TPU v7x, 32 devices: a whole 2x2x4 slice. The times are simulated.
32 devices in a mesh: req: 4 (over x, core), head: 8 (over z, y).
Axes of the slice: x: 2, y: 2, z: 4, core: 2. Of those that a mesh axis runs over, the one named last changes fastest.
Arguments:
- stretch_acts: bfloat16 [8, 256, 2048], P(None, ('req', 'head')), may hold values from -6 to 6
- cache_prefill: bfloat16 [8, 8, 256, 32, 128], P('req', None, 'head'), may hold values from -600 to 600
- stretch_lens: int32 [8], replicated, may hold values from 1 to 256, 1280 in all
- prefix_lens: int32 [8], replicated, may hold values from 1 to 256, 1280 in all
- req_order: int32 [8], replicated, may hold values from 0 to 7, each once
- attn_gain: bfloat16 [2048], replicated, may hold values from 0.25 to 1.75
- in_weight: bfloat16 [2048, 32, 192], P(None, 'head'), may hold values from -0.125 to 0.125
- slopes: float32 [32], P('head'), may hold values from 0.00390625 to 0.5
- out_weight: bfloat16 [32, 64, 2048], P('head'), may hold values from -0.125 to 0.125
- mlp_gain: bfloat16 [2048], replicated, may hold values from 0.25 to 1.75
- up_weight: bfloat16 [2048, 8192], P(None, 'head'), may hold values from -0.125 to 0.125
- down_weight: bfloat16 [8192, 2048], P('head'), may hold values from -0.0625 to 0.0625
Outputs:
- layer_out: bfloat16 [8, 256, 2048], P(None, ('req', 'head'))
- cache_decode: bfloat16 [8, 8, 256, 32, 128], P(None, 'req', None, 'head')
Inputs may be any that keep to these rules, and one draw needn't show every extreme that they name: `stretch_lens`: the entries sum to 1280 and the largest is exactly 256. `prefix_lens`: the entries sum to 1280 and the largest is exactly 256. `req_order`: each request appears once.
All inputs are finite; a program needn't handle non-finite values.
Results may differ from a plain program's by a relative error of at most 0.013.
The roundings to bfloat16 on the way count: a program that leaves them out, or rounds other values in their place, can miss the bound.
Values may be sent and summed in bfloat16 or wider, within the bound.
No kernel may reach another device: no remote copies, remote signals or barrier semaphores. Data moves between devices by JAX's collectives and lax.ppermute only.
A program may use at most 128 MiB of HBM per device.

v0:
```python
import math

import jax
import jax.numpy as jnp
from jax import lax
from jax.sharding import PartitionSpec as P

EPSILON = 1e-05


def layer_norm(values, gain):
    average = jnp.mean(values, axis=-1, keepdims=True)
    centred = values - average
    variance = jnp.mean(centred * centred, axis=-1, keepdims=True)
    return centred * lax.rsqrt(variance + EPSILON) * gain.astype(jnp.float32)


def attend(queries, pairs, prefix_len, slopes, head_dim):
    stretch = queries.shape[0]
    prefix = pairs.shape[0] - stretch
    keys_part = pairs[..., :head_dim]
    values_part = pairs[..., head_dim:]
    scores = jnp.einsum("qhd,khd->hqk", queries, keys_part, preferred_element_type=jnp.float32) * (
        1.0 / math.sqrt(head_dim)
    )
    row_index = jnp.arange(stretch, dtype=jnp.int32)
    key_index = jnp.arange(prefix + stretch, dtype=jnp.int32)
    in_prefix = key_index < prefix
    query_pos = prefix_len + row_index
    key_pos = jnp.where(in_prefix, key_index, prefix_len + key_index - prefix)
    allowed = jnp.where(
        in_prefix[None, :],
        key_index[None, :] < prefix_len,
        (key_index - prefix)[None, :] <= row_index[:, None],
    )
    distance = (query_pos[:, None] - key_pos[None, :]).astype(jnp.float32)
    scores = scores - slopes[:, None, None] * distance[None]
    scores = jnp.where(allowed[None], scores, -jnp.inf)
    highest = jnp.max(scores, axis=-1, keepdims=True)
    expo = jnp.exp(scores - highest)
    soft = (expo / jnp.sum(expo, axis=-1, keepdims=True)).astype(jnp.bfloat16)
    context = jnp.einsum("hqk,khd->qhd", soft, values_part, preferred_element_type=jnp.float32)
    return context.astype(jnp.bfloat16).reshape(stretch, -1)


def local(
    stretch_acts,
    cache_prefill,
    stretch_lens,
    prefix_lens,
    req_order,
    attn_gain,
    in_weight,
    slopes,
    out_weight,
    mlp_gain,
    up_weight,
    down_weight,
):
    req_count = lax.axis_size("req")
    head_count = lax.axis_size("head")
    req_index = lax.axis_index("req")
    head_index = lax.axis_index("head")
    requests = stretch_acts.shape[0]
    stretch_rows = stretch_acts.shape[1]
    features = stretch_acts.shape[2]
    group_size = requests // req_count
    span_rows = head_count * stretch_rows
    stretch_max = req_count * span_rows
    prefix_rows = cache_prefill.shape[2]
    heads_here = in_weight.shape[1]
    pair_width = cache_prefill.shape[4]
    head_dim = pair_width // 2
    members = lax.dynamic_slice_in_dim(req_order, req_index * group_size, group_size)
    member_stretch = jnp.take(stretch_lens, members)
    member_prefix = jnp.take(prefix_lens, members)
    ordered_prefix = jnp.take(prefix_lens, req_order)
    positions = head_index * prefix_rows + jnp.arange(prefix_rows, dtype=jnp.int32)
    keep = positions[None, :] < ordered_prefix[:, None]
    dealt_cache = jnp.where(
        keep[None, :, :, None, None],
        jnp.take(cache_prefill, req_order, axis=1),
        jnp.zeros((), cache_prefill.dtype),
    )
    relaid = lax.all_to_all(
        lax.all_to_all(dealt_cache, "head", split_axis=3, concat_axis=2, tiled=True),
        "req",
        split_axis=1,
        concat_axis=0,
        tiled=True,
    )
    current = relaid[0]
    dealt_acts = jnp.take(stretch_acts, req_order, axis=0)
    dealt_rows = lax.all_to_all(dealt_acts, "req", split_axis=0, concat_axis=1, tiled=True).reshape(
        group_size, req_count, stretch_rows, features
    )
    gathered = lax.all_gather(dealt_rows, "head", axis=2, tiled=True)
    normed = (
        layer_norm(gathered.astype(jnp.float32), attn_gain)
        .astype(jnp.bfloat16)
        .reshape(group_size * stretch_max, features)
    )
    mixed = jnp.dot(
        normed,
        in_weight.reshape(features, heads_here * 3 * head_dim),
        preferred_element_type=jnp.float32,
    )
    mixed = mixed.reshape(group_size, stretch_max, heads_here, 3 * head_dim).astype(jnp.bfloat16)
    contexts = []
    for member in range(group_size):
        pairs = jnp.concatenate([current[member], mixed[member, :, :, head_dim:]], axis=0)
        contexts.append(
            attend(mixed[member, :, :, :head_dim], pairs, member_prefix[member], slopes, head_dim)
        )
    context = jnp.concatenate(contexts, axis=0)
    partial_attn = jnp.dot(
        context,
        out_weight.reshape(heads_here * head_dim, features),
        preferred_element_type=jnp.float32,
    )
    partial_attn = partial_attn.reshape(group_size, req_count, span_rows, features)
    attn_rows = lax.psum_scatter(
        partial_attn.astype(jnp.bfloat16), "head", scatter_dimension=2, tiled=True
    ).astype(jnp.float32)
    residual_rows = dealt_rows.astype(jnp.float32) + attn_rows
    normed_rows = layer_norm(residual_rows, mlp_gain).astype(jnp.bfloat16)
    normed_all = lax.all_gather(normed_rows, "head", axis=2, tiled=True)
    inner = jax.nn.gelu(
        jnp.dot(
            normed_all.reshape(group_size * stretch_max, features),
            up_weight,
            preferred_element_type=jnp.float32,
        ),
        approximate=False,
    ).astype(jnp.bfloat16)
    partial_mlp = jnp.dot(inner, down_weight, preferred_element_type=jnp.float32).reshape(
        group_size, req_count, span_rows, features
    )
    mlp_rows = lax.psum_scatter(
        partial_mlp.astype(jnp.bfloat16), "head", scatter_dimension=2, tiled=True
    ).astype(jnp.float32)
    row_number = (
        jnp.arange(req_count, dtype=jnp.int32)[:, None] * head_count + head_index
    ) * stretch_rows + jnp.arange(stretch_rows, dtype=jnp.int32)[None, :]
    usable = row_number[None] < member_stretch[:, None, None]
    result = jnp.where(
        usable[..., None], residual_rows + mlp_rows, jnp.zeros((), jnp.float32)
    ).astype(jnp.bfloat16)
    returned = lax.all_to_all(result, "req", split_axis=1, concat_axis=0, tiled=True).reshape(
        requests, stretch_rows, features
    )
    inverse = jnp.argsort(req_order)
    layer_out = jnp.take(returned, inverse, axis=0)
    return (layer_out, relaid)


def solution(mesh):
    return jax.shard_map(
        local,
        mesh=mesh,
        in_specs=(
            P(None, ("req", "head"), None),
            P("req", None, "head", None, None),
            P(),
            P(),
            P(),
            P(),
            P(None, "head", None),
            P("head"),
            P("head", None, None),
            P(),
            P(None, "head"),
            P("head", None),
        ),
        out_specs=(P(None, ("req", "head"), None), P(None, "req", None, "head", None)),
        check_vma=False,
    )
```

profile of v0, /device:TPU:1, one launch (start us, length us, event | category | flops | bytes accessed | tf_op | source)
XLA Modules:
  0.0 463.2 jit_solution(14605150824195133511)
XLA Ops:
  7.2 0.8 compare_select_fusion.1
  8.0 1.4 gather_fusion
  10.1 1.5 gather_fusion.3
  11.6 0.8 broadcast_select_fusion.1
  12.4 4.3 all-to-all-start
  16.7 5.3 %gather_fusion.1 = bf16[8,2,32,32,128]{4,3,2,1,0:T(8,128)(2,1)} fusion(bf16[2,8,32,32,128]{4,3,2,1,0:T(8,128)(2,1)} %param.17, s32[1024]{0:T(1024)S(1)} %pad_clamp_fusion.1), kind=kCustom, calls=%fused_computation.5 | custom fusion | bytes 8388640 | tf_op jit(solution)/shard_map/jit(_take)/gather | solution.py:82
  22.0 2.6 select_bitcast_fusion
  24.6 3.6 copy.44
  29.0 6.2 %all-to-all-start.1 = ((bf16[2,8,32,32,128]{4,2,0,1,3:T(8,128)(2,1)}), bf16[2,8,32,32,128]{4,2,0,1,3:T(8,128)(2,1)}, u32[]{:S(2)}, u32[]{:S(2)}) async-start(bf16[2,8,32,32,128]{4,2,0,1,3:T(8,128)(2,1)} %copy.44), calls=%async_computation.1 | async-start | bytes 8388608 | tf_op jit(solution)/shard_map/all_to_all | solution.py:86
  38.6 1.3 iota_compare_fusion.1
  41.2 112.4 %all-to-all-done.1 = bf16[2,8,32,32,128]{4,2,0,1,3:T(8,128)(2,1)} async-done(((bf16[2,8,32,32,128]{4,2,0,1,3:T(8,128)(2,1)}), bf16[2,8,32,32,128]{4,2,0,1,3:T(8,128)(2,1)}, u32[]{:S(2)}, u32[]{:S(2)}) %all-to-all-start.1) | async-done | bytes 4194336 | tf_op jit(solution)/shard_map/all_to_all | solution.py:86
  153.5 3.5 copy.46
  157.0 2.3 copy.47
  159.3 5.9 %all-to-all-start.2 = ((bf16[2,8,256,4,128]{4,2,3,0,1:T(8,128)(2,1)}), bf16[2,8,256,4,128]{4,2,3,0,1:T(8,128)(2,1)}, u32[]{:S(2)}, u32[]{:S(2)}) async-start(bf16[2,8,256,4,128]{4,2,3,0,1:T(8,128)(2,1)} %copy.47), calls=%async_computation.2 | async-start | bytes 8388608 | tf_op jit(solution)/shard_map/all_to_all | solution.py:85
  165.9 0.8 fusion.54
  166.7 1.0 subtract_convert_fusion.1
  167.6 0.9 subtract_convert_fusion
  168.6 2.1 convert_reduce_fusion
  171.5 0.7 fusion.6
  172.4 1.8 fusion.19
  174.2 0.9 copy-done.11
  175.1 37.5 %all-to-all-done.2 = bf16[2,8,256,4,128]{4,2,3,0,1:T(8,128)(2,1)} async-done(((bf16[2,8,256,4,128]{4,2,3,0,1:T(8,128)(2,1)}), bf16[2,8,256,4,128]{4,2,3,0,1:T(8,128)(2,1)}, u32[]{:S(2)}, u32[]{:S(2)}) %all-to-all-start.2) | async-done | bytes 4194336 | tf_op jit(solution)/shard_map/all_to_all | solution.py:85
  212.7 7.4 %copy.49 = bf16[4,2,2,256,4,128]{3,5,4,2,1,0:T(8,128)(2,1)} copy(bf16[4,2,2,256,4,128]{5,3,4,1,2,0:T(8,128)(2,1)} %bitcast.9) | data formatting | bytes 8388608 | tf_op jit(solution)/shard_map/all_to_all | solution.py:85
  220.1 1.1 slice_bitcast_fusion.3
  221.2 1.1 fusion.120
  222.2 1.9 convolution_convert_fusion.3
  224.1 1.1 fusion.119
  225.2 1.2 convolution_convert_fusion.2
  226.6 0.7 convolution_convert_fusion.1
  227.4 2.9 copy.74
  230.3 4.5 reshape.419
  235.5 63.5 %reduce-scatter.7.cloned.1.call-done = bf16[8,16384]{1,0:T(8,128)(2,1)} async-done(((bf16[64,16384]{1,0:T(8,128)(2,1)}), bf16[8,16384]{1,0:T(8,128)(2,1)}) %reduce-scatter.7.cloned.1.call-update) | async-done | bytes 262160
  299.0 1.1 reshape.420
  300.8 0.9 multiply_convert_fusion
  301.8 49.1 %all-gather.5.cloned.1.call-done = bf16[2,4,64,2048]{3,2,0,1:T(8,128)(2,1)} async-done(((bf16[2,4,8,2048]{3,2,0,1:T(8,128)(2,1)}), bf16[2,4,64,2048]{3,2,0,1:T(8,128)(2,1)}) %all-gather.5.cloned.1.call-update) | async-done | bytes 2097168 | tf_op jit(solution)/shard_map/all_gather | solution.py:127
  350.9 1.8 copy.53
  352.7 13.7 %convolution_convert_fusion = bf16[512,2048]{1,0:T(8,128)(2,1)} fusion(bf16[1024,2048]{1,0:T(8,128)(2,1)} %param.27, bf16[512,2048]{1,0:T(8,128)(2,1)S(1)} %bitcast.113, bf16[2048,1024]{1,0:T(8,128)(2,1)} %param.26), kind=kOutput, calls=%fused_computation.19 | convolution fusion | flops 4330094592 | bytes 12582912 | tf_op jit(solution)/shard_map/dot_general | solution.py:136
  366.4 3.2 copy.73
  369.6 2.8 reshape.421
  372.4 1.0 sort.17
  373.6 64.4 %reduce-scatter.9.cloned.1.call-done = bf16[8,16384]{1,0:T(8,128)(2,1)} async-done(((bf16[64,16384]{1,0:T(8,128)(2,1)}), bf16[8,16384]{1,0:T(8,128)(2,1)}) %reduce-scatter.9.cloned.1.call-update) | async-done | bytes 262160
  438.0 1.1 reshape.422
  439.1 1.0 select_convert_fusion
  440.2 5.9 %all-to-all-start.3 = ((bf16[2,4,8,2048]{3,2,0,1:T(8,128)(2,1)}), bf16[2,4,8,2048]{3,2,0,1:T(8,128)(2,1)S(1)}, u32[]{:S(2)}, u32[]{:S(2)}) async-start(bf16[2,4,8,2048]{3,2,0,1:T(8,128)(2,1)} %select_convert_fusion), calls=%async_computation.3 | async-start | bytes 524288 | tf_op jit(solution)/shard_map/all_to_all | solution.py:149
  446.1 7.6 %copy.55 = bf16[8,2,256,4,128]{4,3,2,1,0:T(4,128)(2,1)} copy(bf16[8,2,256,4,128]{2,4,3,1,0:T(8,128)(2,1)} %bitcast.101) | data formatting | bytes 8388608
  453.6 0.7 copy-done.7
  454.4 1.5 gather_fusion.5
  455.9 0.8 broadcast_select_fusion
  (83 shorter events, 9.6 us)
Async XLA Ops:
  7.2 165.2 %copy-start = (bf16[2048,4,192]{0,2,1:T(8,128)(2,1)S(1)}, bf16[2048,4,192]{0,2,1:T(8,128)(2,1)}, u32[]{:S(2)}) copy-start(bf16[2048,4,192]{0,2,1:T(8,128)(2,1)} %param.22) | copy-start | bytes 9437188
  12.4 15.8 %all-to-all-start = ((bf16[8,8,2048]{2,1,0:T(8,128)(2,1)}), bf16[8,8,2048]{2,1,0:T(8,128)(2,1)S(1)}, u32[]{:S(2)}, u32[]{:S(2)}) async-start(bf16[8,8,2048]{2,1,0:T(8,128)(2,1)} %broadcast_select_fusion.1), calls=%async_computation | async-start | bytes 524288 | tf_op jit(solution)/shard_map/all_to_all | solution.py:94
  28.2 7.6 %copy-start.17 = (s32[8]{0:T(128)S(1)}, s32[8]{0:T(128)}, u32[]{:S(2)}) copy-start(s32[8]{0:T(128)} %param.20) | copy-start | bytes 100
  28.2 7.7 %copy-start.2 = (s32[8]{0:T(128)S(1)}, s32[8]{0:T(128)}, u32[]{:S(2)}) copy-start(s32[8]{0:T(128)} %param.19) | copy-start | bytes 100
  28.2 8.4 %copy-start.3 = (s32[8]{0:T(128)S(1)}, s32[8]{0:T(128)}, u32[]{:S(2)}) copy-start(s32[8]{0:T(128)} %param.18) | copy-start | bytes 100
  28.2 9.0 %copy-start.15 = (bf16[2048]{0:T(1024)(128)(2,1)S(1)}, bf16[2048]{0:T(1024)(128)(2,1)}, u32[]{:S(2)}) copy-start(bf16[2048]{0:T(1024)(128)(2,1)} %param.21) | copy-start | bytes 12292
  28.3 0.7 copy-start.5
  29.0 124.6 %all-to-all-start.1 = ((bf16[2,8,32,32,128]{4,2,0,1,3:T(8,128)(2,1)}), bf16[2,8,32,32,128]{4,2,0,1,3:T(8,128)(2,1)}, u32[]{:S(2)}, u32[]{:S(2)}) async-start(bf16[2,8,32,32,128]{4,2,0,1,3:T(8,128)(2,1)} %copy.44), calls=%async_computation.1 | async-start | bytes 8388608 | tf_op jit(solution)/shard_map/all_to_all | solution.py:86
  35.1 133.5 %all-gather.3.cloned.1.call-start = ((), (), s32[]{:S(2)}) async-start(), calls=%async_computation.6 | async-start | bytes 2359296 | tf_op jit(solution)/shard_map/all_gather | solution.py:97
  159.3 53.4 %all-to-all-start.2 = ((bf16[2,8,256,4,128]{4,2,3,0,1:T(8,128)(2,1)}), bf16[2,8,256,4,128]{4,2,3,0,1:T(8,128)(2,1)}, u32[]{:S(2)}, u32[]{:S(2)}) async-start(bf16[2,8,256,4,128]{4,2,3,0,1:T(8,128)(2,1)} %copy.47), calls=%async_computation.2 | async-start | bytes 8388608 | tf_op jit(solution)/shard_map/all_to_all | solution.py:85
  165.3 133.7 %reduce-scatter.7.cloned.1.call-start = ((), (), s32[]{:S(2)}) async-start(), calls=%async_computation.8 | async-start | bytes 2359296
  168.6 2.2 copy-start.4
  174.2 0.9 copy-start.11
  212.7 8.5 %copy-start.10 = (f32[256,512]{1,0:T(8,128)S(1)}, f32[256,512]{1,0:T(8,128)}, u32[]{:S(2)}) copy-start(f32[256,512]{1,0:T(8,128)} %subtract_convert_fusion.1) | copy-start | bytes 1572868
  212.7 8.5 %copy-start.12 = (bf16[2,256,4,192]{1,3,2,0:T(8,128)(2,1)S(1)}, bf16[2,256,4,192]{1,3,2,0:T(8,128)(2,1)}, u32[]{:S(2)}) copy-start(bf16[2,256,4,192]{1,3,2,0:T(8,128)(2,1)} %copy-done.11) | copy-start | bytes 2359300
  212.7 8.5 %copy-start.13 = (pred[256,512]{1,0:T(8,128)(4,1)S(1)}, pred[256,512]{1,0:T(8,128)(4,1)}, u32[]{:S(2)}) copy-start(pred[256,512]{1,0:T(8,128)(4,1)} %get-tuple-element.24) | copy-start | bytes 393220
  212.7 8.5 %copy-start.18 = (f32[4]{0:T(128)S(1)}, f32[4]{0:T(128)}, u32[]{:S(2)}) copy-start(f32[4]{0:T(128)} %param.23) | copy-start | bytes 52
  222.2 1.9 copy-start.9
  225.2 1.3 copy-start.14
  225.2 1.4 copy-start.8
  234.8 0.7 copy-start.16
  234.8 65.4 %copy-start.6 = (bf16[8,8,2048]{2,1,0:T(8,128)(2,1)S(1)}, bf16[8,8,2048]{2,1,0:T(8,128)(2,1)}, u32[]{:S(2)}) copy-start(bf16[8,8,2048]{2,1,0:T(8,128)(2,1)} %copy-done.5) | copy-start | bytes 786436
  234.8 116.1 %all-gather.5.cloned.1.call-start = ((), (), s32[]{:S(2)}) async-start(), calls=%async_computation.7 | async-start | bytes 2359296 | tf_op jit(solution)/shard_map/all_gather | solution.py:127
  301.7 136.3 %reduce-scatter.9.cloned.1.call-start = ((), (), s32[]{:S(2)}) async-start(), calls=%async_computation.9 | async-start | bytes 2359296
  440.2 13.5 %all-to-all-start.3 = ((bf16[2,4,8,2048]{3,2,0,1:T(8,128)(2,1)}), bf16[2,4,8,2048]{3,2,0,1:T(8,128)(2,1)S(1)}, u32[]{:S(2)}, u32[]{:S(2)}) async-start(bf16[2,4,8,2048]{3,2,0,1:T(8,128)(2,1)} %select_convert_fusion), calls=%async_computation.3 | async-start | bytes 524288 | tf_op jit(solution)/shard_map/all_to_all | solution.py:149
  446.1 10.6 %copy-start.1 = (bf16[2048,4,192]{0,2,1:T(8,128)(2,1)S(1)}, bf16[2048,4,192]{0,2,1:T(8,128)(2,1)}, u32[]{:S(2)}) copy-start(bf16[2048,4,192]{0,2,1:T(8,128)(2,1)} %param.22) | copy-start | bytes 9437188
  453.6 0.7 copy-start.7
Sparse Core Ops, SparseCore 0:
  38.7 103.0 all-gather.2
  234.9 64.0 reduce-scatter.6
  301.9 49.0 all-gather.4
  372.6 65.4 reduce-scatter.8
where the time goes:
time: 464 us; the launch traced here: 463 us
  waiting for transfers between devices  328 us (71%)
  local copies, waits for them, and re-layouts  57.7 us (12%)
  starting transfers between devices  22.6 us (5%)
  matrix products  21.5 us (5%)
  other arithmetic  19.6 us (4%)
  between operations  14.1 us (3%)
    unnamed x6, waiting for transfers between devices  129 us
    all_to_all x1, waiting for transfers between devices, local(): lax.all_to_all(dealt_cache, 'head', split_axis=3, concat_axis=2, tiled=True)  112 us
    all_gather x1, waiting for transfers between devices, local(): normed_all = lax.all_gather(normed_rows, 'head', axis=2, tiled=True)  49.1 us
    all_to_all x1, waiting for transfers between devices, local(): lax.all_to_all(lax.all_to_all(dealt_cache, 'head', split_axis=3, concat_a...  37.5 us
    unnamed x45, local copies, waits for them, and re-layouts  26.1 us
    dot_general x1, matrix products, local(): jnp.dot(inner, down_weight, preferred_element_type=jnp.float32)  13.7 us
  transfers between devices with their start and end apart: 8, of which 5 were waited for; matrix products, arithmetic and copies ran while one was open for 9% of the time, Pallas kernels for 0%

commit v1 on v0

--- a/solution.py
+++ b/solution.py
@@ -77,19 +77,25 @@
     ordered_prefix = jnp.take(prefix_lens, req_order)
     positions = head_index * prefix_rows + jnp.arange(prefix_rows, dtype=jnp.int32)
     keep = positions[None, :] < ordered_prefix[:, None]
-    dealt_cache = jnp.where(
-        keep[None, :, :, None, None],
-        jnp.take(cache_prefill, req_order, axis=1),
-        jnp.zeros((), cache_prefill.dtype),
-    )
-    relaid = lax.all_to_all(
-        lax.all_to_all(dealt_cache, "head", split_axis=3, concat_axis=2, tiled=True),
-        "req",
-        split_axis=1,
-        concat_axis=0,
-        tiled=True,
-    )
-    current = relaid[0]
+    local_layers = cache_prefill.shape[0]
+    halves = []
+    for layer in range(local_layers):
+        dealt_cache = jnp.where(
+            keep[None, :, :, None, None],
+            jnp.take(cache_prefill[layer : layer + 1], req_order, axis=1),
+            jnp.zeros((), cache_prefill.dtype),
+        )
+        halves.append(
+            lax.all_to_all(
+                lax.all_to_all(dealt_cache, "head", split_axis=3, concat_axis=2, tiled=True),
+                "req",
+                split_axis=1,
+                concat_axis=0,
+                tiled=True,
+            )
+        )
+    current = halves[0][0]
+    relaid = jnp.stack(halves, axis=1).reshape((req_count * local_layers,) + halves[0].shape[1:])
     dealt_acts = jnp.take(stretch_acts, req_order, axis=0)
     dealt_rows = lax.all_to_all(dealt_acts, "req", split_axis=0, concat_axis=1, tiled=True).reshape(
         group_size, req_count, stretch_rows, features

time: 464 us -> 429 us (0.925)
  waiting for transfers between devices: 328 us -> 269 us
  starting transfers between devices: 22.6 us -> 32.8 us
  local copies, waits for them, and re-layouts: 57.7 us -> 63.7 us
    all_to_all x1 -> x2, waiting for transfers between devices: 112 us -> 54.1 us  [local(): lax.all_to_all(dealt_cache, 'head', split_axis=3, concat_axis=2, tiled=True)]
    all_gather x1, waiting for transfers between devices: 49.1 us -> 75.1 us  [local(): normed_all = lax.all_gather(normed_rows, 'head', axis=2, tiled=True)]
    all_to_all x1 -> x2, waiting for transfers between devices: 37.5 us -> 17.7 us  [local(): lax.all_to_all(lax.all_to_all(dealt_cache, 'head', split_axis=3, concat_a...]
    another operation x0 -> x2, local copies, waits for them, and re-layouts: none -> 10.7 us  [the longest x1 5.49 us: local(): jnp.stack(halves, axis=1)]
    unnamed x6, waiting for transfers between devices: 129 us -> 122 us
    all_to_all x1 -> x2, starting transfers between devices: 5.95 us -> 12.3 us  [local(): lax.all_to_all(lax.all_to_all(dealt_cache, 'head', split_axis=3, concat_a...]
    unnamed x45 -> x44, local copies, waits for them, and re-layouts: 26.1 us -> 21.7 us
    all_to_all x1 -> x2, starting transfers between devices: 6.17 us -> 9.92 us  [local(): lax.all_to_all(dealt_cache, 'head', split_axis=3, concat_axis=2, tiled=True)]
  transfers between devices with their start and end apart: 8 -> 10, of which waited for: 5 -> 5; matrix products, arithmetic and copies ran while one was open for 9% -> 18% of each run, Pallas kernels for 0% -> 0%
where the time goes in v1:
time: 429 us; the launch traced here: 428 us
  waiting for transfers between devices  269 us (63%)
  local copies, waits for them, and re-layouts  63.7 us (15%)
  starting transfers between devices  32.8 us (8%)
  matrix products  25.6 us (6%)
  other arithmetic  22.4 us (5%)
  between operations  14.1 us (3%)
    unnamed x6, waiting for transfers between devices  122 us
    all_gather x1, waiting for transfers between devices, local(): normed_all = lax.all_gather(normed_rows, 'head', axis=2, tiled=True)  75.1 us
    all_to_all x2, waiting for transfers between devices, local(): lax.all_to_all(dealt_cache, 'head', split_axis=3, concat_axis=2, tiled=True)  54.1 us
    unnamed x44, local copies, waits for them, and re-layouts  21.7 us
    all_to_all x2, waiting for transfers between devices, local(): lax.all_to_all(lax.all_to_all(dealt_cache, 'head', split_axis=3, concat_a...  17.7 us
    dot_general x1, matrix products, local(): jnp.dot(inner, down_weight, preferred_element_type=jnp.float32)  14.3 us
    all_to_all x2, starting transfers between devices, local(): lax.all_to_all(lax.all_to_all(dealt_cache, 'head', split_axis=3, concat_a...  12.3 us
    all_to_all x2, starting transfers between devices, local(): lax.all_to_all(dealt_cache, 'head', split_axis=3, concat_axis=2, tiled=True)  9.92 us
  transfers between devices with their start and end apart: 10, of which 5 were waited for; matrix products, arithmetic and copies ran while one was open for 18% of the time, Pallas kernels for 0%

profile of v1, /device:TPU:1, one launch (start us, length us, event | category | flops | bytes accessed | tf_op | source)
XLA Modules:
  0.0 427.7 jit_solution(1506799252785771041)
XLA Ops:
  7.2 0.8 compare_select_fusion.1
  8.0 1.4 gather_fusion
  10.1 1.5 gather_fusion.2
  12.4 4.3 all-to-all-start
  16.7 5.2 %slice_bitcast_fusion = (bf16[8,32,32,128]{3,2,1,0:T(8,128)(2,1)}, bf16[8,32,32,128]{3,2,1,0:T(8,128)(2,1)}) fusion(bf16[2,8,32,32,128]{4,3,2,1,0:T(8,128)(2,1)} %param.19), kind=kLoop, calls=%fused_computation.31 | loop fusion | bytes 8388608 | tf_op jit(solution)/shard_map/jit(_take)/Arg_0.9 | solution.py:85
  21.9 3.7 gather_fusion.6
  25.6 3.7 gather_fusion.3
  29.4 3.5 fusion.12
  32.8 2.1 copy.51
  35.7 6.2 %all-to-all-start.1 = ((bf16[1,8,32,32,128]{4,2,1,0,3:T(8,128)(2,1)}), bf16[1,8,32,32,128]{4,2,1,0,3:T(8,128)(2,1)}, u32[]{:S(2)}, u32[]{:S(2)}) async-start(bf16[1,8,32,32,128]{4,2,1,0,3:T(8,128)(2,1)} %copy.51), calls=%async_computation.1 | async-start | bytes 4194304 | tf_op jit(solution)/shard_map/all_to_all | solution.py:90
  45.3 1.3 iota_compare_fusion.1
  49.3 0.9 subtract_convert_fusion.1
  50.2 0.9 subtract_convert_fusion
  51.1 54.1 %all-to-all-done.1 = bf16[1,8,32,32,128]{4,2,1,0,3:T(8,128)(2,1)} async-done(((bf16[1,8,32,32,128]{4,2,1,0,3:T(8,128)(2,1)}), bf16[1,8,32,32,128]{4,2,1,0,3:T(8,128)(2,1)}, u32[]{:S(2)}, u32[]{:S(2)}) %all-to-all-start.1) | async-done | bytes 2097184 | tf_op jit(solution)/shard_map/all_to_all | solution.py:90
  105.3 2.0 copy.52
  107.3 1.9 copy.53
  109.2 8.0 %all-to-all-start.2 = ((bf16[1,8,256,4,128]{4,2,3,0,1:T(8,128)(2,1)}), bf16[1,8,256,4,128]{4,2,3,0,1:T(8,128)(2,1)}, u32[]{:S(2)}, u32[]{:S(2)}) async-start(bf16[1,8,256,4,128]{4,2,3,0,1:T(8,128)(2,1)} %bitcast.121), calls=%async_computation.2 | async-start | bytes 4194304 | tf_op jit(solution)/shard_map/all_to_all | solution.py:89
  117.3 2.1 convert_reduce_fusion
  121.0 1.8 fusion.21
  122.9 0.9 copy-done.12
  123.8 17.7 %all-to-all-done.2 = bf16[1,8,256,4,128]{4,2,3,0,1:T(8,128)(2,1)} async-done(((bf16[1,8,256,4,128]{4,2,3,0,1:T(8,128)(2,1)}), bf16[1,8,256,4,128]{4,2,3,0,1:T(8,128)(2,1)}, u32[]{:S(2)}, u32[]{:S(2)}) %all-to-all-start.2) | async-done | bytes 2097184 | tf_op jit(solution)/shard_map/all_to_all | solution.py:89
  141.6 2.9 copy.55
  145.2 2.2 fusion.122
  147.4 2.3 convolution_convert_fusion.3
  149.7 2.0 fusion.121
  151.7 2.4 convolution_convert_fusion.2
  154.9 2.9 copy.82
  157.9 4.5 %reshape.468 = bf16[64,16384]{1,0:T(8,128)(2,1)} reshape(bf16[64,2,4,2048]{3,2,1,0:T(4,128)(2,1)} %bitcast.123) | data formatting | bytes 4194304
  163.0 65.3 %reduce-scatter.7.cloned.1.call-done = bf16[8,16384]{1,0:T(8,128)(2,1)} async-done(((bf16[64,16384]{1,0:T(8,128)(2,1)}), bf16[8,16384]{1,0:T(8,128)(2,1)}) %reduce-scatter.7.cloned.1.call-update) | async-done | bytes 262160
  228.3 1.1 reshape.469
  230.2 0.9 multiply_convert_fusion
  231.1 2.1 copy.61
  233.2 3.7 all-to-all-start.4
  237.2 75.1 %all-gather.5.cloned.1.call-done = bf16[2,4,64,2048]{3,2,0,1:T(8,128)(2,1)} async-done(((bf16[2,4,8,2048]{3,2,0,1:T(8,128)(2,1)}), bf16[2,4,64,2048]{3,2,0,1:T(8,128)(2,1)}) %all-gather.5.cloned.1.call-update) | async-done | bytes 2097168 | tf_op jit(solution)/shard_map/all_gather | solution.py:133
  312.3 3.2 copy.59
  315.5 14.3 %convolution_convert_fusion = bf16[512,2048]{1,0:T(8,128)(2,1)} fusion(bf16[1024,2048]{1,0:T(8,128)(2,1)} %param.29, bf16[512,2048]{1,0:T(8,128)(2,1)} %bitcast.134, bf16[2048,1024]{1,0:T(8,128)(2,1)} %param.28), kind=kOutput, calls=%fused_computation.20 | convolution fusion | flops 4330094592 | bytes 12582912 | tf_op jit(solution)/shard_map/dot_general | solution.py:142
  329.7 4.5 %copy.81 = bf16[2,4,64,2048]{3,1,0,2:T(4,128)(2,1)} copy(bf16[2,4,64,2048]{3,2,1,0:T(8,128)(2,1)} %bitcast.135) | data formatting | bytes 4194304
  334.3 4.5 %reshape.470 = bf16[64,16384]{1,0:T(8,128)(2,1)} reshape(bf16[64,2,4,2048]{3,2,1,0:T(4,128)(2,1)} %bitcast.124) | data formatting | bytes 4194304
  338.8 1.0 sort.17
  340.2 1.9 copy.63
  342.1 4.3 %all-to-all-start.5 = ((bf16[1,8,256,4,128]{4,2,3,0,1:T(8,128)(2,1)}), bf16[1,8,256,4,128]{4,2,3,0,1:T(8,128)(2,1)S(1)}, u32[]{:S(2)}, u32[]{:S(2)}) async-start(bf16[1,8,256,4,128]{4,2,3,0,1:T(8,128)(2,1)} %bitcast.44), calls=%async_computation.5 | async-start | bytes 4194304 | tf_op jit(solution)/shard_map/all_to_all | solution.py:89
  346.5 56.0 %reduce-scatter.9.cloned.1.call-done = bf16[8,16384]{1,0:T(8,128)(2,1)} async-done(((bf16[64,16384]{1,0:T(8,128)(2,1)}), bf16[8,16384]{1,0:T(8,128)(2,1)}) %reduce-scatter.9.cloned.1.call-update) | async-done | bytes 262160
  402.6 1.1 reshape.471
  403.7 1.0 select_convert_fusion
  404.7 5.9 %all-to-all-start.3 = ((bf16[2,4,8,2048]{3,2,0,1:T(8,128)(2,1)}), bf16[2,4,8,2048]{3,2,0,1:T(8,128)(2,1)S(1)}, u32[]{:S(2)}, u32[]{:S(2)}) async-start(bf16[2,4,8,2048]{3,2,0,1:T(8,128)(2,1)} %select_convert_fusion), calls=%async_computation.3 | async-start | bytes 524288 | tf_op jit(solution)/shard_map/all_to_all | solution.py:155
  410.6 2.0 pad_maximum_fusion
  412.6 5.5 %copy.65 = bf16[4,2,2,256,4,128]{5,4,3,2,1,0:T(4,128)(2,1)} copy(bf16[4,2,2,256,4,128]{5,3,4,2,0,1:T(8,128)(2,1)S(1)} %pad_maximum_fusion) | data formatting | bytes 8388608 | tf_op jit(solution)/shard_map/stack | solution.py:98
  418.8 1.5 gather_fusion.5
  (93 shorter events, 15.5 us)
Async XLA Ops:
  7.2 113.9 %copy-start = (bf16[2048,4,192]{0,2,1:T(8,128)(2,1)S(1)}, bf16[2048,4,192]{0,2,1:T(8,128)(2,1)}, u32[]{:S(2)}) copy-start(bf16[2048,4,192]{0,2,1:T(8,128)(2,1)} %param.24) | copy-start | bytes 9437188
  12.4 22.6 %all-to-all-start = ((bf16[8,8,2048]{2,1,0:T(8,128)(2,1)}), bf16[8,8,2048]{2,1,0:T(8,128)(2,1)S(1)}, u32[]{:S(2)}, u32[]{:S(2)}) async-start(bf16[8,8,2048]{2,1,0:T(8,128)(2,1)} %broadcast_select_fusion.1), calls=%async_computation | async-start | bytes 524288 | tf_op jit(solution)/shard_map/all_to_all | solution.py:100
  35.0 7.6 %copy-start.17 = (s32[8]{0:T(128)S(1)}, s32[8]{0:T(128)}, u32[]{:S(2)}) copy-start(s32[8]{0:T(128)} %param.22) | copy-start | bytes 100
  35.0 7.7 %copy-start.2 = (s32[8]{0:T(128)S(1)}, s32[8]{0:T(128)}, u32[]{:S(2)}) copy-start(s32[8]{0:T(128)} %param.21) | copy-start | bytes 100
  35.0 8.4 %copy-start.3 = (s32[8]{0:T(128)S(1)}, s32[8]{0:T(128)}, u32[]{:S(2)}) copy-start(s32[8]{0:T(128)} %param.20) | copy-start | bytes 100
  35.0 9.0 %copy-start.15 = (bf16[2048]{0:T(1024)(128)(2,1)S(1)}, bf16[2048]{0:T(1024)(128)(2,1)}, u32[]{:S(2)}) copy-start(bf16[2048]{0:T(1024)(128)(2,1)} %param.23) | copy-start | bytes 12292
  35.0 0.7 copy-start.5
  35.7 69.6 %all-to-all-start.1 = ((bf16[1,8,32,32,128]{4,2,1,0,3:T(8,128)(2,1)}), bf16[1,8,32,32,128]{4,2,1,0,3:T(8,128)(2,1)}, u32[]{:S(2)}, u32[]{:S(2)}) async-start(bf16[1,8,32,32,128]{4,2,1,0,3:T(8,128)(2,1)} %copy.51), calls=%async_computation.1 | async-start | bytes 4194304 | tf_op jit(solution)/shard_map/all_to_all | solution.py:90
  41.9 75.4 %all-gather.3.cloned.1.call-start = ((), (), s32[]{:S(2)}) async-start(), calls=%async_computation.8 | async-start | bytes 2359296 | tf_op jit(solution)/shard_map/all_gather | solution.py:103
  109.2 32.4 %all-to-all-start.2 = ((bf16[1,8,256,4,128]{4,2,3,0,1:T(8,128)(2,1)}), bf16[1,8,256,4,128]{4,2,3,0,1:T(8,128)(2,1)}, u32[]{:S(2)}, u32[]{:S(2)}) async-start(bf16[1,8,256,4,128]{4,2,3,0,1:T(8,128)(2,1)} %bitcast.121), calls=%async_computation.2 | async-start | bytes 4194304 | tf_op jit(solution)/shard_map/all_to_all | solution.py:89
  117.2 111.1 %reduce-scatter.7.cloned.1.call-start = ((), (), s32[]{:S(2)}) async-start(), calls=%async_computation.10 | async-start | bytes 2359296
  117.3 2.2 copy-start.4
  122.9 0.9 copy-start.12
  123.8 21.4 %copy-start.11 = (f32[256,512]{1,0:T(8,128)S(1)}, f32[256,512]{1,0:T(8,128)}, u32[]{:S(2)}) copy-start(f32[256,512]{1,0:T(8,128)} %subtract_convert_fusion.1) | copy-start | bytes 1572868
  123.8 21.4 %copy-start.18 = (f32[4]{0:T(128)S(1)}, f32[4]{0:T(128)}, u32[]{:S(2)}) copy-start(f32[4]{0:T(128)} %param.25) | copy-start | bytes 52
  145.2 4.5 %copy-start.13 = (bf16[256,4,128]{0,2,1:T(8,128)(2,1)}, bf16[256,4,128]{0,2,1:T(8,128)(2,1)S(1)}, u32[]{:S(2)}) copy-start(bf16[256,4,128]{0,2,1:T(8,128)(2,1)S(1)} %get-tuple-element.12) | copy-start | bytes 786436
  145.2 2.2 copy-start.14
  147.4 2.3 copy-start.10
  151.7 2.5 copy-start.9
  162.3 0.7 copy-start.16
  162.3 67.1 %copy-start.6 = (bf16[8,8,2048]{2,1,0:T(8,128)(2,1)S(1)}, bf16[8,8,2048]{2,1,0:T(8,128)(2,1)}, u32[]{:S(2)}) copy-start(bf16[8,8,2048]{2,1,0:T(8,128)(2,1)} %copy-done.5) | copy-start | bytes 786436
  162.3 68.7 %copy-start.7 = (bf16[1,8,32,32,128]{4,3,2,1,0:T(8,128)(2,1)S(1)}, bf16[1,8,32,32,128]{4,3,2,1,0:T(8,128)(2,1)}, u32[]{:S(2)}) copy-start(bf16[1,8,32,32,128]{4,3,2,1,0:T(8,128)(2,1)} %get-tuple-element.17) | copy-start | bytes 6291460
  162.4 149.9 %all-gather.5.cloned.1.call-start = ((), (), s32[]{:S(2)}) async-start(), calls=%async_computation.9 | async-start | bytes 2359296 | tf_op jit(solution)/shard_map/all_gather | solution.py:133
  233.2 106.5 %all-to-all-start.4 = ((bf16[1,8,32,32,128]{4,2,1,0,3:T(8,128)(2,1)}), bf16[1,8,32,32,128]{4,2,1,0,3:T(8,128)(2,1)S(1)}, u32[]{:S(2)}, u32[]{:S(2)}) async-start(bf16[1,8,32,32,128]{4,2,1,0,3:T(8,128)(2,1)} %copy.61), calls=%async_computation.4 | async-start | bytes 4194304 | tf_op jit(solution)/shard_map/all_to_all | solution.py:90
  237.0 165.6 %reduce-scatter.9.cloned.1.call-start = ((), (), s32[]{:S(2)}) async-start(), calls=%async_computation.11 | async-start | bytes 2359296
  342.1 62.7 %all-to-all-start.5 = ((bf16[1,8,256,4,128]{4,2,3,0,1:T(8,128)(2,1)}), bf16[1,8,256,4,128]{4,2,3,0,1:T(8,128)(2,1)S(1)}, u32[]{:S(2)}, u32[]{:S(2)}) async-start(bf16[1,8,256,4,128]{4,2,3,0,1:T(8,128)(2,1)} %bitcast.44), calls=%async_computation.5 | async-start | bytes 4194304 | tf_op jit(solution)/shard_map/all_to_all | solution.py:89
  404.7 13.4 %all-to-all-start.3 = ((bf16[2,4,8,2048]{3,2,0,1:T(8,128)(2,1)}), bf16[2,4,8,2048]{3,2,0,1:T(8,128)(2,1)S(1)}, u32[]{:S(2)}, u32[]{:S(2)}) async-start(bf16[2,4,8,2048]{3,2,0,1:T(8,128)(2,1)} %select_convert_fusion), calls=%async_computation.3 | async-start | bytes 524288 | tf_op jit(solution)/shard_map/all_to_all | solution.py:155
  412.6 8.5 %copy-start.1 = (bf16[2048,4,192]{0,2,1:T(8,128)(2,1)S(1)}, bf16[2048,4,192]{0,2,1:T(8,128)(2,1)}, u32[]{:S(2)}) copy-start(bf16[2048,4,192]{0,2,1:T(8,128)(2,1)} %param.24) | copy-start | bytes 9437188
  418.1 0.7 copy-start.8
Sparse Core Ops, SparseCore 0:
  45.4 70.9 all-gather.2
  162.5 65.8 reduce-scatter.6
  231.2 81.0 all-gather.4
  338.9 63.6 reduce-scatter.8

commit v2 on v1

--- a/solution.py
+++ b/solution.py
@@ -78,24 +78,29 @@
     positions = head_index * prefix_rows + jnp.arange(prefix_rows, dtype=jnp.int32)
     keep = positions[None, :] < ordered_prefix[:, None]
     local_layers = cache_prefill.shape[0]
-    halves = []
+    slots = cache_prefill.shape[1]
+    heads = cache_prefill.shape[3]
+    devices = req_count * head_count
+    chunks = []
     for layer in range(local_layers):
         dealt_cache = jnp.where(
-            keep[None, :, :, None, None],
-            jnp.take(cache_prefill[layer : layer + 1], req_order, axis=1),
+            keep[:, :, None, None],
+            jnp.take(cache_prefill[layer], req_order, axis=0),
             jnp.zeros((), cache_prefill.dtype),
         )
-        halves.append(
-            lax.all_to_all(
-                lax.all_to_all(dealt_cache, "head", split_axis=3, concat_axis=2, tiled=True),
-                "req",
-                split_axis=1,
-                concat_axis=0,
-                tiled=True,
-            )
+        outgoing = (
+            dealt_cache.reshape(req_count, group_size, prefix_rows, head_count, heads // head_count, pair_width)
+            .transpose(0, 3, 1, 2, 4, 5)
+            .reshape(devices, group_size, prefix_rows, heads // head_count, pair_width)
         )
-    current = halves[0][0]
-    relaid = jnp.stack(halves, axis=1).reshape((req_count * local_layers,) + halves[0].shape[1:])
+        incoming = lax.all_to_all(outgoing, ("req", "head"), 0, 0, tiled=True)
+        chunks.append(
+            incoming.reshape(req_count, head_count, group_size, prefix_rows, heads // head_count, pair_width)
+            .transpose(0, 2, 1, 3, 4, 5)
+            .reshape(req_count, group_size, head_count * prefix_rows, heads // head_count, pair_width)
+        )
+    current = chunks[0][0]
+    relaid = jnp.stack(chunks, axis=1).reshape((req_count * local_layers,) + chunks[0].shape[1:])
     dealt_acts = jnp.take(stretch_acts, req_order, axis=0)
     dealt_rows = lax.all_to_all(dealt_acts, "req", split_axis=0, concat_axis=1, tiled=True).reshape(
         group_size, req_count, stretch_rows, features

time: 429 us -> 386 us (0.90)
  waiting for transfers between devices: 269 us -> 241 us
  starting transfers between devices: 32.8 us -> 16.4 us
  blocking collectives: 0 us -> 9.17 us
  local copies, waits for them, and re-layouts: 63.7 us -> 58.5 us
    unnamed x6, waiting for transfers between devices: 122 us -> 81.5 us
    all_gather x1, waiting for transfers between devices: 0.01 us -> 35.8 us  [local(): gathered = lax.all_gather(dealt_rows, 'head', axis=2, tiled=True)]
    all_gather x1, waiting for transfers between devices: 75.1 us -> 48.9 us  [local(): normed_all = lax.all_gather(normed_rows, 'head', axis=2, tiled=True)]
    all_to_all x5 -> x2, starting transfers between devices: 26.5 us -> 10.7 us  [local(): incoming = lax.all_to_all(outgoing, ('req', 'head'), 0, 0, tiled=True)]
    another operation x2 -> x1, local copies, waits for them, and re-layouts: 10.7 us -> 0.27 us  [local(): jnp.stack(chunks, axis=1)]
    all_to_all x0 -> x1, blocking collectives: none -> 9.17 us  [local(): lax.all_to_all(dealt_acts, 'req', split_axis=0, concat_axis=1, tiled=True)]
    all_to_all x5 -> x0, local copies, waits for them, and re-layouts: 9.1 us -> none  [the longest x4 6.25 us: local(): lax.all_to_all(dealt_cache, 'head', split_axis=3, concat_axis=2, tiled=True)]
    transpose x0 -> x4, local copies, waits for them, and re-layouts: none -> 8.91 us  [the longest x2 5.38 us: local(): chunks.append(incoming.reshape(req_count, head_count, group_size, prefix_...]
  transfers between devices with their start and end apart: 10 -> 7, of which waited for: 5 -> 6; matrix products, arithmetic and copies ran while one was open for 18% -> 13% of each run, Pallas kernels for 0% -> 0%
where the time goes in v2:
time: 386 us; the launch traced here: 385 us
  waiting for transfers between devices  241 us (62%)
  local copies, waits for them, and re-layouts  58.5 us (15%)
  matrix products  24.5 us (6%)
  other arithmetic  21.2 us (5%)
  starting transfers between devices  16.4 us (4%)
  between operations  14.1 us (4%)
  blocking collectives  9.17 us (2%)
    unnamed x6, waiting for transfers between devices  81.5 us
    all_to_all x2, waiting for transfers between devices, local(): incoming = lax.all_to_all(outgoing, ('req', 'head'), 0, 0, tiled=True)  75.3 us
    all_gather x1, waiting for transfers between devices, local(): normed_all = lax.all_gather(normed_rows, 'head', axis=2, tiled=True)  48.9 us
    all_gather x1, waiting for transfers between devices, local(): gathered = lax.all_gather(dealt_rows, 'head', axis=2, tiled=True)  35.8 us
    unnamed x41, local copies, waits for them, and re-layouts  25.2 us
    dot_general x1, matrix products, local(): jnp.dot(inner, down_weight, preferred_element_type=jnp.float32)  13.7 us
    all_to_all x2, starting transfers between devices, local(): incoming = lax.all_to_all(outgoing, ('req', 'head'), 0, 0, tiled=True)  10.7 us
    all_to_all x1, blocking collectives, local(): lax.all_to_all(dealt_acts, 'req', split_axis=0, concat_axis=1, tiled=True)  9.17 us
  transfers between devices with their start and end apart: 7, of which 6 were waited for; matrix products, arithmetic and copies ran while one was open for 13% of the time, Pallas kernels for 0%

profile of v2, /device:TPU:1, one launch (start us, length us, event | category | flops | bytes accessed | tf_op | source)
XLA Modules:
  0.0 385.4 jit_solution(10914211351669699215)
XLA Ops:
  8.0 1.4 gather_fusion
  10.1 1.5 gather_fusion.2
  11.7 9.2 %all_to_all.40 = bf16[8,8,2048]{2,1,0:T(8,128)(2,1)} all-to-all(bf16[8,8,2048]{2,1,0:T(8,128)(2,1)S(1)} %broadcast_select_fusion.1), channel_id=1, replica_groups=mesh['req'=4,'head'=8] {'req'}, dimensions={0} | all-to-all | bytes 524288 | tf_op jit(solution)/shard_map/all_to_all | solution.py:105
  20.9 5.2 %slice_bitcast_fusion = (bf16[8,32,32,128]{3,2,1,0:T(8,128)(2,1)}, bf16[8,32,32,128]{3,2,1,0:T(8,128)(2,1)}) fusion(bf16[2,8,32,32,128]{4,3,2,1,0:T(8,128)(2,1)} %param.19), kind=kLoop, calls=%fused_computation.29 | loop fusion | bytes 8388608 | tf_op jit(solution)/shard_map/squeeze | solution.py:88
  26.1 3.7 gather_fusion.6
  29.8 3.8 gather_fusion.3
  33.7 3.5 select_select_fusion
  37.2 0.8 copy.68
  38.0 1.8 copy.69
  39.8 6.1 %all-to-all-start.1 = ((bf16[32,2,32,4,128]{4,2,3,1,0:T(8,128)(2,1)}), bf16[32,2,32,4,128]{4,2,3,1,0:T(8,128)(2,1)}, u32[]{:S(2)}, u32[]{:S(2)}) async-start(bf16[32,2,32,4,128]{4,2,3,1,0:T(8,128)(2,1)} %bitcast.113), calls=%async_computation.1 | async-start | bytes 4194304 | tf_op jit(solution)/shard_map/all_to_all | solution.py:96
  48.9 1.3 iota_compare_fusion.1
  52.3 0.9 subtract_convert_fusion.1
  53.2 0.9 subtract_convert_fusion
  54.1 35.8 %all-gather.3.cloned.1.call-done = bf16[2,4,64,2048]{3,2,0,1:T(8,128)(2,1)} async-done(((bf16[2,4,8,2048]{3,2,0,1:T(8,128)(2,1)}), bf16[2,4,64,2048]{3,2,0,1:T(8,128)(2,1)}) %all-gather.3.cloned.1.call-update) | async-done | bytes 2097168 | tf_op jit(solution)/shard_map/all_gather | solution.py:108
  89.9 2.1 convert_reduce_fusion
  93.7 1.8 fusion.19
  95.5 0.9 copy-done.12
  96.5 15.8 %all-to-all-done.1 = bf16[32,2,32,4,128]{4,2,3,1,0:T(8,128)(2,1)} async-done(((bf16[32,2,32,4,128]{4,2,3,1,0:T(8,128)(2,1)}), bf16[32,2,32,4,128]{4,2,3,1,0:T(8,128)(2,1)}, u32[]{:S(2)}, u32[]{:S(2)}) %all-to-all-start.1) | async-done | bytes 2097184 | tf_op jit(solution)/shard_map/all_to_all | solution.py:96
  112.3 1.1 fusion.118
  113.6 2.0 fusion.121
  115.6 2.2 convolution_convert_fusion.3
  118.0 2.0 fusion.120
  119.9 2.2 convolution_convert_fusion.2
  123.1 2.9 copy.101
  126.0 4.5 %reshape.463 = bf16[64,16384]{1,0:T(8,128)(2,1)} reshape(bf16[64,2,4,2048]{3,2,1,0:T(4,128)(2,1)} %bitcast.117) | data formatting | bytes 4194304
  131.2 63.5 %reduce-scatter.7.cloned.1.call-done = bf16[8,16384]{1,0:T(8,128)(2,1)} async-done(((bf16[64,16384]{1,0:T(8,128)(2,1)}), bf16[8,16384]{1,0:T(8,128)(2,1)}) %reduce-scatter.7.cloned.1.call-update) | async-done | bytes 262160
  194.7 1.1 reshape.464
  196.5 0.9 multiply_convert_fusion
  197.7 48.9 %all-gather.5.cloned.1.call-done = bf16[2,4,64,2048]{3,2,0,1:T(8,128)(2,1)} async-done(((bf16[2,4,8,2048]{3,2,0,1:T(8,128)(2,1)}), bf16[2,4,64,2048]{3,2,0,1:T(8,128)(2,1)}) %all-gather.5.cloned.1.call-update) | async-done | bytes 2097168 | tf_op jit(solution)/shard_map/all_gather | solution.py:138
  246.5 1.8 copy.77
  248.4 13.7 %convolution_convert_fusion = bf16[512,2048]{1,0:T(8,128)(2,1)} fusion(bf16[1024,2048]{1,0:T(8,128)(2,1)} %param.29, bf16[512,2048]{1,0:T(8,128)(2,1)S(1)} %bitcast.127, bf16[2048,1024]{1,0:T(8,128)(2,1)} %param.28), kind=kOutput, calls=%fused_computation.20 | convolution fusion | flops 4330094592 | bytes 12582912 | tf_op jit(solution)/shard_map/dot_general | solution.py:147
  262.0 3.2 copy.100
  265.2 2.8 reshape.465
  268.1 1.6 copy-done.6
  269.6 0.8 copy.80
  270.5 1.8 copy.81
  272.2 4.6 %all-to-all-start.3 = ((bf16[32,2,32,4,128]{4,2,3,1,0:T(8,128)(2,1)}), bf16[32,2,32,4,128]{4,2,3,1,0:T(8,128)(2,1)S(1)}, u32[]{:S(2)}, u32[]{:S(2)}) async-start(bf16[32,2,32,4,128]{4,2,3,1,0:T(8,128)(2,1)} %bitcast.115), calls=%async_computation.3 | async-start | bytes 4194304 | tf_op jit(solution)/shard_map/all_to_all | solution.py:96
  276.9 1.0 sort.17
  278.0 3.5 copy.79
  281.5 59.5 %all-to-all-done.3 = bf16[32,2,32,4,128]{4,2,3,1,0:T(8,128)(2,1)S(1)} async-done(((bf16[32,2,32,4,128]{4,2,3,1,0:T(8,128)(2,1)}), bf16[32,2,32,4,128]{4,2,3,1,0:T(8,128)(2,1)S(1)}, u32[]{:S(2)}, u32[]{:S(2)}) %all-to-all-start.3) | async-done | bytes 2097184 | tf_op jit(solution)/shard_map/all_to_all | solution.py:96
  341.0 1.9 copy.82
  342.9 17.9 %reduce-scatter.9.cloned.1.call-done = bf16[8,16384]{1,0:T(8,128)(2,1)} async-done(((bf16[64,16384]{1,0:T(8,128)(2,1)}), bf16[8,16384]{1,0:T(8,128)(2,1)}) %reduce-scatter.9.cloned.1.call-update) | async-done | bytes 262160
  360.8 1.1 reshape.466
  361.9 1.0 select_convert_fusion
  362.9 5.1 %all-to-all-start.2 = ((bf16[2,4,8,2048]{3,2,0,1:T(8,128)(2,1)}), bf16[2,4,8,2048]{3,2,0,1:T(8,128)(2,1)S(1)}, u32[]{:S(2)}, u32[]{:S(2)}) async-start(bf16[2,4,8,2048]{3,2,0,1:T(8,128)(2,1)} %select_convert_fusion), calls=%async_computation.2 | async-start | bytes 524288 | tf_op jit(solution)/shard_map/all_to_all | solution.py:160
  368.0 2.0 pad_maximum_fusion
  370.3 5.5 %copy.84 = bf16[8,2,256,4,128]{4,3,2,1,0:T(4,128)(2,1)} copy(bf16[8,2,256,4,128]{4,2,3,1,0:T(8,128)(2,1)S(1)} %bitcast.109) | data formatting | bytes 8388608
  376.5 1.5 gather_fusion.5
  (88 shorter events, 13.3 us)
Async XLA Ops:
  7.2 86.5 %copy-start = (bf16[2048,4,192]{0,2,1:T(8,128)(2,1)S(1)}, bf16[2048,4,192]{0,2,1:T(8,128)(2,1)}, u32[]{:S(2)}) copy-start(bf16[2048,4,192]{0,2,1:T(8,128)(2,1)} %param.24) | copy-start | bytes 9437188
  7.2 82.7 %all-gather.3.cloned.1.call-start = ((), (), s32[]{:S(2)}) async-start(), calls=%async_computation.6 | async-start | bytes 2359296 | tf_op jit(solution)/shard_map/all_gather | solution.py:108
  39.8 6.4 %copy-start.15 = (s32[8]{0:T(128)S(1)}, s32[8]{0:T(128)}, u32[]{:S(2)}) copy-start(s32[8]{0:T(128)} %param.22) | copy-start | bytes 100
  39.8 6.5 %copy-start.2 = (s32[8]{0:T(128)S(1)}, s32[8]{0:T(128)}, u32[]{:S(2)}) copy-start(s32[8]{0:T(128)} %param.21) | copy-start | bytes 100
  39.8 7.1 %copy-start.3 = (s32[8]{0:T(128)S(1)}, s32[8]{0:T(128)}, u32[]{:S(2)}) copy-start(s32[8]{0:T(128)} %param.20) | copy-start | bytes 100
  39.8 7.8 %copy-start.13 = (bf16[2048]{0:T(1024)(128)(2,1)S(1)}, bf16[2048]{0:T(1024)(128)(2,1)}, u32[]{:S(2)}) copy-start(bf16[2048]{0:T(1024)(128)(2,1)} %param.23) | copy-start | bytes 12292
  39.8 72.5 %all-to-all-start.1 = ((bf16[32,2,32,4,128]{4,2,3,1,0:T(8,128)(2,1)}), bf16[32,2,32,4,128]{4,2,3,1,0:T(8,128)(2,1)}, u32[]{:S(2)}, u32[]{:S(2)}) async-start(bf16[32,2,32,4,128]{4,2,3,1,0:T(8,128)(2,1)} %bitcast.113), calls=%async_computation.1 | async-start | bytes 4194304 | tf_op jit(solution)/shard_map/all_to_all | solution.py:96
  45.9 148.8 %reduce-scatter.7.cloned.1.call-start = ((), (), s32[]{:S(2)}) async-start(), calls=%async_computation.8 | async-start | bytes 2359296
  89.9 2.2 copy-start.4
  95.5 0.9 copy-start.12
  96.5 17.1 %copy-start.11 = (f32[256,512]{1,0:T(8,128)S(1)}, f32[256,512]{1,0:T(8,128)}, u32[]{:S(2)}) copy-start(f32[256,512]{1,0:T(8,128)} %subtract_convert_fusion.1) | copy-start | bytes 1572868
  96.5 17.1 %copy-start.16 = (f32[4]{0:T(128)S(1)}, f32[4]{0:T(128)}, u32[]{:S(2)}) copy-start(f32[4]{0:T(128)} %param.25) | copy-start | bytes 52
  115.5 2.4 copy-start.10
  119.9 2.4 copy-start.9
  130.5 0.7 copy-start.14
  130.5 65.3 %copy-start.5 = (bf16[8,8,2048]{2,1,0:T(8,128)(2,1)S(1)}, bf16[8,8,2048]{2,1,0:T(8,128)(2,1)}, u32[]{:S(2)}) copy-start(bf16[8,8,2048]{2,1,0:T(8,128)(2,1)} %all_to_all.40) | copy-start | bytes 786436
  130.5 116.0 %all-gather.5.cloned.1.call-start = ((), (), s32[]{:S(2)}) async-start(), calls=%async_computation.7 | async-start | bytes 2359296 | tf_op jit(solution)/shard_map/all_gather | solution.py:138
  197.4 163.4 %reduce-scatter.9.cloned.1.call-start = ((), (), s32[]{:S(2)}) async-start(), calls=%async_computation.9 | async-start | bytes 2359296
  268.0 1.6 copy-start.6
  272.2 68.8 %all-to-all-start.3 = ((bf16[32,2,32,4,128]{4,2,3,1,0:T(8,128)(2,1)}), bf16[32,2,32,4,128]{4,2,3,1,0:T(8,128)(2,1)S(1)}, u32[]{:S(2)}, u32[]{:S(2)}) async-start(bf16[32,2,32,4,128]{4,2,3,1,0:T(8,128)(2,1)} %bitcast.115), calls=%async_computation.3 | async-start | bytes 4194304 | tf_op jit(solution)/shard_map/all_to_all | solution.py:96
  342.9 25.2 %copy-start.7 = (bf16[4,2,8,32,4,128]{5,3,2,4,1,0:T(8,128)(2,1)S(1)}, bf16[4,2,8,32,4,128]{5,3,2,4,1,0:T(8,128)(2,1)}, u32[]{:S(2)}) copy-start(bf16[4,2,8,32,4,128]{5,3,2,4,1,0:T(8,128)(2,1)} %copy.79) | copy-start | bytes 6291460
  362.9 12.9 %all-to-all-start.2 = ((bf16[2,4,8,2048]{3,2,0,1:T(8,128)(2,1)}), bf16[2,4,8,2048]{3,2,0,1:T(8,128)(2,1)S(1)}, u32[]{:S(2)}, u32[]{:S(2)}) async-start(bf16[2,4,8,2048]{3,2,0,1:T(8,128)(2,1)} %select_convert_fusion), calls=%async_computation.2 | async-start | bytes 524288 | tf_op jit(solution)/shard_map/all_to_all | solution.py:160
  370.3 8.5 %copy-start.1 = (bf16[2048,4,192]{0,2,1:T(8,128)(2,1)S(1)}, bf16[2048,4,192]{0,2,1:T(8,128)(2,1)}, u32[]{:S(2)}) copy-start(bf16[2048,4,192]{0,2,1:T(8,128)(2,1)} %param.24) | copy-start | bytes 9437188
  375.8 0.7 copy-start.8
Sparse Core Ops, SparseCore 0:
  21.0 68.8 all-gather.2
  130.6 63.9 reduce-scatter.6
  197.5 48.9 all-gather.4
  268.2 92.5 reduce-scatter.8

commit v3 on v2

--- a/solution.py
+++ b/solution.py
@@ -41,6 +41,14 @@
     soft = (expo / jnp.sum(expo, axis=-1, keepdims=True)).astype(jnp.bfloat16)
     context = jnp.einsum("hqk,khd->qhd", soft, values_part, preferred_element_type=jnp.float32)
     return context.astype(jnp.bfloat16).reshape(stretch, -1)
+
+
+def head_sum(partial, head_count, stretch_rows):
+    shape = partial.shape[:2] + (head_count, stretch_rows) + partial.shape[3:]
+    pieces = lax.all_to_all(
+        partial.astype(jnp.bfloat16).reshape(shape), "head", split_axis=2, concat_axis=2, tiled=True
+    )
+    return jnp.sum(pieces.astype(jnp.float32), axis=2)
 
 
 def local(
@@ -130,9 +138,7 @@
         preferred_element_type=jnp.float32,
     )
     partial_attn = partial_attn.reshape(group_size, req_count, span_rows, features)
-    attn_rows = lax.psum_scatter(
-        partial_attn.astype(jnp.bfloat16), "head", scatter_dimension=2, tiled=True
-    ).astype(jnp.float32)
+    attn_rows = head_sum(partial_attn, head_count, stretch_rows)
     residual_rows = dealt_rows.astype(jnp.float32) + attn_rows
     normed_rows = layer_norm(residual_rows, mlp_gain).astype(jnp.bfloat16)
     normed_all = lax.all_gather(normed_rows, "head", axis=2, tiled=True)
@@ -147,9 +153,7 @@
     partial_mlp = jnp.dot(inner, down_weight, preferred_element_type=jnp.float32).reshape(
         group_size, req_count, span_rows, features
     )
-    mlp_rows = lax.psum_scatter(
-        partial_mlp.astype(jnp.bfloat16), "head", scatter_dimension=2, tiled=True
-    ).astype(jnp.float32)
+    mlp_rows = head_sum(partial_mlp, head_count, stretch_rows)
     row_number = (
         jnp.arange(req_count, dtype=jnp.int32)[:, None] * head_count + head_index
     ) * stretch_rows + jnp.arange(stretch_rows, dtype=jnp.int32)[None, :]

time: 386 us -> 355 us (0.920)
  waiting for transfers between devices: 241 us -> 213 us
  local copies, waits for them, and re-layouts: 58.5 us -> 47.4 us
  starting transfers between devices: 16.4 us -> 22.6 us
    all_to_all x0 -> x2, waiting for transfers between devices: none -> 88.5 us  [head_sum(): lax.all_to_all(partial.astype(jnp.bfloat16).reshape(shape), 'head', split...]
    unnamed x6 -> x2, waiting for transfers between devices: 81.5 us -> 0.03 us
    all_to_all x2, waiting for transfers between devices: 75.3 us -> 16 us  [local(): incoming = lax.all_to_all(outgoing, ('req', 'head'), 0, 0, tiled=True)]
    all_gather x1, waiting for transfers between devices: 48.9 us -> 72.8 us  [local(): normed_all = lax.all_gather(normed_rows, 'head', axis=2, tiled=True)]
    unnamed x41, local copies, waits for them, and re-layouts: 25.2 us -> 9.04 us
    all_to_all x0 -> x2, starting transfers between devices: none -> 7.34 us  [head_sum(): lax.all_to_all(partial.astype(jnp.bfloat16).reshape(shape), 'head', split...]
  transfers between devices with their start and end apart: 7 -> 7, of which waited for: 6 -> 5; matrix products, arithmetic and copies ran while one was open for 13% -> 19% of each run, Pallas kernels for 0% -> 0%
where the time goes in v3:
time: 355 us; the launch traced here: 354 us
  waiting for transfers between devices  213 us (60%)
  local copies, waits for them, and re-layouts  47.4 us (13%)
  matrix products  26.8 us (8%)
  starting transfers between devices  22.6 us (6%)
  other arithmetic  21.2 us (6%)
  between operations  14.4 us (4%)
  blocking collectives  9.06 us (3%)
    all_to_all x2, waiting for transfers between devices, head_sum(): lax.all_to_all(partial.astype(jnp.bfloat16).reshape(shape), 'head', split...  88.5 us
    all_gather x1, waiting for transfers between devices, local(): normed_all = lax.all_gather(normed_rows, 'head', axis=2, tiled=True)  72.8 us
    all_gather x1, waiting for transfers between devices, local(): gathered = lax.all_gather(dealt_rows, 'head', axis=2, tiled=True)  35.4 us
    all_to_all x2, waiting for transfers between devices, local(): incoming = lax.all_to_all(outgoing, ('req', 'head'), 0, 0, tiled=True)  16 us
    dot_general x1, matrix products, local(): jnp.dot(inner, down_weight, preferred_element_type=jnp.float32)  14.3 us
    all_to_all x2, starting transfers between devices, local(): incoming = lax.all_to_all(outgoing, ('req', 'head'), 0, 0, tiled=True)  10.5 us
    all_to_all x1, blocking collectives, local(): lax.all_to_all(dealt_acts, 'req', split_axis=0, concat_axis=1, tiled=True)  9.06 us
    unnamed x41, local copies, waits for them, and re-layouts  9.04 us
  transfers between devices with their start and end apart: 7, of which 5 were waited for; matrix products, arithmetic and copies ran while one was open for 19% of the time, Pallas kernels for 0%

profile of v3, /device:TPU:1, one launch (start us, length us, event | category | flops | bytes accessed | tf_op | source)
XLA Modules:
  0.0 354.2 jit_solution(10485192841990364266)
XLA Ops:
  7.2 0.8 compare_select_fusion.1
  8.0 1.4 gather_fusion
  10.1 1.5 gather_fusion.2
  11.7 9.1 %all_to_all.50 = bf16[8,8,2048]{2,1,0:T(8,128)(2,1)S(1)} all-to-all(bf16[8,8,2048]{2,1,0:T(8,128)(2,1)S(1)} %broadcast_select_fusion.1), channel_id=1, replica_groups=mesh['req'=4,'head'=8] {'req'}, dimensions={0} | all-to-all | bytes 524288 | tf_op jit(solution)/shard_map/all_to_all | solution.py:113
  21.5 5.2 %slice_bitcast_fusion = (bf16[8,32,32,128]{3,2,1,0:T(8,128)(2,1)}, bf16[8,32,32,128]{3,2,1,0:T(8,128)(2,1)}) fusion(bf16[2,8,32,32,128]{4,3,2,1,0:T(8,128)(2,1)} %param.19), kind=kLoop, calls=%fused_computation.30 | loop fusion | bytes 8388608 | tf_op jit(solution)/shard_map/squeeze | solution.py:96
  26.7 3.7 %gather_fusion.6 = bf16[8,32,32,128]{3,2,1,0:T(8,128)(2,1)} fusion(bf16[8,32,32,128]{3,2,1,0:T(8,128)(2,1)} %get-tuple-element.17, s32[1024]{0:T(1024)S(1)} %pad_clamp_fusion.1), kind=kCustom, calls=%fused_computation.5.clone | custom fusion | bytes 4194336 | tf_op jit(solution)/shard_map/jit(_take)/gather | solution.py:96
  30.4 3.8 %gather_fusion.3 = bf16[8,32,32,128]{3,2,1,0:T(8,128)(2,1)} fusion(bf16[8,32,32,128]{3,2,1,0:T(8,128)(2,1)} %get-tuple-element.18, s32[1024]{0:T(1024)S(1)} %pad_clamp_fusion.1), kind=kCustom, calls=%fused_computation.2.clone | custom fusion | bytes 4194336 | tf_op jit(solution)/shard_map/jit(_take)/gather | solution.py:96
  34.3 3.5 select_select_fusion
  37.8 0.8 copy.72
  38.6 1.8 copy.73
  40.4 5.7 %all-to-all-start.1 = ((bf16[32,2,32,4,128]{4,2,3,1,0:T(8,128)(2,1)}), bf16[32,2,32,4,128]{4,2,3,1,0:T(8,128)(2,1)}, u32[]{:S(2)}, u32[]{:S(2)}) async-start(bf16[32,2,32,4,128]{4,2,3,1,0:T(8,128)(2,1)} %bitcast.118), calls=%async_computation.1 | async-start | bytes 4194304 | tf_op jit(solution)/shard_map/all_to_all | solution.py:104
  48.8 1.3 iota_compare_fusion.1
  52.1 0.8 fusion.55
  52.9 0.9 subtract_convert_fusion.1
  53.8 0.9 subtract_convert_fusion
  54.7 35.4 %all-gather.3.cloned.1.call-done = bf16[2,4,64,2048]{3,2,1,0:T(8,128)(2,1)} async-done(((bf16[2,4,8,2048]{3,2,1,0:T(8,128)(2,1)}), bf16[2,4,64,2048]{3,2,1,0:T(8,128)(2,1)}) %all-gather.3.cloned.1.call-update) | async-done | bytes 2097168 | tf_op jit(solution)/shard_map/all_gather | solution.py:116
  90.1 2.1 convert_reduce_fusion
  93.8 1.8 fusion.20
  95.6 0.9 copy-done.13
  96.6 16.0 %all-to-all-done.1 = bf16[32,2,32,4,128]{4,2,3,1,0:T(8,128)(2,1)} async-done(((bf16[32,2,32,4,128]{4,2,3,1,0:T(8,128)(2,1)}), bf16[32,2,32,4,128]{4,2,3,1,0:T(8,128)(2,1)}, u32[]{:S(2)}, u32[]{:S(2)}) %all-to-all-start.1) | async-done | bytes 2097184 | tf_op jit(solution)/shard_map/all_to_all | solution.py:104
  112.5 1.1 fusion.119
  113.8 2.0 fusion.122
  115.8 2.9 convolution_convert_fusion.3
  118.8 2.0 fusion.121
  120.8 2.2 convolution_convert_fusion.2
  123.1 0.8 copy.78
  123.9 1.7 fusion.9
  125.6 1.6 copy.79
  127.2 3.7 %all-to-all-start.2 = ((bf16[2,4,8,8,2048]{4,3,1,0,2:T(8,128)(2,1)}), bf16[2,4,8,8,2048]{4,3,1,0,2:T(8,128)(2,1)S(1)}, u32[]{:S(2)}, u32[]{:S(2)}) async-start(bf16[2,4,8,8,2048]{4,3,1,0,2:T(8,128)(2,1)} %copy.79), calls=%async_computation.2 | async-start | bytes 4194304 | tf_op jit(solution)/shard_map/all_to_all | solution.py:48
  131.0 47.3 %all-to-all-done.2 = bf16[2,4,8,8,2048]{4,3,1,0,2:T(8,128)(2,1)S(1)} async-done(((bf16[2,4,8,8,2048]{4,3,1,0,2:T(8,128)(2,1)}), bf16[2,4,8,8,2048]{4,3,1,0,2:T(8,128)(2,1)S(1)}, u32[]{:S(2)}, u32[]{:S(2)}) %all-to-all-start.2) | async-done | bytes 2097184 | tf_op jit(solution)/shard_map/all_to_all | solution.py:48
  179.1 0.8 multiply_convert_fusion
  180.4 0.8 copy.85
  181.2 1.8 copy.86
  182.9 4.8 %all-to-all-start.5 = ((bf16[32,2,32,4,128]{4,2,3,1,0:T(8,128)(2,1)}), bf16[32,2,32,4,128]{4,2,3,1,0:T(8,128)(2,1)S(1)}, u32[]{:S(2)}, u32[]{:S(2)}) async-start(bf16[32,2,32,4,128]{4,2,3,1,0:T(8,128)(2,1)} %bitcast.120), calls=%async_computation.5 | async-start | bytes 4194304 | tf_op jit(solution)/shard_map/all_to_all | solution.py:104
  187.7 72.8 %all-gather.5.cloned.1.call-done = bf16[2,4,64,2048]{3,2,1,0:T(8,128)(2,1)} async-done(((bf16[2,4,8,2048]{3,2,1,0:T(8,128)(2,1)}), bf16[2,4,64,2048]{3,2,1,0:T(8,128)(2,1)}) %all-gather.5.cloned.1.call-update) | async-done | bytes 2097168 | tf_op jit(solution)/shard_map/all_gather | solution.py:144
  260.5 14.3 %convolution_convert_fusion = bf16[512,2048]{1,0:T(8,128)(2,1)} fusion(bf16[1024,2048]{1,0:T(8,128)(2,1)} %param.29, bf16[512,2048]{1,0:T(8,128)(2,1)} %bitcast.134, bf16[2048,1024]{1,0:T(8,128)(2,1)} %param.28), kind=kOutput, calls=%fused_computation.22 | convolution fusion | flops 4330094592 | bytes 12582912 | tf_op jit(solution)/shard_map/dot_general | solution.py:153
  274.8 3.1 copy.81
  277.9 1.3 copy-done.6
  279.2 3.6 %all-to-all-start.3 = ((bf16[2,4,8,8,2048]{4,3,1,0,2:T(8,128)(2,1)}), bf16[2,4,8,8,2048]{4,3,1,0,2:T(8,128)(2,1)S(1)}, u32[]{:S(2)}, u32[]{:S(2)}) async-start(bf16[2,4,8,8,2048]{4,3,1,0,2:T(8,128)(2,1)} %copy.81), calls=%async_computation.3 | async-start | bytes 4194304 | tf_op jit(solution)/shard_map/all_to_all | solution.py:48
  282.8 1.0 sort.17
  284.0 3.6 %copy.84 = bf16[4,2,8,32,4,128]{5,3,2,4,1,0:T(8,128)(2,1)} copy(bf16[4,2,8,32,4,128]{5,3,4,1,2,0:T(8,128)(2,1)} %bitcast.7) | data formatting | bytes 4194304 | tf_op jit(solution)/shard_map/transpose | solution.py:107
  287.6 1.9 copy.87
  289.5 41.1 %all-to-all-done.3 = bf16[2,4,8,8,2048]{4,3,1,0,2:T(8,128)(2,1)S(1)} async-done(((bf16[2,4,8,8,2048]{4,3,1,0,2:T(8,128)(2,1)}), bf16[2,4,8,8,2048]{4,3,1,0,2:T(8,128)(2,1)S(1)}, u32[]{:S(2)}, u32[]{:S(2)}) %all-to-all-start.3) | async-done | bytes 2097184 | tf_op jit(solution)/shard_map/all_to_all | solution.py:48
  331.9 4.7 %all-to-all-start.4 = ((bf16[2,4,8,2048]{3,2,0,1:T(8,128)(2,1)}), bf16[2,4,8,2048]{3,2,0,1:T(8,128)(2,1)S(1)}, u32[]{:S(2)}, u32[]{:S(2)}) async-start(bf16[2,4,8,2048]{3,2,0,1:T(8,128)(2,1)} %copy.83), calls=%async_computation.4 | async-start | bytes 524288 | tf_op jit(solution)/shard_map/all_to_all | solution.py:164
  336.5 2.0 pad_maximum_fusion
  338.8 5.5 %copy.89 = bf16[8,2,256,4,128]{4,3,2,1,0:T(4,128)(2,1)} copy(bf16[8,2,256,4,128]{4,2,3,1,0:T(8,128)(2,1)S(1)} %bitcast.115) | data formatting | bytes 8388608
  345.0 1.5 gather_fusion.5
  346.5 0.8 broadcast_select_fusion
  (90 shorter events, 11.8 us)
Async XLA Ops:
  7.2 86.6 %copy-start = (bf16[2048,4,192]{0,2,1:T(8,128)(2,1)S(1)}, bf16[2048,4,192]{0,2,1:T(8,128)(2,1)}, u32[]{:S(2)}) copy-start(bf16[2048,4,192]{0,2,1:T(8,128)(2,1)} %param.24) | copy-start | bytes 9437188
  7.2 82.9 %all-gather.3.cloned.1.call-start = ((), (), s32[]{:S(2)}) async-start(), calls=%async_computation.6 | async-start | bytes 2359296 | tf_op jit(solution)/shard_map/all_gather | solution.py:116
  40.4 5.8 %copy-start.18 = (s32[8]{0:T(128)S(1)}, s32[8]{0:T(128)}, u32[]{:S(2)}) copy-start(s32[8]{0:T(128)} %param.22) | copy-start | bytes 100
  40.4 5.8 %copy-start.2 = (s32[8]{0:T(128)S(1)}, s32[8]{0:T(128)}, u32[]{:S(2)}) copy-start(s32[8]{0:T(128)} %param.21) | copy-start | bytes 100
  40.4 6.5 %copy-start.3 = (s32[8]{0:T(128)S(1)}, s32[8]{0:T(128)}, u32[]{:S(2)}) copy-start(s32[8]{0:T(128)} %param.20) | copy-start | bytes 100
  40.4 7.1 %copy-start.16 = (bf16[2048]{0:T(1024)(128)(2,1)S(1)}, bf16[2048]{0:T(1024)(128)(2,1)}, u32[]{:S(2)}) copy-start(bf16[2048]{0:T(1024)(128)(2,1)} %param.23) | copy-start | bytes 12292
  40.4 72.1 %all-to-all-start.1 = ((bf16[32,2,32,4,128]{4,2,3,1,0:T(8,128)(2,1)}), bf16[32,2,32,4,128]{4,2,3,1,0:T(8,128)(2,1)}, u32[]{:S(2)}, u32[]{:S(2)}) async-start(bf16[32,2,32,4,128]{4,2,3,1,0:T(8,128)(2,1)} %bitcast.118), calls=%async_computation.1 | async-start | bytes 4194304 | tf_op jit(solution)/shard_map/all_to_all | solution.py:104
  90.1 2.2 copy-start.4
  95.6 0.9 copy-start.13
  96.5 17.3 %copy-start.12 = (f32[256,512]{1,0:T(8,128)S(1)}, f32[256,512]{1,0:T(8,128)}, u32[]{:S(2)}) copy-start(f32[256,512]{1,0:T(8,128)} %subtract_convert_fusion.1) | copy-start | bytes 1572868
  96.5 17.3 %copy-start.14 = (pred[256,512]{1,0:T(8,128)(4,1)S(1)}, pred[256,512]{1,0:T(8,128)(4,1)}, u32[]{:S(2)}) copy-start(pred[256,512]{1,0:T(8,128)(4,1)} %get-tuple-element.23) | copy-start | bytes 393220
  96.5 17.3 %copy-start.19 = (f32[4]{0:T(128)S(1)}, f32[4]{0:T(128)}, u32[]{:S(2)}) copy-start(f32[4]{0:T(128)} %param.25) | copy-start | bytes 52
  115.8 3.0 copy-start.11
  120.8 2.3 copy-start.15
  120.8 3.1 copy-start.10
  127.2 3.8 %copy-start.17 = (bf16[2048]{0:T(1024)(128)(2,1)S(1)}, bf16[2048]{0:T(1024)(128)(2,1)}, u32[]{:S(2)}) copy-start(bf16[2048]{0:T(1024)(128)(2,1)} %param.27) | copy-start | bytes 12292
  127.2 51.2 %all-to-all-start.2 = ((bf16[2,4,8,8,2048]{4,3,1,0,2:T(8,128)(2,1)}), bf16[2,4,8,8,2048]{4,3,1,0,2:T(8,128)(2,1)S(1)}, u32[]{:S(2)}, u32[]{:S(2)}) async-start(bf16[2,4,8,8,2048]{4,3,1,0,2:T(8,128)(2,1)} %copy.79), calls=%async_computation.2 | async-start | bytes 4194304 | tf_op jit(solution)/shard_map/all_to_all | solution.py:48
  130.9 129.6 %all-gather.5.cloned.1.call-start = ((), (), s32[]{:S(2)}) async-start(), calls=%async_computation.7 | async-start | bytes 2359296 | tf_op jit(solution)/shard_map/all_gather | solution.py:144
  178.7 1.7 copy-start.5
  182.9 95.0 %all-to-all-start.5 = ((bf16[32,2,32,4,128]{4,2,3,1,0:T(8,128)(2,1)}), bf16[32,2,32,4,128]{4,2,3,1,0:T(8,128)(2,1)S(1)}, u32[]{:S(2)}, u32[]{:S(2)}) async-start(bf16[32,2,32,4,128]{4,2,3,1,0:T(8,128)(2,1)} %bitcast.120), calls=%async_computation.5 | async-start | bytes 4194304 | tf_op jit(solution)/shard_map/all_to_all | solution.py:104
  277.9 1.3 copy-start.6
  279.2 51.4 %all-to-all-start.3 = ((bf16[2,4,8,8,2048]{4,3,1,0,2:T(8,128)(2,1)}), bf16[2,4,8,8,2048]{4,3,1,0,2:T(8,128)(2,1)S(1)}, u32[]{:S(2)}, u32[]{:S(2)}) async-start(bf16[2,4,8,8,2048]{4,3,1,0,2:T(8,128)(2,1)} %copy.81), calls=%async_computation.3 | async-start | bytes 4194304 | tf_op jit(solution)/shard_map/all_to_all | solution.py:48
  284.0 3.6 %copy-start.7 = (bf16[32,2,32,4,128]{4,2,3,1,0:T(8,128)(2,1)S(1)}, bf16[32,2,32,4,128]{4,2,3,1,0:T(8,128)(2,1)}, u32[]{:S(2)}) copy-start(bf16[32,2,32,4,128]{4,2,3,1,0:T(8,128)(2,1)} %copy-done.6) | copy-start | bytes 6291460
  331.0 5.5 %copy-start.8 = (bf16[4,2,8,32,4,128]{5,3,2,4,1,0:T(8,128)(2,1)S(1)}, bf16[4,2,8,32,4,128]{5,3,2,4,1,0:T(8,128)(2,1)}, u32[]{:S(2)}) copy-start(bf16[4,2,8,32,4,128]{5,3,2,4,1,0:T(8,128)(2,1)} %copy.84) | copy-start | bytes 6291460
  331.9 12.4 %all-to-all-start.4 = ((bf16[2,4,8,2048]{3,2,0,1:T(8,128)(2,1)}), bf16[2,4,8,2048]{3,2,0,1:T(8,128)(2,1)S(1)}, u32[]{:S(2)}, u32[]{:S(2)}) async-start(bf16[2,4,8,2048]{3,2,0,1:T(8,128)(2,1)} %copy.83), calls=%async_computation.4 | async-start | bytes 524288 | tf_op jit(solution)/shard_map/all_to_all | solution.py:164
  338.8 8.5 %copy-start.1 = (bf16[2048,4,192]{0,2,1:T(8,128)(2,1)S(1)}, bf16[2048,4,192]{0,2,1:T(8,128)(2,1)}, u32[]{:S(2)}) copy-start(bf16[2048,4,192]{0,2,1:T(8,128)(2,1)} %param.24) | copy-start | bytes 9437188
  344.3 0.7 copy-start.9
Sparse Core Ops, SparseCore 0:
  21.6 68.4 all-gather.2
  180.0 80.4 all-gather.4

commit v4 on v3

--- a/solution.py
+++ b/solution.py
@@ -91,11 +91,10 @@
     devices = req_count * head_count
     chunks = []
     for layer in range(local_layers):
-        dealt_cache = jnp.where(
-            keep[:, :, None, None],
-            jnp.take(cache_prefill[layer], req_order, axis=0),
-            jnp.zeros((), cache_prefill.dtype),
+        taken = jnp.stack(
+            [lax.dynamic_index_in_dim(cache_prefill[layer], req_order[slot], 0, False) for slot in range(slots)]
         )
+        dealt_cache = jnp.where(keep[:, :, None, None], taken, jnp.zeros((), cache_prefill.dtype))
         outgoing = (
             dealt_cache.reshape(req_count, group_size, prefix_rows, head_count, heads // head_count, pair_width)
             .transpose(0, 3, 1, 2, 4, 5)

time: 355 us -> 385 us (1.085)
  local copies, waits for them, and re-layouts: 47.4 us -> 65.2 us
  between operations: 14.4 us -> 29.2 us
  blocking collectives: 9.06 us -> 0 us
  starting transfers between devices: 22.6 us -> 27.8 us
    unnamed x41 -> x67, local copies, waits for them, and re-layouts: 9.04 us -> 28.2 us
    all_gather x1, waiting for transfers between devices: 35.4 us -> 47.2 us  [local(): gathered = lax.all_gather(dealt_rows, 'head', axis=2, tiled=True)]
    all_to_all x2, waiting for transfers between devices: 16 us -> 4.56 us  [local(): incoming = lax.all_to_all(outgoing, ('req', 'head'), 0, 0, tiled=True)]
    all_to_all x1 -> x0, blocking collectives: 9.06 us -> none  [local(): lax.all_to_all(dealt_acts, 'req', split_axis=0, concat_axis=1, tiled=True)]
    gather x2 -> x0, local copies, waits for them, and re-layouts: 7.51 us -> none  [local(): jnp.take(cache_prefill[layer], req_order, axis=0)]
    slice x0 -> x2, local copies, waits for them, and re-layouts: none -> 5.85 us  [the longest x1 5.17 us: local(): cache_prefill[layer]]
    squeeze x1 -> x0, local copies, waits for them, and re-layouts: 5.18 us -> none  [local(): cache_prefill[layer]]
    all_to_all x0 -> x1, starting transfers between devices: none -> 4.26 us  [local(): lax.all_to_all(dealt_acts, 'req', split_axis=0, concat_axis=1, tiled=True)]
  transfers between devices with their start and end apart: 7 -> 8, of which waited for: 5 -> 5; matrix products, arithmetic and copies ran while one was open for 19% -> 22% of each run, Pallas kernels for 0% -> 0%
where the time goes in v4:
time: 385 us; the launch traced here: 384 us
  waiting for transfers between devices  213 us (55%)
  local copies, waits for them, and re-layouts  65.2 us (17%)
  between operations  29.2 us (8%)
  starting transfers between devices  27.8 us (7%)
  matrix products  26.8 us (7%)
  other arithmetic  21.8 us (6%)
    all_to_all x2, waiting for transfers between devices, head_sum(): lax.all_to_all(partial.astype(jnp.bfloat16).reshape(shape), 'head', split...  88.5 us
    all_gather x1, waiting for transfers between devices, local(): normed_all = lax.all_gather(normed_rows, 'head', axis=2, tiled=True)  72.8 us
    all_gather x1, waiting for transfers between devices, local(): gathered = lax.all_gather(dealt_rows, 'head', axis=2, tiled=True)  47.2 us
    unnamed x67, local copies, waits for them, and re-layouts  28.2 us
    dot_general x1, matrix products, local(): jnp.dot(inner, down_weight, preferred_element_type=jnp.float32)  14.3 us
    all_to_all x2, starting transfers between devices, local(): incoming = lax.all_to_all(outgoing, ('req', 'head'), 0, 0, tiled=True)  11.5 us
  transfers between devices with their start and end apart: 8, of which 5 were waited for; matrix products, arithmetic and copies ran while one was open for 22% of the time, Pallas kernels for 0%

profile of v4, /device:TPU:1, one launch (start us, length us, event | category | flops | bytes accessed | tf_op | source)
XLA Modules:
  0.0 383.8 jit_solution(986323598534315497)
XLA Ops:
  8.0 1.4 gather_fusion
  10.1 1.5 gather_fusion.2
  12.4 4.3 %all-to-all-start = ((bf16[8,8,2048]{2,1,0:T(8,128)(2,1)}), bf16[8,8,2048]{2,1,0:T(8,128)(2,1)S(1)}, u32[]{:S(2)}, u32[]{:S(2)}) async-start(bf16[8,8,2048]{2,1,0:T(8,128)(2,1)} %broadcast_select_fusion.1), calls=%async_computation | async-start | bytes 524288 | tf_op jit(solution)/shard_map/all_to_all | solution.py:112
  27.2 5.2 %fusion.119 = (bf16[1,8,32,32,128]{4,3,2,1,0:T(8,128)(2,1)}, bf16[1,8,32,32,128]{4,3,2,1,0:T(8,128)(2,1)}) fusion(bf16[2,8,32,32,128]{4,3,2,1,0:T(8,128)(2,1)} %param.17), kind=kLoop, calls=%fused_computation.217 | loop fusion | bytes 8388608 | tf_op jit(solution)/shard_map/slice | solution.py:95
  37.2 4.2 %constant_dynamic-slice_fusion = (bf16[1,1,32,32,128]{4,3,2,1,0:T(8,128)(2,1)}, bf16[1,1,32,32,128]{4,3,2,1,0:T(8,128)(2,1)}, bf16[1,1,32,32,128]{4,3,2,1,0:T(8,...) fusion(bf16[1,8,32,32,128]{4,3,2,1,0:T(8,128)(2,1)} %get-tuple-, ...), kind=kLoop, calls=%fused_computation.133 | loop fusion | bytes 8388640 | tf_op jit(solution)/shard_map/jit(dynamic_index_in_dim)/dynamic_slice | solution.py:95
  43.2 1.8 bitcast_dynamic-update-slice_fusion.14
  45.0 1.8 bitcast_dynamic-update-slice_fusion.13
  46.8 1.8 bitcast_dynamic-update-slice_fusion.12
  48.5 1.8 bitcast_dynamic-update-slice_fusion.11
  55.2 1.9 bitcast_dynamic-update-slice_fusion.4
  57.1 1.8 bitcast_dynamic-update-slice_fusion.3
  58.8 1.8 bitcast_dynamic-update-slice_fusion.2
  60.6 1.8 bitcast_dynamic-update-slice_fusion.1
  62.4 1.8 bitcast_dynamic-update-slice_fusion
  64.1 3.3 select_bitcast_fusion
  67.5 1.7 copy.124
  69.2 6.8 %all-to-all-start.1 = ((bf16[32,2,32,4,128]{4,2,3,1,0:T(8,128)(2,1)}), bf16[32,2,32,4,128]{4,2,3,1,0:T(8,128)(2,1)}, u32[]{:S(2)}, u32[]{:S(2)}) async-start(bf16[32,2,32,4,128]{4,2,3,1,0:T(8,128)(2,1)} %bitcast.154), calls=%async_computation.1 | async-start | bytes 4194304 | tf_op jit(solution)/shard_map/all_to_all | solution.py:103
  78.7 1.3 iota_compare_fusion.1
  82.7 0.9 subtract_convert_fusion.1
  83.6 0.9 subtract_convert_fusion
  84.5 47.2 %all-gather.3.cloned.1.call-done = bf16[2,4,64,2048]{3,2,1,0:T(8,128)(2,1)} async-done(((bf16[2,4,8,2048]{3,2,1,0:T(8,128)(2,1)}), bf16[2,4,64,2048]{3,2,1,0:T(8,128)(2,1)}) %all-gather.3.cloned.1.call-update) | async-done | bytes 2097168 | tf_op jit(solution)/shard_map/all_gather | solution.py:115
  131.7 2.1 convert_reduce_fusion
  135.4 1.8 fusion.20
  138.1 4.6 %all-to-all-done.1 = bf16[32,2,32,4,128]{4,2,3,1,0:T(8,128)(2,1)} async-done(((bf16[32,2,32,4,128]{4,2,3,1,0:T(8,128)(2,1)}), bf16[32,2,32,4,128]{4,2,3,1,0:T(8,128)(2,1)}, u32[]{:S(2)}, u32[]{:S(2)}) %all-to-all-start.1) | async-done | bytes 2097184 | tf_op jit(solution)/shard_map/all_to_all | solution.py:103
  142.7 1.1 fusion.120
  144.0 2.0 fusion.124
  146.0 2.9 convolution_convert_fusion.3
  149.0 2.0 fusion.123
  151.0 2.2 convolution_convert_fusion.2
  154.1 1.7 fusion.9
  155.8 1.6 copy.130
  157.4 3.7 all-to-all-start.2
  161.2 47.4 %all-to-all-done.2 = bf16[2,4,8,8,2048]{4,3,1,0,2:T(8,128)(2,1)S(1)} async-done(((bf16[2,4,8,8,2048]{4,3,1,0,2:T(8,128)(2,1)}), bf16[2,4,8,8,2048]{4,3,1,0,2:T(8,128)(2,1)S(1)}, u32[]{:S(2)}, u32[]{:S(2)}) %all-to-all-start.2) | async-done | bytes 2097184 | tf_op jit(solution)/shard_map/all_to_all | solution.py:48
  210.6 2.0 copy.144
  212.6 4.7 %all-to-all-start.5 = ((bf16[32,2,32,4,128]{4,2,3,1,0:T(8,128)(2,1)}), bf16[32,2,32,4,128]{4,2,3,1,0:T(8,128)(2,1)S(1)}, u32[]{:S(2)}, u32[]{:S(2)}) async-start(bf16[32,2,32,4,128]{4,2,3,1,0:T(8,128)(2,1)} %bitcast.156), calls=%async_computation.5 | async-start | bytes 4194304 | tf_op jit(solution)/shard_map/all_to_all | solution.py:103
  217.3 72.8 %all-gather.5.cloned.1.call-done = bf16[2,4,64,2048]{3,2,1,0:T(8,128)(2,1)} async-done(((bf16[2,4,8,2048]{3,2,1,0:T(8,128)(2,1)}), bf16[2,4,64,2048]{3,2,1,0:T(8,128)(2,1)}) %all-gather.5.cloned.1.call-update) | async-done | bytes 2097168 | tf_op jit(solution)/shard_map/all_gather | solution.py:143
  290.1 14.3 %convolution_convert_fusion = bf16[512,2048]{1,0:T(8,128)(2,1)} fusion(bf16[1024,2048]{1,0:T(8,128)(2,1)} %param.27, bf16[512,2048]{1,0:T(8,128)(2,1)} %bitcast.170, bf16[2048,1024]{1,0:T(8,128)(2,1)} %param.26), kind=kOutput, calls=%fused_computation.20 | convolution fusion | flops 4330094592 | bytes 12582912 | tf_op jit(solution)/shard_map/dot_general | solution.py:152
  304.4 3.2 copy.132
  307.5 1.3 copy-done.6
  308.8 3.6 all-to-all-start.3
  312.5 1.0 sort.17
  313.6 3.6 copy.135
  317.2 1.9 copy.145
  319.1 41.1 %all-to-all-done.3 = bf16[2,4,8,8,2048]{4,3,1,0,2:T(8,128)(2,1)S(1)} async-done(((bf16[2,4,8,8,2048]{4,3,1,0,2:T(8,128)(2,1)}), bf16[2,4,8,8,2048]{4,3,1,0,2:T(8,128)(2,1)S(1)}, u32[]{:S(2)}, u32[]{:S(2)}) %all-to-all-start.3) | async-done | bytes 2097184 | tf_op jit(solution)/shard_map/all_to_all | solution.py:48
  361.5 4.7 %all-to-all-start.4 = ((bf16[2,4,8,2048]{3,2,0,1:T(8,128)(2,1)}), bf16[2,4,8,2048]{3,2,0,1:T(8,128)(2,1)S(1)}, u32[]{:S(2)}, u32[]{:S(2)}) async-start(bf16[2,4,8,2048]{3,2,0,1:T(8,128)(2,1)} %copy.134), calls=%async_computation.4 | async-start | bytes 524288 | tf_op jit(solution)/shard_map/all_to_all | solution.py:163
  366.1 2.0 pad_maximum_fusion
  368.4 5.5 %copy.147 = bf16[8,2,256,4,128]{4,3,2,1,0:T(4,128)(2,1)} copy(bf16[8,2,256,4,128]{4,2,3,1,0:T(8,128)(2,1)S(1)} %bitcast.151) | data formatting | bytes 8388608
  374.6 1.5 gather_fusion.4
  (118 shorter events, 23.9 us)
Async XLA Ops:
  7.2 128.2 %copy-start = (bf16[2048,4,192]{0,2,1:T(8,128)(2,1)S(1)}, bf16[2048,4,192]{0,2,1:T(8,128)(2,1)}, u32[]{:S(2)}) copy-start(bf16[2048,4,192]{0,2,1:T(8,128)(2,1)} %param.22) | copy-start | bytes 9437188
  7.2 9.5 %copy-start.22 = (s32[8]{0:T(128)S(1)}, s32[8]{0:T(128)}, u32[]{:S(2)}) copy-start(s32[8]{0:T(128)} %param.20) | copy-start | bytes 100
  12.4 42.0 %all-to-all-start = ((bf16[8,8,2048]{2,1,0:T(8,128)(2,1)}), bf16[8,8,2048]{2,1,0:T(8,128)(2,1)S(1)}, u32[]{:S(2)}, u32[]{:S(2)}) async-start(bf16[8,8,2048]{2,1,0:T(8,128)(2,1)} %broadcast_select_fusion.1), calls=%async_computation | async-start | bytes 524288 | tf_op jit(solution)/shard_map/all_to_all | solution.py:112
  16.7 115.0 %all-gather.3.cloned.1.call-start = ((), (), s32[]{:S(2)}) async-start(), calls=%async_computation.6 | async-start | bytes 2359296 | tf_op jit(solution)/shard_map/all_gather | solution.py:115
  43.1 7.1 %copy-start.16 = (bf16[1,1,32,32,128]{4,3,2,1,0:T(8,128)(2,1)S(1)}, bf16[1,1,32,32,128]{4,3,2,1,0:T(8,128)(2,1)}, u32[]{:S(2)}) copy-start(bf16[1,1,32,32,128]{4,3,2,1,0:T(8,128)(2,1)} %get-tuple-element.61) | copy-start | bytes 786436
  43.1 7.9 %copy-start.15 = (bf16[1,1,32,32,128]{4,3,2,1,0:T(8,128)(2,1)S(1)}, bf16[1,1,32,32,128]{4,3,2,1,0:T(8,128)(2,1)}, u32[]{:S(2)}) copy-start(bf16[1,1,32,32,128]{4,3,2,1,0:T(8,128)(2,1)} %get-tuple-element.62) | copy-start | bytes 786436
  43.1 8.8 %copy-start.14 = (bf16[1,1,32,32,128]{4,3,2,1,0:T(8,128)(2,1)S(1)}, bf16[1,1,32,32,128]{4,3,2,1,0:T(8,128)(2,1)}, u32[]{:S(2)}) copy-start(bf16[1,1,32,32,128]{4,3,2,1,0:T(8,128)(2,1)} %get-tuple-element.63) | copy-start | bytes 786436
  43.2 9.6 %copy-start.13 = (bf16[1,1,32,32,128]{4,3,2,1,0:T(8,128)(2,1)S(1)}, bf16[1,1,32,32,128]{4,3,2,1,0:T(8,128)(2,1)}, u32[]{:S(2)}) copy-start(bf16[1,1,32,32,128]{4,3,2,1,0:T(8,128)(2,1)} %get-tuple-element.24) | copy-start | bytes 786436
  43.2 10.4 %copy-start.12 = (bf16[1,1,32,32,128]{4,3,2,1,0:T(8,128)(2,1)S(1)}, bf16[1,1,32,32,128]{4,3,2,1,0:T(8,128)(2,1)}, u32[]{:S(2)}) copy-start(bf16[1,1,32,32,128]{4,3,2,1,0:T(8,128)(2,1)} %get-tuple-element.23) | copy-start | bytes 786436
  55.2 8.9 %copy-start.9 = (bf16[8,32,32,128]{3,1,2,0:T(8,128)(2,1)S(1)}, bf16[8,32,32,128]{3,1,2,0:T(8,128)(2,1)}, u32[]{:S(2)}) copy-start(bf16[8,32,32,128]{3,1,2,0:T(8,128)(2,1)} %bitcast_dynamic-update-slice_fusion.8) | copy-start | bytes 6291460
  69.1 6.9 %copy-start.2 = (s32[8]{0:T(128)S(1)}, s32[8]{0:T(128)}, u32[]{:S(2)}) copy-start(s32[8]{0:T(128)} %param.19) | copy-start | bytes 100
  69.1 7.5 %copy-start.3 = (s32[8]{0:T(128)S(1)}, s32[8]{0:T(128)}, u32[]{:S(2)}) copy-start(s32[8]{0:T(128)} %param.18) | copy-start | bytes 100
  69.1 8.2 %copy-start.23 = (bf16[2048]{0:T(1024)(128)(2,1)S(1)}, bf16[2048]{0:T(1024)(128)(2,1)}, u32[]{:S(2)}) copy-start(bf16[2048]{0:T(1024)(128)(2,1)} %param.21) | copy-start | bytes 12292
  69.2 73.5 %all-to-all-start.1 = ((bf16[32,2,32,4,128]{4,2,3,1,0:T(8,128)(2,1)}), bf16[32,2,32,4,128]{4,2,3,1,0:T(8,128)(2,1)}, u32[]{:S(2)}, u32[]{:S(2)}) async-start(bf16[32,2,32,4,128]{4,2,3,1,0:T(8,128)(2,1)} %bitcast.154), calls=%async_computation.1 | async-start | bytes 4194304 | tf_op jit(solution)/shard_map/all_to_all | solution.py:103
  131.7 2.2 copy-start.4
  137.2 0.9 copy-start.19
  138.1 5.9 %copy-start.18 = (f32[256,512]{1,0:T(8,128)S(1)}, f32[256,512]{1,0:T(8,128)}, u32[]{:S(2)}) copy-start(f32[256,512]{1,0:T(8,128)} %subtract_convert_fusion.1) | copy-start | bytes 1572868
  138.1 5.9 %copy-start.20 = (pred[256,512]{1,0:T(8,128)(4,1)S(1)}, pred[256,512]{1,0:T(8,128)(4,1)}, u32[]{:S(2)}) copy-start(pred[256,512]{1,0:T(8,128)(4,1)} %get-tuple-element.38) | copy-start | bytes 393220
  138.1 5.9 %copy-start.25 = (f32[4]{0:T(128)S(1)}, f32[4]{0:T(128)}, u32[]{:S(2)}) copy-start(f32[4]{0:T(128)} %param.23) | copy-start | bytes 52
  145.9 3.0 copy-start.17
  151.0 2.3 copy-start.21
  151.0 3.1 copy-start.11
  157.4 3.8 copy-start.24
  157.4 51.2 %all-to-all-start.2 = ((bf16[2,4,8,8,2048]{4,3,1,0,2:T(8,128)(2,1)}), bf16[2,4,8,8,2048]{4,3,1,0,2:T(8,128)(2,1)S(1)}, u32[]{:S(2)}, u32[]{:S(2)}) async-start(bf16[2,4,8,8,2048]{4,3,1,0,2:T(8,128)(2,1)} %copy.130), calls=%async_computation.2 | async-start | bytes 4194304 | tf_op jit(solution)/shard_map/all_to_all | solution.py:48
  161.1 129.0 %all-gather.5.cloned.1.call-start = ((), (), s32[]{:S(2)}) async-start(), calls=%async_computation.7 | async-start | bytes 2359296 | tf_op jit(solution)/shard_map/all_gather | solution.py:143
  208.9 1.7 copy-start.5
  212.6 94.9 %all-to-all-start.5 = ((bf16[32,2,32,4,128]{4,2,3,1,0:T(8,128)(2,1)}), bf16[32,2,32,4,128]{4,2,3,1,0:T(8,128)(2,1)S(1)}, u32[]{:S(2)}, u32[]{:S(2)}) async-start(bf16[32,2,32,4,128]{4,2,3,1,0:T(8,128)(2,1)} %bitcast.156), calls=%async_computation.5 | async-start | bytes 4194304 | tf_op jit(solution)/shard_map/all_to_all | solution.py:103
  307.5 1.3 copy-start.6
  308.8 51.4 %all-to-all-start.3 = ((bf16[2,4,8,8,2048]{4,3,1,0,2:T(8,128)(2,1)}), bf16[2,4,8,8,2048]{4,3,1,0,2:T(8,128)(2,1)S(1)}, u32[]{:S(2)}, u32[]{:S(2)}) async-start(bf16[2,4,8,8,2048]{4,3,1,0,2:T(8,128)(2,1)} %copy.132), calls=%async_computation.3 | async-start | bytes 4194304 | tf_op jit(solution)/shard_map/all_to_all | solution.py:48
  313.6 3.6 copy-start.7
  360.6 5.5 %copy-start.8 = (bf16[4,2,8,32,4,128]{5,3,2,4,1,0:T(8,128)(2,1)S(1)}, bf16[4,2,8,32,4,128]{5,3,2,4,1,0:T(8,128)(2,1)}, u32[]{:S(2)}) copy-start(bf16[4,2,8,32,4,128]{5,3,2,4,1,0:T(8,128)(2,1)} %copy.135) | copy-start | bytes 6291460
  361.5 12.4 %all-to-all-start.4 = ((bf16[2,4,8,2048]{3,2,0,1:T(8,128)(2,1)}), bf16[2,4,8,2048]{3,2,0,1:T(8,128)(2,1)S(1)}, u32[]{:S(2)}, u32[]{:S(2)}) async-start(bf16[2,4,8,2048]{3,2,0,1:T(8,128)(2,1)} %copy.134), calls=%async_computation.4 | async-start | bytes 524288 | tf_op jit(solution)/shard_map/all_to_all | solution.py:163
  368.4 8.5 %copy-start.1 = (bf16[2048,4,192]{0,2,1:T(8,128)(2,1)S(1)}, bf16[2048,4,192]{0,2,1:T(8,128)(2,1)}, u32[]{:S(2)}) copy-start(bf16[2048,4,192]{0,2,1:T(8,128)(2,1)} %param.22) | copy-start | bytes 9437188
  373.9 0.7 copy-start.10
Sparse Core Ops, SparseCore 0:
  55.3 76.3 all-gather.2
  210.3 79.7 all-gather.4

commit v5 on v3

--- a/solution.py
+++ b/solution.py
@@ -98,69 +98,57 @@
         )
         outgoing = (
             dealt_cache.reshape(req_count, group_size, prefix_rows, head_count, heads // head_count, pair_width)
-            .transpose(0, 3, 1, 2, 4, 5)
-            .reshape(devices, group_size, prefix_rows, heads // head_count, pair_width)
+            .transpose(1, 0, 3, 2, 4, 5)
+            .reshape(group_size, devices, 1, prefix_rows, heads // head_count, pair_width)
         )
-        incoming = lax.all_to_all(outgoing, ("req", "head"), 0, 0, tiled=True)
-        chunks.append(
-            incoming.reshape(req_count, head_count, group_size, prefix_rows, heads // head_count, pair_width)
-            .transpose(0, 2, 1, 3, 4, 5)
-            .reshape(req_count, group_size, head_count * prefix_rows, heads // head_count, pair_width)
-        )
-    current = chunks[0][0]
-    relaid = jnp.stack(chunks, axis=1).reshape((req_count * local_layers,) + chunks[0].shape[1:])
+        for member in range(group_size):
+            incoming = lax.all_to_all(outgoing[member], ("req", "head"), 0, 0, tiled=True)
+            chunks.append(
+                incoming.reshape(req_count, head_count * prefix_rows, heads // head_count, pair_width)
+            )
+    relaid = jnp.stack(chunks, axis=1).reshape(
+        (req_count * local_layers, group_size) + chunks[0].shape[1:]
+    )
     dealt_acts = jnp.take(stretch_acts, req_order, axis=0)
     dealt_rows = lax.all_to_all(dealt_acts, "req", split_axis=0, concat_axis=1, tiled=True).reshape(
         group_size, req_count, stretch_rows, features
     )
-    gathered = lax.all_gather(dealt_rows, "head", axis=2, tiled=True)
-    normed = (
-        layer_norm(gathered.astype(jnp.float32), attn_gain)
-        .astype(jnp.bfloat16)
-        .reshape(group_size * stretch_max, features)
-    )
-    mixed = jnp.dot(
-        normed,
-        in_weight.reshape(features, heads_here * 3 * head_dim),
-        preferred_element_type=jnp.float32,
-    )
-    mixed = mixed.reshape(group_size, stretch_max, heads_here, 3 * head_dim).astype(jnp.bfloat16)
-    contexts = []
-    for member in range(group_size):
-        pairs = jnp.concatenate([current[member], mixed[member, :, :, head_dim:]], axis=0)
-        contexts.append(
-            attend(mixed[member, :, :, :head_dim], pairs, member_prefix[member], slopes, head_dim)
-        )
-    context = jnp.concatenate(contexts, axis=0)
-    partial_attn = jnp.dot(
-        context,
-        out_weight.reshape(heads_here * head_dim, features),
-        preferred_element_type=jnp.float32,
-    )
-    partial_attn = partial_attn.reshape(group_size, req_count, span_rows, features)
-    attn_rows = head_sum(partial_attn, head_count, stretch_rows)
-    residual_rows = dealt_rows.astype(jnp.float32) + attn_rows
-    normed_rows = layer_norm(residual_rows, mlp_gain).astype(jnp.bfloat16)
-    normed_all = lax.all_gather(normed_rows, "head", axis=2, tiled=True)
-    inner = jax.nn.gelu(
-        jnp.dot(
-            normed_all.reshape(group_size * stretch_max, features),
-            up_weight,
-            preferred_element_type=jnp.float32,
-        ),
-        approximate=False,
-    ).astype(jnp.bfloat16)
-    partial_mlp = jnp.dot(inner, down_weight, preferred_element_type=jnp.float32).reshape(
-        group_size, req_count, span_rows, features
-    )
-    mlp_rows = head_sum(partial_mlp, head_count, stretch_rows)
     row_number = (
         jnp.arange(req_count, dtype=jnp.int32)[:, None] * head_count + head_index
     ) * stretch_rows + jnp.arange(stretch_rows, dtype=jnp.int32)[None, :]
-    usable = row_number[None] < member_stretch[:, None, None]
-    result = jnp.where(
-        usable[..., None], residual_rows + mlp_rows, jnp.zeros((), jnp.float32)
-    ).astype(jnp.bfloat16)
+    results = []
+    for member in range(group_size):
+        own_rows = dealt_rows[member]
+        gathered = lax.all_gather(own_rows, "head", axis=1, tiled=True)
+        normed = layer_norm(gathered.astype(jnp.float32), attn_gain).astype(jnp.bfloat16).reshape(stretch_max, features)
+        mixed = jnp.dot(
+            normed,
+            in_weight.reshape(features, heads_here * 3 * head_dim),
+            preferred_element_type=jnp.float32,
+        )
+        mixed = mixed.reshape(stretch_max, heads_here, 3 * head_dim).astype(jnp.bfloat16)
+        pairs = jnp.concatenate([chunks[member][0], mixed[:, :, head_dim:]], axis=0)
+        context = attend(mixed[:, :, :head_dim], pairs, member_prefix[member], slopes, head_dim)
+        partial_attn = jnp.dot(
+            context,
+            out_weight.reshape(heads_here * head_dim, features),
+            preferred_element_type=jnp.float32,
+        )
+        attn_rows = head_sum(partial_attn.reshape(1, req_count, span_rows, features), head_count, stretch_rows)[0]
+        residual_rows = own_rows.astype(jnp.float32) + attn_rows
+        normed_rows = layer_norm(residual_rows, mlp_gain).astype(jnp.bfloat16)
+        normed_all = lax.all_gather(normed_rows, "head", axis=1, tiled=True)
+        inner = jax.nn.gelu(
+            jnp.dot(normed_all.reshape(stretch_max, features), up_weight, preferred_element_type=jnp.float32),
+            approximate=False,
+        ).astype(jnp.bfloat16)
+        partial_mlp = jnp.dot(inner, down_weight, preferred_element_type=jnp.float32)
+        mlp_rows = head_sum(partial_mlp.reshape(1, req_count, span_rows, features), head_count, stretch_rows)[0]
+        usable = row_number < member_stretch[member]
+        results.append(
+            jnp.where(usable[..., None], residual_rows + mlp_rows, jnp.zeros((), jnp.float32)).astype(jnp.bfloat16)
+        )
+    result = jnp.stack(results)
     returned = lax.all_to_all(result, "req", split_axis=1, concat_axis=0, tiled=True).reshape(
         requests, stretch_rows, features
     )

time: 355 us -> 388 us (1.093)
  starting transfers between devices: 22.6 us -> 41.7 us
  waiting for transfers between devices: 213 us -> 200 us
  other arithmetic: 21.2 us -> 33.4 us
  local copies, waits for them, and re-layouts: 47.4 us -> 55.3 us
  matrix products: 26.8 us -> 33.2 us
    all_to_all x2 -> x4, waiting for transfers between devices: 88.5 us -> 51.5 us  [head_sum(): lax.all_to_all(partial.astype(jnp.bfloat16).reshape(shape), 'head', split...]
    all_to_all x2 -> x4, waiting for transfers between devices: 16 us -> 34.9 us  [local(): lax.all_to_all(outgoing[member], ('req', 'head'), 0, 0, tiled=True)]
    all_to_all x2 -> x4, starting transfers between devices: 7.34 us -> 17.2 us  [head_sum(): lax.all_to_all(partial.astype(jnp.bfloat16).reshape(shape), 'head', split...]
    all_to_all x2 -> x4, starting transfers between devices: 10.5 us -> 19.6 us  [local(): lax.all_to_all(outgoing[member], ('req', 'head'), 0, 0, tiled=True)]
    transpose x4 -> x0, local copies, waits for them, and re-layouts: 9.06 us -> none  [the longest x2 5.52 us: local(): chunks.append(incoming.reshape(req_count, head_count, group_size, prefix_...]
    slice x4 -> x10, local copies, waits for them, and re-layouts: 1.72 us -> 10.7 us  [the longest x4 7.83 us: local(): outgoing[member]]
    all_to_all x1 -> x4, local copies, waits for them, and re-layouts: 0.72 us -> 7.4 us  [local(): lax.all_to_all(outgoing[member], ('req', 'head'), 0, 0, tiled=True)]
    dot_general x1 -> x2, matrix products: 14.3 us -> 18.6 us  [local(): jnp.dot(inner, down_weight, preferred_element_type=jnp.float32)]
  transfers between devices with their start and end apart: 7 -> 13, of which waited for: 5 -> 9; matrix products, arithmetic and copies ran while one was open for 19% -> 29% of each run, Pallas kernels for 0% -> 0%
where the time goes in v5:
time: 388 us; the launch traced here: 386 us
  waiting for transfers between devices  200 us (52%)
  local copies, waits for them, and re-layouts  55.3 us (14%)
  starting transfers between devices  41.7 us (11%)
  other arithmetic  33.4 us (9%)
  matrix products  33.2 us (9%)
  between operations  14.3 us (4%)
  blocking collectives  9.06 us (2%)
    all_gather x2, waiting for transfers between devices, local(): normed_all = lax.all_gather(normed_rows, 'head', axis=1, tiled=True)  56.4 us
    all_gather x2, waiting for transfers between devices, local(): gathered = lax.all_gather(own_rows, 'head', axis=1, tiled=True)  55.6 us
    all_to_all x4, waiting for transfers between devices, head_sum(): lax.all_to_all(partial.astype(jnp.bfloat16).reshape(shape), 'head', split...  51.5 us
    all_to_all x4, waiting for transfers between devices, local(): lax.all_to_all(outgoing[member], ('req', 'head'), 0, 0, tiled=True)  34.9 us
    all_to_all x4, starting transfers between devices, local(): lax.all_to_all(outgoing[member], ('req', 'head'), 0, 0, tiled=True)  19.6 us
    dot_general x2, matrix products, local(): jnp.dot(inner, down_weight, preferred_element_type=jnp.float32)  18.6 us
    all_to_all x4, starting transfers between devices, head_sum(): lax.all_to_all(partial.astype(jnp.bfloat16).reshape(shape), 'head', split...  17.2 us
    all_to_all x1, blocking collectives, local(): lax.all_to_all(dealt_acts, 'req', split_axis=0, concat_axis=1, tiled=True)  9.06 us
  transfers between devices with their start and end apart: 13, of which 9 were waited for; matrix products, arithmetic and copies ran while one was open for 29% of the time, Pallas kernels for 0%

profile of v5, /device:TPU:1, one launch (start us, length us, event | category | flops | bytes accessed | tf_op | source)
XLA Modules:
  0.0 386.5 jit_solution(13026984027722912634)
XLA Ops:
  10.1 1.5 gather_fusion.2
  11.7 9.1 %all_to_all.70 = bf16[8,8,2048]{2,1,0:T(8,128)(2,1)S(1)} all-to-all(bf16[8,8,2048]{2,1,0:T(8,128)(2,1)S(1)} %broadcast_select_fusion.1), channel_id=1, replica_groups=mesh['req'=4,'head'=8] {'req'}, dimensions={0} | all-to-all | bytes 524288 | tf_op jit(solution)/shard_map/all_to_all | solution.py:113
  21.5 5.2 %slice_bitcast_fusion = (bf16[8,32,32,128]{3,2,1,0:T(8,128)(2,1)}, bf16[8,32,32,128]{3,2,1,0:T(8,128)(2,1)}) fusion(bf16[2,8,32,32,128]{4,3,2,1,0:T(8,128)(2,1)} %param.19), kind=kLoop, calls=%fused_computation.38 | loop fusion | bytes 8388608 | tf_op jit(solution)/shard_map/squeeze | solution.py:96
  26.7 3.7 gather_fusion.6
  30.4 3.8 gather_fusion.3
  34.2 3.5 select_select_fusion
  37.7 2.0 fusion.237
  41.2 5.7 %all-to-all-start.1 = ((bf16[32,1,32,4,128]{4,2,3,1,0:T(8,128)(2,1)}), bf16[32,1,32,4,128]{4,2,3,1,0:T(8,128)(2,1)}, u32[]{:S(2)}, u32[]{:S(2)}) async-start(bf16[32,1,32,4,128]{4,2,3,1,0:T(8,128)(2,1)} %bitcast.169), calls=%async_computation.1 | async-start | bytes 2097152 | tf_op jit(solution)/shard_map/all_to_all | solution.py:105
  49.8 2.7 copy.65
  56.9 16.8 %all-gather.13.cloned.1.call-done = bf16[1,4,64,2048]{3,2,0,1:T(8,128)(2,1)} async-done(((bf16[1,4,8,2048]{3,2,0,1:T(8,128)(2,1)}), bf16[1,4,64,2048]{3,2,0,1:T(8,128)(2,1)}) %all-gather.13.cloned.1.call-update) | async-done | bytes 1048592 | tf_op jit(solution)/shard_map/all_gather | solution.py:122
  73.7 1.4 convert_reduce_fusion
  75.2 38.8 %all-gather.11.cloned.1.call-done = bf16[1,4,64,2048]{3,2,1,0:T(8,128)(2,1)} async-done(((bf16[1,4,8,2048]{3,2,1,0:T(8,128)(2,1)}), bf16[1,4,64,2048]{3,2,1,0:T(8,128)(2,1)}) %all-gather.11.cloned.1.call-update) | async-done | bytes 1048592 | tf_op jit(solution)/shard_map/all_gather | solution.py:122
  115.4 2.2 fusion.17
  117.6 4.8 %all-to-all-start.4 = ((bf16[32,1,32,4,128]{4,2,3,1,0:T(8,128)(2,1)}), bf16[32,1,32,4,128]{4,2,3,1,0:T(8,128)(2,1)}, u32[]{:S(2)}, u32[]{:S(2)}) async-start(bf16[32,1,32,4,128]{4,2,3,1,0:T(8,128)(2,1)} %bitcast.170), calls=%async_computation.4 | async-start | bytes 2097152 | tf_op jit(solution)/shard_map/all_to_all | solution.py:105
  122.5 1.6 fusion.11
  124.8 3.2 fusion.19
  132.7 1.8 copy.60
  134.5 2.3 fusion.241
  136.8 2.6 fusion.26
  140.3 1.8 fusion.6
  143.2 6.4 %all-to-all-done.4 = bf16[32,1,32,4,128]{4,2,3,1,0:T(8,128)(2,1)} async-done(((bf16[32,1,32,4,128]{4,2,3,1,0:T(8,128)(2,1)}), bf16[32,1,32,4,128]{4,2,3,1,0:T(8,128)(2,1)}, u32[]{:S(2)}, u32[]{:S(2)}) %all-to-all-start.4) | async-done | bytes 1048608 | tf_op jit(solution)/shard_map/all_to_all | solution.py:105
  149.5 4.4 %all-to-all-start.2 = ((bf16[1,4,8,8,2048]{4,3,1,0,2:T(8,128)(2,1)}), bf16[1,4,8,8,2048]{4,3,1,0,2:T(8,128)(2,1)}, u32[]{:S(2)}, u32[]{:S(2)}) async-start(bf16[1,4,8,8,2048]{4,3,1,0,2:T(8,128)(2,1)} %copy.62), calls=%async_computation.2 | async-start | bytes 2097152 | tf_op jit(solution)/shard_map/all_to_all | solution.py:48
  156.3 2.2 fusion.23
  158.5 1.5 copy.66
  160.2 2.0 fusion.244
  162.2 2.3 fusion.27
  166.3 12.5 %all-to-all-done.2 = bf16[1,4,8,8,2048]{4,3,1,0,2:T(8,128)(2,1)} async-done(((bf16[1,4,8,8,2048]{4,3,1,0,2:T(8,128)(2,1)}), bf16[1,4,8,8,2048]{4,3,1,0,2:T(8,128)(2,1)}, u32[]{:S(2)}, u32[]{:S(2)}) %all-to-all-start.2) | async-done | bytes 1048608 | tf_op jit(solution)/shard_map/all_to_all | solution.py:48
  178.8 4.5 %all-to-all-start.5 = ((bf16[1,4,8,8,2048]{4,3,1,0,2:T(8,128)(2,1)}), bf16[1,4,8,8,2048]{4,3,1,0,2:T(8,128)(2,1)}, u32[]{:S(2)}, u32[]{:S(2)}) async-start(bf16[1,4,8,8,2048]{4,3,1,0,2:T(8,128)(2,1)} %copy.69), calls=%async_computation.5 | async-start | bytes 2097152 | tf_op jit(solution)/shard_map/all_to_all | solution.py:48
  184.2 1.8 fusion.236
  187.5 20.6 %all-to-all-done.5 = bf16[1,4,8,8,2048]{4,3,1,0,2:T(8,128)(2,1)} async-done(((bf16[1,4,8,8,2048]{4,3,1,0,2:T(8,128)(2,1)}), bf16[1,4,8,8,2048]{4,3,1,0,2:T(8,128)(2,1)}, u32[]{:S(2)}, u32[]{:S(2)}) %all-to-all-start.5) | async-done | bytes 1048608 | tf_op jit(solution)/shard_map/all_to_all | solution.py:48
  208.1 5.4 %all-to-all-start.8 = ((bf16[32,1,32,4,128]{4,2,3,1,0:T(8,128)(2,1)}), bf16[32,1,32,4,128]{4,2,3,1,0:T(8,128)(2,1)S(1)}, u32[]{:S(2)}, u32[]{:S(2)}) async-start(bf16[32,1,32,4,128]{4,2,3,1,0:T(8,128)(2,1)} %bitcast.172), calls=%async_computation.8 | async-start | bytes 2097152 | tf_op jit(solution)/shard_map/all_to_all | solution.py:105
  216.2 28.5 %all-to-all-done.8 = bf16[32,1,32,4,128]{4,2,3,1,0:T(8,128)(2,1)S(1)} async-done(((bf16[32,1,32,4,128]{4,2,3,1,0:T(8,128)(2,1)}), bf16[32,1,32,4,128]{4,2,3,1,0:T(8,128)(2,1)S(1)}, u32[]{:S(2)}, u32[]{:S(2)}) %all-to-all-start.8) | async-done | bytes 1048608 | tf_op jit(solution)/shard_map/all_to_all | solution.py:105
  244.7 3.8 all-to-all-start.9
  249.0 20.2 %all-gather.9.cloned.1.call-done = bf16[4,64,2048]{2,1,0:T(8,128)(2,1)} async-done(((bf16[4,8,2048]{2,1,0:T(8,128)(2,1)}), bf16[4,64,2048]{2,1,0:T(8,128)(2,1)}) %all-gather.9.cloned.1.call-update) | async-done | bytes 1048592 | tf_op jit(solution)/shard_map/all_gather | solution.py:140
  269.3 9.3 %convolution_convert_fusion = bf16[256,2048]{1,0:T(8,128)(2,1)} fusion(bf16[1024,2048]{1,0:T(8,128)(2,1)} %param.29, bf16[256,2048]{1,0:T(8,128)(2,1)} %bitcast.182, bf16[2048,1024]{1,0:T(8,128)(2,1)} %param.28), kind=kOutput, calls=%fused_computation.18 | convolution fusion | flops 2165047296 | bytes 10485760 | tf_op jit(solution)/shard_map/dot_general | solution.py:145
  278.6 2.4 copy.70
  280.9 4.0 %all-to-all-start.6 = ((bf16[1,4,8,8,2048]{4,3,1,0,2:T(8,128)(2,1)}), bf16[1,4,8,8,2048]{4,3,1,0,2:T(8,128)(2,1)S(1)}, u32[]{:S(2)}, u32[]{:S(2)}) async-start(bf16[1,4,8,8,2048]{4,3,1,0,2:T(8,128)(2,1)} %copy.70), calls=%async_computation.6 | async-start | bytes 2097152 | tf_op jit(solution)/shard_map/all_to_all | solution.py:48
  284.9 36.2 %all-gather.7.cloned.1.call-done = bf16[4,64,2048]{2,1,0:T(8,128)(2,1)} async-done(((bf16[4,8,2048]{2,1,0:T(8,128)(2,1)}), bf16[4,64,2048]{2,1,0:T(8,128)(2,1)}) %all-gather.7.cloned.1.call-update) | async-done | bytes 1048592 | tf_op jit(solution)/shard_map/all_gather | solution.py:140
  321.1 9.3 %convolution_convert_fusion.2 = bf16[256,2048]{1,0:T(8,128)(2,1)} fusion(bf16[1024,2048]{1,0:T(8,128)(2,1)} %param.29, bf16[256,2048]{1,0:T(8,128)(2,1)} %bitcast.183, bf16[2048,1024]{1,0:T(8,128)(2,1)} %param.28), kind=kOutput, calls=%fused_computation.20 | convolution fusion | flops 2165047296 | bytes 10485760 | tf_op jit(solution)/shard_map/dot_general | solution.py:145
  330.4 2.3 copy.63
  332.7 4.2 %all-to-all-start.3 = ((bf16[1,4,8,8,2048]{4,3,1,0,2:T(8,128)(2,1)}), bf16[1,4,8,8,2048]{4,3,1,0,2:T(8,128)(2,1)}, u32[]{:S(2)}, u32[]{:S(2)}) async-start(bf16[1,4,8,8,2048]{4,3,1,0,2:T(8,128)(2,1)} %copy.63), calls=%async_computation.3 | async-start | bytes 2097152 | tf_op jit(solution)/shard_map/all_to_all | solution.py:48
  339.3 2.3 copy.75
  341.6 2.3 copy.76
  344.0 18.3 %all-to-all-done.3 = bf16[1,4,8,8,2048]{4,3,1,0,2:T(8,128)(2,1)} async-done(((bf16[1,4,8,8,2048]{4,3,1,0,2:T(8,128)(2,1)}), bf16[1,4,8,8,2048]{4,3,1,0,2:T(8,128)(2,1)}, u32[]{:S(2)}, u32[]{:S(2)}) %all-to-all-start.3) | async-done | bytes 1048608 | tf_op jit(solution)/shard_map/all_to_all | solution.py:48
  364.6 4.7 %all-to-all-start.7 = ((bf16[2,4,8,2048]{3,2,0,1:T(8,128)(2,1)}), bf16[2,4,8,2048]{3,2,0,1:T(8,128)(2,1)S(1)}, u32[]{:S(2)}, u32[]{:S(2)}) async-start(bf16[2,4,8,2048]{3,2,0,1:T(8,128)(2,1)} %copy.71), calls=%async_computation.7 | async-start | bytes 524288 | tf_op jit(solution)/shard_map/all_to_all | solution.py:152
  369.3 1.8 pad_maximum_fusion
  371.4 5.5 %copy.78 = bf16[8,2,256,4,128]{4,3,2,1,0:T(4,128)(2,1)} copy(bf16[8,2,256,4,128]{4,2,3,1,0:T(8,128)(2,1)S(1)} %bitcast.156) | data formatting | bytes 8388608
  377.6 1.5 gather_fusion.5
  (122 shorter events, 37.7 us)
Async XLA Ops:
  7.2 120.8 %copy-start = (bf16[2048,4,192]{0,2,1:T(8,128)(2,1)S(1)}, bf16[2048,4,192]{0,2,1:T(8,128)(2,1)}, u32[]{:S(2)}) copy-start(bf16[2048,4,192]{0,2,1:T(8,128)(2,1)} %param.24) | copy-start | bytes 9437188
  7.2 66.5 %all-gather.13.cloned.1.call-start = ((), (), s32[]{:S(2)}) async-start(), calls=%async_computation.13 | async-start | bytes 1179648 | tf_op jit(solution)/shard_map/all_gather | solution.py:122
  39.7 7.9 %copy-start.17 = (s32[8]{0:T(128)S(1)}, s32[8]{0:T(128)}, u32[]{:S(2)}) copy-start(s32[8]{0:T(128)} %param.22) | copy-start | bytes 100
  39.7 8.0 %copy-start.2 = (s32[8]{0:T(128)S(1)}, s32[8]{0:T(128)}, u32[]{:S(2)}) copy-start(s32[8]{0:T(128)} %param.21) | copy-start | bytes 100
  39.7 8.6 %copy-start.3 = (s32[8]{0:T(128)S(1)}, s32[8]{0:T(128)}, u32[]{:S(2)}) copy-start(s32[8]{0:T(128)} %param.20) | copy-start | bytes 100
  41.2 8.6 %copy-start.15 = (bf16[2048]{0:T(1024)(128)(2,1)S(1)}, bf16[2048]{0:T(1024)(128)(2,1)}, u32[]{:S(2)}) copy-start(bf16[2048]{0:T(1024)(128)(2,1)} %param.23) | copy-start | bytes 12292
  41.2 76.5 %all-to-all-start.1 = ((bf16[32,1,32,4,128]{4,2,3,1,0:T(8,128)(2,1)}), bf16[32,1,32,4,128]{4,2,3,1,0:T(8,128)(2,1)}, u32[]{:S(2)}, u32[]{:S(2)}) async-start(bf16[32,1,32,4,128]{4,2,3,1,0:T(8,128)(2,1)} %bitcast.169), calls=%async_computation.1 | async-start | bytes 2097152 | tf_op jit(solution)/shard_map/all_to_all | solution.py:105
  46.9 67.1 %all-gather.11.cloned.1.call-start = ((), (), s32[]{:S(2)}) async-start(), calls=%async_computation.12 | async-start | bytes 1179648 | tf_op jit(solution)/shard_map/all_gather | solution.py:122
  56.0 78.5 %copy-start.14 = (pred[256,512]{1,0:T(8,128)(4,1)}, pred[256,512]{1,0:T(8,128)(4,1)S(1)}, u32[]{:S(2)}) copy-start(pred[256,512]{1,0:T(8,128)(4,1)S(1)} %get-tuple-element.32) | copy-start | bytes 393220
  117.6 31.9 %all-to-all-start.4 = ((bf16[32,1,32,4,128]{4,2,3,1,0:T(8,128)(2,1)}), bf16[32,1,32,4,128]{4,2,3,1,0:T(8,128)(2,1)}, u32[]{:S(2)}, u32[]{:S(2)}) async-start(bf16[32,1,32,4,128]{4,2,3,1,0:T(8,128)(2,1)} %bitcast.170), calls=%async_computation.4 | async-start | bytes 2097152 | tf_op jit(solution)/shard_map/all_to_all | solution.py:105
  129.0 3.8 copy-start.12
  129.0 5.6 %copy-start.19 = (f32[4]{0:T(128)S(1)}, f32[4]{0:T(128)}, u32[]{:S(2)}) copy-start(f32[4]{0:T(128)} %param.25) | copy-start | bytes 52
  131.0 1.0 copy-start.5
  149.5 29.3 %all-to-all-start.2 = ((bf16[1,4,8,8,2048]{4,3,1,0,2:T(8,128)(2,1)}), bf16[1,4,8,8,2048]{4,3,1,0,2:T(8,128)(2,1)}, u32[]{:S(2)}, u32[]{:S(2)}) async-start(bf16[1,4,8,8,2048]{4,3,1,0,2:T(8,128)(2,1)} %copy.62), calls=%async_computation.2 | async-start | bytes 2097152 | tf_op jit(solution)/shard_map/all_to_all | solution.py:48
  158.5 1.6 copy-start.11
  158.5 1.7 copy-start.10
  158.5 1.7 copy-start.13
  162.2 2.5 copy-start.7
  165.2 18.2 %copy-start.16 = (bf16[2048]{0:T(1024)(128)(2,1)S(1)}, bf16[2048]{0:T(1024)(128)(2,1)}, u32[]{:S(2)}) copy-start(bf16[2048]{0:T(1024)(128)(2,1)} %param.27) | copy-start | bytes 12292
  165.2 18.2 %copy-start.4 = (bf16[8,32,32,128]{3,2,1,0:T(8,128)(2,1)S(1)}, bf16[8,32,32,128]{3,2,1,0:T(8,128)(2,1)}, u32[]{:S(2)}) copy-start(bf16[8,32,32,128]{3,2,1,0:T(8,128)(2,1)} %get-tuple-element.33) | copy-start | bytes 6291460
  178.8 29.3 %all-to-all-start.5 = ((bf16[1,4,8,8,2048]{4,3,1,0,2:T(8,128)(2,1)}), bf16[1,4,8,8,2048]{4,3,1,0,2:T(8,128)(2,1)}, u32[]{:S(2)}, u32[]{:S(2)}) async-start(bf16[1,4,8,8,2048]{4,3,1,0,2:T(8,128)(2,1)} %copy.69), calls=%async_computation.5 | async-start | bytes 2097152 | tf_op jit(solution)/shard_map/all_to_all | solution.py:48
  208.1 36.6 %all-to-all-start.8 = ((bf16[32,1,32,4,128]{4,2,3,1,0:T(8,128)(2,1)}), bf16[32,1,32,4,128]{4,2,3,1,0:T(8,128)(2,1)S(1)}, u32[]{:S(2)}, u32[]{:S(2)}) async-start(bf16[32,1,32,4,128]{4,2,3,1,0:T(8,128)(2,1)} %bitcast.172), calls=%async_computation.8 | async-start | bytes 2097152 | tf_op jit(solution)/shard_map/all_to_all | solution.py:105
  213.5 55.8 %all-gather.9.cloned.1.call-start = ((), (), s32[]{:S(2)}) async-start(), calls=%async_computation.11 | async-start | bytes 1179648 | tf_op jit(solution)/shard_map/all_gather | solution.py:140
  244.7 33.8 %copy-start.8 = (bf16[32,1,32,4,128]{4,2,3,1,0:T(8,128)(2,1)}, bf16[32,1,32,4,128]{4,2,3,1,0:T(8,128)(2,1)S(1)}, u32[]{:S(2)}) copy-start(bf16[32,1,32,4,128]{4,2,3,1,0:T(8,128)(2,1)S(1)} %all-to-all-done.8) | copy-start | bytes 3145732
  244.7 36.2 %all-to-all-start.9 = ((bf16[32,1,32,4,128]{4,2,3,1,0:T(8,128)(2,1)}), bf16[32,1,32,4,128]{4,2,3,1,0:T(8,128)(2,1)}, u32[]{:S(2)}, u32[]{:S(2)}) async-start(bf16[32,1,32,4,128]{4,2,3,1,0:T(8,128)(2,1)} %bitcast.171), calls=%async_computation.9 | async-start | bytes 2097152 | tf_op jit(solution)/shard_map/all_to_all | solution.py:105
  248.5 72.6 %all-gather.7.cloned.1.call-start = ((), (), s32[]{:S(2)}) async-start(), calls=%async_computation.10 | async-start | bytes 1179648 | tf_op jit(solution)/shard_map/all_gather | solution.py:140
  280.9 51.8 %all-to-all-start.6 = ((bf16[1,4,8,8,2048]{4,3,1,0,2:T(8,128)(2,1)}), bf16[1,4,8,8,2048]{4,3,1,0,2:T(8,128)(2,1)S(1)}, u32[]{:S(2)}, u32[]{:S(2)}) async-start(bf16[1,4,8,8,2048]{4,3,1,0,2:T(8,128)(2,1)} %copy.70), calls=%async_computation.6 | async-start | bytes 2097152 | tf_op jit(solution)/shard_map/all_to_all | solution.py:48
  330.4 6.6 %copy-start.18 = (s32[8]{0:T(128)S(1)}, s32[8]{0:T(128)}, u32[]{:S(2)}) copy-start(s32[8]{0:T(128)} %param.22) | copy-start | bytes 100
  332.7 29.7 %all-to-all-start.3 = ((bf16[1,4,8,8,2048]{4,3,1,0,2:T(8,128)(2,1)}), bf16[1,4,8,8,2048]{4,3,1,0,2:T(8,128)(2,1)}, u32[]{:S(2)}, u32[]{:S(2)}) async-start(bf16[1,4,8,8,2048]{4,3,1,0,2:T(8,128)(2,1)} %copy.63), calls=%async_computation.3 | async-start | bytes 2097152 | tf_op jit(solution)/shard_map/all_to_all | solution.py:48
  344.0 25.3 %copy-start.6 = (bf16[32,1,32,4,128]{4,2,0,3,1:T(8,128)(2,1)S(1)}, bf16[32,1,32,4,128]{4,2,0,3,1:T(8,128)(2,1)}, u32[]{:S(2)}) copy-start(bf16[32,1,32,4,128]{4,2,0,3,1:T(8,128)(2,1)} %copy-done.5) | copy-start | bytes 3145732
  364.6 12.3 %all-to-all-start.7 = ((bf16[2,4,8,2048]{3,2,0,1:T(8,128)(2,1)}), bf16[2,4,8,2048]{3,2,0,1:T(8,128)(2,1)S(1)}, u32[]{:S(2)}, u32[]{:S(2)}) async-start(bf16[2,4,8,2048]{3,2,0,1:T(8,128)(2,1)} %copy.71), calls=%async_computation.7 | async-start | bytes 524288 | tf_op jit(solution)/shard_map/all_to_all | solution.py:152
  371.4 8.5 %copy-start.1 = (bf16[2048,4,192]{0,2,1:T(8,128)(2,1)S(1)}, bf16[2048,4,192]{0,2,1:T(8,128)(2,1)}, u32[]{:S(2)}) copy-start(bf16[2048,4,192]{0,2,1:T(8,128)(2,1)} %param.24) | copy-start | bytes 9437188
  376.9 0.7 copy-start.9
Sparse Core Ops, SparseCore 0:
  21.6 52.0 all-gather.12
  75.9 38.0 all-gather.10
  216.5 52.7 all-gather.8
  271.9 49.1 all-gather.6

commit v6 on v3

--- a/solution.py
+++ b/solution.py
@@ -138,10 +138,10 @@
         preferred_element_type=jnp.float32,
     )
     partial_attn = partial_attn.reshape(group_size, req_count, span_rows, features)
-    attn_rows = head_sum(partial_attn, head_count, stretch_rows)
-    residual_rows = dealt_rows.astype(jnp.float32) + attn_rows
-    normed_rows = layer_norm(residual_rows, mlp_gain).astype(jnp.bfloat16)
-    normed_all = lax.all_gather(normed_rows, "head", axis=2, tiled=True)
+    attn_all = lax.psum(partial_attn.astype(jnp.bfloat16), "head").astype(jnp.float32)
+    residual_all = gathered.astype(jnp.float32) + attn_all
+    normed_all = layer_norm(residual_all, mlp_gain).astype(jnp.bfloat16)
+    residual_rows = lax.dynamic_slice_in_dim(residual_all, head_index * stretch_rows, stretch_rows, axis=2)
     inner = jax.nn.gelu(
         jnp.dot(
             normed_all.reshape(group_size * stretch_max, features),
@@ -154,6 +154,7 @@
         group_size, req_count, span_rows, features
     )
     mlp_rows = head_sum(partial_mlp, head_count, stretch_rows)
+    relaid, mlp_rows = lax.optimization_barrier((relaid, mlp_rows))
     row_number = (
         jnp.arange(req_count, dtype=jnp.int32)[:, None] * head_count + head_index
     ) * stretch_rows + jnp.arange(stretch_rows, dtype=jnp.int32)[None, :]

time: 355 us -> 355 us (level)
  other arithmetic: 21.2 us -> 25.7 us
    psum x0 -> x1, waiting for transfers between devices: none -> 124 us  [local(): lax.psum(partial_attn.astype(jnp.bfloat16), 'head').astype(jnp.float32)]
    all_gather x1 -> x0, waiting for transfers between devices: 72.8 us -> none  [local(): normed_all = lax.all_gather(normed_rows, 'head', axis=2, tiled=True)]
    all_to_all x2 -> x1, waiting for transfers between devices: 88.5 us -> 39.4 us  [head_sum(): lax.all_to_all(partial.astype(jnp.bfloat16).reshape(shape), 'head', split...]
    add x0 -> x1, other arithmetic: none -> 4.29 us  [local(): residual_all = gathered.astype(jnp.float32) + attn_all]
    all_to_all x2 -> x1, starting transfers between devices: 7.34 us -> 4.34 us  [head_sum(): lax.all_to_all(partial.astype(jnp.bfloat16).reshape(shape), 'head', split...]
    unnamed x41 -> x35, local copies, waits for them, and re-layouts: 9.04 us -> 9.66 us
  transfers between devices with their start and end apart: 7 -> 6, of which waited for: 5 -> 4; matrix products, arithmetic and copies ran while one was open for 19% -> 20% of each run, Pallas kernels for 0% -> 0%
where the time goes in v6:
time: 355 us; the launch traced here: 354 us
  waiting for transfers between devices  215 us (61%)
  local copies, waits for them, and re-layouts  45 us (13%)
  other arithmetic  25.7 us (7%)
  matrix products  25.1 us (7%)
  starting transfers between devices  19.7 us (6%)
  between operations  14.4 us (4%)
  blocking collectives  9.06 us (3%)
    psum x1, waiting for transfers between devices, local(): lax.psum(partial_attn.astype(jnp.bfloat16), 'head').astype(jnp.float32)  124 us
    all_to_all x1, waiting for transfers between devices, head_sum(): lax.all_to_all(partial.astype(jnp.bfloat16).reshape(shape), 'head', split...  39.4 us
    all_gather x1, waiting for transfers between devices, local(): gathered = lax.all_gather(dealt_rows, 'head', axis=2, tiled=True)  36.1 us
    all_to_all x2, waiting for transfers between devices, local(): incoming = lax.all_to_all(outgoing, ('req', 'head'), 0, 0, tiled=True)  16 us
    dot_general x1, matrix products, local(): jnp.dot(inner, down_weight, preferred_element_type=jnp.float32)  12.9 us
    all_to_all x2, starting transfers between devices, local(): incoming = lax.all_to_all(outgoing, ('req', 'head'), 0, 0, tiled=True)  9.96 us
    unnamed x35, local copies, waits for them, and re-layouts  9.66 us
    all_to_all x1, blocking collectives, local(): lax.all_to_all(dealt_acts, 'req', split_axis=0, concat_axis=1, tiled=True)  9.06 us
  transfers between devices with their start and end apart: 6, of which 4 were waited for; matrix products, arithmetic and copies ran while one was open for 20% of the time, Pallas kernels for 0%

profile of v6, /device:TPU:1, one launch (start us, length us, event | category | flops | bytes accessed | tf_op | source)
XLA Modules:
  0.0 354.3 jit_solution(11144420402726880255)
XLA Ops:
  7.2 0.8 compare_select_fusion.1
  8.0 1.4 gather_fusion
  10.1 1.5 gather_fusion.2
  11.7 9.1 %all_to_all.45 = bf16[8,8,2048]{2,1,0:T(8,128)(2,1)S(1)} all-to-all(bf16[8,8,2048]{2,1,0:T(8,128)(2,1)S(1)} %broadcast_select_fusion.1), channel_id=1, replica_groups=mesh['req'=4,'head'=8] {'req'}, dimensions={0} | all-to-all | bytes 524288 | tf_op jit(solution)/shard_map/all_to_all | solution.py:113
  20.8 0.7 copy.72
  21.5 5.2 %slice_bitcast_fusion.1 = (bf16[8,32,32,128]{3,2,1,0:T(8,128)(2,1)}, bf16[8,32,32,128]{3,2,1,0:T(8,128)(2,1)}) fusion(bf16[2,8,32,32,128]{4,3,2,1,0:T(8,128)(2,1)} %param.19), kind=kLoop, calls=%fused_computation.51 | loop fusion | bytes 8388608 | tf_op jit(solution)/shard_map/squeeze | solution.py:96
  26.7 3.7 %gather_fusion.3 = bf16[8,32,32,128]{3,2,1,0:T(8,128)(2,1)} fusion(bf16[8,32,32,128]{3,2,1,0:T(8,128)(2,1)} %get-tuple-element.21, s32[1024]{0:T(1024)S(1)} %pad_clamp_fusion.1), kind=kCustom, calls=%fused_computation.2.clone | custom fusion | bytes 4194336 | tf_op jit(solution)/shard_map/jit(_take)/gather | solution.py:96
  30.4 3.8 %gather_fusion.5 = bf16[8,32,32,128]{3,2,1,0:T(8,128)(2,1)} fusion(bf16[8,32,32,128]{3,2,1,0:T(8,128)(2,1)} %get-tuple-element.22, s32[1024]{0:T(1024)S(1)} %pad_clamp_fusion.1), kind=kCustom, calls=%fused_computation.5.clone | custom fusion | bytes 4194336 | tf_op jit(solution)/shard_map/jit(_take)/gather | solution.py:96
  34.3 3.5 select_select_fusion.1
  37.8 0.8 copy.54
  38.6 1.8 copy.55
  40.4 5.7 %all-to-all-start.1 = ((bf16[32,2,32,4,128]{4,2,3,1,0:T(8,128)(2,1)}), bf16[32,2,32,4,128]{4,2,3,1,0:T(8,128)(2,1)}, u32[]{:S(2)}, u32[]{:S(2)}) async-start(bf16[32,2,32,4,128]{4,2,3,1,0:T(8,128)(2,1)} %bitcast.101), calls=%async_computation.1 | async-start | bytes 4194304 | tf_op jit(solution)/shard_map/all_to_all | solution.py:104
  49.1 1.2 iota_compare_fusion.1
  52.3 0.9 subtract_convert_fusion
  53.2 0.9 subtract_convert_fusion.1
  54.1 36.1 %all-gather.2.cloned.1.call-done = bf16[2,4,64,2048]{3,2,1,0:T(8,128)(2,1)} async-done(((bf16[2,4,8,2048]{3,2,1,0:T(8,128)(2,1)}), bf16[2,4,64,2048]{3,2,1,0:T(8,128)(2,1)}) %all-gather.2.cloned.1.call-update) | async-done | bytes 2097168 | tf_op jit(solution)/shard_map/all_gather | solution.py:116
  90.1 2.1 convert_reduce_fusion
  93.1 0.7 fusion.6
  93.8 1.8 fusion.19
  95.6 0.9 copy-done.12
  96.6 16.0 %all-to-all-done.1 = bf16[32,2,32,4,128]{4,2,3,1,0:T(8,128)(2,1)} async-done(((bf16[32,2,32,4,128]{4,2,3,1,0:T(8,128)(2,1)}), bf16[32,2,32,4,128]{4,2,3,1,0:T(8,128)(2,1)}, u32[]{:S(2)}, u32[]{:S(2)}) %all-to-all-start.1) | async-done | bytes 2097184 | tf_op jit(solution)/shard_map/all_to_all | solution.py:104
  112.5 1.1 fusion.118
  113.8 2.0 fusion.120
  115.8 2.2 convolution_convert_fusion.2
  118.2 2.0 fusion.121
  120.2 2.2 convolution_convert_fusion.3
  122.6 2.0 convolution_convert_fusion.1
  124.6 0.8 copy.62
  125.4 1.8 copy.63
  127.2 4.2 %all-to-all-start.2 = ((bf16[32,2,32,4,128]{4,2,3,1,0:T(8,128)(2,1)}), bf16[32,2,32,4,128]{4,2,3,1,0:T(8,128)(2,1)}, u32[]{:S(2)}, u32[]{:S(2)}) async-start(bf16[32,2,32,4,128]{4,2,3,1,0:T(8,128)(2,1)} %bitcast.102), calls=%async_computation.2 | async-start | bytes 4194304 | tf_op jit(solution)/shard_map/all_to_all | solution.py:104
  131.5 123.8 %all-reduce.2.cloned.1.call-done = bf16[2,4,64,2048]{3,2,1,0:T(8,128)(2,1)} async-done(((bf16[2,4,64,2048]{3,2,1,0:T(8,128)(2,1)}), bf16[2,4,64,2048]{3,2,1,0:T(8,128)(2,1)}) %all-reduce.2.cloned.1.call-update) | async-done | bytes 2097168 | tf_op jit(solution)/shard_map/psum | solution.py:141
  255.3 4.3 %convert_add_fusion = (f32[2,4,64,2048]{3,2,1,0:T(8,128)}, f32[2,4,64]{2,1,0:T(4,128)S(1)}) fusion(bf16[2,4,64,2048]{3,2,1,0:T(8,128)(2,1)S(1)} %copy-done.5, bf16[2,4,64,2048]{3,2,1,0:T(8,128)(2,1)} %all-reduce.2.cloned.1.call-done), kind=kLoop, calls=%fused_computation.9 | loop fusion | flops 4193792 | bytes 8390656 | tf_op jit(solution)/shard_map/add | solution.py:142
  259.6 0.9 multiply_reduce_fusion
  260.6 2.2 multiply_convert_fusion
  262.8 12.9 %convolution_convert_fusion = bf16[512,2048]{1,0:T(8,128)(2,1)S(1)} fusion(bf16[1024,2048]{1,0:T(8,128)(2,1)} %param.29, bf16[512,2048]{1,0:T(8,128)(2,1)} %bitcast.107, bf16[2048,1024]{1,0:T(8,128)(2,1)} %param.28), kind=kOutput, calls=%fused_computation.24 | convolution fusion | flops 4330094592 | bytes 12582912 | tf_op jit(solution)/shard_map/dot_general | solution.py:153
  275.7 1.6 copy.66
  277.4 4.3 %all-to-all-start.3 = ((bf16[2,4,8,8,2048]{4,3,1,0,2:T(8,128)(2,1)}), bf16[2,4,8,8,2048]{4,3,1,0,2:T(8,128)(2,1)S(1)}, u32[]{:S(2)}, u32[]{:S(2)}) async-start(bf16[2,4,8,8,2048]{4,3,1,0,2:T(8,128)(2,1)} %copy.66), calls=%async_computation.3 | async-start | bytes 4194304 | tf_op jit(solution)/shard_map/all_to_all | solution.py:48
  281.7 1.0 sort.17
  282.8 2.2 copy.61
  285.0 2.2 copy.64
  287.5 2.2 copy.65
  289.7 39.4 %all-to-all-done.3 = bf16[2,4,8,8,2048]{4,3,1,0,2:T(8,128)(2,1)S(1)} async-done(((bf16[2,4,8,8,2048]{4,3,1,0,2:T(8,128)(2,1)}), bf16[2,4,8,8,2048]{4,3,1,0,2:T(8,128)(2,1)S(1)}, u32[]{:S(2)}, u32[]{:S(2)}) %all-to-all-start.3) | async-done | bytes 2097184 | tf_op jit(solution)/shard_map/all_to_all | solution.py:48
  329.5 1.1 select_convert_fusion
  330.6 0.7 copy.67
  331.3 5.2 %all-to-all-start.4 = ((bf16[2,4,8,2048]{3,2,0,1:T(8,128)(2,1)}), bf16[2,4,8,2048]{3,2,0,1:T(8,128)(2,1)S(1)}, u32[]{:S(2)}, u32[]{:S(2)}) async-start(bf16[2,4,8,2048]{3,2,0,1:T(8,128)(2,1)} %copy.67), calls=%async_computation.4 | async-start | bytes 524288 | tf_op jit(solution)/shard_map/all_to_all | solution.py:165
  336.5 7.9 %copy.68 = bf16[8,2,256,4,128]{4,3,2,1,0:T(4,128)(2,1)} copy(bf16[8,2,256,4,128]{4,2,3,1,0:T(8,128)(2,1)} %bitcast.100) | data formatting | bytes 8388608
  345.1 1.5 gather_fusion.6
  346.6 0.8 broadcast_select_fusion
  (80 shorter events, 8.8 us)
Async XLA Ops:
  7.2 86.6 %copy-start = (bf16[2048,4,192]{0,2,1:T(8,128)(2,1)S(1)}, bf16[2048,4,192]{0,2,1:T(8,128)(2,1)}, u32[]{:S(2)}) copy-start(bf16[2048,4,192]{0,2,1:T(8,128)(2,1)} %param.24) | copy-start | bytes 9437188
  7.2 83.0 %all-gather.2.cloned.1.call-start = ((), (), s32[]{:S(2)}) async-start(), calls=%async_computation.5 | async-start | bytes 2359296 | tf_op jit(solution)/shard_map/all_gather | solution.py:116
  40.4 6.0 %copy-start.15 = (s32[8]{0:T(128)S(1)}, s32[8]{0:T(128)}, u32[]{:S(2)}) copy-start(s32[8]{0:T(128)} %param.22) | copy-start | bytes 100
  40.4 6.1 %copy-start.2 = (s32[8]{0:T(128)S(1)}, s32[8]{0:T(128)}, u32[]{:S(2)}) copy-start(s32[8]{0:T(128)} %param.21) | copy-start | bytes 100
  40.4 6.7 %copy-start.3 = (s32[8]{0:T(128)S(1)}, s32[8]{0:T(128)}, u32[]{:S(2)}) copy-start(s32[8]{0:T(128)} %param.20) | copy-start | bytes 100
  40.4 7.3 %copy-start.13 = (bf16[2048]{0:T(1024)(128)(2,1)S(1)}, bf16[2048]{0:T(1024)(128)(2,1)}, u32[]{:S(2)}) copy-start(bf16[2048]{0:T(1024)(128)(2,1)} %param.23) | copy-start | bytes 12292
  40.4 72.1 %all-to-all-start.1 = ((bf16[32,2,32,4,128]{4,2,3,1,0:T(8,128)(2,1)}), bf16[32,2,32,4,128]{4,2,3,1,0:T(8,128)(2,1)}, u32[]{:S(2)}, u32[]{:S(2)}) async-start(bf16[32,2,32,4,128]{4,2,3,1,0:T(8,128)(2,1)} %bitcast.101), calls=%async_computation.1 | async-start | bytes 4194304 | tf_op jit(solution)/shard_map/all_to_all | solution.py:104
  46.1 209.2 %all-reduce.2.cloned.1.call-start = ((), (), s32[]{:S(2)}) async-start(), calls=%async_computation.6 | async-start | bytes 4194304 | tf_op jit(solution)/shard_map/psum | solution.py:141
  90.1 2.2 copy-start.4
  95.6 0.9 copy-start.12
  96.5 17.3 %copy-start.11 = (f32[256,512]{1,0:T(8,128)S(1)}, f32[256,512]{1,0:T(8,128)}, u32[]{:S(2)}) copy-start(f32[256,512]{1,0:T(8,128)} %subtract_convert_fusion) | copy-start | bytes 1572868
  96.5 17.3 %copy-start.16 = (f32[4]{0:T(128)S(1)}, f32[4]{0:T(128)}, u32[]{:S(2)}) copy-start(f32[4]{0:T(128)} %param.25) | copy-start | bytes 52
  115.8 2.4 copy-start.10
  120.1 2.4 copy-start.9
  122.6 2.0 copy-start.7
  127.2 4.3 %copy-start.14 = (bf16[2048]{0:T(1024)(128)(2,1)S(1)}, bf16[2048]{0:T(1024)(128)(2,1)}, u32[]{:S(2)}) copy-start(bf16[2048]{0:T(1024)(128)(2,1)} %param.27) | copy-start | bytes 12292
  127.2 128.1 %copy-start.5 = (bf16[2,4,64,2048]{3,2,1,0:T(8,128)(2,1)S(1)}, bf16[2,4,64,2048]{3,2,1,0:T(8,128)(2,1)}, u32[]{:S(2)}) copy-start(bf16[2,4,64,2048]{3,2,1,0:T(8,128)(2,1)} %all-gather.2.cloned.1.call-done) | copy-start | bytes 6291460
  127.2 150.1 %all-to-all-start.2 = ((bf16[32,2,32,4,128]{4,2,3,1,0:T(8,128)(2,1)}), bf16[32,2,32,4,128]{4,2,3,1,0:T(8,128)(2,1)}, u32[]{:S(2)}, u32[]{:S(2)}) async-start(bf16[32,2,32,4,128]{4,2,3,1,0:T(8,128)(2,1)} %bitcast.102), calls=%async_computation.2 | async-start | bytes 4194304 | tf_op jit(solution)/shard_map/all_to_all | solution.py:104
  255.3 4.3 %copy-start.6 = (bf16[2,4,64,2048]{3,2,1,0:T(8,128)(2,1)S(1)}, bf16[2,4,64,2048]{3,2,1,0:T(8,128)(2,1)}, u32[]{:S(2)}) copy-start(bf16[2,4,64,2048]{3,2,1,0:T(8,128)(2,1)} %all-reduce.2.cloned.1.call-done) | copy-start | bytes 6291460
  277.4 51.8 %all-to-all-start.3 = ((bf16[2,4,8,8,2048]{4,3,1,0,2:T(8,128)(2,1)}), bf16[2,4,8,8,2048]{4,3,1,0,2:T(8,128)(2,1)S(1)}, u32[]{:S(2)}, u32[]{:S(2)}) async-start(bf16[2,4,8,8,2048]{4,3,1,0,2:T(8,128)(2,1)} %copy.66), calls=%async_computation.3 | async-start | bytes 4194304 | tf_op jit(solution)/shard_map/all_to_all | solution.py:48
  331.3 13.1 %all-to-all-start.4 = ((bf16[2,4,8,2048]{3,2,0,1:T(8,128)(2,1)}), bf16[2,4,8,2048]{3,2,0,1:T(8,128)(2,1)S(1)}, u32[]{:S(2)}, u32[]{:S(2)}) async-start(bf16[2,4,8,2048]{3,2,0,1:T(8,128)(2,1)} %copy.67), calls=%async_computation.4 | async-start | bytes 524288 | tf_op jit(solution)/shard_map/all_to_all | solution.py:165
  336.5 10.9 %copy-start.1 = (bf16[2048,4,192]{0,2,1:T(8,128)(2,1)S(1)}, bf16[2048,4,192]{0,2,1:T(8,128)(2,1)}, u32[]{:S(2)}) copy-start(bf16[2048,4,192]{0,2,1:T(8,128)(2,1)} %param.24) | copy-start | bytes 9437188
  344.4 0.7 copy-start.8
Sparse Core Ops, SparseCore 0:
  21.6 68.4 all-gather.1
  124.7 130.5 all-reduce.1

commit v7 on v3

--- a/solution.py
+++ b/solution.py
@@ -90,10 +90,13 @@
     heads = cache_prefill.shape[3]
     devices = req_count * head_count
     chunks = []
+    dealt_acts = jnp.take(stretch_acts, req_order, axis=0)
+    later_layers = cache_prefill[1:]
     for layer in range(local_layers):
+        source = cache_prefill[0] if layer == 0 else later_layers[layer - 1]
         dealt_cache = jnp.where(
             keep[:, :, None, None],
-            jnp.take(cache_prefill[layer], req_order, axis=0),
+            jnp.take(source, req_order, axis=0),
             jnp.zeros((), cache_prefill.dtype),
         )
         outgoing = (
@@ -101,7 +104,11 @@
             .transpose(0, 3, 1, 2, 4, 5)
             .reshape(devices, group_size, prefix_rows, heads // head_count, pair_width)
         )
+        if layer == 0:
+            outgoing, dealt_acts = lax.optimization_barrier((outgoing, dealt_acts))
         incoming = lax.all_to_all(outgoing, ("req", "head"), 0, 0, tiled=True)
+        if layer == 0:
+            incoming, later_layers = lax.optimization_barrier((incoming, later_layers))
         chunks.append(
             incoming.reshape(req_count, head_count, group_size, prefix_rows, heads // head_count, pair_width)
             .transpose(0, 2, 1, 3, 4, 5)
@@ -109,7 +116,6 @@
         )
     current = chunks[0][0]
     relaid = jnp.stack(chunks, axis=1).reshape((req_count * local_layers,) + chunks[0].shape[1:])
-    dealt_acts = jnp.take(stretch_acts, req_order, axis=0)
     dealt_rows = lax.all_to_all(dealt_acts, "req", split_axis=0, concat_axis=1, tiled=True).reshape(
         group_size, req_count, stretch_rows, features
     )
@@ -154,6 +160,7 @@
         group_size, req_count, span_rows, features
     )
     mlp_rows = head_sum(partial_mlp, head_count, stretch_rows)
+    relaid, mlp_rows = lax.optimization_barrier((relaid, mlp_rows))
     row_number = (
         jnp.arange(req_count, dtype=jnp.int32)[:, None] * head_count + head_index
     ) * stretch_rows + jnp.arange(stretch_rows, dtype=jnp.int32)[None, :]

time: 355 us -> 361 us (1.017)
  waiting for transfers between devices: 213 us -> 221 us
    all_gather x1, waiting for transfers between devices: 35.4 us -> 63.7 us  [local(): gathered = lax.all_gather(dealt_rows, 'head', axis=2, tiled=True)]
    all_to_all x2, waiting for transfers between devices: 16 us -> 0.01 us  [local(): incoming = lax.all_to_all(outgoing, ('req', 'head'), 0, 0, tiled=True)]
    squeeze x1 -> x0, local copies, waits for them, and re-layouts: 5.18 us -> none  [local(): cache_prefill[layer]]
    slice x0 -> x1, local copies, waits for them, and re-layouts: none -> 5.18 us  [local(): later_layers = cache_prefill[1:]]
    all_gather x1, waiting for transfers between devices: 72.8 us -> 68.4 us  [local(): normed_all = lax.all_gather(normed_rows, 'head', axis=2, tiled=True)]
    unnamed x41 -> x45, local copies, waits for them, and re-layouts: 9.04 us -> 11 us
  transfers between devices with their start and end apart: 7 -> 7, of which waited for: 5 -> 4; matrix products, arithmetic and copies ran while one was open for 19% -> 14% of each run, Pallas kernels for 0% -> 0%
where the time goes in v7:
time: 361 us; the launch traced here: 360 us
  waiting for transfers between devices  221 us (61%)
  local copies, waits for them, and re-layouts  47.7 us (13%)
  matrix products  26.8 us (7%)
  starting transfers between devices  23.1 us (6%)
  other arithmetic  18.8 us (5%)
  between operations  14.5 us (4%)
  blocking collectives  9.06 us (3%)
    all_to_all x2, waiting for transfers between devices, head_sum(): lax.all_to_all(partial.astype(jnp.bfloat16).reshape(shape), 'head', split...  88.4 us
    all_gather x1, waiting for transfers between devices, local(): normed_all = lax.all_gather(normed_rows, 'head', axis=2, tiled=True)  68.4 us
    all_gather x1, waiting for transfers between devices, local(): gathered = lax.all_gather(dealt_rows, 'head', axis=2, tiled=True)  63.7 us
    dot_general x1, matrix products, local(): jnp.dot(inner, down_weight, preferred_element_type=jnp.float32)  14.3 us
    unnamed x45, local copies, waits for them, and re-layouts  11 us
    all_to_all x2, starting transfers between devices, local(): incoming = lax.all_to_all(outgoing, ('req', 'head'), 0, 0, tiled=True)  10.5 us
    all_to_all x1, blocking collectives, local(): lax.all_to_all(dealt_acts, 'req', split_axis=0, concat_axis=1, tiled=True)  9.06 us
    all_to_all x2, starting transfers between devices, head_sum(): lax.all_to_all(partial.astype(jnp.bfloat16).reshape(shape), 'head', split...  7.6 us
  transfers between devices with their start and end apart: 7, of which 4 were waited for; matrix products, arithmetic and copies ran while one was open for 14% of the time, Pallas kernels for 0%

profile of v7, /device:TPU:1, one launch (start us, length us, event | category | flops | bytes accessed | tf_op | source)
XLA Modules:
  0.0 360.5 jit_solution(2317743694310252925)
XLA Ops:
  7.2 0.8 compare_select_fusion.2
  8.0 1.4 gather_fusion
  10.1 5.2 %fusion.119 = (bf16[1,8,32,32,128]{4,3,2,1,0:T(8,128)(2,1)}, bf16[8,32,32,128]{3,2,1,0:T(8,128)(2,1)}) fusion(bf16[2,8,32,32,128]{4,3,2,1,0:T(8,128)(2,1)} %param.19), kind=kLoop, calls=%fused_computation.188 | loop fusion | bytes 8388608 | tf_op jit(solution)/shard_map/slice | solution.py:94
  15.3 3.7 %gather_fusion.2 = bf16[8,32,32,128]{3,2,1,0:T(8,128)(2,1)} fusion(bf16[8,32,32,128]{3,2,1,0:T(8,128)(2,1)} %get-tuple-element.30, s32[1024]{0:T(1024)S(1)} %pad_clamp_fusion.1), kind=kCustom, calls=%fused_computation.1.clone | custom fusion | bytes 4194336 | tf_op jit(solution)/shard_map/jit(_take)/gather | solution.py:99
  19.1 1.8 select_select_fusion.1
  20.8 0.8 copy.71
  21.7 1.8 copy.72
  23.4 1.5 gather_fusion.3
  25.1 9.1 %all_to_all.50 = bf16[8,8,2048]{2,1,0:T(8,128)(2,1)S(1)} all-to-all(bf16[8,8,2048]{2,1,0:T(8,128)(2,1)S(1)} %broadcast_select_fusion.1), channel_id=1, replica_groups=mesh['req'=4,'head'=8] {'req'}, dimensions={0} | all-to-all | bytes 524288 | tf_op jit(solution)/shard_map/all_to_all | solution.py:119
  34.1 0.7 copy_bitcast_fusion
  34.9 5.8 %all-to-all-start.1 = ((bf16[32,2,32,4,128]{4,2,3,1,0:T(8,128)(2,1)}), bf16[32,2,32,4,128]{4,2,3,1,0:T(8,128)(2,1)}, u32[]{:S(2)}, u32[]{:S(2)}) async-start(bf16[32,2,32,4,128]{4,2,3,1,0:T(8,128)(2,1)} %bitcast.117), calls=%async_computation.1 | async-start | bytes 4194304 | tf_op jit(solution)/shard_map/all_to_all | solution.py:109
  43.9 1.2 iota_compare_fusion.1
  47.1 0.8 fusion.55
  47.9 0.9 subtract_convert_fusion.1
  48.8 0.9 subtract_convert_fusion
  49.7 63.7 %all-gather.3.cloned.1.call-done = bf16[2,4,64,2048]{3,2,1,0:T(8,128)(2,1)} async-done(((bf16[2,4,8,2048]{3,2,1,0:T(8,128)(2,1)}), bf16[2,4,64,2048]{3,2,1,0:T(8,128)(2,1)}) %all-gather.3.cloned.1.call-update) | async-done | bytes 2097168 | tf_op jit(solution)/shard_map/all_gather | solution.py:122
  113.4 2.1 convert_reduce_fusion
  117.0 1.8 fusion.20
  118.9 0.9 copy-done.11
  119.8 1.1 fusion.120
  121.1 2.0 fusion.123
  123.1 2.9 convolution_convert_fusion.3
  126.2 2.0 fusion.122
  128.1 2.2 convolution_convert_fusion.2
  130.4 0.8 copy.78
  131.3 1.7 fusion.9
  132.9 1.6 copy.79
  134.5 3.7 %all-to-all-start.2 = ((bf16[2,4,8,8,2048]{4,3,1,0,2:T(8,128)(2,1)}), bf16[2,4,8,8,2048]{4,3,1,0,2:T(8,128)(2,1)S(1)}, u32[]{:S(2)}, u32[]{:S(2)}) async-start(bf16[2,4,8,8,2048]{4,3,1,0,2:T(8,128)(2,1)} %copy.79), calls=%async_computation.2 | async-start | bytes 4194304 | tf_op jit(solution)/shard_map/all_to_all | solution.py:48
  138.5 47.5 %all-to-all-done.2 = bf16[2,4,8,8,2048]{4,3,1,0,2:T(8,128)(2,1)S(1)} async-done(((bf16[2,4,8,8,2048]{4,3,1,0,2:T(8,128)(2,1)}), bf16[2,4,8,8,2048]{4,3,1,0,2:T(8,128)(2,1)S(1)}, u32[]{:S(2)}, u32[]{:S(2)}) %all-to-all-start.2) | async-done | bytes 2097184 | tf_op jit(solution)/shard_map/all_to_all | solution.py:48
  186.8 0.8 multiply_convert_fusion
  187.7 2.5 gather_fusion.5
  190.7 0.8 copy.82
  191.5 2.0 copy.83
  193.6 4.7 %all-to-all-start.3 = ((bf16[32,2,32,4,128]{4,2,3,1,0:T(8,128)(2,1)}), bf16[32,2,32,4,128]{4,2,3,1,0:T(8,128)(2,1)S(1)}, u32[]{:S(2)}, u32[]{:S(2)}) async-start(bf16[32,2,32,4,128]{4,2,3,1,0:T(8,128)(2,1)} %bitcast.119), calls=%async_computation.3 | async-start | bytes 4194304 | tf_op jit(solution)/shard_map/all_to_all | solution.py:109
  198.3 68.4 %all-gather.5.cloned.1.call-done = bf16[2,4,64,2048]{3,2,1,0:T(8,128)(2,1)} async-done(((bf16[2,4,8,2048]{3,2,1,0:T(8,128)(2,1)}), bf16[2,4,64,2048]{3,2,1,0:T(8,128)(2,1)}) %all-gather.5.cloned.1.call-update) | async-done | bytes 2097168 | tf_op jit(solution)/shard_map/all_gather | solution.py:150
  266.6 14.3 %convolution_convert_fusion = bf16[512,2048]{1,0:T(8,128)(2,1)} fusion(bf16[1024,2048]{1,0:T(8,128)(2,1)} %param.29, bf16[512,2048]{1,0:T(8,128)(2,1)} %bitcast.134, bf16[2048,1024]{1,0:T(8,128)(2,1)} %param.28), kind=kOutput, calls=%fused_computation.22 | convolution fusion | flops 4330094592 | bytes 12582912 | tf_op jit(solution)/shard_map/dot_general | solution.py:159
  280.9 3.2 copy.86
  284.1 1.3 copy-done.5
  285.4 3.9 %all-to-all-start.4 = ((bf16[2,4,8,8,2048]{4,3,1,0,2:T(8,128)(2,1)}), bf16[2,4,8,8,2048]{4,3,1,0,2:T(8,128)(2,1)S(1)}, u32[]{:S(2)}, u32[]{:S(2)}) async-start(bf16[2,4,8,8,2048]{4,3,1,0,2:T(8,128)(2,1)} %copy.86), calls=%async_computation.4 | async-start | bytes 4194304 | tf_op jit(solution)/shard_map/all_to_all | solution.py:48
  289.3 1.0 sort.17
  290.4 2.3 copy.81
  293.7 2.2 copy.85
  295.9 40.9 %all-to-all-done.4 = bf16[2,4,8,8,2048]{4,3,1,0,2:T(8,128)(2,1)S(1)} async-done(((bf16[2,4,8,8,2048]{4,3,1,0,2:T(8,128)(2,1)}), bf16[2,4,8,8,2048]{4,3,1,0,2:T(8,128)(2,1)S(1)}, u32[]{:S(2)}, u32[]{:S(2)}) %all-to-all-start.4) | async-done | bytes 2097184 | tf_op jit(solution)/shard_map/all_to_all | solution.py:48
  337.3 0.7 copy.88
  338.0 4.7 %all-to-all-start.5 = ((bf16[2,4,8,2048]{3,2,0,1:T(8,128)(2,1)}), bf16[2,4,8,2048]{3,2,0,1:T(8,128)(2,1)S(1)}, u32[]{:S(2)}, u32[]{:S(2)}) async-start(bf16[2,4,8,2048]{3,2,0,1:T(8,128)(2,1)} %copy.88), calls=%async_computation.5 | async-start | bytes 524288 | tf_op jit(solution)/shard_map/all_to_all | solution.py:171
  342.7 7.9 %copy.89 = bf16[8,2,256,4,128]{4,3,2,1,0:T(4,128)(2,1)} copy(bf16[8,2,256,4,128]{4,2,3,1,0:T(8,128)(2,1)} %bitcast.114) | data formatting | bytes 8388608
  351.3 1.5 gather_fusion.6
  352.8 0.8 broadcast_select_fusion
  (95 shorter events, 11.8 us)
Async XLA Ops:
  7.2 109.8 %copy-start = (bf16[2048,4,192]{0,2,1:T(8,128)(2,1)S(1)}, bf16[2048,4,192]{0,2,1:T(8,128)(2,1)}, u32[]{:S(2)}) copy-start(bf16[2048,4,192]{0,2,1:T(8,128)(2,1)} %param.24) | copy-start | bytes 9437188
  7.2 106.2 %all-gather.3.cloned.1.call-start = ((), (), s32[]{:S(2)}) async-start(), calls=%async_computation.6 | async-start | bytes 2359296 | tf_op jit(solution)/shard_map/all_gather | solution.py:122
  10.1 14.8 %copy-start.14 = (pred[8]{0:T(512)(128)(4,1)}, pred[8]{0:T(512)(128)(4,1)S(1)}, u32[]{:S(2)}) copy-start(pred[8]{0:T(512)(128)(4,1)S(1)} %get-tuple-element.28) | copy-start | bytes 28
  34.9 5.8 %copy-start.19 = (s32[8]{0:T(128)S(1)}, s32[8]{0:T(128)}, u32[]{:S(2)}) copy-start(s32[8]{0:T(128)} %param.22) | copy-start | bytes 100
  34.9 5.9 %copy-start.2 = (s32[8]{0:T(128)S(1)}, s32[8]{0:T(128)}, u32[]{:S(2)}) copy-start(s32[8]{0:T(128)} %param.21) | copy-start | bytes 100
  34.9 6.6 %copy-start.3 = (s32[8]{0:T(128)S(1)}, s32[8]{0:T(128)}, u32[]{:S(2)}) copy-start(s32[8]{0:T(128)} %param.20) | copy-start | bytes 100
  34.9 7.2 %copy-start.16 = (bf16[2048]{0:T(1024)(128)(2,1)S(1)}, bf16[2048]{0:T(1024)(128)(2,1)}, u32[]{:S(2)}) copy-start(bf16[2048]{0:T(1024)(128)(2,1)} %param.23) | copy-start | bytes 12292
  34.9 84.9 %all-to-all-start.1 = ((bf16[32,2,32,4,128]{4,2,3,1,0:T(8,128)(2,1)}), bf16[32,2,32,4,128]{4,2,3,1,0:T(8,128)(2,1)}, u32[]{:S(2)}, u32[]{:S(2)}) async-start(bf16[32,2,32,4,128]{4,2,3,1,0:T(8,128)(2,1)} %bitcast.117), calls=%async_computation.1 | async-start | bytes 4194304 | tf_op jit(solution)/shard_map/all_to_all | solution.py:109
  113.4 2.2 copy-start.4
  118.8 0.9 copy-start.11
  119.7 1.4 copy-start.10
  119.7 1.4 copy-start.12
  119.7 1.4 copy-start.21
  123.1 3.0 copy-start.9
  128.1 2.3 copy-start.13
  128.1 3.1 copy-start.8
  134.5 4.0 %copy-start.17 = (bf16[2048]{0:T(1024)(128)(2,1)S(1)}, bf16[2048]{0:T(1024)(128)(2,1)}, u32[]{:S(2)}) copy-start(bf16[2048]{0:T(1024)(128)(2,1)} %param.27) | copy-start | bytes 12292
  134.5 51.6 %all-to-all-start.2 = ((bf16[2,4,8,8,2048]{4,3,1,0,2:T(8,128)(2,1)}), bf16[2,4,8,8,2048]{4,3,1,0,2:T(8,128)(2,1)S(1)}, u32[]{:S(2)}, u32[]{:S(2)}) async-start(bf16[2,4,8,8,2048]{4,3,1,0,2:T(8,128)(2,1)} %copy.79), calls=%async_computation.2 | async-start | bytes 4194304 | tf_op jit(solution)/shard_map/all_to_all | solution.py:48
  138.2 128.4 %all-gather.5.cloned.1.call-start = ((), (), s32[]{:S(2)}) async-start(), calls=%async_computation.7 | async-start | bytes 2359296 | tf_op jit(solution)/shard_map/all_gather | solution.py:150
  187.7 2.6 copy-start.15
  193.6 90.5 %all-to-all-start.3 = ((bf16[32,2,32,4,128]{4,2,3,1,0:T(8,128)(2,1)}), bf16[32,2,32,4,128]{4,2,3,1,0:T(8,128)(2,1)S(1)}, u32[]{:S(2)}, u32[]{:S(2)}) async-start(bf16[32,2,32,4,128]{4,2,3,1,0:T(8,128)(2,1)} %bitcast.119), calls=%async_computation.3 | async-start | bytes 4194304 | tf_op jit(solution)/shard_map/all_to_all | solution.py:109
  284.1 5.2 %copy-start.20 = (s32[8]{0:T(128)S(1)}, s32[8]{0:T(128)}, u32[]{:S(2)}) copy-start(s32[8]{0:T(128)} %param.22) | copy-start | bytes 100
  284.1 6.3 %copy-start.18 = (s32[2]{0:T(128)S(1)}, s32[2]{0:T(128)}, u32[]{:S(2)}) copy-start(s32[2]{0:T(128)} %get-tuple-element.37) | copy-start | bytes 28
  284.1 1.3 copy-start.5
  285.4 51.4 %all-to-all-start.4 = ((bf16[2,4,8,8,2048]{4,3,1,0,2:T(8,128)(2,1)}), bf16[2,4,8,8,2048]{4,3,1,0,2:T(8,128)(2,1)S(1)}, u32[]{:S(2)}, u32[]{:S(2)}) async-start(bf16[2,4,8,8,2048]{4,3,1,0,2:T(8,128)(2,1)} %copy.86), calls=%async_computation.4 | async-start | bytes 4194304 | tf_op jit(solution)/shard_map/all_to_all | solution.py:48
  290.4 2.3 copy-start.6
  338.0 12.6 %all-to-all-start.5 = ((bf16[2,4,8,2048]{3,2,0,1:T(8,128)(2,1)}), bf16[2,4,8,2048]{3,2,0,1:T(8,128)(2,1)S(1)}, u32[]{:S(2)}, u32[]{:S(2)}) async-start(bf16[2,4,8,2048]{3,2,0,1:T(8,128)(2,1)} %copy.88), calls=%async_computation.5 | async-start | bytes 524288 | tf_op jit(solution)/shard_map/all_to_all | solution.py:171
  342.7 10.9 %copy-start.1 = (bf16[2048,4,192]{0,2,1:T(8,128)(2,1)S(1)}, bf16[2048,4,192]{0,2,1:T(8,128)(2,1)}, u32[]{:S(2)}) copy-start(bf16[2048,4,192]{0,2,1:T(8,128)(2,1)} %param.24) | copy-start | bytes 9437188
  350.6 0.7 copy-start.7
Sparse Core Ops, SparseCore 0:
  35.0 78.3 all-gather.2
  187.8 78.8 all-gather.4

commit v8 on v3

--- a/solution.py
+++ b/solution.py
@@ -44,11 +44,25 @@
 
 
 def head_sum(partial, head_count, stretch_rows):
-    shape = partial.shape[:2] + (head_count, stretch_rows) + partial.shape[3:]
-    pieces = lax.all_to_all(
-        partial.astype(jnp.bfloat16).reshape(shape), "head", split_axis=2, concat_axis=2, tiled=True
-    )
-    return jnp.sum(pieces.astype(jnp.float32), axis=2)
+    inner_size = 4 if head_count % 4 == 0 else head_count
+    outer_size = head_count // inner_size
+    me = lax.axis_index("head")
+    outer_me, inner_me = me // inner_size, me % inner_size
+    blocks = partial.astype(jnp.bfloat16).reshape(
+        partial.shape[:2] + (outer_size, inner_size, stretch_rows) + partial.shape[3:]
+    )
+    level_one = lax.dynamic_index_in_dim(blocks, inner_me, 3, False).astype(jnp.float32)
+    for shift in range(1, inner_size):
+        pairs = [(j, (j // inner_size) * inner_size + (j % inner_size + shift) % inner_size) for j in range(head_count)]
+        sent = lax.dynamic_index_in_dim(blocks, (inner_me + shift) % inner_size, 3, False)
+        level_one = level_one + lax.ppermute(sent, "head", pairs).astype(jnp.float32)
+    rounded_one = level_one.astype(jnp.bfloat16)
+    total = lax.dynamic_index_in_dim(level_one, outer_me, 2, False)
+    for shift in range(1, outer_size):
+        pairs = [(j, ((j // inner_size + shift) % outer_size) * inner_size + j % inner_size) for j in range(head_count)]
+        sent = lax.dynamic_index_in_dim(rounded_one, (outer_me + shift) % outer_size, 2, False)
+        total = total + lax.ppermute(sent, "head", pairs).astype(jnp.float32)
+    return total
 
 
 def local(
@@ -154,6 +168,7 @@
         group_size, req_count, span_rows, features
     )
     mlp_rows = head_sum(partial_mlp, head_count, stretch_rows)
+    relaid, mlp_rows = lax.optimization_barrier((relaid, mlp_rows))
     row_number = (
         jnp.arange(req_count, dtype=jnp.int32)[:, None] * head_count + head_index
     ) * stretch_rows + jnp.arange(stretch_rows, dtype=jnp.int32)[None, :]

time: 355 us -> 333 us (0.938)
  waiting for transfers between devices: 213 us -> 191 us
  local copies, waits for them, and re-layouts: 47.4 us -> 52.6 us
  starting transfers between devices: 22.6 us -> 17.6 us
    all_to_all x2 -> x0, waiting for transfers between devices: 88.5 us -> none  [head_sum(): lax.all_to_all(partial.astype(jnp.bfloat16).reshape(shape), 'head', split...]
    ppermute x0 -> x8, waiting for transfers between devices: none -> 66.9 us  [the longest x6 46.2 us: head_sum(): lax.ppermute(sent, 'head', pairs).astype(jnp.float32)]
    all_to_all x2 -> x0, starting transfers between devices: 7.34 us -> none  [head_sum(): lax.all_to_all(partial.astype(jnp.bfloat16).reshape(shape), 'head', split...]
    unnamed x41 -> x47, local copies, waits for them, and re-layouts: 9.04 us -> 13.5 us
    ppermute x0 -> x8, starting transfers between devices: none -> 4.41 us  [the longest x6 4.33 us: head_sum(): lax.ppermute(sent, 'head', pairs).astype(jnp.float32)]
    convert_element_type x2 -> x1, local copies, waits for them, and re-layouts: 3.86 us -> 0.14 us  [local(): normed = layer_norm(gathered.astype(jnp.float32), attn_gain).astype(jnp.b...]
  transfers between devices with their start and end apart: 7 -> 13, of which waited for: 5 -> 10; matrix products, arithmetic and copies ran while one was open for 19% -> 21% of each run, Pallas kernels for 0% -> 0%
where the time goes in v8:
time: 333 us; the launch traced here: 332 us
  waiting for transfers between devices  191 us (57%)
  local copies, waits for them, and re-layouts  52.6 us (16%)
  matrix products  25.2 us (8%)
  other arithmetic  22 us (7%)
  starting transfers between devices  17.6 us (5%)
  between operations  14.7 us (4%)
  blocking collectives  9.17 us (3%)
    all_gather x1, waiting for transfers between devices, local(): normed_all = lax.all_gather(normed_rows, 'head', axis=2, tiled=True)  71.8 us
    ppermute x6, waiting for transfers between devices, head_sum(): lax.ppermute(sent, 'head', pairs).astype(jnp.float32)  46.2 us
    all_gather x1, waiting for transfers between devices, local(): gathered = lax.all_gather(dealt_rows, 'head', axis=2, tiled=True)  35.9 us
    ppermute x2, waiting for transfers between devices, head_sum(): total = total + lax.ppermute(sent, 'head', pairs).astype(jnp.float32)  20.7 us
    all_to_all x2, waiting for transfers between devices, local(): incoming = lax.all_to_all(outgoing, ('req', 'head'), 0, 0, tiled=True)  15.8 us
    dot_general x1, matrix products, local(): jnp.dot(inner, down_weight, preferred_element_type=jnp.float32)  14.3 us
    unnamed x47, local copies, waits for them, and re-layouts  13.5 us
    all_to_all x1, blocking collectives, local(): lax.all_to_all(dealt_acts, 'req', split_axis=0, concat_axis=1, tiled=True)  9.17 us
  transfers between devices with their start and end apart: 13, of which 10 were waited for; matrix products, arithmetic and copies ran while one was open for 21% of the time, Pallas kernels for 0%

profile of v8, /device:TPU:1, one launch (start us, length us, event | category | flops | bytes accessed | tf_op | source)
XLA Modules:
  0.0 331.9 jit_solution(6121935259771760552)
XLA Ops:
  8.0 1.6 gather_fusion.2
  9.7 1.3 gather_fusion
  11.7 9.2 %all_to_all.40 = bf16[8,8,2048]{2,1,0:T(8,128)(2,1)} all-to-all(bf16[8,8,2048]{2,1,0:T(8,128)(2,1)S(1)} %broadcast_select_fusion.1), channel_id=1, replica_groups=mesh['req'=4,'head'=8] {'req'}, dimensions={0} | all-to-all | bytes 524288 | tf_op jit(solution)/shard_map/all_to_all | solution.py:127
  20.9 5.2 %slice_bitcast_fusion = (bf16[8,32,32,128]{3,2,1,0:T(8,128)(2,1)}, bf16[8,32,32,128]{3,2,1,0:T(8,128)(2,1)}) fusion(bf16[2,8,32,32,128]{4,3,2,1,0:T(8,128)(2,1)} %param.19), kind=kLoop, calls=%fused_computation.40 | loop fusion | bytes 8388608 | tf_op jit(solution)/shard_map/squeeze | solution.py:110
  26.1 3.8 %gather_fusion.5 = bf16[8,32,32,128]{3,2,1,0:T(8,128)(2,1)} fusion(bf16[8,32,32,128]{3,2,1,0:T(8,128)(2,1)} %get-tuple-element.19, s32[1024]{0:T(1024)S(1)} %pad_clamp_fusion.1), kind=kCustom, calls=%fused_computation.5.clone | custom fusion | bytes 4194336 | tf_op jit(solution)/shard_map/jit(_take)/gather | solution.py:110
  29.9 3.8 %gather_fusion.3 = bf16[8,32,32,128]{3,2,1,0:T(8,128)(2,1)} fusion(bf16[8,32,32,128]{3,2,1,0:T(8,128)(2,1)} %get-tuple-element.20, s32[1024]{0:T(1024)S(1)} %pad_clamp_fusion.1), kind=kCustom, calls=%fused_computation.2.clone | custom fusion | bytes 4194336 | tf_op jit(solution)/shard_map/jit(_take)/gather | solution.py:110
  33.7 3.5 %select_select_fusion = (bf16[8,32,32,128]{3,2,1,0:T(8,128)(2,1)}, bf16[8,32,32,128]{3,2,1,0:T(8,128)(2,1)S(1)}) fusion(bf16[8,32,32,128]{3,2,1,0:T(8,128)(2,1)} %gather_fusion.5, pred[8]{0:T(512)(128)(4,1)S(1)} %get-tuple-element.18, pred[8,32]{1,0:T(8,128)(4,1)S(1)} %broadcast_compare_fusion, bf16[8,32,32,128]{3,2,1,0:T(8,128)(2,1)} %gather_fusion.3), kind=kLoop, calls=%fused_computation.25 | loop fusion | flops 4194304 | bytes 8388872 | tf_op jit(solution)/shard_map/jit(_where)/select_n | solution.py:108
  38.0 1.8 copy.58
  39.8 6.1 %all-to-all-start.1 = ((bf16[32,2,32,4,128]{4,2,3,1,0:T(8,128)(2,1)}), bf16[32,2,32,4,128]{4,2,3,1,0:T(8,128)(2,1)}, u32[]{:S(2)}, u32[]{:S(2)}) async-start(bf16[32,2,32,4,128]{4,2,3,1,0:T(8,128)(2,1)} %bitcast.139), calls=%async_computation.1 | async-start | bytes 4194304 | tf_op jit(solution)/shard_map/all_to_all | solution.py:118
  48.9 1.2 iota_compare_fusion.1
  52.2 0.9 subtract_convert_fusion
  53.1 0.9 subtract_convert_fusion.1
  54.0 35.9 %all-gather.3.cloned.1.call-done = bf16[2,4,64,2048]{3,2,0,1:T(8,128)(2,1)} async-done(((bf16[2,4,8,2048]{3,2,0,1:T(8,128)(2,1)}), bf16[2,4,64,2048]{3,2,0,1:T(8,128)(2,1)}) %all-gather.3.cloned.1.call-update) | async-done | bytes 2097168 | tf_op jit(solution)/shard_map/all_gather | solution.py:130
  90.0 2.1 convert_reduce_fusion
  93.8 1.8 fusion.19
  95.6 0.9 copy-done.18
  96.5 15.8 %all-to-all-done.1 = bf16[32,2,32,4,128]{4,2,3,1,0:T(8,128)(2,1)} async-done(((bf16[32,2,32,4,128]{4,2,3,1,0:T(8,128)(2,1)}), bf16[32,2,32,4,128]{4,2,3,1,0:T(8,128)(2,1)}, u32[]{:S(2)}, u32[]{:S(2)}) %all-to-all-start.1) | async-done | bytes 2097184 | tf_op jit(solution)/shard_map/all_to_all | solution.py:118
  112.3 1.1 fusion.126
  113.6 2.0 fusion.128
  115.6 2.2 convolution_convert_fusion.2
  118.0 2.0 fusion.129
  120.0 2.2 convolution_convert_fusion.3
  123.1 1.0 constant_dynamic-slice_fusion.7
  124.3 2.1 collective-permute-start.1
  126.8 10.2 %collective-permute-done.2 = bf16[2,4,2,8,2048]{4,3,1,0,2:T(8,128)(2,1)} collective-permute-done((bf16[2,4,2,8,2048]{4,3,1,0,2:T(8,128)(2,1)S(1)}, bf16[2,4,2,8,2048]{4,3,1,0,2:T(8,128)(2,1)}, u32[]{:S(2)}, u32[]{:S(2)}) %collective-permute-start.2) | collective-permute-done | bytes 524320 | tf_op jit(solution)/shard_map/ppermute | solution.py:58
  136.9 12.9 %collective-permute-done.1 = bf16[2,4,2,8,2048]{4,3,1,0,2:T(8,128)(2,1)S(1)} collective-permute-done((bf16[2,4,2,8,2048]{4,3,1,0,2:T(8,128)(2,1)S(1)}, bf16[2,4,2,8,2048]{4,3,1,0,2:T(8,128)(2,1)S(1)}, u32[]{:S(2)}, u32[]{:S(2)}) %collective-permute-start.1) | collective-permute-done | bytes 524320 | tf_op jit(solution)/shard_map/ppermute | solution.py:58
  151.4 1.7 fusion.26
  154.2 13.8 %collective-permute-done.3 = bf16[2,4,8,2048]{3,2,0,1:T(8,128)(2,1)} collective-permute-done((bf16[2,4,8,2048]{3,2,0,1:T(8,128)(2,1)}, bf16[2,4,8,2048]{3,2,0,1:T(8,128)(2,1)}, u32[]{:S(2)}, u32[]{:S(2)}) %collective-permute-start.3) | collective-permute-done | bytes 262176 | tf_op jit(solution)/shard_map/ppermute | solution.py:64
  168.0 1.3 fusion.124
  171.2 1.8 copy.73
  173.0 2.9 all-to-all-start.2
  175.9 1.0 sort.17
  176.9 71.8 %all-gather.5.cloned.1.call-done = bf16[2,4,64,2048]{3,2,0,1:T(8,128)(2,1)} async-done(((bf16[2,4,8,2048]{3,2,0,1:T(8,128)(2,1)}), bf16[2,4,64,2048]{3,2,0,1:T(8,128)(2,1)}) %all-gather.5.cloned.1.call-update) | async-done | bytes 2097168 | tf_op jit(solution)/shard_map/all_gather | solution.py:158
  248.7 3.2 copy.76
  251.9 14.3 %convolution_convert_fusion = bf16[512,2048]{1,0:T(8,128)(2,1)} fusion(bf16[1024,2048]{1,0:T(8,128)(2,1)} %param.29, bf16[512,2048]{1,0:T(8,128)(2,1)} %bitcast.150, bf16[2048,1024]{1,0:T(8,128)(2,1)} %param.28), kind=kOutput, calls=%fused_computation.20 | convolution fusion | flops 4330094592 | bytes 12582912 | tf_op jit(solution)/shard_map/dot_general | solution.py:167
  266.2 1.7 constant_dynamic-slice_fusion.3
  268.0 1.1 collective-permute-start.5
  270.1 10.9 %collective-permute-done.6 = bf16[2,4,2,8,2048]{4,3,1,0,2:T(8,128)(2,1)S(1)} collective-permute-done((bf16[2,4,2,8,2048]{4,3,1,0,2:T(8,128)(2,1)S(1)}, bf16[2,4,2,8,2048]{4,3,1,0,2:T(8,128)(2,1)S(1)}, u32[]{:S(2)}, u32[]{:S(2)}) %collective-permute-start.6) | collective-permute-done | bytes 524320 | tf_op jit(solution)/shard_map/ppermute | solution.py:58
  281.0 10.8 %collective-permute-done.5 = bf16[2,4,2,8,2048]{4,3,1,0,2:T(8,128)(2,1)S(1)} collective-permute-done((bf16[2,4,2,8,2048]{4,3,1,0,2:T(8,128)(2,1)S(1)}, bf16[2,4,2,8,2048]{4,3,1,0,2:T(8,128)(2,1)S(1)}, u32[]{:S(2)}, u32[]{:S(2)}) %collective-permute-start.5) | collective-permute-done | bytes 524320 | tf_op jit(solution)/shard_map/ppermute | solution.py:58
  291.8 1.4 collective-permute-done.4
  293.5 1.0 copy-done.7
  294.6 3.5 %copy.71 = bf16[4,2,8,32,4,128]{5,3,2,4,1,0:T(8,128)(2,1)} copy(bf16[4,2,8,32,4,128]{5,3,4,1,2,0:T(8,128)(2,1)} %bitcast.7) | data formatting | bytes 4194304 | tf_op jit(solution)/shard_map/transpose | solution.py:121
  298.7 1.0 copy-done.6
  300.1 2.2 copy.75
  302.4 7.0 %collective-permute-done.7 = bf16[2,4,8,2048]{3,2,0,1:T(8,128)(2,1)S(1)} collective-permute-done((bf16[2,4,8,2048]{3,2,0,1:T(8,128)(2,1)S(1)}, bf16[2,4,8,2048]{3,2,0,1:T(8,128)(2,1)S(1)}, u32[]{:S(2)}, u32[]{:S(2)}) %collective-permute-start.7) | collective-permute-done | bytes 262176 | tf_op jit(solution)/shard_map/ppermute | solution.py:64
  310.2 3.9 %all-to-all-start.3 = ((bf16[2,4,8,2048]{3,2,0,1:T(8,128)(2,1)}), bf16[2,4,8,2048]{3,2,0,1:T(8,128)(2,1)S(1)}, u32[]{:S(2)}, u32[]{:S(2)}) async-start(bf16[2,4,8,2048]{3,2,0,1:T(8,128)(2,1)} %select_convert_fusion), calls=%async_computation.3 | async-start | bytes 524288 | tf_op jit(solution)/shard_map/all_to_all | solution.py:179
  314.1 7.9 %copy.83 = bf16[8,2,256,4,128]{4,3,2,1,0:T(4,128)(2,1)} copy(bf16[8,2,256,4,128]{4,2,3,1,0:T(8,128)(2,1)} %bitcast.138) | data formatting | bytes 8388608
  322.7 1.5 gather_fusion.6
  (119 shorter events, 20.2 us)
Async XLA Ops:
  7.2 86.6 %copy-start = (bf16[2048,4,192]{0,2,1:T(8,128)(2,1)S(1)}, bf16[2048,4,192]{0,2,1:T(8,128)(2,1)}, u32[]{:S(2)}) copy-start(bf16[2048,4,192]{0,2,1:T(8,128)(2,1)} %param.24) | copy-start | bytes 9437188
  7.2 82.8 %all-gather.3.cloned.1.call-start = ((), (), s32[]{:S(2)}) async-start(), calls=%async_computation.4 | async-start | bytes 2359296 | tf_op jit(solution)/shard_map/all_gather | solution.py:130
  39.8 6.4 %copy-start.21 = (s32[8]{0:T(128)S(1)}, s32[8]{0:T(128)}, u32[]{:S(2)}) copy-start(s32[8]{0:T(128)} %param.22) | copy-start | bytes 100
  39.8 6.5 %copy-start.2 = (s32[8]{0:T(128)S(1)}, s32[8]{0:T(128)}, u32[]{:S(2)}) copy-start(s32[8]{0:T(128)} %param.21) | copy-start | bytes 100
  39.8 7.2 %copy-start.3 = (s32[8]{0:T(128)S(1)}, s32[8]{0:T(128)}, u32[]{:S(2)}) copy-start(s32[8]{0:T(128)} %param.20) | copy-start | bytes 100
  39.8 7.8 %copy-start.19 = (bf16[2048]{0:T(1024)(128)(2,1)S(1)}, bf16[2048]{0:T(1024)(128)(2,1)}, u32[]{:S(2)}) copy-start(bf16[2048]{0:T(1024)(128)(2,1)} %param.23) | copy-start | bytes 12292
  39.8 72.5 %all-to-all-start.1 = ((bf16[32,2,32,4,128]{4,2,3,1,0:T(8,128)(2,1)}), bf16[32,2,32,4,128]{4,2,3,1,0:T(8,128)(2,1)}, u32[]{:S(2)}, u32[]{:S(2)}) async-start(bf16[32,2,32,4,128]{4,2,3,1,0:T(8,128)(2,1)} %bitcast.139), calls=%async_computation.1 | async-start | bytes 4194304 | tf_op jit(solution)/shard_map/all_to_all | solution.py:118
  45.9 202.8 %all-gather.5.cloned.1.call-start = ((), (), s32[]{:S(2)}) async-start(), calls=%async_computation.5 | async-start | bytes 2359296 | tf_op jit(solution)/shard_map/all_gather | solution.py:158
  90.0 2.2 copy-start.4
  95.6 0.9 copy-start.18
  96.5 17.1 %copy-start.15 = (f32[256,512]{1,0:T(8,128)S(1)}, f32[256,512]{1,0:T(8,128)}, u32[]{:S(2)}) copy-start(f32[256,512]{1,0:T(8,128)} %subtract_convert_fusion) | copy-start | bytes 1572868
  96.5 17.1 %copy-start.22 = (f32[4]{0:T(128)S(1)}, f32[4]{0:T(128)}, u32[]{:S(2)}) copy-start(f32[4]{0:T(128)} %param.25) | copy-start | bytes 52
  115.6 2.4 copy-start.14
  120.0 2.4 copy-start.13
  124.1 27.3 %copy-start.11 = (bf16[2,4,2,1,8,2048]{5,4,3,2,1,0:T(8,128)(2,1)S(1)}, bf16[2,4,2,1,8,2048]{5,4,3,2,1,0:T(8,128)(2,1)}, u32[]{:S(2)}) copy-start(bf16[2,4,2,1,8,2048]{5,4,3,2,1,0:T(8,128)(2,1)} %get-tuple-element.25) | copy-start | bytes 1572868
  124.2 12.8 %collective-permute-start.2 = (bf16[2,4,2,8,2048]{4,3,1,0,2:T(8,128)(2,1)S(1)}, bf16[2,4,2,8,2048]{4,3,1,0,2:T(8,128)(2,1)}, u32[]{:S(2)}, u32[]{:S(2)}) collective-permute-start(bf16[2,4,2,8,2048]{4,3,1,0,2:T(8,128)(2,1)S(1)} %bitcast.157), channel_id=1, source_target_pairs={{0,3},{1,0},{2,1},{3,2},{4,7},{5,4},{6,5},{7,6},{8,11},{9,8},{10,9... | collective-permute-start | bytes 1572872 | tf_op jit(solution)/shard_map/ppermute | solution.py:58
  124.3 25.5 %collective-permute-start.1 = (bf16[2,4,2,8,2048]{4,3,1,0,2:T(8,128)(2,1)S(1)}, bf16[2,4,2,8,2048]{4,3,1,0,2:T(8,128)(2,1)S(1)}, u32[]{:S(2)}, u32[]{:S(2)}) collective-permute-start(bf16[2,4,2,8,2048]{4,3,1,0,2:T(8,128)(2,1)S(1)} %bitcast.158), channel_id=1, source_target_pairs={{0,2},{1,3},{2,0},{3,1},{4,6},{5,7},{6,4},{7,5},{8,10},{9,11},{10,... | collective-permute-start | bytes 1572872 | tf_op jit(solution)/shard_map/ppermute | solution.py:58
  126.4 23.4 %collective-permute-start = (bf16[2,4,2,8,2048]{4,3,1,0,2:T(8,128)(2,1)S(1)}, bf16[2,4,2,8,2048]{4,3,1,0,2:T(8,128)(2,1)S(1)}, u32[]{:S(2)}, u32[]{:S(2)}) collective-permute-start(bf16[2,4,2,8,2048]{4,3,1,0,2:T(8,128)(2,1)S(1)} %bitcast.159), channel_id=1, source_target_pairs={{0,1},{1,2},{2,3},{3,0},{4,5},{5,6},{6,7},{7,4},{8,9},{9,10},{10,1... | collective-permute-start | bytes 1572872 | tf_op jit(solution)/shard_map/ppermute | solution.py:58
  149.8 0.8 copy-start.16
  150.6 0.8 copy-start.17
  151.4 2.5 copy-start.20
  151.4 16.6 %copy-start.10 = (bf16[8,8,2048]{2,1,0:T(8,128)(2,1)S(1)}, bf16[8,8,2048]{2,1,0:T(8,128)(2,1)}, u32[]{:S(2)}) copy-start(bf16[8,8,2048]{2,1,0:T(8,128)(2,1)} %all_to_all.40) | copy-start | bytes 786436
  153.1 1.0 copy-start.9
  153.1 17.2 %copy-start.5 = (bf16[8,32,32,128]{3,2,1,0:T(8,128)(2,1)S(1)}, bf16[8,32,32,128]{3,2,1,0:T(8,128)(2,1)}, u32[]{:S(2)}) copy-start(bf16[8,32,32,128]{3,2,1,0:T(8,128)(2,1)} %get-tuple-element.35) | copy-start | bytes 6291460
  153.9 14.0 %collective-permute-start.3 = (bf16[2,4,8,2048]{3,2,0,1:T(8,128)(2,1)}, bf16[2,4,8,2048]{3,2,0,1:T(8,128)(2,1)}, u32[]{:S(2)}, u32[]{:S(2)}) collective-permute-start(bf16[2,4,8,2048]{3,2,0,1:T(8,128)(2,1)} %copy.69), channel_id=1, source_target_pairs={{0,4},{1,5},{2,6},{3,7},{4,0},{5,1},{6,2},{7,3},{8,12},{9,13},{10,... | collective-permute-start | bytes 786440 | tf_op jit(solution)/shard_map/ppermute | solution.py:64
  173.0 125.2 %all-to-all-start.2 = ((bf16[32,2,32,4,128]{4,2,3,1,0:T(8,128)(2,1)}), bf16[32,2,32,4,128]{4,2,3,1,0:T(8,128)(2,1)S(1)}, u32[]{:S(2)}, u32[]{:S(2)}) async-start(bf16[32,2,32,4,128]{4,2,3,1,0:T(8,128)(2,1)} %bitcast.141), calls=%async_computation.2 | async-start | bytes 4194304 | tf_op jit(solution)/shard_map/all_to_all | solution.py:118
  267.9 13.1 %collective-permute-start.6 = (bf16[2,4,2,8,2048]{4,3,1,0,2:T(8,128)(2,1)S(1)}, bf16[2,4,2,8,2048]{4,3,1,0,2:T(8,128)(2,1)S(1)}, u32[]{:S(2)}, u32[]{:S(2)}) collective-permute-start(bf16[2,4,2,8,2048]{4,3,1,0,2:T(8,128)(2,1)S(1)} %bitcast.160), channel_id=1, source_target_pairs={{0,3},{1,0},{2,1},{3,2},{4,7},{5,4},{6,5},{7,6},{8,11},{9,8},{10,9... | collective-permute-start | bytes 1572872 | tf_op jit(solution)/shard_map/ppermute | solution.py:58
  268.0 23.8 %collective-permute-start.5 = (bf16[2,4,2,8,2048]{4,3,1,0,2:T(8,128)(2,1)S(1)}, bf16[2,4,2,8,2048]{4,3,1,0,2:T(8,128)(2,1)S(1)}, u32[]{:S(2)}, u32[]{:S(2)}) collective-permute-start(bf16[2,4,2,8,2048]{4,3,1,0,2:T(8,128)(2,1)S(1)} %bitcast.161), channel_id=1, source_target_pairs={{0,2},{1,3},{2,0},{3,1},{4,6},{5,7},{6,4},{7,5},{8,10},{9,11},{10,... | collective-permute-start | bytes 1572872 | tf_op jit(solution)/shard_map/ppermute | solution.py:58
  269.1 24.1 %collective-permute-start.4 = (bf16[2,4,2,8,2048]{4,3,1,0,2:T(8,128)(2,1)S(1)}, bf16[2,4,2,8,2048]{4,3,1,0,2:T(8,128)(2,1)S(1)}, u32[]{:S(2)}, u32[]{:S(2)}) collective-permute-start(bf16[2,4,2,8,2048]{4,3,1,0,2:T(8,128)(2,1)S(1)} %bitcast.162), channel_id=1, source_target_pairs={{0,1},{1,2},{2,3},{3,0},{4,5},{5,6},{6,7},{7,4},{8,9},{9,10},{10,1... | collective-permute-start | bytes 1572872 | tf_op jit(solution)/shard_map/ppermute | solution.py:58
  293.5 1.0 copy-start.7
  294.6 14.8 %collective-permute-start.7 = (bf16[2,4,8,2048]{3,2,0,1:T(8,128)(2,1)S(1)}, bf16[2,4,8,2048]{3,2,0,1:T(8,128)(2,1)S(1)}, u32[]{:S(2)}, u32[]{:S(2)}) collective-permute-start(bf16[2,4,8,2048]{3,2,0,1:T(8,128)(2,1)S(1)} %copy.81), channel_id=1, source_target_pairs={{0,4},{1,5},{2,6},{3,7},{4,0},{5,1},{6,2},{7,3},{8,12},{9,13},{10,... | collective-permute-start | bytes 786440 | tf_op jit(solution)/shard_map/ppermute | solution.py:64
  298.1 1.6 copy-start.6
  300.1 9.2 %copy-start.8 = (f32[2,4,2,8,2048]{4,3,1,0,2:T(8,128)S(1)}, f32[2,4,2,8,2048]{4,3,1,0,2:T(8,128)}, u32[]{:S(2)}) copy-start(f32[2,4,2,8,2048]{4,3,1,0,2:T(8,128)} %copy-done.7) | copy-start | bytes 3145732
  310.2 11.8 %all-to-all-start.3 = ((bf16[2,4,8,2048]{3,2,0,1:T(8,128)(2,1)}), bf16[2,4,8,2048]{3,2,0,1:T(8,128)(2,1)S(1)}, u32[]{:S(2)}, u32[]{:S(2)}) async-start(bf16[2,4,8,2048]{3,2,0,1:T(8,128)(2,1)} %select_convert_fusion), calls=%async_computation.3 | async-start | bytes 524288 | tf_op jit(solution)/shard_map/all_to_all | solution.py:179
  314.1 10.9 %copy-start.1 = (bf16[2048,4,192]{0,2,1:T(8,128)(2,1)S(1)}, bf16[2048,4,192]{0,2,1:T(8,128)(2,1)}, u32[]{:S(2)}) copy-start(bf16[2048,4,192]{0,2,1:T(8,128)(2,1)} %param.24) | copy-start | bytes 9437188
  322.0 0.7 copy-start.12
Sparse Core Ops, SparseCore 0:
  21.0 68.8 all-gather.2
  170.5 78.1 all-gather.4

commit v9 on v8

--- a/solution.py
+++ b/solution.py
@@ -63,6 +63,25 @@
         sent = lax.dynamic_index_in_dim(rounded_one, (outer_me + shift) % outer_size, 2, False)
         total = total + lax.ppermute(sent, "head", pairs).astype(jnp.float32)
     return total
+
+
+def head_gather(rows, head_count):
+    inner_size = 4 if head_count % 4 == 0 else head_count
+    outer_size = head_count // inner_size
+    me = lax.axis_index("head")
+    outer_me, inner_me = me // inner_size, me % inner_size
+    held = [rows]
+    for shift in range(1, outer_size):
+        pairs = [(j, ((j // inner_size + shift) % outer_size) * inner_size + j % inner_size) for j in range(head_count)]
+        held.append(lax.ppermute(rows, "head", pairs))
+    by_outer = jnp.take(jnp.stack(held), (outer_me - jnp.arange(outer_size)) % outer_size, axis=0)
+    held = [by_outer]
+    for shift in range(1, inner_size):
+        pairs = [(j, (j // inner_size) * inner_size + (j % inner_size + shift) % inner_size) for j in range(head_count)]
+        held.append(lax.ppermute(by_outer, "head", pairs))
+    by_inner = jnp.take(jnp.stack(held), (inner_me - jnp.arange(inner_size)) % inner_size, axis=0)
+    gathered = jnp.moveaxis(by_inner, (0, 1), (3, 2))
+    return gathered.reshape(rows.shape[:2] + (head_count * rows.shape[2],) + rows.shape[3:])
 
 
 def local(
@@ -127,7 +146,7 @@
     dealt_rows = lax.all_to_all(dealt_acts, "req", split_axis=0, concat_axis=1, tiled=True).reshape(
         group_size, req_count, stretch_rows, features
     )
-    gathered = lax.all_gather(dealt_rows, "head", axis=2, tiled=True)
+    gathered = head_gather(dealt_rows, head_count)
     normed = (
         layer_norm(gathered.astype(jnp.float32), attn_gain)
         .astype(jnp.bfloat16)
@@ -155,7 +174,7 @@
     attn_rows = head_sum(partial_attn, head_count, stretch_rows)
     residual_rows = dealt_rows.astype(jnp.float32) + attn_rows
     normed_rows = layer_norm(residual_rows, mlp_gain).astype(jnp.bfloat16)
-    normed_all = lax.all_gather(normed_rows, "head", axis=2, tiled=True)
+    normed_all = head_gather(normed_rows, head_count)
     inner = jax.nn.gelu(
         jnp.dot(
             normed_all.reshape(group_size * stretch_max, features),

time: 333 us -> 378 us (1.14)
  waiting for transfers between devices: 191 us -> 211 us
  starting transfers between devices: 17.6 us -> 35.2 us
  other arithmetic: 22 us -> 39.2 us
  between operations: 14.7 us -> 1.38 us
  local copies, waits for them, and re-layouts: 52.6 us -> 63 us
  blocking collectives: 9.17 us -> 0 us
    ppermute x0 -> x8, waiting for transfers between devices: none -> 150 us  [the longest x2 107 us: head_gather(): held.append(lax.ppermute(rows, 'head', pairs))]
    all_gather x2 -> x0, waiting for transfers between devices: 108 us -> none  [the longest x1 71.8 us: local(): normed_all = lax.all_gather(normed_rows, 'head', axis=2, tiled=True)]
    all_to_all x2, waiting for transfers between devices: 15.8 us -> 0.01 us  [local(): incoming = lax.all_to_all(outgoing, ('req', 'head'), 0, 0, tiled=True)]
    gather x0 -> x4, local copies, waits for them, and re-layouts: none -> 11.7 us  [the longest x2 7.49 us: head_gather(): jnp.take(jnp.stack(held), (inner_me - jnp.arange(inner_size)) % inner_siz...]
    all_to_all x1 -> x0, blocking collectives: 9.17 us -> none  [local(): lax.all_to_all(dealt_acts, 'req', split_axis=0, concat_axis=1, tiled=True)]
    another operation x0 -> x7, other arithmetic: none -> 7.6 us  [head_gather(): jnp.stack(held)]
    ppermute x0 -> x8, starting transfers between devices: none -> 7.5 us  [the longest x6 5.08 us: head_gather(): held.append(lax.ppermute(by_outer, 'head', pairs))]
    ppermute x2, waiting for transfers between devices: 20.7 us -> 15.6 us  [head_sum(): total = total + lax.ppermute(sent, 'head', pairs).astype(jnp.float32)]
  transfers between devices with their start and end apart: 13 -> 20, of which waited for: 10 -> 13; matrix products, arithmetic and copies ran while one was open for 21% -> 26% of each run, Pallas kernels for 0% -> 0%
where the time goes in v9:
time: 378 us; the launch traced here: 376 us
  waiting for transfers between devices  211 us (56%)
  local copies, waits for them, and re-layouts  63 us (17%)
  other arithmetic  39.2 us (10%)
  starting transfers between devices  35.2 us (9%)
  matrix products  26.8 us (7%)
    ppermute x2, waiting for transfers between devices, head_gather(): held.append(lax.ppermute(rows, 'head', pairs))  107 us
    ppermute x6, waiting for transfers between devices, head_sum(): lax.ppermute(sent, 'head', pairs).astype(jnp.float32)  44.8 us
    ppermute x6, waiting for transfers between devices, head_gather(): held.append(lax.ppermute(by_outer, 'head', pairs))  43.7 us
    ppermute x2, waiting for transfers between devices, head_sum(): total = total + lax.ppermute(sent, 'head', pairs).astype(jnp.float32)  15.6 us
    dot_general x1, matrix products, local(): jnp.dot(inner, down_weight, preferred_element_type=jnp.float32)  14.3 us
    unnamed x53, local copies, waits for them, and re-layouts  13.2 us
    all_to_all x2, starting transfers between devices, local(): incoming = lax.all_to_all(outgoing, ('req', 'head'), 0, 0, tiled=True)  12.1 us
    another operation x7, other arithmetic, head_gather(): jnp.stack(held)  7.6 us
  transfers between devices with their start and end apart: 20, of which 13 were waited for; matrix products, arithmetic and copies ran while one was open for 26% of the time, Pallas kernels for 0%

profile of v9, /device:TPU:1, one launch (start us, length us, event | category | flops | bytes accessed | tf_op | source)
XLA Modules:
  0.0 376.3 jit_solution(6161178947345547940)
XLA Ops:
  5.9 4.3 %all-to-all-start = ((bf16[8,8,2048]{2,1,0:T(8,128)(2,1)}), bf16[8,8,2048]{2,1,0:T(8,128)(2,1)S(1)}, u32[]{:S(2)}, u32[]{:S(2)}) async-start(bf16[8,8,2048]{2,1,0:T(8,128)(2,1)} %broadcast_select_fusion.4), calls=%async_computation | async-start | bytes 524288 | tf_op jit(solution)/shard_map/all_to_all | solution.py:146
  14.8 1.9 iota_compare_fusion.1
  18.1 5.2 %slice_bitcast_fusion = (bf16[8,32,32,128]{3,2,1,0:T(8,128)(2,1)}, bf16[8,32,32,128]{3,2,1,0:T(8,128)(2,1)}) fusion(bf16[2,8,32,32,128]{4,3,2,1,0:T(8,128)(2,1)} %param.23), kind=kLoop, calls=%fused_computation.47 | loop fusion | bytes 8388608 | tf_op jit(solution)/shard_map/squeeze | solution.py:129
  23.3 3.7 gather_fusion.7
  27.0 3.7 gather_fusion.3
  30.8 3.5 select_select_fusion
  35.1 1.8 copy.60
  40.2 6.8 %all-to-all-start.1 = ((bf16[32,2,32,4,128]{4,2,3,1,0:T(8,128)(2,1)}), bf16[32,2,32,4,128]{4,2,3,1,0:T(8,128)(2,1)}, u32[]{:S(2)}, u32[]{:S(2)}) async-start(bf16[32,2,32,4,128]{4,2,3,1,0:T(8,128)(2,1)} %bitcast.170), calls=%async_computation.1 | async-start | bytes 4194304 | tf_op jit(solution)/shard_map/all_to_all | solution.py:137
  47.0 2.4 collective-permute-start
  50.0 56.3 %collective-permute-done = bf16[2,4,8,2048]{3,2,0,1:T(8,128)(2,1)S(1)} collective-permute-done((bf16[2,4,8,2048]{3,2,0,1:T(8,128)(2,1)S(1)}, bf16[2,4,8,2048]{3,2,0,1:T(8,128)(2,1)S(1)}, u32[]{:S(2)}, u32[]{:S(2)}) %collective-permute-start) | collective-permute-done | bytes 262176 | tf_op jit(solution)/shard_map/ppermute | solution.py:76
  107.2 2.4 gather_fusion.4
  109.6 1.9 broadcast_select_fusion.2
  111.5 2.4 collective-permute-start.2
  115.9 8.6 %collective-permute-done.3 = bf16[2,2,4,8,2048]{4,3,1,2,0:T(8,128)(2,1)} collective-permute-done((bf16[2,2,4,8,2048]{4,3,1,2,0:T(8,128)(2,1)}, bf16[2,2,4,8,2048]{4,3,1,2,0:T(8,128)(2,1)}, u32[]{:S(2)}, u32[]{:S(2)}) %collective-permute-start.3) | collective-permute-done | bytes 524320 | tf_op jit(solution)/shard_map/ppermute | solution.py:81
  124.4 12.2 %collective-permute-done.2 = bf16[2,2,4,8,2048]{4,3,1,2,0:T(8,128)(2,1)} collective-permute-done((bf16[2,2,4,8,2048]{4,3,1,2,0:T(8,128)(2,1)}, bf16[2,2,4,8,2048]{4,3,1,2,0:T(8,128)(2,1)}, u32[]{:S(2)}, u32[]{:S(2)}) %collective-permute-start.2) | collective-permute-done | bytes 524320 | tf_op jit(solution)/shard_map/ppermute | solution.py:81
  136.8 2.9 pad_maximum_fusion.1
  139.8 3.8 gather_fusion.5
  143.5 2.3 bitcast_reduce_fusion
  147.8 1.8 fusion.19
  151.9 2.0 fusion.130
  153.8 2.9 convolution_convert_fusion.2
  156.9 2.0 fusion.131
  158.9 2.2 convolution_convert_fusion.3
  162.0 1.7 convolution_convert_fusion.1
  165.8 2.5 collective-permute-start.5
  168.7 9.3 %collective-permute-done.6 = bf16[2,4,2,8,2048]{4,3,1,0,2:T(8,128)(2,1)S(1)} collective-permute-done((bf16[2,4,2,8,2048]{4,3,1,0,2:T(8,128)(2,1)S(1)}, bf16[2,4,2,8,2048]{4,3,1,0,2:T(8,128)(2,1)S(1)}, u32[]{:S(2)}, u32[]{:S(2)}) %collective-permute-start.6) | collective-permute-done | bytes 524320 | tf_op jit(solution)/shard_map/ppermute | solution.py:58
  177.9 13.1 %collective-permute-done.5 = bf16[2,4,2,8,2048]{4,3,1,0,2:T(8,128)(2,1)S(1)} collective-permute-done((bf16[2,4,2,8,2048]{4,3,1,0,2:T(8,128)(2,1)S(1)}, bf16[2,4,2,8,2048]{4,3,1,0,2:T(8,128)(2,1)S(1)}, u32[]{:S(2)}, u32[]{:S(2)}) %collective-permute-start.5) | collective-permute-done | bytes 524320 | tf_op jit(solution)/shard_map/ppermute | solution.py:58
  192.6 2.0 fusion.26
  196.3 1.8 copy.75
  198.0 5.3 %all-to-all-start.2 = ((bf16[32,2,32,4,128]{4,2,3,1,0:T(8,128)(2,1)}), bf16[32,2,32,4,128]{4,2,3,1,0:T(8,128)(2,1)S(1)}, u32[]{:S(2)}, u32[]{:S(2)}) async-start(bf16[32,2,32,4,128]{4,2,3,1,0:T(8,128)(2,1)} %bitcast.172), calls=%async_computation.2 | async-start | bytes 4194304 | tf_op jit(solution)/shard_map/all_to_all | solution.py:137
  204.4 9.5 %collective-permute-done.7 = bf16[2,4,8,2048]{3,2,0,1:T(8,128)(2,1)} collective-permute-done((bf16[2,4,8,2048]{3,2,0,1:T(8,128)(2,1)}, bf16[2,4,8,2048]{3,2,0,1:T(8,128)(2,1)}, u32[]{:S(2)}, u32[]{:S(2)}) %collective-permute-start.7) | collective-permute-done | bytes 262176 | tf_op jit(solution)/shard_map/ppermute | solution.py:64
  215.8 50.4 %collective-permute-done.8 = bf16[2,4,8,2048]{3,2,0,1:T(8,128)(2,1)S(1)} collective-permute-done((bf16[2,4,8,2048]{3,2,0,1:T(8,128)(2,1)S(1)}, bf16[2,4,8,2048]{3,2,0,1:T(8,128)(2,1)S(1)}, u32[]{:S(2)}, u32[]{:S(2)}) %collective-permute-start.8) | collective-permute-done | bytes 262176 | tf_op jit(solution)/shard_map/ppermute | solution.py:76
  267.1 1.7 gather_fusion.8
  269.0 2.6 collective-permute-start.10
  271.7 10.2 %collective-permute-done.11 = bf16[2,2,4,8,2048]{4,3,1,2,0:T(8,128)(2,1)S(1)} collective-permute-done((bf16[2,2,4,8,2048]{4,3,1,2,0:T(8,128)(2,1)S(1)}, bf16[2,2,4,8,2048]{4,3,1,2,0:T(8,128)(2,1)S(1)}, u32[]{:S(2)}, u32[]{:S(2)}) %collective-permute-start.11) | collective-permute-done | bytes 524320 | tf_op jit(solution)/shard_map/ppermute | solution.py:81
  282.0 12.4 %collective-permute-done.10 = bf16[2,2,4,8,2048]{4,3,1,2,0:T(8,128)(2,1)S(1)} collective-permute-done((bf16[2,2,4,8,2048]{4,3,1,2,0:T(8,128)(2,1)S(1)}, bf16[2,2,4,8,2048]{4,3,1,2,0:T(8,128)(2,1)S(1)}, u32[]{:S(2)}, u32[]{:S(2)}) %collective-permute-start.10) | collective-permute-done | bytes 524320 | tf_op jit(solution)/shard_map/ppermute | solution.py:81
  296.0 3.7 gather_fusion.9
  299.7 1.9 select_bitcast_fusion
  303.0 14.3 %convolution_convert_fusion = bf16[512,2048]{1,0:T(8,128)(2,1)} fusion(bf16[1024,2048]{1,0:T(8,128)(2,1)} %param.33, bf16[512,2048]{1,0:T(8,128)(2,1)} %bitcast.182, bf16[2048,1024]{1,0:T(8,128)(2,1)} %param.32), kind=kOutput, calls=%fused_computation.24 | convolution fusion | flops 4330094592 | bytes 12582912 | tf_op jit(solution)/shard_map/dot_general | solution.py:186
  317.3 1.7 constant_dynamic-slice_fusion.3
  320.0 2.7 collective-permute-start.13
  322.9 9.6 %collective-permute-done.14 = bf16[2,4,2,8,2048]{4,3,1,0,2:T(8,128)(2,1)S(1)} collective-permute-done((bf16[2,4,2,8,2048]{4,3,1,0,2:T(8,128)(2,1)S(1)}, bf16[2,4,2,8,2048]{4,3,1,0,2:T(8,128)(2,1)S(1)}, u32[]{:S(2)}, u32[]{:S(2)}) %collective-permute-start.14) | collective-permute-done | bytes 524320 | tf_op jit(solution)/shard_map/ppermute | solution.py:58
  332.5 12.9 %collective-permute-done.13 = bf16[2,4,2,8,2048]{4,3,1,0,2:T(8,128)(2,1)S(1)} collective-permute-done((bf16[2,4,2,8,2048]{4,3,1,0,2:T(8,128)(2,1)S(1)}, bf16[2,4,2,8,2048]{4,3,1,0,2:T(8,128)(2,1)S(1)}, u32[]{:S(2)}, u32[]{:S(2)}) %collective-permute-start.13) | collective-permute-done | bytes 524320 | tf_op jit(solution)/shard_map/ppermute | solution.py:58
  346.8 3.5 copy.73
  352.3 2.2 copy.77
  354.5 6.1 %collective-permute-done.15 = bf16[2,4,8,2048]{3,2,0,1:T(8,128)(2,1)S(1)} collective-permute-done((bf16[2,4,8,2048]{3,2,0,1:T(8,128)(2,1)S(1)}, bf16[2,4,8,2048]{3,2,0,1:T(8,128)(2,1)S(1)}, u32[]{:S(2)}, u32[]{:S(2)}) %collective-permute-start.15) | collective-permute-done | bytes 262176 | tf_op jit(solution)/shard_map/ppermute | solution.py:64
  361.5 3.9 %all-to-all-start.3 = ((bf16[2,4,8,2048]{3,2,0,1:T(8,128)(2,1)}), bf16[2,4,8,2048]{3,2,0,1:T(8,128)(2,1)S(1)}, u32[]{:S(2)}, u32[]{:S(2)}) async-start(bf16[2,4,8,2048]{3,2,0,1:T(8,128)(2,1)} %select_convert_fusion), calls=%async_computation.3 | async-start | bytes 524288 | tf_op jit(solution)/shard_map/all_to_all | solution.py:198
  365.4 7.9 %copy.85 = bf16[8,2,256,4,128]{4,3,2,1,0:T(4,128)(2,1)} copy(bf16[8,2,256,4,128]{4,2,3,1,0:T(8,128)(2,1)} %bitcast.169) | data formatting | bytes 8388608
  (156 shorter events, 45.3 us)
Async XLA Ops:
  0.6 147.1 %copy-start = (bf16[2048,4,192]{0,2,1:T(8,128)(2,1)S(1)}, bf16[2048,4,192]{0,2,1:T(8,128)(2,1)}, u32[]{:S(2)}) copy-start(bf16[2048,4,192]{0,2,1:T(8,128)(2,1)} %param.28) | copy-start | bytes 9437188
  0.6 9.5 %copy-start.23 = (s32[8]{0:T(128)S(1)}, s32[8]{0:T(128)}, u32[]{:S(2)}) copy-start(s32[8]{0:T(128)} %param.26) | copy-start | bytes 100
  0.7 9.6 %copy-start.2 = (s32[8]{0:T(128)S(1)}, s32[8]{0:T(128)}, u32[]{:S(2)}) copy-start(s32[8]{0:T(128)} %param.25) | copy-start | bytes 100
  0.7 10.3 %copy-start.3 = (s32[8]{0:T(128)S(1)}, s32[8]{0:T(128)}, u32[]{:S(2)}) copy-start(s32[8]{0:T(128)} %param.24) | copy-start | bytes 100
  5.9 34.3 %all-to-all-start = ((bf16[8,8,2048]{2,1,0:T(8,128)(2,1)}), bf16[8,8,2048]{2,1,0:T(8,128)(2,1)S(1)}, u32[]{:S(2)}, u32[]{:S(2)}) async-start(bf16[8,8,2048]{2,1,0:T(8,128)(2,1)} %broadcast_select_fusion.4), calls=%async_computation | async-start | bytes 524288 | tf_op jit(solution)/shard_map/all_to_all | solution.py:146
  18.1 89.1 %copy-start.20 = (s32[1024]{0:T(1024)}, s32[1024]{0:T(1024)S(1)}, u32[]{:S(2)}) copy-start(s32[1024]{0:T(1024)S(1)} %pad_clamp_fusion.2) | copy-start | bytes 12292
  40.2 110.3 %all-to-all-start.1 = ((bf16[32,2,32,4,128]{4,2,3,1,0:T(8,128)(2,1)}), bf16[32,2,32,4,128]{4,2,3,1,0:T(8,128)(2,1)}, u32[]{:S(2)}, u32[]{:S(2)}) async-start(bf16[32,2,32,4,128]{4,2,3,1,0:T(8,128)(2,1)} %bitcast.170), calls=%async_computation.1 | async-start | bytes 4194304 | tf_op jit(solution)/shard_map/all_to_all | solution.py:137
  47.0 59.3 %collective-permute-start = (bf16[2,4,8,2048]{3,2,0,1:T(8,128)(2,1)S(1)}, bf16[2,4,8,2048]{3,2,0,1:T(8,128)(2,1)S(1)}, u32[]{:S(2)}, u32[]{:S(2)}) collective-permute-start(bf16[2,4,8,2048]{3,2,0,1:T(8,128)(2,1)S(1)} %bitcast.178), channel_id=1, source_target_pairs={{0,4},{1,5},{2,6},{3,7},{4,0},{5,1},{6,2},{7,3},{8,12},{9,13},{10,... | collective-permute-start | bytes 786440 | tf_op jit(solution)/shard_map/ppermute | solution.py:76
  111.5 12.9 %collective-permute-start.3 = (bf16[2,2,4,8,2048]{4,3,1,2,0:T(8,128)(2,1)}, bf16[2,2,4,8,2048]{4,3,1,2,0:T(8,128)(2,1)}, u32[]{:S(2)}, u32[]{:S(2)}) collective-permute-start(bf16[2,2,4,8,2048]{4,3,1,2,0:T(8,128)(2,1)} %broadcast_select_fusion.2), channel_id=1, source_target_pairs={{0,3},{1,0},{2,1},{3,2},{4,7},{5,4},{6,5},{7,6},{8,11},{9,8},{10,9... | collective-permute-start | bytes 1572872 | tf_op jit(solution)/shard_map/ppermute | solution.py:81
  111.5 25.1 %collective-permute-start.2 = (bf16[2,2,4,8,2048]{4,3,1,2,0:T(8,128)(2,1)}, bf16[2,2,4,8,2048]{4,3,1,2,0:T(8,128)(2,1)}, u32[]{:S(2)}, u32[]{:S(2)}) collective-permute-start(bf16[2,2,4,8,2048]{4,3,1,2,0:T(8,128)(2,1)} %broadcast_select_fusion.2), channel_id=1, source_target_pairs={{0,2},{1,3},{2,0},{3,1},{4,6},{5,7},{6,4},{7,5},{8,10},{9,11},{10,... | collective-permute-start | bytes 1572872 | tf_op jit(solution)/shard_map/ppermute | solution.py:81
  113.9 22.9 %collective-permute-start.1 = (bf16[2,2,4,8,2048]{4,3,1,2,0:T(8,128)(2,1)}, bf16[2,2,4,8,2048]{4,3,1,2,0:T(8,128)(2,1)}, u32[]{:S(2)}, u32[]{:S(2)}) collective-permute-start(bf16[2,2,4,8,2048]{4,3,1,2,0:T(8,128)(2,1)} %broadcast_select_fusion.2), channel_id=1, source_target_pairs={{0,1},{1,2},{2,3},{3,0},{4,5},{5,6},{6,7},{7,4},{8,9},{9,10},{10,1... | collective-permute-start | bytes 1572872 | tf_op jit(solution)/shard_map/ppermute | solution.py:81
  143.5 2.3 copy-start.4
  149.6 0.9 copy-start.17
  150.5 1.4 copy-start.13
  150.5 1.4 copy-start.18
  150.5 1.4 copy-start.25
  153.8 3.0 copy-start.12
  158.9 2.3 copy-start.19
  158.9 3.1 copy-start.11
  164.7 13.2 %collective-permute-start.6 = (bf16[2,4,2,8,2048]{4,3,1,0,2:T(8,128)(2,1)S(1)}, bf16[2,4,2,8,2048]{4,3,1,0,2:T(8,128)(2,1)S(1)}, u32[]{:S(2)}, u32[]{:S(2)}) collective-permute-start(bf16[2,4,2,8,2048]{4,3,1,0,2:T(8,128)(2,1)S(1)} %bitcast.189), channel_id=1, source_target_pairs={{0,3},{1,0},{2,1},{3,2},{4,7},{5,4},{6,5},{7,6},{8,11},{9,8},{10,9... | collective-permute-start | bytes 1572872 | tf_op jit(solution)/shard_map/ppermute | solution.py:58
  165.8 25.2 %collective-permute-start.5 = (bf16[2,4,2,8,2048]{4,3,1,0,2:T(8,128)(2,1)S(1)}, bf16[2,4,2,8,2048]{4,3,1,0,2:T(8,128)(2,1)S(1)}, u32[]{:S(2)}, u32[]{:S(2)}) collective-permute-start(bf16[2,4,2,8,2048]{4,3,1,0,2:T(8,128)(2,1)S(1)} %bitcast.190), channel_id=1, source_target_pairs={{0,2},{1,3},{2,0},{3,1},{4,6},{5,7},{6,4},{7,5},{8,10},{9,11},{10,... | collective-permute-start | bytes 1572872 | tf_op jit(solution)/shard_map/ppermute | solution.py:58
  168.3 22.7 %collective-permute-start.4 = (bf16[2,4,2,8,2048]{4,3,1,0,2:T(8,128)(2,1)S(1)}, bf16[2,4,2,8,2048]{4,3,1,0,2:T(8,128)(2,1)S(1)}, u32[]{:S(2)}, u32[]{:S(2)}) collective-permute-start(bf16[2,4,2,8,2048]{4,3,1,0,2:T(8,128)(2,1)S(1)} %bitcast.191), channel_id=1, source_target_pairs={{0,1},{1,2},{2,3},{3,0},{4,5},{5,6},{6,7},{7,4},{8,9},{9,10},{10,1... | collective-permute-start | bytes 1572872 | tf_op jit(solution)/shard_map/ppermute | solution.py:58
  177.9 13.1 %copy-start.14 = (bf16[2,4,2,8,2048]{4,3,1,0,2:T(8,128)(2,1)}, bf16[2,4,2,8,2048]{4,3,1,0,2:T(8,128)(2,1)S(1)}, u32[]{:S(2)}) copy-start(bf16[2,4,2,8,2048]{4,3,1,0,2:T(8,128)(2,1)S(1)} %collective-permute-done.6) | copy-start | bytes 1572868
  191.0 0.8 copy-start.15
  191.8 0.8 copy-start.16
  192.6 2.9 copy-start.5
  194.6 1.7 copy-start.9
  195.4 18.5 %collective-permute-start.7 = (bf16[2,4,8,2048]{3,2,0,1:T(8,128)(2,1)}, bf16[2,4,8,2048]{3,2,0,1:T(8,128)(2,1)}, u32[]{:S(2)}, u32[]{:S(2)}) collective-permute-start(bf16[2,4,8,2048]{3,2,0,1:T(8,128)(2,1)} %copy.71), channel_id=1, source_target_pairs={{0,4},{1,5},{2,6},{3,7},{4,0},{5,1},{6,2},{7,3},{8,12},{9,13},{10,... | collective-permute-start | bytes 786440 | tf_op jit(solution)/shard_map/ppermute | solution.py:64
  198.0 5.3 %copy-start.21 = (bf16[2048]{0:T(1024)(128)(2,1)S(1)}, bf16[2048]{0:T(1024)(128)(2,1)}, u32[]{:S(2)}) copy-start(bf16[2048]{0:T(1024)(128)(2,1)} %param.31) | copy-start | bytes 12292
  198.0 5.4 %copy-start.24 = (s32[8]{0:T(128)S(1)}, s32[8]{0:T(128)}, u32[]{:S(2)}) copy-start(s32[8]{0:T(128)} %param.26) | copy-start | bytes 100
  198.0 152.3 %all-to-all-start.2 = ((bf16[32,2,32,4,128]{4,2,3,1,0:T(8,128)(2,1)}), bf16[32,2,32,4,128]{4,2,3,1,0:T(8,128)(2,1)S(1)}, u32[]{:S(2)}, u32[]{:S(2)}) async-start(bf16[32,2,32,4,128]{4,2,3,1,0:T(8,128)(2,1)} %bitcast.172), calls=%async_computation.2 | async-start | bytes 4194304 | tf_op jit(solution)/shard_map/all_to_all | solution.py:137
  215.6 50.6 %collective-permute-start.8 = (bf16[2,4,8,2048]{3,2,0,1:T(8,128)(2,1)S(1)}, bf16[2,4,8,2048]{3,2,0,1:T(8,128)(2,1)S(1)}, u32[]{:S(2)}, u32[]{:S(2)}) collective-permute-start(bf16[2,4,8,2048]{3,2,0,1:T(8,128)(2,1)S(1)} %multiply_convert_fusion), channel_id=1, source_target_pairs={{0,4},{1,5},{2,6},{3,7},{4,0},{5,1},{6,2},{7,3},{8,12},{9,13},{10,... | collective-permute-start | bytes 786440 | tf_op jit(solution)/shard_map/ppermute | solution.py:76
  268.9 13.1 %collective-permute-start.11 = (bf16[2,2,4,8,2048]{4,3,1,2,0:T(8,128)(2,1)S(1)}, bf16[2,2,4,8,2048]{4,3,1,2,0:T(8,128)(2,1)S(1)}, u32[]{:S(2)}, u32[]{:S(2)}) collective-permute-start(bf16[2,2,4,8,2048]{4,3,1,2,0:T(8,128)(2,1)S(1)} %broadcast_select_fusion.1), channel_id=1, source_target_pairs={{0,3},{1,0},{2,1},{3,2},{4,7},{5,4},{6,5},{7,6},{8,11},{9,8},{10,9... | collective-permute-start | bytes 1572872 | tf_op jit(solution)/shard_map/ppermute | solution.py:81
  269.0 25.4 %collective-permute-start.10 = (bf16[2,2,4,8,2048]{4,3,1,2,0:T(8,128)(2,1)S(1)}, bf16[2,2,4,8,2048]{4,3,1,2,0:T(8,128)(2,1)S(1)}, u32[]{:S(2)}, u32[]{:S(2)}) collective-permute-start(bf16[2,2,4,8,2048]{4,3,1,2,0:T(8,128)(2,1)S(1)} %broadcast_select_fusion.1), channel_id=1, source_target_pairs={{0,2},{1,3},{2,0},{3,1},{4,6},{5,7},{6,4},{7,5},{8,10},{9,11},{10,... | collective-permute-start | bytes 1572872 | tf_op jit(solution)/shard_map/ppermute | solution.py:81
  271.6 22.8 %collective-permute-start.9 = (bf16[2,2,4,8,2048]{4,3,1,2,0:T(8,128)(2,1)S(1)}, bf16[2,2,4,8,2048]{4,3,1,2,0:T(8,128)(2,1)S(1)}, u32[]{:S(2)}, u32[]{:S(2)}) collective-permute-start(bf16[2,2,4,8,2048]{4,3,1,2,0:T(8,128)(2,1)S(1)} %broadcast_select_fusion.1), channel_id=1, source_target_pairs={{0,1},{1,2},{2,3},{3,0},{4,5},{5,6},{6,7},{7,4},{8,9},{9,10},{10,1... | collective-permute-start | bytes 1572872 | tf_op jit(solution)/shard_map/ppermute | solution.py:81
  319.0 3.8 %copy-start.22 = (s32[2]{0:T(128)S(1)}, s32[2]{0:T(128)}, u32[]{:S(2)}) copy-start(s32[2]{0:T(128)} %get-tuple-element.39) | copy-start | bytes 28
  319.1 13.4 %collective-permute-start.14 = (bf16[2,4,2,8,2048]{4,3,1,0,2:T(8,128)(2,1)S(1)}, bf16[2,4,2,8,2048]{4,3,1,0,2:T(8,128)(2,1)S(1)}, u32[]{:S(2)}, u32[]{:S(2)}) collective-permute-start(bf16[2,4,2,8,2048]{4,3,1,0,2:T(8,128)(2,1)S(1)} %bitcast.192), channel_id=1, source_target_pairs={{0,3},{1,0},{2,1},{3,2},{4,7},{5,4},{6,5},{7,6},{8,11},{9,8},{10,9... | collective-permute-start | bytes 1572872 | tf_op jit(solution)/shard_map/ppermute | solution.py:58
  320.0 25.4 %collective-permute-start.13 = (bf16[2,4,2,8,2048]{4,3,1,0,2:T(8,128)(2,1)S(1)}, bf16[2,4,2,8,2048]{4,3,1,0,2:T(8,128)(2,1)S(1)}, u32[]{:S(2)}, u32[]{:S(2)}) collective-permute-start(bf16[2,4,2,8,2048]{4,3,1,0,2:T(8,128)(2,1)S(1)} %bitcast.193), channel_id=1, source_target_pairs={{0,2},{1,3},{2,0},{3,1},{4,6},{5,7},{6,4},{7,5},{8,10},{9,11},{10,... | collective-permute-start | bytes 1572872 | tf_op jit(solution)/shard_map/ppermute | solution.py:58
  322.7 22.7 %collective-permute-start.12 = (bf16[2,4,2,8,2048]{4,3,1,0,2:T(8,128)(2,1)S(1)}, bf16[2,4,2,8,2048]{4,3,1,0,2:T(8,128)(2,1)S(1)}, u32[]{:S(2)}, u32[]{:S(2)}) collective-permute-start(bf16[2,4,2,8,2048]{4,3,1,0,2:T(8,128)(2,1)S(1)} %bitcast.194), channel_id=1, source_target_pairs={{0,1},{1,2},{2,3},{3,0},{4,5},{5,6},{6,7},{7,4},{8,9},{9,10},{10,1... | collective-permute-start | bytes 1572872 | tf_op jit(solution)/shard_map/ppermute | solution.py:58
  345.7 1.0 copy-start.7
  346.7 13.9 %collective-permute-start.15 = (bf16[2,4,8,2048]{3,2,0,1:T(8,128)(2,1)S(1)}, bf16[2,4,8,2048]{3,2,0,1:T(8,128)(2,1)S(1)}, u32[]{:S(2)}, u32[]{:S(2)}) collective-permute-start(bf16[2,4,8,2048]{3,2,0,1:T(8,128)(2,1)S(1)} %copy.83), channel_id=1, source_target_pairs={{0,4},{1,5},{2,6},{3,7},{4,0},{5,1},{6,2},{7,3},{8,12},{9,13},{10,... | collective-permute-start | bytes 786440 | tf_op jit(solution)/shard_map/ppermute | solution.py:64
  350.3 1.6 copy-start.6
  352.3 8.4 %copy-start.8 = (f32[2,4,2,8,2048]{4,3,1,0,2:T(8,128)S(1)}, f32[2,4,2,8,2048]{4,3,1,0,2:T(8,128)}, u32[]{:S(2)}) copy-start(f32[2,4,2,8,2048]{4,3,1,0,2:T(8,128)} %copy-done.7) | copy-start | bytes 3145732
  361.5 11.8 %all-to-all-start.3 = ((bf16[2,4,8,2048]{3,2,0,1:T(8,128)(2,1)}), bf16[2,4,8,2048]{3,2,0,1:T(8,128)(2,1)S(1)}, u32[]{:S(2)}, u32[]{:S(2)}) async-start(bf16[2,4,8,2048]{3,2,0,1:T(8,128)(2,1)} %select_convert_fusion), calls=%async_computation.3 | async-start | bytes 524288 | tf_op jit(solution)/shard_map/all_to_all | solution.py:198
  365.4 10.9 %copy-start.1 = (bf16[2048,4,192]{0,2,1:T(8,128)(2,1)S(1)}, bf16[2048,4,192]{0,2,1:T(8,128)(2,1)}, u32[]{:S(2)}) copy-start(bf16[2048,4,192]{0,2,1:T(8,128)(2,1)} %param.28) | copy-start | bytes 9437188
  373.3 0.7 copy-start.10

commit v10 on v8

--- a/solution.py
+++ b/solution.py
@@ -63,6 +63,12 @@
         sent = lax.dynamic_index_in_dim(rounded_one, (outer_me + shift) % outer_size, 2, False)
         total = total + lax.ppermute(sent, "head", pairs).astype(jnp.float32)
     return total
+
+
+def land(incoming, req_count, head_count):
+    shape = (req_count, head_count) + incoming.shape[1:]
+    landed = incoming.reshape(shape).transpose(0, 2, 1, 3, 4, 5)
+    return landed.reshape(landed.shape[:2] + (-1,) + landed.shape[4:])
 
 
 def local(
@@ -104,6 +110,7 @@
     heads = cache_prefill.shape[3]
     devices = req_count * head_count
     chunks = []
+    deferred = []
     for layer in range(local_layers):
         dealt_cache = jnp.where(
             keep[:, :, None, None],
@@ -115,14 +122,11 @@
             .transpose(0, 3, 1, 2, 4, 5)
             .reshape(devices, group_size, prefix_rows, heads // head_count, pair_width)
         )
-        incoming = lax.all_to_all(outgoing, ("req", "head"), 0, 0, tiled=True)
-        chunks.append(
-            incoming.reshape(req_count, head_count, group_size, prefix_rows, heads // head_count, pair_width)
-            .transpose(0, 2, 1, 3, 4, 5)
-            .reshape(req_count, group_size, head_count * prefix_rows, heads // head_count, pair_width)
-        )
+        if layer == 0:
+            chunks.append(land(lax.all_to_all(outgoing, ("req", "head"), 0, 0, tiled=True), req_count, head_count))
+        else:
+            deferred.append(outgoing)
     current = chunks[0][0]
-    relaid = jnp.stack(chunks, axis=1).reshape((req_count * local_layers,) + chunks[0].shape[1:])
     dealt_acts = jnp.take(stretch_acts, req_order, axis=0)
     dealt_rows = lax.all_to_all(dealt_acts, "req", split_axis=0, concat_axis=1, tiled=True).reshape(
         group_size, req_count, stretch_rows, features
@@ -156,6 +160,10 @@
     residual_rows = dealt_rows.astype(jnp.float32) + attn_rows
     normed_rows = layer_norm(residual_rows, mlp_gain).astype(jnp.bfloat16)
     normed_all = lax.all_gather(normed_rows, "head", axis=2, tiled=True)
+    deferred, normed_all = lax.optimization_barrier((deferred, normed_all))
+    for outgoing in deferred:
+        chunks.append(land(lax.all_to_all(outgoing, ("req", "head"), 0, 0, tiled=True), req_count, head_count))
+    relaid = jnp.stack(chunks, axis=1).reshape((req_count * local_layers,) + chunks[0].shape[1:])
     inner = jax.nn.gelu(
         jnp.dot(
             normed_all.reshape(group_size * stretch_max, features),

time: 333 us -> 329 us (0.988); the launches traced: 332 us -> 324 us
  waiting for transfers between devices: 191 us -> 177 us
  starting transfers between devices: 17.6 us -> 24.7 us
    all_gather x1, waiting for transfers between devices: 71.8 us -> 43 us  [local(): normed_all = lax.all_gather(normed_rows, 'head', axis=2, tiled=True)]
    ppermute x6, waiting for transfers between devices: 46.2 us -> 59.7 us  [head_sum(): lax.ppermute(sent, 'head', pairs).astype(jnp.float32)]
    unnamed x47 -> x43, local copies, waits for them, and re-layouts: 13.5 us -> 11.8 us
  transfers between devices with their start and end apart: 13 -> 13, of which waited for: 10 -> 10; matrix products, arithmetic and copies ran while one was open for 21% -> 20% of each run, Pallas kernels for 0% -> 0%
where the time goes in v10:
time: 329 us; the launch traced here: 324 us
  waiting for transfers between devices  177 us (54%)
  local copies, waits for them, and re-layouts  50.8 us (15%)
  matrix products  25.2 us (8%)
  starting transfers between devices  24.7 us (8%)
  other arithmetic  22.2 us (7%)
  between operations  14.6 us (4%)
  blocking collectives  9.17 us (3%)
    ppermute x6, waiting for transfers between devices, head_sum(): lax.ppermute(sent, 'head', pairs).astype(jnp.float32)  59.7 us
    all_gather x1, waiting for transfers between devices, local(): normed_all = lax.all_gather(normed_rows, 'head', axis=2, tiled=True)  43 us
    all_gather x1, waiting for transfers between devices, local(): gathered = lax.all_gather(dealt_rows, 'head', axis=2, tiled=True)  35.7 us
    ppermute x2, waiting for transfers between devices, head_sum(): total = total + lax.ppermute(sent, 'head', pairs).astype(jnp.float32)  22.6 us
    all_to_all x2, waiting for transfers between devices, local(): lax.all_to_all(outgoing, ('req', 'head'), 0, 0, tiled=True)  15.8 us
    dot_general x1, matrix products, local(): jnp.dot(inner, down_weight, preferred_element_type=jnp.float32)  14.3 us
    unnamed x43, local copies, waits for them, and re-layouts  11.8 us
    all_to_all x2, starting transfers between devices, local(): lax.all_to_all(outgoing, ('req', 'head'), 0, 0, tiled=True)  10.7 us
  transfers between devices with their start and end apart: 13, of which 10 were waited for; matrix products, arithmetic and copies ran while one was open for 20% of the time, Pallas kernels for 0%

profile of v10, /device:TPU:1, one launch (start us, length us, event | category | flops | bytes accessed | tf_op | source)
XLA Modules:
  0.0 323.6 jit_solution(10944904907828797788)
XLA Ops:
  8.0 1.4 gather_fusion
  10.1 1.5 gather_fusion.2
  11.7 9.2 %all_to_all.40 = bf16[8,8,2048]{2,1,0:T(8,128)(2,1)} all-to-all(bf16[8,8,2048]{2,1,0:T(8,128)(2,1)S(1)} %broadcast_select_fusion.1), channel_id=1, replica_groups=mesh['req'=4,'head'=8] {'req'}, dimensions={0} | all-to-all | bytes 524288 | tf_op jit(solution)/shard_map/all_to_all | solution.py:131
  20.9 5.2 %slice_bitcast_fusion = (bf16[8,32,32,128]{3,2,1,0:T(8,128)(2,1)}, bf16[8,32,32,128]{3,2,1,0:T(8,128)(2,1)}) fusion(bf16[2,8,32,32,128]{4,3,2,1,0:T(8,128)(2,1)} %param.19), kind=kLoop, calls=%fused_computation.40 | loop fusion | bytes 8388608 | tf_op jit(solution)/shard_map/squeeze | solution.py:117
  26.1 3.7 %gather_fusion.5 = bf16[8,32,32,128]{3,2,1,0:T(8,128)(2,1)} fusion(bf16[8,32,32,128]{3,2,1,0:T(8,128)(2,1)} %get-tuple-element.23, s32[1024]{0:T(1024)S(1)} %pad_clamp_fusion.1), kind=kCustom, calls=%fused_computation.5.clone | custom fusion | bytes 4194336 | tf_op jit(solution)/shard_map/jit(_take)/gather | solution.py:117
  29.8 3.8 %gather_fusion.3 = bf16[8,32,32,128]{3,2,1,0:T(8,128)(2,1)} fusion(bf16[8,32,32,128]{3,2,1,0:T(8,128)(2,1)} %get-tuple-element.24, s32[1024]{0:T(1024)S(1)} %pad_clamp_fusion.1), kind=kCustom, calls=%fused_computation.2.clone | custom fusion | bytes 4194336 | tf_op jit(solution)/shard_map/jit(_take)/gather | solution.py:117
  33.7 3.5 %select_select_fusion = (bf16[8,32,32,128]{3,2,1,0:T(8,128)(2,1)}, bf16[8,32,32,128]{3,2,1,0:T(8,128)(2,1)S(1)}) fusion(bf16[8,32,32,128]{3,2,1,0:T(8,128)(2,1)} %gather_fusion.5, pred[8]{0:T(512)(128)(4,1)S(1)} %get-tuple-element.22, pred[8,32]{1,0:T(8,128)(4,1)S(1)} %broadcast_compare_fusion, bf16[8,32,32,128]{3,2,1,0:T(8,128)(2,1)} %gather_fusion.3), kind=kLoop, calls=%fused_computation.25 | loop fusion | flops 4194304 | bytes 8388872 | tf_op jit(solution)/shard_map/jit(_where)/select_n | solution.py:115
  38.0 1.8 copy.58
  39.8 6.1 %all-to-all-start.1 = ((bf16[32,2,32,4,128]{4,2,3,1,0:T(8,128)(2,1)}), bf16[32,2,32,4,128]{4,2,3,1,0:T(8,128)(2,1)}, u32[]{:S(2)}, u32[]{:S(2)}) async-start(bf16[32,2,32,4,128]{4,2,3,1,0:T(8,128)(2,1)} %bitcast.139), calls=%async_computation.1 | async-start | bytes 4194304 | tf_op jit(solution)/shard_map/all_to_all | solution.py:126
  49.0 1.3 iota_compare_fusion.1
  54.2 35.7 %all-gather.3.cloned.1.call-done = bf16[2,4,64,2048]{3,2,0,1:T(8,128)(2,1)} async-done(((bf16[2,4,8,2048]{3,2,0,1:T(8,128)(2,1)}), bf16[2,4,64,2048]{3,2,0,1:T(8,128)(2,1)}) %all-gather.3.cloned.1.call-update) | async-done | bytes 2097168 | tf_op jit(solution)/shard_map/all_gather | solution.py:134
  89.9 2.1 convert_reduce_fusion
  93.7 1.8 fusion.19
  96.5 15.8 %all-to-all-done.1 = bf16[32,2,32,4,128]{4,2,3,1,0:T(8,128)(2,1)} async-done(((bf16[32,2,32,4,128]{4,2,3,1,0:T(8,128)(2,1)}), bf16[32,2,32,4,128]{4,2,3,1,0:T(8,128)(2,1)}, u32[]{:S(2)}, u32[]{:S(2)}) %all-to-all-start.1) | async-done | bytes 2097184 | tf_op jit(solution)/shard_map/all_to_all | solution.py:126
  112.3 1.1 fusion.126
  113.6 2.0 fusion.129
  115.6 2.2 convolution_convert_fusion.3
  118.0 2.0 fusion.128
  119.9 2.2 convolution_convert_fusion.2
  123.1 1.0 constant_dynamic-slice_fusion.7
  124.1 0.9 collective-permute-start
  125.2 1.8 collective-permute-start.2
  127.0 10.8 %collective-permute-done = bf16[2,4,2,8,2048]{4,3,1,0,2:T(8,128)(2,1)} collective-permute-done((bf16[2,4,2,8,2048]{4,3,1,0,2:T(8,128)(2,1)S(1)}, bf16[2,4,2,8,2048]{4,3,1,0,2:T(8,128)(2,1)}, u32[]{:S(2)}, u32[]{:S(2)}) %collective-permute-start) | collective-permute-done | bytes 524320 | tf_op jit(solution)/shard_map/ppermute | solution.py:58
  137.8 0.9 collective-permute-done.1
  138.8 11.4 %collective-permute-done.2 = bf16[2,4,2,8,2048]{4,3,1,0,2:T(8,128)(2,1)S(1)} collective-permute-done((bf16[2,4,2,8,2048]{4,3,1,0,2:T(8,128)(2,1)S(1)}, bf16[2,4,2,8,2048]{4,3,1,0,2:T(8,128)(2,1)S(1)}, u32[]{:S(2)}, u32[]{:S(2)}) %collective-permute-start.2) | collective-permute-done | bytes 524320 | tf_op jit(solution)/shard_map/ppermute | solution.py:58
  151.0 1.7 fusion.26
  153.8 14.2 %collective-permute-done.3 = bf16[2,4,8,2048]{3,2,0,1:T(8,128)(2,1)} collective-permute-done((bf16[2,4,8,2048]{3,2,0,1:T(8,128)(2,1)}, bf16[2,4,8,2048]{3,2,0,1:T(8,128)(2,1)}, u32[]{:S(2)}, u32[]{:S(2)}) %collective-permute-start.3) | collective-permute-done | bytes 262176 | tf_op jit(solution)/shard_map/ppermute | solution.py:64
  168.0 1.3 fusion.124
  171.3 1.8 copy.73
  173.0 1.0 sort.17
  174.0 43.0 %all-gather.5.cloned.1.call-done = bf16[2,4,64,2048]{3,2,0,1:T(8,128)(2,1)} async-done(((bf16[2,4,8,2048]{3,2,0,1:T(8,128)(2,1)}), bf16[2,4,64,2048]{3,2,0,1:T(8,128)(2,1)}) %all-gather.5.cloned.1.call-update) | async-done | bytes 2097168 | tf_op jit(solution)/shard_map/all_gather | solution.py:162
  217.0 3.2 copy.76
  220.1 4.6 %all-to-all-start.2 = ((bf16[32,2,32,4,128]{4,2,3,1,0:T(8,128)(2,1)}), bf16[32,2,32,4,128]{4,2,3,1,0:T(8,128)(2,1)S(1)}, u32[]{:S(2)}, u32[]{:S(2)}) async-start(bf16[32,2,32,4,128]{4,2,3,1,0:T(8,128)(2,1)} %bitcast.44), calls=%async_computation.2 | async-start | bytes 4194304 | tf_op jit(solution)/shard_map/all_to_all | solution.py:165
  224.8 14.3 %convolution_convert_fusion = bf16[512,2048]{1,0:T(8,128)(2,1)} fusion(bf16[1024,2048]{1,0:T(8,128)(2,1)} %param.29, bf16[512,2048]{1,0:T(8,128)(2,1)} %bitcast.148, bf16[2048,1024]{1,0:T(8,128)(2,1)} %param.28), kind=kOutput, calls=%fused_computation.20 | convolution fusion | flops 4330094592 | bytes 12582912 | tf_op jit(solution)/shard_map/dot_general | solution.py:175
  239.0 1.7 constant_dynamic-slice_fusion.3
  240.8 1.4 collective-permute-start.4
  242.3 1.2 collective-permute-start.5
  243.5 1.5 collective-permute-start.6
  245.1 27.2 %collective-permute-done.4 = bf16[2,4,2,8,2048]{4,3,1,0,2:T(8,128)(2,1)S(1)} collective-permute-done((bf16[2,4,2,8,2048]{4,3,1,0,2:T(8,128)(2,1)S(1)}, bf16[2,4,2,8,2048]{4,3,1,0,2:T(8,128)(2,1)S(1)}, u32[]{:S(2)}, u32[]{:S(2)}) %collective-permute-start.4) | collective-permute-done | bytes 524320 | tf_op jit(solution)/shard_map/ppermute | solution.py:58
  272.3 9.4 %collective-permute-done.6 = bf16[2,4,2,8,2048]{4,3,1,0,2:T(8,128)(2,1)S(1)} collective-permute-done((bf16[2,4,2,8,2048]{4,3,1,0,2:T(8,128)(2,1)S(1)}, bf16[2,4,2,8,2048]{4,3,1,0,2:T(8,128)(2,1)S(1)}, u32[]{:S(2)}, u32[]{:S(2)}) %collective-permute-start.6) | collective-permute-done | bytes 524320 | tf_op jit(solution)/shard_map/ppermute | solution.py:58
  282.1 1.8 collective-permute-start.7
  283.9 3.5 %copy.71 = bf16[4,2,8,32,4,128]{5,3,2,4,1,0:T(8,128)(2,1)} copy(bf16[4,2,8,32,4,128]{5,3,4,1,2,0:T(8,128)(2,1)} %bitcast.7) | data formatting | bytes 4194304 | tf_op jit(solution)/shard_map/transpose | solution.py:70
  287.4 8.4 %collective-permute-done.7 = bf16[2,4,8,2048]{3,2,0,1:T(8,128)(2,1)S(1)} collective-permute-done((bf16[2,4,8,2048]{3,2,0,1:T(8,128)(2,1)S(1)}, bf16[2,4,8,2048]{3,2,0,1:T(8,128)(2,1)S(1)}, u32[]{:S(2)}, u32[]{:S(2)}) %collective-permute-start.7) | collective-permute-done | bytes 262176 | tf_op jit(solution)/shard_map/ppermute | solution.py:64
  296.4 1.0 copy-done.6
  297.8 2.2 copy.75
  300.9 4.9 %all-to-all-start.3 = ((bf16[2,4,8,2048]{3,2,0,1:T(8,128)(2,1)}), bf16[2,4,8,2048]{3,2,0,1:T(8,128)(2,1)S(1)}, u32[]{:S(2)}, u32[]{:S(2)}) async-start(bf16[2,4,8,2048]{3,2,0,1:T(8,128)(2,1)} %select_convert_fusion), calls=%async_computation.3 | async-start | bytes 524288 | tf_op jit(solution)/shard_map/all_to_all | solution.py:187
  305.8 7.9 %copy.83 = bf16[8,2,256,4,128]{4,3,2,1,0:T(4,128)(2,1)} copy(bf16[8,2,256,4,128]{4,2,3,1,0:T(8,128)(2,1)} %bitcast.138) | data formatting | bytes 8388608
  314.4 1.5 gather_fusion.6
  (115 shorter events, 21.1 us)
Async XLA Ops:
  7.2 86.5 %copy-start = (bf16[2048,4,192]{0,2,1:T(8,128)(2,1)S(1)}, bf16[2048,4,192]{0,2,1:T(8,128)(2,1)}, u32[]{:S(2)}) copy-start(bf16[2048,4,192]{0,2,1:T(8,128)(2,1)} %param.24) | copy-start | bytes 9437188
  7.2 82.7 %all-gather.3.cloned.1.call-start = ((), (), s32[]{:S(2)}) async-start(), calls=%async_computation.4 | async-start | bytes 2359296 | tf_op jit(solution)/shard_map/all_gather | solution.py:134
  39.8 6.4 %copy-start.19 = (s32[8]{0:T(128)S(1)}, s32[8]{0:T(128)}, u32[]{:S(2)}) copy-start(s32[8]{0:T(128)} %param.22) | copy-start | bytes 100
  39.8 6.5 %copy-start.2 = (s32[8]{0:T(128)S(1)}, s32[8]{0:T(128)}, u32[]{:S(2)}) copy-start(s32[8]{0:T(128)} %param.21) | copy-start | bytes 100
  39.8 7.2 %copy-start.3 = (s32[8]{0:T(128)S(1)}, s32[8]{0:T(128)}, u32[]{:S(2)}) copy-start(s32[8]{0:T(128)} %param.20) | copy-start | bytes 100
  39.8 7.8 %copy-start.17 = (bf16[2048]{0:T(1024)(128)(2,1)S(1)}, bf16[2048]{0:T(1024)(128)(2,1)}, u32[]{:S(2)}) copy-start(bf16[2048]{0:T(1024)(128)(2,1)} %param.23) | copy-start | bytes 12292
  39.8 72.5 %all-to-all-start.1 = ((bf16[32,2,32,4,128]{4,2,3,1,0:T(8,128)(2,1)}), bf16[32,2,32,4,128]{4,2,3,1,0:T(8,128)(2,1)}, u32[]{:S(2)}, u32[]{:S(2)}) async-start(bf16[32,2,32,4,128]{4,2,3,1,0:T(8,128)(2,1)} %bitcast.139), calls=%async_computation.1 | async-start | bytes 4194304 | tf_op jit(solution)/shard_map/all_to_all | solution.py:126
  45.9 171.1 %all-gather.5.cloned.1.call-start = ((), (), s32[]{:S(2)}) async-start(), calls=%async_computation.5 | async-start | bytes 2359296 | tf_op jit(solution)/shard_map/all_gather | solution.py:162
  89.9 2.2 copy-start.4
  95.5 0.9 copy-start.16
  96.4 17.1 %copy-start.13 = (f32[256,512]{1,0:T(8,128)S(1)}, f32[256,512]{1,0:T(8,128)}, u32[]{:S(2)}) copy-start(f32[256,512]{1,0:T(8,128)} %subtract_convert_fusion.1) | copy-start | bytes 1572868
  96.4 17.1 %copy-start.20 = (f32[4]{0:T(128)S(1)}, f32[4]{0:T(128)}, u32[]{:S(2)}) copy-start(f32[4]{0:T(128)} %param.25) | copy-start | bytes 52
  115.6 2.4 copy-start.12
  119.9 2.4 copy-start.11
  124.1 26.9 %copy-start.9 = (bf16[2,4,2,1,8,2048]{5,4,3,2,1,0:T(8,128)(2,1)S(1)}, bf16[2,4,2,1,8,2048]{5,4,3,2,1,0:T(8,128)(2,1)}, u32[]{:S(2)}) copy-start(bf16[2,4,2,1,8,2048]{5,4,3,2,1,0:T(8,128)(2,1)} %get-tuple-element.29) | copy-start | bytes 1572868
  124.1 13.7 %collective-permute-start = (bf16[2,4,2,8,2048]{4,3,1,0,2:T(8,128)(2,1)S(1)}, bf16[2,4,2,8,2048]{4,3,1,0,2:T(8,128)(2,1)}, u32[]{:S(2)}, u32[]{:S(2)}) collective-permute-start(bf16[2,4,2,8,2048]{4,3,1,0,2:T(8,128)(2,1)S(1)} %bitcast.156), channel_id=1, source_target_pairs={{0,1},{1,2},{2,3},{3,0},{4,5},{5,6},{6,7},{7,4},{8,9},{9,10},{10,1... | collective-permute-start | bytes 1572872 | tf_op jit(solution)/shard_map/ppermute | solution.py:58
  125.1 13.7 %collective-permute-start.1 = (bf16[2,4,2,8,2048]{4,3,1,0,2:T(8,128)(2,1)S(1)}, bf16[2,4,2,8,2048]{4,3,1,0,2:T(8,128)(2,1)S(1)}, u32[]{:S(2)}, u32[]{:S(2)}) collective-permute-start(bf16[2,4,2,8,2048]{4,3,1,0,2:T(8,128)(2,1)S(1)} %bitcast.157), channel_id=1, source_target_pairs={{0,2},{1,3},{2,0},{3,1},{4,6},{5,7},{6,4},{7,5},{8,10},{9,11},{10,... | collective-permute-start | bytes 1572872 | tf_op jit(solution)/shard_map/ppermute | solution.py:58
  125.2 24.9 %collective-permute-start.2 = (bf16[2,4,2,8,2048]{4,3,1,0,2:T(8,128)(2,1)S(1)}, bf16[2,4,2,8,2048]{4,3,1,0,2:T(8,128)(2,1)S(1)}, u32[]{:S(2)}, u32[]{:S(2)}) collective-permute-start(bf16[2,4,2,8,2048]{4,3,1,0,2:T(8,128)(2,1)S(1)} %bitcast.158), channel_id=1, source_target_pairs={{0,3},{1,0},{2,1},{3,2},{4,7},{5,4},{6,5},{7,6},{8,11},{9,8},{10,9... | collective-permute-start | bytes 1572872 | tf_op jit(solution)/shard_map/ppermute | solution.py:58
  138.8 11.4 %copy-start.14 = (bf16[2,4,2,8,2048]{4,3,1,0,2:T(8,128)(2,1)}, bf16[2,4,2,8,2048]{4,3,1,0,2:T(8,128)(2,1)S(1)}, u32[]{:S(2)}) copy-start(bf16[2,4,2,8,2048]{4,3,1,0,2:T(8,128)(2,1)S(1)} %collective-permute-done.1) | copy-start | bytes 1572868
  150.2 0.8 copy-start.15
  151.0 2.5 copy-start.18
  151.0 17.0 %copy-start.8 = (bf16[8,8,2048]{2,1,0:T(8,128)(2,1)S(1)}, bf16[8,8,2048]{2,1,0:T(8,128)(2,1)}, u32[]{:S(2)}) copy-start(bf16[8,8,2048]{2,1,0:T(8,128)(2,1)} %all_to_all.40) | copy-start | bytes 786436
  152.7 1.1 copy-start.7
  152.7 17.7 %copy-start.5 = (bf16[8,32,32,128]{3,2,1,0:T(8,128)(2,1)S(1)}, bf16[8,32,32,128]{3,2,1,0:T(8,128)(2,1)}, u32[]{:S(2)}) copy-start(bf16[8,32,32,128]{3,2,1,0:T(8,128)(2,1)} %get-tuple-element.39) | copy-start | bytes 6291460
  153.5 14.5 %collective-permute-start.3 = (bf16[2,4,8,2048]{3,2,0,1:T(8,128)(2,1)}, bf16[2,4,8,2048]{3,2,0,1:T(8,128)(2,1)}, u32[]{:S(2)}, u32[]{:S(2)}) collective-permute-start(bf16[2,4,8,2048]{3,2,0,1:T(8,128)(2,1)} %copy.69), channel_id=1, source_target_pairs={{0,4},{1,5},{2,6},{3,7},{4,0},{5,1},{6,2},{7,3},{8,12},{9,13},{10,... | collective-permute-start | bytes 786440 | tf_op jit(solution)/shard_map/ppermute | solution.py:64
  220.1 75.7 %all-to-all-start.2 = ((bf16[32,2,32,4,128]{4,2,3,1,0:T(8,128)(2,1)}), bf16[32,2,32,4,128]{4,2,3,1,0:T(8,128)(2,1)S(1)}, u32[]{:S(2)}, u32[]{:S(2)}) async-start(bf16[32,2,32,4,128]{4,2,3,1,0:T(8,128)(2,1)} %bitcast.44), calls=%async_computation.2 | async-start | bytes 4194304 | tf_op jit(solution)/shard_map/all_to_all | solution.py:165
  240.8 31.5 %collective-permute-start.4 = (bf16[2,4,2,8,2048]{4,3,1,0,2:T(8,128)(2,1)S(1)}, bf16[2,4,2,8,2048]{4,3,1,0,2:T(8,128)(2,1)S(1)}, u32[]{:S(2)}, u32[]{:S(2)}) collective-permute-start(bf16[2,4,2,8,2048]{4,3,1,0,2:T(8,128)(2,1)S(1)} %bitcast.159), channel_id=1, source_target_pairs={{0,1},{1,2},{2,3},{3,0},{4,5},{5,6},{6,7},{7,4},{8,9},{9,10},{10,1... | collective-permute-start | bytes 1572872 | tf_op jit(solution)/shard_map/ppermute | solution.py:58
  242.3 30.0 %collective-permute-start.5 = (bf16[2,4,2,8,2048]{4,3,1,0,2:T(8,128)(2,1)S(1)}, bf16[2,4,2,8,2048]{4,3,1,0,2:T(8,128)(2,1)S(1)}, u32[]{:S(2)}, u32[]{:S(2)}) collective-permute-start(bf16[2,4,2,8,2048]{4,3,1,0,2:T(8,128)(2,1)S(1)} %bitcast.160), channel_id=1, source_target_pairs={{0,2},{1,3},{2,0},{3,1},{4,6},{5,7},{6,4},{7,5},{8,10},{9,11},{10,... | collective-permute-start | bytes 1572872 | tf_op jit(solution)/shard_map/ppermute | solution.py:58
  243.5 38.1 %collective-permute-start.6 = (bf16[2,4,2,8,2048]{4,3,1,0,2:T(8,128)(2,1)S(1)}, bf16[2,4,2,8,2048]{4,3,1,0,2:T(8,128)(2,1)S(1)}, u32[]{:S(2)}, u32[]{:S(2)}) collective-permute-start(bf16[2,4,2,8,2048]{4,3,1,0,2:T(8,128)(2,1)S(1)} %bitcast.161), channel_id=1, source_target_pairs={{0,3},{1,0},{2,1},{3,2},{4,7},{5,4},{6,5},{7,6},{8,11},{9,8},{10,9... | collective-permute-start | bytes 1572872 | tf_op jit(solution)/shard_map/ppermute | solution.py:58
  282.1 13.7 %collective-permute-start.7 = (bf16[2,4,8,2048]{3,2,0,1:T(8,128)(2,1)S(1)}, bf16[2,4,8,2048]{3,2,0,1:T(8,128)(2,1)S(1)}, u32[]{:S(2)}, u32[]{:S(2)}) collective-permute-start(bf16[2,4,8,2048]{3,2,0,1:T(8,128)(2,1)S(1)} %copy.81), channel_id=1, source_target_pairs={{0,4},{1,5},{2,6},{3,7},{4,0},{5,1},{6,2},{7,3},{8,12},{9,13},{10,... | collective-permute-start | bytes 786440 | tf_op jit(solution)/shard_map/ppermute | solution.py:64
  295.8 1.6 copy-start.6
  300.9 12.9 %all-to-all-start.3 = ((bf16[2,4,8,2048]{3,2,0,1:T(8,128)(2,1)}), bf16[2,4,8,2048]{3,2,0,1:T(8,128)(2,1)S(1)}, u32[]{:S(2)}, u32[]{:S(2)}) async-start(bf16[2,4,8,2048]{3,2,0,1:T(8,128)(2,1)} %select_convert_fusion), calls=%async_computation.3 | async-start | bytes 524288 | tf_op jit(solution)/shard_map/all_to_all | solution.py:187
  305.8 10.9 %copy-start.1 = (bf16[2048,4,192]{0,2,1:T(8,128)(2,1)S(1)}, bf16[2048,4,192]{0,2,1:T(8,128)(2,1)}, u32[]{:S(2)}) copy-start(bf16[2048,4,192]{0,2,1:T(8,128)(2,1)} %param.24) | copy-start | bytes 9437188
  313.7 0.7 copy-start.10
Sparse Core Ops, SparseCore 0:
  21.0 68.8 all-gather.2
  170.6 46.3 all-gather.4

commit v11 on v10

--- a/solution.py
+++ b/solution.py
@@ -111,10 +111,12 @@
     devices = req_count * head_count
     chunks = []
     deferred = []
+    later_layers = cache_prefill[1:]
     for layer in range(local_layers):
+        source = cache_prefill[0] if layer == 0 else later_layers[layer - 1]
         dealt_cache = jnp.where(
             keep[:, :, None, None],
-            jnp.take(cache_prefill[layer], req_order, axis=0),
+            jnp.take(source, req_order, axis=0),
             jnp.zeros((), cache_prefill.dtype),
         )
         outgoing = (
@@ -123,7 +125,9 @@
             .reshape(devices, group_size, prefix_rows, heads // head_count, pair_width)
         )
         if layer == 0:
-            chunks.append(land(lax.all_to_all(outgoing, ("req", "head"), 0, 0, tiled=True), req_count, head_count))
+            incoming = lax.all_to_all(outgoing, ("req", "head"), 0, 0, tiled=True)
+            incoming, later_layers = lax.optimization_barrier((incoming, later_layers))
+            chunks.append(land(incoming, req_count, head_count))
         else:
             deferred.append(outgoing)
     current = chunks[0][0]

time: 329 us -> 321 us (0.976)
    all_to_all x2 -> x1, waiting for transfers between devices: 15.8 us -> 0.01 us  [local(): lax.all_to_all(outgoing, ('req', 'head'), 0, 0, tiled=True)]
    all_gather x1, waiting for transfers between devices: 35.7 us -> 50.3 us  [local(): gathered = lax.all_gather(dealt_rows, 'head', axis=2, tiled=True)]
    all_to_all x2 -> x1, starting transfers between devices: 10.7 us -> 4.61 us  [local(): lax.all_to_all(outgoing, ('req', 'head'), 0, 0, tiled=True)]
    all_to_all x0 -> x1, starting transfers between devices: none -> 6.11 us  [local(): incoming = lax.all_to_all(outgoing, ('req', 'head'), 0, 0, tiled=True)]
    squeeze x1 -> x0, local copies, waits for them, and re-layouts: 5.17 us -> none  [local(): cache_prefill[layer]]
    slice x0 -> x1, local copies, waits for them, and re-layouts: none -> 5.17 us  [local(): later_layers = cache_prefill[1:]]
    all_gather x1, waiting for transfers between devices: 43 us -> 39.5 us  [local(): normed_all = lax.all_gather(normed_rows, 'head', axis=2, tiled=True)]
    unnamed x43 -> x39, local copies, waits for them, and re-layouts: 11.8 us -> 10.7 us
where the time goes in v11:
time: 321 us; the launch traced here: 315 us
  waiting for transfers between devices  174 us (54%)
  local copies, waits for them, and re-layouts  48 us (15%)
  matrix products  25.2 us (8%)
  starting transfers between devices  24.8 us (8%)
  other arithmetic  19.6 us (6%)
  between operations  14.7 us (5%)
  blocking collectives  9.17 us (3%)
    ppermute x6, waiting for transfers between devices, head_sum(): lax.ppermute(sent, 'head', pairs).astype(jnp.float32)  59.7 us
    all_gather x1, waiting for transfers between devices, local(): gathered = lax.all_gather(dealt_rows, 'head', axis=2, tiled=True)  50.3 us
    all_gather x1, waiting for transfers between devices, local(): normed_all = lax.all_gather(normed_rows, 'head', axis=2, tiled=True)  39.5 us
    ppermute x2, waiting for transfers between devices, head_sum(): total = total + lax.ppermute(sent, 'head', pairs).astype(jnp.float32)  22.8 us
    dot_general x1, matrix products, local(): jnp.dot(inner, down_weight, preferred_element_type=jnp.float32)  14.3 us
    unnamed x39, local copies, waits for them, and re-layouts  10.7 us
    all_to_all x1, blocking collectives, local(): lax.all_to_all(dealt_acts, 'req', split_axis=0, concat_axis=1, tiled=True)  9.17 us
    ppermute x6, starting transfers between devices, head_sum(): lax.ppermute(sent, 'head', pairs).astype(jnp.float32)  6.95 us
  transfers between devices with their start and end apart: 13, of which 10 were waited for; matrix products, arithmetic and copies ran while one was open for 20% of the time, Pallas kernels for 0%

profile of v11, /device:TPU:1, one launch (start us, length us, event | category | flops | bytes accessed | tf_op | source)
XLA Modules:
  0.0 315.1 jit_solution(10662462286563790245)
XLA Ops:
  8.0 1.4 gather_fusion
  10.1 1.5 gather_fusion.2
  11.7 9.2 %all_to_all.40 = bf16[8,8,2048]{2,1,0:T(8,128)(2,1)} all-to-all(bf16[8,8,2048]{2,1,0:T(8,128)(2,1)S(1)} %broadcast_select_fusion.1), channel_id=1, replica_groups=mesh['req'=4,'head'=8] {'req'}, dimensions={0} | all-to-all | bytes 524288 | tf_op jit(solution)/shard_map/all_to_all | solution.py:135
  20.9 5.2 %fusion.126 = (bf16[1,8,32,32,128]{4,3,2,1,0:T(8,128)(2,1)}, bf16[8,32,32,128]{3,2,1,0:T(8,128)(2,1)}) fusion(bf16[2,8,32,32,128]{4,3,2,1,0:T(8,128)(2,1)} %param.19), kind=kLoop, calls=%fused_computation.214 | loop fusion | bytes 8388608 | tf_op jit(solution)/shard_map/slice | solution.py:114
  26.1 3.7 %gather_fusion.3 = bf16[8,32,32,128]{3,2,1,0:T(8,128)(2,1)} fusion(bf16[8,32,32,128]{3,2,1,0:T(8,128)(2,1)} %get-tuple-element.28, s32[1024]{0:T(1024)S(1)} %pad_clamp_fusion.1), kind=kCustom, calls=%fused_computation.2.clone | custom fusion | bytes 4194336 | tf_op jit(solution)/shard_map/jit(_take)/gather | solution.py:119
  29.9 1.8 select_select_fusion.1
  32.5 1.8 copy.58
  34.3 6.1 %all-to-all-start.1 = ((bf16[32,2,32,4,128]{4,2,3,1,0:T(8,128)(2,1)}), bf16[32,2,32,4,128]{4,2,3,1,0:T(8,128)(2,1)}, u32[]{:S(2)}, u32[]{:S(2)}) async-start(bf16[32,2,32,4,128]{4,2,3,1,0:T(8,128)(2,1)} %bitcast.138), calls=%async_computation.1 | async-start | bytes 4194304 | tf_op jit(solution)/shard_map/all_to_all | solution.py:128
  43.5 1.3 iota_compare_fusion.1
  47.8 0.9 subtract_convert_fusion
  48.7 50.3 %all-gather.3.cloned.1.call-done = bf16[2,4,64,2048]{3,2,0,1:T(8,128)(2,1)} async-done(((bf16[2,4,8,2048]{3,2,0,1:T(8,128)(2,1)}), bf16[2,4,64,2048]{3,2,0,1:T(8,128)(2,1)}) %all-gather.3.cloned.1.call-update) | async-done | bytes 2097168 | tf_op jit(solution)/shard_map/all_gather | solution.py:138
  99.0 2.1 convert_reduce_fusion
  102.8 1.8 fusion.19
  105.6 1.4 all-to-all-done.1
  107.0 1.1 fusion.127
  108.3 2.0 fusion.130
  110.3 2.2 convolution_convert_fusion.3
  112.7 2.0 fusion.129
  114.6 2.2 convolution_convert_fusion.2
  117.8 1.0 constant_dynamic-slice_fusion.7
  118.9 1.2 collective-permute-start
  120.2 1.5 collective-permute-start.2
  121.7 10.8 %collective-permute-done = bf16[2,4,2,8,2048]{4,3,1,0,2:T(8,128)(2,1)} collective-permute-done((bf16[2,4,2,8,2048]{4,3,1,0,2:T(8,128)(2,1)S(1)}, bf16[2,4,2,8,2048]{4,3,1,0,2:T(8,128)(2,1)}, u32[]{:S(2)}, u32[]{:S(2)}) %collective-permute-start) | collective-permute-done | bytes 524320 | tf_op jit(solution)/shard_map/ppermute | solution.py:58
  132.6 0.9 collective-permute-done.1
  133.5 11.4 %collective-permute-done.2 = bf16[2,4,2,8,2048]{4,3,1,0,2:T(8,128)(2,1)S(1)} collective-permute-done((bf16[2,4,2,8,2048]{4,3,1,0,2:T(8,128)(2,1)S(1)}, bf16[2,4,2,8,2048]{4,3,1,0,2:T(8,128)(2,1)S(1)}, u32[]{:S(2)}, u32[]{:S(2)}) %collective-permute-start.2) | collective-permute-done | bytes 524320 | tf_op jit(solution)/shard_map/ppermute | solution.py:58
  144.9 1.4 fusion.26
  146.5 14.4 %collective-permute-done.3 = bf16[2,4,8,2048]{3,2,0,1:T(8,128)(2,1)S(1)} collective-permute-done((bf16[2,4,8,2048]{3,2,0,1:T(8,128)(2,1)S(1)}, bf16[2,4,8,2048]{3,2,0,1:T(8,128)(2,1)S(1)}, u32[]{:S(2)}, u32[]{:S(2)}) %collective-permute-start.3) | collective-permute-done | bytes 262176 | tf_op jit(solution)/shard_map/ppermute | solution.py:64
  162.2 0.9 sort.17
  163.2 2.5 gather_fusion.5
  167.0 2.0 copy.73
  169.0 39.5 %all-gather.5.cloned.1.call-done = bf16[2,4,64,2048]{3,2,0,1:T(8,128)(2,1)} async-done(((bf16[2,4,8,2048]{3,2,0,1:T(8,128)(2,1)}), bf16[2,4,64,2048]{3,2,0,1:T(8,128)(2,1)}) %all-gather.5.cloned.1.call-update) | async-done | bytes 2097168 | tf_op jit(solution)/shard_map/all_gather | solution.py:166
  208.5 3.2 %copy.76 = bf16[2,4,64,2048]{3,2,1,0:T(8,128)(2,1)} copy(bf16[2,4,64,2048]{3,2,0,1:T(8,128)(2,1)} %all-gather.5.cloned.1.call-done) | data formatting | bytes 4194304 | tf_op jit(solution)/shard_map/optimization_barrier | solution.py:167
  211.7 4.6 %all-to-all-start.2 = ((bf16[32,2,32,4,128]{4,2,3,1,0:T(8,128)(2,1)}), bf16[32,2,32,4,128]{4,2,3,1,0:T(8,128)(2,1)S(1)}, u32[]{:S(2)}, u32[]{:S(2)}) async-start(bf16[32,2,32,4,128]{4,2,3,1,0:T(8,128)(2,1)} %bitcast.44), calls=%async_computation.2 | async-start | bytes 4194304 | tf_op jit(solution)/shard_map/all_to_all | solution.py:169
  216.3 14.3 %convolution_convert_fusion = bf16[512,2048]{1,0:T(8,128)(2,1)} fusion(bf16[1024,2048]{1,0:T(8,128)(2,1)} %param.29, bf16[512,2048]{1,0:T(8,128)(2,1)} %bitcast.148, bf16[2048,1024]{1,0:T(8,128)(2,1)} %param.28), kind=kOutput, calls=%fused_computation.20 | convolution fusion | flops 4330094592 | bytes 12582912 | tf_op jit(solution)/shard_map/dot_general | solution.py:179
  230.6 1.7 constant_dynamic-slice_fusion.3
  232.3 1.4 collective-permute-start.4
  233.8 1.3 collective-permute-start.5
  235.1 1.5 collective-permute-start.6
  236.7 27.2 %collective-permute-done.4 = bf16[2,4,2,8,2048]{4,3,1,0,2:T(8,128)(2,1)S(1)} collective-permute-done((bf16[2,4,2,8,2048]{4,3,1,0,2:T(8,128)(2,1)S(1)}, bf16[2,4,2,8,2048]{4,3,1,0,2:T(8,128)(2,1)S(1)}, u32[]{:S(2)}, u32[]{:S(2)}) %collective-permute-start.4) | collective-permute-done | bytes 524320 | tf_op jit(solution)/shard_map/ppermute | solution.py:58
  263.8 9.4 %collective-permute-done.6 = bf16[2,4,2,8,2048]{4,3,1,0,2:T(8,128)(2,1)S(1)} collective-permute-done((bf16[2,4,2,8,2048]{4,3,1,0,2:T(8,128)(2,1)S(1)}, bf16[2,4,2,8,2048]{4,3,1,0,2:T(8,128)(2,1)S(1)}, u32[]{:S(2)}, u32[]{:S(2)}) %collective-permute-start.6) | collective-permute-done | bytes 524320 | tf_op jit(solution)/shard_map/ppermute | solution.py:58
  273.6 1.8 collective-permute-start.7
  275.5 3.5 %copy.71 = bf16[4,2,8,32,4,128]{5,3,2,4,1,0:T(8,128)(2,1)} copy(bf16[4,2,8,32,4,128]{5,3,4,1,2,0:T(8,128)(2,1)} %bitcast.7) | data formatting | bytes 4194304 | tf_op jit(solution)/shard_map/transpose | solution.py:70
  279.0 8.4 %collective-permute-done.7 = bf16[2,4,8,2048]{3,2,0,1:T(8,128)(2,1)S(1)} collective-permute-done((bf16[2,4,8,2048]{3,2,0,1:T(8,128)(2,1)S(1)}, bf16[2,4,8,2048]{3,2,0,1:T(8,128)(2,1)S(1)}, u32[]{:S(2)}, u32[]{:S(2)}) %collective-permute-start.7) | collective-permute-done | bytes 262176 | tf_op jit(solution)/shard_map/ppermute | solution.py:64
  288.0 1.0 copy-done.5
  289.4 2.2 copy.75
  292.4 4.9 %all-to-all-start.3 = ((bf16[2,4,8,2048]{3,2,0,1:T(8,128)(2,1)}), bf16[2,4,8,2048]{3,2,0,1:T(8,128)(2,1)S(1)}, u32[]{:S(2)}, u32[]{:S(2)}) async-start(bf16[2,4,8,2048]{3,2,0,1:T(8,128)(2,1)} %select_convert_fusion), calls=%async_computation.3 | async-start | bytes 524288 | tf_op jit(solution)/shard_map/all_to_all | solution.py:191
  297.4 7.9 %copy.83 = bf16[8,2,256,4,128]{4,3,2,1,0:T(4,128)(2,1)} copy(bf16[8,2,256,4,128]{4,2,3,1,0:T(8,128)(2,1)} %bitcast.137) | data formatting | bytes 8388608
  306.0 1.5 gather_fusion.6
  (112 shorter events, 19.2 us)
Async XLA Ops:
  7.2 95.6 %copy-start = (bf16[2048,4,192]{0,2,1:T(8,128)(2,1)S(1)}, bf16[2048,4,192]{0,2,1:T(8,128)(2,1)}, u32[]{:S(2)}) copy-start(bf16[2048,4,192]{0,2,1:T(8,128)(2,1)} %param.24) | copy-start | bytes 9437188
  7.2 91.8 %all-gather.3.cloned.1.call-start = ((), (), s32[]{:S(2)}) async-start(), calls=%async_computation.4 | async-start | bytes 2359296 | tf_op jit(solution)/shard_map/all_gather | solution.py:138
  34.3 6.4 %copy-start.15 = (s32[8]{0:T(128)S(1)}, s32[8]{0:T(128)}, u32[]{:S(2)}) copy-start(s32[8]{0:T(128)} %param.22) | copy-start | bytes 100
  34.3 6.5 %copy-start.2 = (s32[8]{0:T(128)S(1)}, s32[8]{0:T(128)}, u32[]{:S(2)}) copy-start(s32[8]{0:T(128)} %param.21) | copy-start | bytes 100
  34.3 7.2 %copy-start.3 = (s32[8]{0:T(128)S(1)}, s32[8]{0:T(128)}, u32[]{:S(2)}) copy-start(s32[8]{0:T(128)} %param.20) | copy-start | bytes 100
  34.3 7.8 %copy-start.13 = (bf16[2048]{0:T(1024)(128)(2,1)S(1)}, bf16[2048]{0:T(1024)(128)(2,1)}, u32[]{:S(2)}) copy-start(bf16[2048]{0:T(1024)(128)(2,1)} %param.23) | copy-start | bytes 12292
  34.3 72.7 %all-to-all-start.1 = ((bf16[32,2,32,4,128]{4,2,3,1,0:T(8,128)(2,1)}), bf16[32,2,32,4,128]{4,2,3,1,0:T(8,128)(2,1)}, u32[]{:S(2)}, u32[]{:S(2)}) async-start(bf16[32,2,32,4,128]{4,2,3,1,0:T(8,128)(2,1)} %bitcast.138), calls=%async_computation.1 | async-start | bytes 4194304 | tf_op jit(solution)/shard_map/all_to_all | solution.py:128
  40.4 168.1 %all-gather.5.cloned.1.call-start = ((), (), s32[]{:S(2)}) async-start(), calls=%async_computation.5 | async-start | bytes 2359296 | tf_op jit(solution)/shard_map/all_gather | solution.py:166
  99.0 2.2 copy-start.4
  104.6 0.9 copy-start.12
  105.5 2.7 copy-start.11
  105.5 2.7 copy-start.17
  110.2 2.4 copy-start.10
  112.6 2.0 copy-start.18
  114.6 2.4 copy-start.9
  118.8 26.1 %copy-start.7 = (bf16[2,4,2,1,8,2048]{5,4,3,2,1,0:T(8,128)(2,1)S(1)}, bf16[2,4,2,1,8,2048]{5,4,3,2,1,0:T(8,128)(2,1)}, u32[]{:S(2)}) copy-start(bf16[2,4,2,1,8,2048]{5,4,3,2,1,0:T(8,128)(2,1)} %get-tuple-element.33) | copy-start | bytes 1572868
  118.9 13.7 %collective-permute-start = (bf16[2,4,2,8,2048]{4,3,1,0,2:T(8,128)(2,1)S(1)}, bf16[2,4,2,8,2048]{4,3,1,0,2:T(8,128)(2,1)}, u32[]{:S(2)}, u32[]{:S(2)}) collective-permute-start(bf16[2,4,2,8,2048]{4,3,1,0,2:T(8,128)(2,1)S(1)} %bitcast.156), channel_id=1, source_target_pairs={{0,1},{1,2},{2,3},{3,0},{4,5},{5,6},{6,7},{7,4},{8,9},{9,10},{10,1... | collective-permute-start | bytes 1572872 | tf_op jit(solution)/shard_map/ppermute | solution.py:58
  120.1 13.4 %collective-permute-start.1 = (bf16[2,4,2,8,2048]{4,3,1,0,2:T(8,128)(2,1)S(1)}, bf16[2,4,2,8,2048]{4,3,1,0,2:T(8,128)(2,1)S(1)}, u32[]{:S(2)}, u32[]{:S(2)}) collective-permute-start(bf16[2,4,2,8,2048]{4,3,1,0,2:T(8,128)(2,1)S(1)} %bitcast.157), channel_id=1, source_target_pairs={{0,2},{1,3},{2,0},{3,1},{4,6},{5,7},{6,4},{7,5},{8,10},{9,11},{10,... | collective-permute-start | bytes 1572872 | tf_op jit(solution)/shard_map/ppermute | solution.py:58
  120.2 24.7 %collective-permute-start.2 = (bf16[2,4,2,8,2048]{4,3,1,0,2:T(8,128)(2,1)S(1)}, bf16[2,4,2,8,2048]{4,3,1,0,2:T(8,128)(2,1)S(1)}, u32[]{:S(2)}, u32[]{:S(2)}) collective-permute-start(bf16[2,4,2,8,2048]{4,3,1,0,2:T(8,128)(2,1)S(1)} %bitcast.158), channel_id=1, source_target_pairs={{0,3},{1,0},{2,1},{3,2},{4,7},{5,4},{6,5},{7,6},{8,11},{9,8},{10,9... | collective-permute-start | bytes 1572872 | tf_op jit(solution)/shard_map/ppermute | solution.py:58
  144.9 1.6 copy-start.14
  144.9 16.0 %copy-start.6 = (bf16[8,8,2048]{2,1,0:T(8,128)(2,1)S(1)}, bf16[8,8,2048]{2,1,0:T(8,128)(2,1)}, u32[]{:S(2)}) copy-start(bf16[8,8,2048]{2,1,0:T(8,128)(2,1)} %all_to_all.40) | copy-start | bytes 786436
  146.3 15.9 %copy-start.16 = (s32[8]{0:T(128)S(1)}, s32[8]{0:T(128)}, u32[]{:S(2)}) copy-start(s32[8]{0:T(128)} %param.22) | copy-start | bytes 100
  146.4 14.5 %collective-permute-start.3 = (bf16[2,4,8,2048]{3,2,0,1:T(8,128)(2,1)S(1)}, bf16[2,4,8,2048]{3,2,0,1:T(8,128)(2,1)S(1)}, u32[]{:S(2)}, u32[]{:S(2)}) collective-permute-start(bf16[2,4,8,2048]{3,2,0,1:T(8,128)(2,1)S(1)} %copy.69), channel_id=1, source_target_pairs={{0,4},{1,5},{2,6},{3,7},{4,0},{5,1},{6,2},{7,3},{8,12},{9,13},{10,... | collective-permute-start | bytes 786440 | tf_op jit(solution)/shard_map/ppermute | solution.py:64
  211.7 75.7 %all-to-all-start.2 = ((bf16[32,2,32,4,128]{4,2,3,1,0:T(8,128)(2,1)}), bf16[32,2,32,4,128]{4,2,3,1,0:T(8,128)(2,1)S(1)}, u32[]{:S(2)}, u32[]{:S(2)}) async-start(bf16[32,2,32,4,128]{4,2,3,1,0:T(8,128)(2,1)} %bitcast.44), calls=%async_computation.2 | async-start | bytes 4194304 | tf_op jit(solution)/shard_map/all_to_all | solution.py:169
  232.3 31.5 %collective-permute-start.4 = (bf16[2,4,2,8,2048]{4,3,1,0,2:T(8,128)(2,1)S(1)}, bf16[2,4,2,8,2048]{4,3,1,0,2:T(8,128)(2,1)S(1)}, u32[]{:S(2)}, u32[]{:S(2)}) collective-permute-start(bf16[2,4,2,8,2048]{4,3,1,0,2:T(8,128)(2,1)S(1)} %bitcast.159), channel_id=1, source_target_pairs={{0,1},{1,2},{2,3},{3,0},{4,5},{5,6},{6,7},{7,4},{8,9},{9,10},{10,1... | collective-permute-start | bytes 1572872 | tf_op jit(solution)/shard_map/ppermute | solution.py:58
  233.8 30.0 %collective-permute-start.5 = (bf16[2,4,2,8,2048]{4,3,1,0,2:T(8,128)(2,1)S(1)}, bf16[2,4,2,8,2048]{4,3,1,0,2:T(8,128)(2,1)S(1)}, u32[]{:S(2)}, u32[]{:S(2)}) collective-permute-start(bf16[2,4,2,8,2048]{4,3,1,0,2:T(8,128)(2,1)S(1)} %bitcast.160), channel_id=1, source_target_pairs={{0,2},{1,3},{2,0},{3,1},{4,6},{5,7},{6,4},{7,5},{8,10},{9,11},{10,... | collective-permute-start | bytes 1572872 | tf_op jit(solution)/shard_map/ppermute | solution.py:58
  235.1 38.1 %collective-permute-start.6 = (bf16[2,4,2,8,2048]{4,3,1,0,2:T(8,128)(2,1)S(1)}, bf16[2,4,2,8,2048]{4,3,1,0,2:T(8,128)(2,1)S(1)}, u32[]{:S(2)}, u32[]{:S(2)}) collective-permute-start(bf16[2,4,2,8,2048]{4,3,1,0,2:T(8,128)(2,1)S(1)} %bitcast.161), channel_id=1, source_target_pairs={{0,3},{1,0},{2,1},{3,2},{4,7},{5,4},{6,5},{7,6},{8,11},{9,8},{10,9... | collective-permute-start | bytes 1572872 | tf_op jit(solution)/shard_map/ppermute | solution.py:58
  273.6 13.7 %collective-permute-start.7 = (bf16[2,4,8,2048]{3,2,0,1:T(8,128)(2,1)S(1)}, bf16[2,4,8,2048]{3,2,0,1:T(8,128)(2,1)S(1)}, u32[]{:S(2)}, u32[]{:S(2)}) collective-permute-start(bf16[2,4,8,2048]{3,2,0,1:T(8,128)(2,1)S(1)} %copy.81), channel_id=1, source_target_pairs={{0,4},{1,5},{2,6},{3,7},{4,0},{5,1},{6,2},{7,3},{8,12},{9,13},{10,... | collective-permute-start | bytes 786440 | tf_op jit(solution)/shard_map/ppermute | solution.py:64
  287.4 1.6 copy-start.5
  292.4 12.9 %all-to-all-start.3 = ((bf16[2,4,8,2048]{3,2,0,1:T(8,128)(2,1)}), bf16[2,4,8,2048]{3,2,0,1:T(8,128)(2,1)S(1)}, u32[]{:S(2)}, u32[]{:S(2)}) async-start(bf16[2,4,8,2048]{3,2,0,1:T(8,128)(2,1)} %select_convert_fusion), calls=%async_computation.3 | async-start | bytes 524288 | tf_op jit(solution)/shard_map/all_to_all | solution.py:191
  297.4 10.9 %copy-start.1 = (bf16[2048,4,192]{0,2,1:T(8,128)(2,1)S(1)}, bf16[2048,4,192]{0,2,1:T(8,128)(2,1)}, u32[]{:S(2)}) copy-start(bf16[2048,4,192]{0,2,1:T(8,128)(2,1)} %param.24) | copy-start | bytes 9437188
  305.3 0.7 copy-start.8
Sparse Core Ops, SparseCore 0:
  21.0 77.9 all-gather.2
  162.3 46.1 all-gather.4

commit v12 on v11

--- a/solution.py
+++ b/solution.py
@@ -131,6 +131,8 @@
         else:
             deferred.append(outgoing)
     current = chunks[0][0]
+    for outgoing in deferred:
+        chunks.append(land(lax.all_to_all(outgoing, ("req", "head"), 0, 0, tiled=True), req_count, head_count))
     dealt_acts = jnp.take(stretch_acts, req_order, axis=0)
     dealt_rows = lax.all_to_all(dealt_acts, "req", split_axis=0, concat_axis=1, tiled=True).reshape(
         group_size, req_count, stretch_rows, features
@@ -161,13 +163,11 @@
     )
     partial_attn = partial_attn.reshape(group_size, req_count, span_rows, features)
     attn_rows = head_sum(partial_attn, head_count, stretch_rows)
+    attn_rows, later_chunks = lax.optimization_barrier((attn_rows, chunks[1:]))
+    relaid = jnp.stack(chunks[:1] + later_chunks, axis=1).reshape((req_count * local_layers,) + chunks[0].shape[1:])
     residual_rows = dealt_rows.astype(jnp.float32) + attn_rows
     normed_rows = layer_norm(residual_rows, mlp_gain).astype(jnp.bfloat16)
     normed_all = lax.all_gather(normed_rows, "head", axis=2, tiled=True)
-    deferred, normed_all = lax.optimization_barrier((deferred, normed_all))
-    for outgoing in deferred:
-        chunks.append(land(lax.all_to_all(outgoing, ("req", "head"), 0, 0, tiled=True), req_count, head_count))
-    relaid = jnp.stack(chunks, axis=1).reshape((req_count * local_layers,) + chunks[0].shape[1:])
     inner = jax.nn.gelu(
         jnp.dot(
             normed_all.reshape(group_size * stretch_max, features),

time: 321 us -> 327 us (1.019); the launches traced: 315 us -> 325 us
  waiting for transfers between devices: 174 us -> 180 us
    all_gather x1, waiting for transfers between devices: 39.5 us -> 45.6 us  [local(): normed_all = lax.all_gather(normed_rows, 'head', axis=2, tiled=True)]
    unnamed x39 -> x35, local copies, waits for them, and re-layouts: 10.7 us -> 9.75 us
  transfers between devices with their start and end apart: 13 -> 13, of which waited for: 10 -> 10; matrix products, arithmetic and copies ran while one was open for 20% -> 19% of each run, Pallas kernels for 0% -> 0%
where the time goes in v12:
time: 327 us; the launch traced here: 325 us
  waiting for transfers between devices  180 us (55%)
  local copies, waits for them, and re-layouts  49.1 us (15%)
  matrix products  27.9 us (9%)
  starting transfers between devices  23.4 us (7%)
  other arithmetic  21.6 us (7%)
  between operations  14.6 us (4%)
  blocking collectives  9.17 us (3%)
    ppermute x6, waiting for transfers between devices, head_sum(): lax.ppermute(sent, 'head', pairs).astype(jnp.float32)  62.6 us
    all_gather x1, waiting for transfers between devices, local(): gathered = lax.all_gather(dealt_rows, 'head', axis=2, tiled=True)  49.8 us
    all_gather x1, waiting for transfers between devices, local(): normed_all = lax.all_gather(normed_rows, 'head', axis=2, tiled=True)  45.6 us
    ppermute x2, waiting for transfers between devices, head_sum(): total = total + lax.ppermute(sent, 'head', pairs).astype(jnp.float32)  19.9 us
    dot_general x1, matrix products, local(): jnp.dot(inner, down_weight, preferred_element_type=jnp.float32)  13.7 us
    unnamed x35, local copies, waits for them, and re-layouts  9.75 us
    all_to_all x1, blocking collectives, local(): lax.all_to_all(dealt_acts, 'req', split_axis=0, concat_axis=1, tiled=True)  9.17 us
  transfers between devices with their start and end apart: 13, of which 10 were waited for; matrix products, arithmetic and copies ran while one was open for 19% of the time, Pallas kernels for 0%

profile of v12, /device:TPU:1, one launch (start us, length us, event | category | flops | bytes accessed | tf_op | source)
XLA Modules:
  0.0 325.4 jit_solution(3831834161780009817)
XLA Ops:
  8.0 1.6 gather_fusion.2
  9.7 1.3 gather_fusion
  11.7 9.2 %all_to_all.40 = bf16[8,8,2048]{2,1,0:T(8,128)(2,1)} all-to-all(bf16[8,8,2048]{2,1,0:T(8,128)(2,1)S(1)} %broadcast_select_fusion.1), channel_id=1, replica_groups=mesh['req'=4,'head'=8] {'req'}, dimensions={0} | all-to-all | bytes 524288 | tf_op jit(solution)/shard_map/all_to_all | solution.py:137
  20.9 5.2 %fusion.124 = (bf16[1,8,32,32,128]{4,3,2,1,0:T(8,128)(2,1)}, bf16[8,32,32,128]{3,2,1,0:T(8,128)(2,1)}) fusion(bf16[2,8,32,32,128]{4,3,2,1,0:T(8,128)(2,1)} %param.19), kind=kLoop, calls=%fused_computation.214 | loop fusion | bytes 8388608 | tf_op jit(solution)/shard_map/slice | solution.py:114
  26.1 3.7 %gather_fusion.3 = bf16[8,32,32,128]{3,2,1,0:T(8,128)(2,1)} fusion(bf16[8,32,32,128]{3,2,1,0:T(8,128)(2,1)} %get-tuple-element.26, s32[1024]{0:T(1024)S(1)} %pad_clamp_fusion.1), kind=kCustom, calls=%fused_computation.2.clone | custom fusion | bytes 4194336 | tf_op jit(solution)/shard_map/jit(_take)/gather | solution.py:119
  29.9 1.8 select_select_fusion.1
  32.6 1.8 copy.57
  34.3 6.1 %all-to-all-start.1 = ((bf16[32,2,32,4,128]{4,2,3,1,0:T(8,128)(2,1)}), bf16[32,2,32,4,128]{4,2,3,1,0:T(8,128)(2,1)}, u32[]{:S(2)}, u32[]{:S(2)}) async-start(bf16[32,2,32,4,128]{4,2,3,1,0:T(8,128)(2,1)} %bitcast.144), calls=%async_computation.1 | async-start | bytes 4194304 | tf_op jit(solution)/shard_map/all_to_all | solution.py:128
  43.3 1.3 iota_compare_fusion.1
  49.2 49.8 %all-gather.3.cloned.1.call-done = bf16[2,4,64,2048]{3,2,0,1:T(8,128)(2,1)} async-done(((bf16[2,4,8,2048]{3,2,0,1:T(8,128)(2,1)}), bf16[2,4,64,2048]{3,2,0,1:T(8,128)(2,1)}) %all-gather.3.cloned.1.call-update) | async-done | bytes 2097168 | tf_op jit(solution)/shard_map/all_gather | solution.py:140
  99.0 2.1 convert_reduce_fusion
  102.7 2.7 fusion.19
  105.5 1.6 all-to-all-done.1
  107.0 2.5 gather_fusion.5
  110.9 2.0 copy.71
  112.9 3.3 %all-to-all-start.2 = ((bf16[32,2,32,4,128]{4,2,3,1,0:T(8,128)(2,1)}), bf16[32,2,32,4,128]{4,2,3,1,0:T(8,128)(2,1)S(1)}, u32[]{:S(2)}, u32[]{:S(2)}) async-start(bf16[32,2,32,4,128]{4,2,3,1,0:T(8,128)(2,1)} %bitcast.146), calls=%async_computation.2 | async-start | bytes 4194304 | tf_op jit(solution)/shard_map/all_to_all | solution.py:135
  117.3 1.1 fusion.125
  118.7 2.3 fusion.127
  121.0 3.2 convolution_convert_fusion.2
  124.2 2.0 fusion.128
  126.2 2.2 convolution_convert_fusion.3
  128.6 1.9 convolution_convert_fusion.1
  130.5 1.0 constant_dynamic-slice_fusion.7
  132.3 2.4 collective-permute-start.2
  136.9 30.6 %collective-permute-done.2 = bf16[2,4,2,8,2048]{4,3,1,0,2:T(8,128)(2,1)} collective-permute-done((bf16[2,4,2,8,2048]{4,3,1,0,2:T(8,128)(2,1)}, bf16[2,4,2,8,2048]{4,3,1,0,2:T(8,128)(2,1)}, u32[]{:S(2)}, u32[]{:S(2)}) %collective-permute-start.2) | collective-permute-done | bytes 524320 | tf_op jit(solution)/shard_map/ppermute | solution.py:58
  167.6 11.2 %collective-permute-done.1 = bf16[2,4,2,8,2048]{4,3,1,0,2:T(8,128)(2,1)} collective-permute-done((bf16[2,4,2,8,2048]{4,3,1,0,2:T(8,128)(2,1)}, bf16[2,4,2,8,2048]{4,3,1,0,2:T(8,128)(2,1)}, u32[]{:S(2)}, u32[]{:S(2)}) %collective-permute-start.1) | collective-permute-done | bytes 524320 | tf_op jit(solution)/shard_map/ppermute | solution.py:58
  178.8 1.7 fusion.26
  180.5 1.0 copy-done.7
  181.7 13.5 %collective-permute-done.3 = bf16[2,4,8,2048]{3,2,0,1:T(8,128)(2,1)S(1)} collective-permute-done((bf16[2,4,8,2048]{3,2,0,1:T(8,128)(2,1)S(1)}, bf16[2,4,8,2048]{3,2,0,1:T(8,128)(2,1)S(1)}, u32[]{:S(2)}, u32[]{:S(2)}) %collective-permute-start.3) | collective-permute-done | bytes 262176 | tf_op jit(solution)/shard_map/ppermute | solution.py:64
  195.2 1.1 copy_add_fusion.1
  196.3 1.9 copy.72
  199.5 1.0 sort.17
  200.4 45.6 %all-gather.5.cloned.1.call-done = bf16[2,4,64,2048]{3,2,0,1:T(8,128)(2,1)} async-done(((bf16[2,4,8,2048]{3,2,0,1:T(8,128)(2,1)}), bf16[2,4,64,2048]{3,2,0,1:T(8,128)(2,1)}) %all-gather.5.cloned.1.call-update) | async-done | bytes 2097168 | tf_op jit(solution)/shard_map/all_gather | solution.py:170
  246.1 1.8 copy.75
  247.9 13.7 %convolution_convert_fusion = bf16[512,2048]{1,0:T(8,128)(2,1)} fusion(bf16[1024,2048]{1,0:T(8,128)(2,1)} %param.29, bf16[512,2048]{1,0:T(8,128)(2,1)S(1)} %bitcast.154, bf16[2048,1024]{1,0:T(8,128)(2,1)} %param.28), kind=kOutput, calls=%fused_computation.20 | convolution fusion | flops 4330094592 | bytes 12582912 | tf_op jit(solution)/shard_map/dot_general | solution.py:179
  261.6 1.8 constant_dynamic-slice_fusion.3
  263.4 1.5 collective-permute-start.6
  265.1 1.5 collective-permute-start.4
  266.8 8.3 %collective-permute-done.6 = bf16[2,4,2,8,2048]{4,3,1,0,2:T(8,128)(2,1)S(1)} collective-permute-done((bf16[2,4,2,8,2048]{4,3,1,0,2:T(8,128)(2,1)S(1)}, bf16[2,4,2,8,2048]{4,3,1,0,2:T(8,128)(2,1)S(1)}, u32[]{:S(2)}, u32[]{:S(2)}) %collective-permute-start.6) | collective-permute-done | bytes 524320 | tf_op jit(solution)/shard_map/ppermute | solution.py:58
  275.1 11.3 %collective-permute-done.5 = bf16[2,4,2,8,2048]{4,3,1,0,2:T(8,128)(2,1)S(1)} collective-permute-done((bf16[2,4,2,8,2048]{4,3,1,0,2:T(8,128)(2,1)S(1)}, bf16[2,4,2,8,2048]{4,3,1,0,2:T(8,128)(2,1)S(1)}, u32[]{:S(2)}, u32[]{:S(2)}) %collective-permute-start.5) | collective-permute-done | bytes 524320 | tf_op jit(solution)/shard_map/ppermute | solution.py:58
  286.4 1.1 collective-permute-done.4
  287.9 2.6 collective-permute-start.7
  290.6 2.3 copy.73
  293.3 2.2 copy.74
  295.5 6.3 %collective-permute-done.7 = bf16[2,4,8,2048]{3,2,0,1:T(8,128)(2,1)S(1)} collective-permute-done((bf16[2,4,8,2048]{3,2,0,1:T(8,128)(2,1)S(1)}, bf16[2,4,8,2048]{3,2,0,1:T(8,128)(2,1)S(1)}, u32[]{:S(2)}, u32[]{:S(2)}) %collective-permute-start.7) | collective-permute-done | bytes 262176 | tf_op jit(solution)/shard_map/ppermute | solution.py:64
  302.7 5.0 %all-to-all-start.3 = ((bf16[2,4,8,2048]{3,2,0,1:T(8,128)(2,1)}), bf16[2,4,8,2048]{3,2,0,1:T(8,128)(2,1)S(1)}, u32[]{:S(2)}, u32[]{:S(2)}) async-start(bf16[2,4,8,2048]{3,2,0,1:T(8,128)(2,1)} %select_convert_fusion), calls=%async_computation.3 | async-start | bytes 524288 | tf_op jit(solution)/shard_map/all_to_all | solution.py:191
  307.7 7.9 %copy.82 = bf16[8,2,256,4,128]{4,3,2,1,0:T(4,128)(2,1)} copy(bf16[8,2,256,4,128]{4,2,3,1,0:T(8,128)(2,1)} %bitcast.140) | data formatting | bytes 8388608
  316.3 1.5 gather_fusion.6
  (109 shorter events, 22.3 us)
Async XLA Ops:
  7.2 95.6 %copy-start = (bf16[2048,4,192]{0,2,1:T(8,128)(2,1)S(1)}, bf16[2048,4,192]{0,2,1:T(8,128)(2,1)}, u32[]{:S(2)}) copy-start(bf16[2048,4,192]{0,2,1:T(8,128)(2,1)} %param.24) | copy-start | bytes 9437188
  7.2 91.8 %all-gather.3.cloned.1.call-start = ((), (), s32[]{:S(2)}) async-start(), calls=%async_computation.4 | async-start | bytes 2359296 | tf_op jit(solution)/shard_map/all_gather | solution.py:140
  34.3 6.2 %copy-start.15 = (s32[8]{0:T(128)S(1)}, s32[8]{0:T(128)}, u32[]{:S(2)}) copy-start(s32[8]{0:T(128)} %param.22) | copy-start | bytes 100
  34.3 6.3 %copy-start.2 = (s32[8]{0:T(128)S(1)}, s32[8]{0:T(128)}, u32[]{:S(2)}) copy-start(s32[8]{0:T(128)} %param.21) | copy-start | bytes 100
  34.3 6.9 %copy-start.3 = (s32[8]{0:T(128)S(1)}, s32[8]{0:T(128)}, u32[]{:S(2)}) copy-start(s32[8]{0:T(128)} %param.20) | copy-start | bytes 100
  34.3 7.6 %copy-start.13 = (bf16[2048]{0:T(1024)(128)(2,1)S(1)}, bf16[2048]{0:T(1024)(128)(2,1)}, u32[]{:S(2)}) copy-start(bf16[2048]{0:T(1024)(128)(2,1)} %param.23) | copy-start | bytes 12292
  34.3 72.7 %all-to-all-start.1 = ((bf16[32,2,32,4,128]{4,2,3,1,0:T(8,128)(2,1)}), bf16[32,2,32,4,128]{4,2,3,1,0:T(8,128)(2,1)}, u32[]{:S(2)}, u32[]{:S(2)}) async-start(bf16[32,2,32,4,128]{4,2,3,1,0:T(8,128)(2,1)} %bitcast.144), calls=%async_computation.1 | async-start | bytes 4194304 | tf_op jit(solution)/shard_map/all_to_all | solution.py:128
  99.0 2.2 copy-start.4
  112.9 3.6 %copy-start.10 = (bf16[2,256,4,192]{1,3,2,0:T(8,128)(2,1)S(1)}, bf16[2,256,4,192]{1,3,2,0:T(8,128)(2,1)}, u32[]{:S(2)}) copy-start(bf16[2,256,4,192]{1,3,2,0:T(8,128)(2,1)} %fusion.19) | copy-start | bytes 2359300
  112.9 83.5 %all-to-all-start.2 = ((bf16[32,2,32,4,128]{4,2,3,1,0:T(8,128)(2,1)}), bf16[32,2,32,4,128]{4,2,3,1,0:T(8,128)(2,1)S(1)}, u32[]{:S(2)}, u32[]{:S(2)}) async-start(bf16[32,2,32,4,128]{4,2,3,1,0:T(8,128)(2,1)} %bitcast.146), calls=%async_computation.2 | async-start | bytes 4194304 | tf_op jit(solution)/shard_map/all_to_all | solution.py:135
  116.2 2.5 copy-start.16
  116.2 129.9 %all-gather.5.cloned.1.call-start = ((), (), s32[]{:S(2)}) async-start(), calls=%async_computation.5 | async-start | bytes 2359296 | tf_op jit(solution)/shard_map/all_gather | solution.py:170
  121.0 3.2 copy-start.9
  121.0 3.2 copy-start.11
  126.2 2.2 copy-start.12
  132.3 35.2 %collective-permute-start.2 = (bf16[2,4,2,8,2048]{4,3,1,0,2:T(8,128)(2,1)}, bf16[2,4,2,8,2048]{4,3,1,0,2:T(8,128)(2,1)}, u32[]{:S(2)}, u32[]{:S(2)}) collective-permute-start(bf16[2,4,2,8,2048]{4,3,1,0,2:T(8,128)(2,1)} %bitcast.137), channel_id=1, source_target_pairs={{0,3},{1,0},{2,1},{3,2},{4,7},{5,4},{6,5},{7,6},{8,11},{9,8},{10,9... | collective-permute-start | bytes 1572872 | tf_op jit(solution)/shard_map/ppermute | solution.py:58
  135.6 43.3 %collective-permute-start.1 = (bf16[2,4,2,8,2048]{4,3,1,0,2:T(8,128)(2,1)}, bf16[2,4,2,8,2048]{4,3,1,0,2:T(8,128)(2,1)}, u32[]{:S(2)}, u32[]{:S(2)}) collective-permute-start(bf16[2,4,2,8,2048]{4,3,1,0,2:T(8,128)(2,1)} %bitcast.138), channel_id=1, source_target_pairs={{0,2},{1,3},{2,0},{3,1},{4,6},{5,7},{6,4},{7,5},{8,10},{9,11},{10,... | collective-permute-start | bytes 1572872 | tf_op jit(solution)/shard_map/ppermute | solution.py:58
  136.6 42.2 %collective-permute-start = (bf16[2,4,2,8,2048]{4,3,1,0,2:T(8,128)(2,1)}, bf16[2,4,2,8,2048]{4,3,1,0,2:T(8,128)(2,1)S(1)}, u32[]{:S(2)}, u32[]{:S(2)}) collective-permute-start(bf16[2,4,2,8,2048]{4,3,1,0,2:T(8,128)(2,1)} %bitcast.139), channel_id=1, source_target_pairs={{0,1},{1,2},{2,3},{3,0},{4,5},{5,6},{6,7},{7,4},{8,9},{9,10},{10,1... | collective-permute-start | bytes 1572872 | tf_op jit(solution)/shard_map/ppermute | solution.py:58
  178.8 2.8 copy-start.14
  180.5 1.0 copy-start.7
  181.6 13.7 %collective-permute-start.3 = (bf16[2,4,8,2048]{3,2,0,1:T(8,128)(2,1)S(1)}, bf16[2,4,8,2048]{3,2,0,1:T(8,128)(2,1)S(1)}, u32[]{:S(2)}, u32[]{:S(2)}) collective-permute-start(bf16[2,4,8,2048]{3,2,0,1:T(8,128)(2,1)S(1)} %copy.68), channel_id=1, source_target_pairs={{0,4},{1,5},{2,6},{3,7},{4,0},{5,1},{6,2},{7,3},{8,12},{9,13},{10,... | collective-permute-start | bytes 786440 | tf_op jit(solution)/shard_map/ppermute | solution.py:64
  196.3 1.9 copy-start.5
  263.4 11.7 %collective-permute-start.6 = (bf16[2,4,2,8,2048]{4,3,1,0,2:T(8,128)(2,1)S(1)}, bf16[2,4,2,8,2048]{4,3,1,0,2:T(8,128)(2,1)S(1)}, u32[]{:S(2)}, u32[]{:S(2)}) collective-permute-start(bf16[2,4,2,8,2048]{4,3,1,0,2:T(8,128)(2,1)S(1)} %bitcast.161), channel_id=1, source_target_pairs={{0,3},{1,0},{2,1},{3,2},{4,7},{5,4},{6,5},{7,6},{8,11},{9,8},{10,9... | collective-permute-start | bytes 1572872 | tf_op jit(solution)/shard_map/ppermute | solution.py:58
  265.0 21.4 %collective-permute-start.5 = (bf16[2,4,2,8,2048]{4,3,1,0,2:T(8,128)(2,1)S(1)}, bf16[2,4,2,8,2048]{4,3,1,0,2:T(8,128)(2,1)S(1)}, u32[]{:S(2)}, u32[]{:S(2)}) collective-permute-start(bf16[2,4,2,8,2048]{4,3,1,0,2:T(8,128)(2,1)S(1)} %bitcast.162), channel_id=1, source_target_pairs={{0,2},{1,3},{2,0},{3,1},{4,6},{5,7},{6,4},{7,5},{8,10},{9,11},{10,... | collective-permute-start | bytes 1572872 | tf_op jit(solution)/shard_map/ppermute | solution.py:58
  265.1 22.4 %collective-permute-start.4 = (bf16[2,4,2,8,2048]{4,3,1,0,2:T(8,128)(2,1)S(1)}, bf16[2,4,2,8,2048]{4,3,1,0,2:T(8,128)(2,1)S(1)}, u32[]{:S(2)}, u32[]{:S(2)}) collective-permute-start(bf16[2,4,2,8,2048]{4,3,1,0,2:T(8,128)(2,1)S(1)} %bitcast.163), channel_id=1, source_target_pairs={{0,1},{1,2},{2,3},{3,0},{4,5},{5,6},{6,7},{7,4},{8,9},{9,10},{10,1... | collective-permute-start | bytes 1572872 | tf_op jit(solution)/shard_map/ppermute | solution.py:58
  287.9 13.9 %collective-permute-start.7 = (bf16[2,4,8,2048]{3,2,0,1:T(8,128)(2,1)S(1)}, bf16[2,4,8,2048]{3,2,0,1:T(8,128)(2,1)S(1)}, u32[]{:S(2)}, u32[]{:S(2)}) collective-permute-start(bf16[2,4,8,2048]{3,2,0,1:T(8,128)(2,1)S(1)} %copy.80), channel_id=1, source_target_pairs={{0,4},{1,5},{2,6},{3,7},{4,0},{5,1},{6,2},{7,3},{8,12},{9,13},{10,... | collective-permute-start | bytes 786440 | tf_op jit(solution)/shard_map/ppermute | solution.py:64
  290.6 2.3 copy-start.6
  302.7 12.9 %all-to-all-start.3 = ((bf16[2,4,8,2048]{3,2,0,1:T(8,128)(2,1)}), bf16[2,4,8,2048]{3,2,0,1:T(8,128)(2,1)S(1)}, u32[]{:S(2)}, u32[]{:S(2)}) async-start(bf16[2,4,8,2048]{3,2,0,1:T(8,128)(2,1)} %select_convert_fusion), calls=%async_computation.3 | async-start | bytes 524288 | tf_op jit(solution)/shard_map/all_to_all | solution.py:191
  307.7 10.9 %copy-start.1 = (bf16[2048,4,192]{0,2,1:T(8,128)(2,1)S(1)}, bf16[2048,4,192]{0,2,1:T(8,128)(2,1)}, u32[]{:S(2)}) copy-start(bf16[2048,4,192]{0,2,1:T(8,128)(2,1)} %param.24) | copy-start | bytes 9437188
  315.6 0.7 copy-start.8
Sparse Core Ops, SparseCore 0:
  21.0 77.8 all-gather.2
  199.6 46.4 all-gather.4

commit v13 on v11

--- a/solution.py
+++ b/solution.py
@@ -63,6 +63,25 @@
         sent = lax.dynamic_index_in_dim(rounded_one, (outer_me + shift) % outer_size, 2, False)
         total = total + lax.ppermute(sent, "head", pairs).astype(jnp.float32)
     return total
+
+
+def head_gather(rows, head_count):
+    inner_size = 4 if head_count % 4 == 0 else head_count
+    outer_size = head_count // inner_size
+    me = lax.axis_index("head")
+    outer_me, inner_me = me // inner_size, me % inner_size
+    held = [rows]
+    for shift in range(1, outer_size):
+        pairs = [(j, ((j // inner_size + shift) % outer_size) * inner_size + j % inner_size) for j in range(head_count)]
+        held.append(lax.ppermute(rows, "head", pairs))
+    by_outer = jnp.take(jnp.stack(held), (outer_me - jnp.arange(outer_size)) % outer_size, axis=0)
+    held = [by_outer]
+    for shift in range(1, inner_size):
+        pairs = [(j, (j // inner_size) * inner_size + (j % inner_size + shift) % inner_size) for j in range(head_count)]
+        held.append(lax.ppermute(by_outer, "head", pairs))
+    by_inner = jnp.take(jnp.stack(held), (inner_me - jnp.arange(inner_size)) % inner_size, axis=0)
+    gathered = jnp.moveaxis(by_inner, (0, 1), (3, 2))
+    return gathered.reshape(rows.shape[:2] + (head_count * rows.shape[2],) + rows.shape[3:])
 
 
 def land(incoming, req_count, head_count):
@@ -109,6 +128,11 @@
     slots = cache_prefill.shape[1]
     heads = cache_prefill.shape[3]
     devices = req_count * head_count
+    dealt_acts = jnp.take(stretch_acts, req_order, axis=0)
+    dealt_rows = lax.all_to_all(dealt_acts, "req", split_axis=0, concat_axis=1, tiled=True).reshape(
+        group_size, req_count, stretch_rows, features
+    )
+    gathered = head_gather(dealt_rows, head_count)
     chunks = []
     deferred = []
     later_layers = cache_prefill[1:]
@@ -125,17 +149,13 @@
             .reshape(devices, group_size, prefix_rows, heads // head_count, pair_width)
         )
         if layer == 0:
+            outgoing, gathered = lax.optimization_barrier((outgoing, gathered))
             incoming = lax.all_to_all(outgoing, ("req", "head"), 0, 0, tiled=True)
             incoming, later_layers = lax.optimization_barrier((incoming, later_layers))
             chunks.append(land(incoming, req_count, head_count))
         else:
             deferred.append(outgoing)
     current = chunks[0][0]
-    dealt_acts = jnp.take(stretch_acts, req_order, axis=0)
-    dealt_rows = lax.all_to_all(dealt_acts, "req", split_axis=0, concat_axis=1, tiled=True).reshape(
-        group_size, req_count, stretch_rows, features
-    )
-    gathered = lax.all_gather(dealt_rows, "head", axis=2, tiled=True)
     normed = (
         layer_norm(gathered.astype(jnp.float32), attn_gain)
         .astype(jnp.bfloat16)
@@ -163,7 +183,7 @@
     attn_rows = head_sum(partial_attn, head_count, stretch_rows)
     residual_rows = dealt_rows.astype(jnp.float32) + attn_rows
     normed_rows = layer_norm(residual_rows, mlp_gain).astype(jnp.bfloat16)
-    normed_all = lax.all_gather(normed_rows, "head", axis=2, tiled=True)
+    normed_all = head_gather(normed_rows, head_count)
     deferred, normed_all = lax.optimization_barrier((deferred, normed_all))
     for outgoing in deferred:
         chunks.append(land(lax.all_to_all(outgoing, ("req", "head"), 0, 0, tiled=True), req_count, head_count))

time: 321 us -> 340 us (1.059)
  other arithmetic: 19.6 us -> 34 us
  between operations: 14.7 us -> 1.44 us
  local copies, waits for them, and re-layouts: 48 us -> 60.7 us
  starting transfers between devices: 24.8 us -> 37.2 us
  blocking collectives: 9.17 us -> 0 us
    all_gather x2 -> x0, waiting for transfers between devices: 89.8 us -> none  [the longest x1 50.3 us: local(): gathered = lax.all_gather(dealt_rows, 'head', axis=2, tiled=True)]
    ppermute x0 -> x8, waiting for transfers between devices: none -> 59.2 us  [the longest x6 36.1 us: head_gather(): held.append(lax.ppermute(by_outer, 'head', pairs))]
    all_to_all x1, waiting for transfers between devices: 1.44 us -> 35.6 us  [local(): incoming = lax.all_to_all(outgoing, ('req', 'head'), 0, 0, tiled=True)]
    gather x0 -> x4, local copies, waits for them, and re-layouts: none -> 9.86 us  [the longest x2 5.69 us: head_gather(): jnp.take(jnp.stack(held), (inner_me - jnp.arange(inner_size)) % inner_siz...]
    all_to_all x1 -> x0, blocking collectives: 9.17 us -> none  [local(): lax.all_to_all(dealt_acts, 'req', split_axis=0, concat_axis=1, tiled=True)]
    ppermute x0 -> x8, starting transfers between devices: none -> 7.73 us  [the longest x6 4.67 us: head_gather(): held.append(lax.ppermute(by_outer, 'head', pairs))]
    another operation x0 -> x7, other arithmetic: none -> 6.28 us  [head_gather(): jnp.stack(held)]
    all_to_all x0 -> x1, starting transfers between devices: none -> 4.26 us  [local(): lax.all_to_all(dealt_acts, 'req', split_axis=0, concat_axis=1, tiled=True)]
  transfers between devices with their start and end apart: 13 -> 20, of which waited for: 10 -> 15; matrix products, arithmetic and copies ran while one was open for 20% -> 20% of each run, Pallas kernels for 0% -> 0%
where the time goes in v13:
time: 340 us; the launch traced here: 334 us
  waiting for transfers between devices  174 us (51%)
  local copies, waits for them, and re-layouts  60.7 us (18%)
  starting transfers between devices  37.2 us (11%)
  other arithmetic  34 us (10%)
  matrix products  26.8 us (8%)
    ppermute x6, waiting for transfers between devices, head_sum(): lax.ppermute(sent, 'head', pairs).astype(jnp.float32)  59.9 us
    ppermute x6, waiting for transfers between devices, head_gather(): held.append(lax.ppermute(by_outer, 'head', pairs))  36.1 us
    all_to_all x1, waiting for transfers between devices, local(): incoming = lax.all_to_all(outgoing, ('req', 'head'), 0, 0, tiled=True)  35.6 us
    ppermute x2, waiting for transfers between devices, head_gather(): held.append(lax.ppermute(rows, 'head', pairs))  23.2 us
    ppermute x2, waiting for transfers between devices, head_sum(): total = total + lax.ppermute(sent, 'head', pairs).astype(jnp.float32)  18.9 us
    dot_general x1, matrix products, local(): jnp.dot(inner, down_weight, preferred_element_type=jnp.float32)  14.3 us
    unnamed x65, local copies, waits for them, and re-layouts  10.6 us
    all_to_all x1, starting transfers between devices, local(): incoming = lax.all_to_all(outgoing, ('req', 'head'), 0, 0, tiled=True)  8.11 us
  transfers between devices with their start and end apart: 20, of which 15 were waited for; matrix products, arithmetic and copies ran while one was open for 20% of the time, Pallas kernels for 0%

profile of v13, /device:TPU:1, one launch (start us, length us, event | category | flops | bytes accessed | tf_op | source)
XLA Modules:
  0.0 333.9 jit_solution(14308277320382644223)
XLA Ops:
  5.9 4.3 %all-to-all-start = ((bf16[8,8,2048]{2,1,0:T(8,128)(2,1)}), bf16[8,8,2048]{2,1,0:T(8,128)(2,1)S(1)}, u32[]{:S(2)}, u32[]{:S(2)}) async-start(bf16[8,8,2048]{2,1,0:T(8,128)(2,1)} %broadcast_select_fusion.3), calls=%async_computation | async-start | bytes 524288 | tf_op jit(solution)/shard_map/all_to_all | solution.py:132
  10.3 5.2 %fusion.128 = (bf16[1,8,32,32,128]{4,3,2,1,0:T(8,128)(2,1)}, bf16[8,32,32,128]{3,2,1,0:T(8,128)(2,1)}) fusion(bf16[2,8,32,32,128]{4,3,2,1,0:T(8,128)(2,1)} %param.23), kind=kLoop, calls=%fused_computation.240 | loop fusion | bytes 8388608 | tf_op jit(solution)/shard_map/slice | solution.py:138
  15.4 3.7 %gather_fusion.3 = bf16[8,32,32,128]{3,2,1,0:T(8,128)(2,1)} fusion(bf16[8,32,32,128]{3,2,1,0:T(8,128)(2,1)} %get-tuple-element.38, s32[1024]{0:T(1024)S(1)} %pad_clamp_fusion.3), kind=kCustom, calls=%fused_computation.2.clone | custom fusion | bytes 4194336 | tf_op jit(solution)/shard_map/jit(_take)/gather | solution.py:143
  19.4 3.0 collective-permute-start
  22.4 2.8 select_select_fusion.1
  25.1 9.5 %collective-permute-done = bf16[2,4,8,2048]{3,2,1,0:T(8,128)(2,1)S(1)} collective-permute-done((bf16[2,4,8,2048]{3,2,1,0:T(8,128)(2,1)S(1)}, bf16[2,4,8,2048]{3,2,1,0:T(8,128)(2,1)S(1)}, u32[]{:S(2)}, u32[]{:S(2)}) %collective-permute-start) | collective-permute-done | bytes 262176 | tf_op jit(solution)/shard_map/ppermute | solution.py:76
  35.5 2.4 gather_fusion.4
  37.9 1.9 broadcast_select_fusion.1
  42.2 2.4 copy.108
  44.6 1.8 copy.109
  48.9 4.1 %collective-permute-done.2 = bf16[2,2,4,8,2048]{4,3,2,1,0:T(8,128)(2,1)} collective-permute-done((bf16[2,2,4,8,2048]{4,3,2,1,0:T(8,128)(2,1)}, bf16[2,2,4,8,2048]{4,3,2,1,0:T(8,128)(2,1)}, u32[]{:S(2)}, u32[]{:S(2)}) %collective-permute-start.2) | collective-permute-done | bytes 524320 | tf_op jit(solution)/shard_map/ppermute | solution.py:81
  53.0 9.9 %collective-permute-done.3 = bf16[2,2,4,8,2048]{4,3,2,1,0:T(8,128)(2,1)} collective-permute-done((bf16[2,2,4,8,2048]{4,3,2,1,0:T(8,128)(2,1)}, bf16[2,2,4,8,2048]{4,3,2,1,0:T(8,128)(2,1)}, u32[]{:S(2)}, u32[]{:S(2)}) %collective-permute-start.3) | collective-permute-done | bytes 524320 | tf_op jit(solution)/shard_map/ppermute | solution.py:81
  62.9 1.9 collective-permute-done.1
  64.8 2.9 pad_maximum_fusion.1
  67.7 3.6 %gather_fusion.5 = bf16[4,2,2,4,8,2048]{5,4,3,2,1,0:T(8,128)(2,1)} fusion(bf16[4,2,2,4,8,2048]{5,4,3,2,1,0:T(8,128)(2,1)} %pad_maximum_fusion.1, s32[1024]{0:T(1024)S(1)} %pad_clamp_fusion.1), kind=kCustom, calls=%fused_computation.4.clone | custom fusion | bytes 4194320 | tf_op jit(solution)/shard_map/jit(_take)/gather | solution.py:82
  71.3 1.9 select_bitcast_fusion.1
  74.6 8.1 %all-to-all-start.1 = ((bf16[32,2,32,4,128]{4,2,3,1,0:T(8,128)(2,1)}), bf16[32,2,32,4,128]{4,2,3,1,0:T(8,128)(2,1)}, u32[]{:S(2)}, u32[]{:S(2)}) async-start(bf16[32,2,32,4,128]{4,2,3,1,0:T(8,128)(2,1)} %bitcast.170), calls=%async_computation.1 | async-start | bytes 4194304 | tf_op jit(solution)/shard_map/all_to_all | solution.py:153
  90.5 1.9 convert_reduce_fusion
  93.9 1.8 fusion.19
  96.6 35.6 %all-to-all-done.1 = bf16[32,2,32,4,128]{4,2,3,1,0:T(8,128)(2,1)} async-done(((bf16[32,2,32,4,128]{4,2,3,1,0:T(8,128)(2,1)}), bf16[32,2,32,4,128]{4,2,3,1,0:T(8,128)(2,1)}, u32[]{:S(2)}, u32[]{:S(2)}) %all-to-all-start.1) | async-done | bytes 2097184 | tf_op jit(solution)/shard_map/all_to_all | solution.py:153
  133.5 2.0 fusion.132
  135.5 2.9 convolution_convert_fusion.3
  138.6 2.0 fusion.131
  140.6 2.2 convolution_convert_fusion.2
  143.7 1.7 convolution_convert_fusion.1
  149.1 11.0 %collective-permute-done.4 = bf16[2,4,2,8,2048]{4,3,1,0,2:T(8,128)(2,1)} collective-permute-done((bf16[2,4,2,8,2048]{4,3,1,0,2:T(8,128)(2,1)S(1)}, bf16[2,4,2,8,2048]{4,3,1,0,2:T(8,128)(2,1)}, u32[]{:S(2)}, u32[]{:S(2)}) %collective-permute-start.4) | collective-permute-done | bytes 524320 | tf_op jit(solution)/shard_map/ppermute | solution.py:58
  161.1 11.4 %collective-permute-done.6 = bf16[2,4,2,8,2048]{4,3,1,0,2:T(8,128)(2,1)S(1)} collective-permute-done((bf16[2,4,2,8,2048]{4,3,1,0,2:T(8,128)(2,1)S(1)}, bf16[2,4,2,8,2048]{4,3,1,0,2:T(8,128)(2,1)S(1)}, u32[]{:S(2)}, u32[]{:S(2)}) %collective-permute-start.6) | collective-permute-done | bytes 524320 | tf_op jit(solution)/shard_map/ppermute | solution.py:58
  175.0 2.7 gather_fusion.7
  177.6 10.5 %collective-permute-done.7 = bf16[2,4,8,2048]{3,2,1,0:T(8,128)(2,1)S(1)} collective-permute-done((bf16[2,4,8,2048]{3,2,1,0:T(8,128)(2,1)S(1)}, bf16[2,4,8,2048]{3,2,1,0:T(8,128)(2,1)S(1)}, u32[]{:S(2)}, u32[]{:S(2)}) %collective-permute-start.7) | collective-permute-done | bytes 262176 | tf_op jit(solution)/shard_map/ppermute | solution.py:64
  190.0 13.7 %collective-permute-done.8 = bf16[2,4,8,2048]{3,2,1,0:T(8,128)(2,1)S(1)} collective-permute-done((bf16[2,4,8,2048]{3,2,1,0:T(8,128)(2,1)S(1)}, bf16[2,4,8,2048]{3,2,1,0:T(8,128)(2,1)S(1)}, u32[]{:S(2)}, u32[]{:S(2)}) %collective-permute-start.8) | collective-permute-done | bytes 262176 | tf_op jit(solution)/shard_map/ppermute | solution.py:76
  204.5 1.7 gather_fusion.8
  206.5 2.3 collective-permute-start.11
  210.1 2.0 copy.122
  212.3 8.1 %collective-permute-done.9 = bf16[2,2,4,8,2048]{4,3,2,1,0:T(8,128)(2,1)S(1)} collective-permute-done((bf16[2,2,4,8,2048]{4,3,2,1,0:T(8,128)(2,1)S(1)}, bf16[2,2,4,8,2048]{4,3,2,1,0:T(8,128)(2,1)S(1)}, u32[]{:S(2)}, u32[]{:S(2)}) %collective-permute-start.9) | collective-permute-done | bytes 524320 | tf_op jit(solution)/shard_map/ppermute | solution.py:81
  220.4 12.0 %collective-permute-done.11 = bf16[2,2,4,8,2048]{4,3,2,1,0:T(8,128)(2,1)S(1)} collective-permute-done((bf16[2,2,4,8,2048]{4,3,2,1,0:T(8,128)(2,1)S(1)}, bf16[2,2,4,8,2048]{4,3,2,1,0:T(8,128)(2,1)S(1)}, u32[]{:S(2)}, u32[]{:S(2)}) %collective-permute-start.11) | collective-permute-done | bytes 524320 | tf_op jit(solution)/shard_map/ppermute | solution.py:81
  232.7 2.1 gather_fusion.9
  234.8 1.9 select_bitcast_fusion
  238.3 3.6 %all-to-all-start.2 = ((bf16[32,2,32,4,128]{4,2,3,1,0:T(8,128)(2,1)}), bf16[32,2,32,4,128]{4,2,3,1,0:T(8,128)(2,1)S(1)}, u32[]{:S(2)}, u32[]{:S(2)}) async-start(bf16[32,2,32,4,128]{4,2,3,1,0:T(8,128)(2,1)} %bitcast.51), calls=%async_computation.2 | async-start | bytes 4194304 | tf_op jit(solution)/shard_map/all_to_all | solution.py:189
  241.9 14.3 %convolution_convert_fusion = bf16[512,2048]{1,0:T(8,128)(2,1)} fusion(bf16[1024,2048]{1,0:T(8,128)(2,1)} %param.33, bf16[512,2048]{1,0:T(8,128)(2,1)} %bitcast.179, bf16[2048,1024]{1,0:T(8,128)(2,1)} %param.32), kind=kOutput, calls=%fused_computation.24 | convolution fusion | flops 4330094592 | bytes 12582912 | tf_op jit(solution)/shard_map/dot_general | solution.py:199
  256.2 1.7 constant_dynamic-slice_fusion.3
  262.3 27.1 %collective-permute-done.12 = bf16[2,4,2,8,2048]{4,3,1,0,2:T(8,128)(2,1)S(1)} collective-permute-done((bf16[2,4,2,8,2048]{4,3,1,0,2:T(8,128)(2,1)S(1)}, bf16[2,4,2,8,2048]{4,3,1,0,2:T(8,128)(2,1)S(1)}, u32[]{:S(2)}, u32[]{:S(2)}) %collective-permute-start.12) | collective-permute-done | bytes 524320 | tf_op jit(solution)/shard_map/ppermute | solution.py:58
  289.4 9.4 %collective-permute-done.14 = bf16[2,4,2,8,2048]{4,3,1,0,2:T(8,128)(2,1)S(1)} collective-permute-done((bf16[2,4,2,8,2048]{4,3,1,0,2:T(8,128)(2,1)S(1)}, bf16[2,4,2,8,2048]{4,3,1,0,2:T(8,128)(2,1)S(1)}, u32[]{:S(2)}, u32[]{:S(2)}) %collective-permute-start.14) | collective-permute-done | bytes 524320 | tf_op jit(solution)/shard_map/ppermute | solution.py:58
  299.1 1.8 collective-permute-start.15
  301.0 3.5 %copy.120 = bf16[4,2,8,32,4,128]{5,3,2,4,1,0:T(8,128)(2,1)} copy(bf16[4,2,8,32,4,128]{5,3,4,1,2,0:T(8,128)(2,1)} %bitcast.15) | data formatting | bytes 4194304 | tf_op jit(solution)/shard_map/transpose | solution.py:89
  304.5 8.4 %collective-permute-done.15 = bf16[2,4,8,2048]{3,2,1,0:T(8,128)(2,1)S(1)} collective-permute-done((bf16[2,4,8,2048]{3,2,1,0:T(8,128)(2,1)S(1)}, bf16[2,4,8,2048]{3,2,1,0:T(8,128)(2,1)S(1)}, u32[]{:S(2)}, u32[]{:S(2)}) %collective-permute-start.15) | collective-permute-done | bytes 262176 | tf_op jit(solution)/shard_map/ppermute | solution.py:64
  314.9 2.2 copy.125
  318.0 4.9 %all-to-all-start.3 = ((bf16[2,4,8,2048]{3,2,0,1:T(8,128)(2,1)}), bf16[2,4,8,2048]{3,2,0,1:T(8,128)(2,1)S(1)}, u32[]{:S(2)}, u32[]{:S(2)}) async-start(bf16[2,4,8,2048]{3,2,0,1:T(8,128)(2,1)} %copy.130), calls=%async_computation.3 | async-start | bytes 524288 | tf_op jit(solution)/shard_map/all_to_all | solution.py:211
  322.9 7.9 %copy.131 = bf16[8,2,256,4,128]{4,3,2,1,0:T(4,128)(2,1)} copy(bf16[8,2,256,4,128]{4,2,3,1,0:T(8,128)(2,1)} %bitcast.169) | data formatting | bytes 8388608
  (170 shorter events, 48.7 us)
Async XLA Ops:
  0.6 93.2 %copy-start = (bf16[2048,4,192]{0,2,1:T(8,128)(2,1)S(1)}, bf16[2048,4,192]{0,2,1:T(8,128)(2,1)}, u32[]{:S(2)}) copy-start(bf16[2048,4,192]{0,2,1:T(8,128)(2,1)} %param.28) | copy-start | bytes 9437188
  1.5 14.0 %copy-start.17 = (s32[1024]{0:T(1024)}, s32[1024]{0:T(1024)S(1)}, u32[]{:S(2)}) copy-start(s32[1024]{0:T(1024)S(1)} %pad_clamp_fusion.3) | copy-start | bytes 12292
  3.6 18.8 %copy-start.20 = (pred[8]{0:T(512)(128)(4,1)}, pred[8]{0:T(512)(128)(4,1)S(1)}, u32[]{:S(2)}) copy-start(pred[8]{0:T(512)(128)(4,1)S(1)} %get-tuple-element.36) | copy-start | bytes 28
  5.9 13.4 %all-to-all-start = ((bf16[8,8,2048]{2,1,0:T(8,128)(2,1)}), bf16[8,8,2048]{2,1,0:T(8,128)(2,1)S(1)}, u32[]{:S(2)}, u32[]{:S(2)}) async-start(bf16[8,8,2048]{2,1,0:T(8,128)(2,1)} %broadcast_select_fusion.3), calls=%async_computation | async-start | bytes 524288 | tf_op jit(solution)/shard_map/all_to_all | solution.py:132
  10.2 37.5 %copy-start.18 = (pred[2]{0:T(512)(128)(4,1)}, pred[2]{0:T(512)(128)(4,1)S(1)}, u32[]{:S(2)}) copy-start(pred[2]{0:T(512)(128)(4,1)S(1)} %compare_and_fusion.2) | copy-start | bytes 10
  10.2 25.2 %copy-start.23 = (s32[1024]{0:T(1024)}, s32[1024]{0:T(1024)S(1)}, u32[]{:S(2)}) copy-start(s32[1024]{0:T(1024)S(1)} %pad_clamp_fusion.2) | copy-start | bytes 12292
  10.3 57.5 %copy-start.22 = (s32[1024]{0:T(1024)}, s32[1024]{0:T(1024)S(1)}, u32[]{:S(2)}) copy-start(s32[1024]{0:T(1024)S(1)} %pad_clamp_fusion.1) | copy-start | bytes 12292
  15.4 3.7 %copy-start.29 = (s32[8]{0:T(128)S(1)}, s32[8]{0:T(128)}, u32[]{:S(2)}) copy-start(s32[8]{0:T(128)} %param.26) | copy-start | bytes 100
  19.3 5.8 %copy-start.15 = (pred[8,32]{1,0:T(8,128)(4,1)}, pred[8,32]{1,0:T(8,128)(4,1)S(1)}, u32[]{:S(2)}) copy-start(pred[8,32]{1,0:T(8,128)(4,1)S(1)} %broadcast_compare_fusion) | copy-start | bytes 772
  19.4 15.2 %collective-permute-start = (bf16[2,4,8,2048]{3,2,1,0:T(8,128)(2,1)S(1)}, bf16[2,4,8,2048]{3,2,1,0:T(8,128)(2,1)S(1)}, u32[]{:S(2)}, u32[]{:S(2)}) collective-permute-start(bf16[2,4,8,2048]{3,2,1,0:T(8,128)(2,1)S(1)} %get-tuple-element.52), channel_id=1, source_target_pairs={{0,4},{1,5},{2,6},{3,7},{4,0},{5,1},{6,2},{7,3},{8,12},{9,13},{10,... | collective-permute-start | bytes 786440 | tf_op jit(solution)/shard_map/ppermute | solution.py:76
  39.8 13.1 %collective-permute-start.2 = (bf16[2,2,4,8,2048]{4,3,2,1,0:T(8,128)(2,1)}, bf16[2,2,4,8,2048]{4,3,2,1,0:T(8,128)(2,1)}, u32[]{:S(2)}, u32[]{:S(2)}) collective-permute-start(bf16[2,2,4,8,2048]{4,3,2,1,0:T(8,128)(2,1)} %broadcast_select_fusion.1), channel_id=1, source_target_pairs={{0,2},{1,3},{2,0},{3,1},{4,6},{5,7},{6,4},{7,5},{8,10},{9,11},{10,... | collective-permute-start | bytes 1572872 | tf_op jit(solution)/shard_map/ppermute | solution.py:81
  40.5 22.4 %collective-permute-start.3 = (bf16[2,2,4,8,2048]{4,3,2,1,0:T(8,128)(2,1)}, bf16[2,2,4,8,2048]{4,3,2,1,0:T(8,128)(2,1)}, u32[]{:S(2)}, u32[]{:S(2)}) collective-permute-start(bf16[2,2,4,8,2048]{4,3,2,1,0:T(8,128)(2,1)} %broadcast_select_fusion.1), channel_id=1, source_target_pairs={{0,3},{1,0},{2,1},{3,2},{4,7},{5,4},{6,5},{7,6},{8,11},{9,8},{10,9... | collective-permute-start | bytes 1572872 | tf_op jit(solution)/shard_map/ppermute | solution.py:81
  42.1 22.7 %collective-permute-start.1 = (bf16[2,2,4,8,2048]{4,3,2,1,0:T(8,128)(2,1)}, bf16[2,2,4,8,2048]{4,3,2,1,0:T(8,128)(2,1)}, u32[]{:S(2)}, u32[]{:S(2)}) collective-permute-start(bf16[2,2,4,8,2048]{4,3,2,1,0:T(8,128)(2,1)} %broadcast_select_fusion.1), channel_id=1, source_target_pairs={{0,1},{1,2},{2,3},{3,0},{4,5},{5,6},{6,7},{7,4},{8,9},{9,10},{10,1... | collective-permute-start | bytes 1572872 | tf_op jit(solution)/shard_map/ppermute | solution.py:81
  42.1 29.2 %copy-start.26 = (pred[4]{0:T(512)(128)(4,1)}, pred[4]{0:T(512)(128)(4,1)S(1)}, u32[]{:S(2)}) copy-start(pred[4]{0:T(512)(128)(4,1)S(1)} %compare_and_fusion.1) | copy-start | bytes 16
  44.6 1.8 copy-start.24
  44.6 1.8 copy-start.2
  44.6 2.5 copy-start.3
  74.6 57.7 %all-to-all-start.1 = ((bf16[32,2,32,4,128]{4,2,3,1,0:T(8,128)(2,1)}), bf16[32,2,32,4,128]{4,2,3,1,0:T(8,128)(2,1)}, u32[]{:S(2)}, u32[]{:S(2)}) async-start(bf16[32,2,32,4,128]{4,2,3,1,0:T(8,128)(2,1)} %bitcast.170), calls=%async_computation.1 | async-start | bytes 4194304 | tf_op jit(solution)/shard_map/all_to_all | solution.py:153
  82.7 9.7 %copy-start.4 = (bf16[2,4,2,4,8,2048]{5,4,3,2,1,0:T(8,128)(2,1)S(1)}, bf16[2,4,2,4,8,2048]{5,4,3,2,1,0:T(8,128)(2,1)}, u32[]{:S(2)}) copy-start(bf16[2,4,2,4,8,2048]{5,4,3,2,1,0:T(8,128)(2,1)} %copy.110) | copy-start | bytes 6291460
  96.6 36.9 %copy-start.11 = (f32[256,512]{1,0:T(8,128)S(1)}, f32[256,512]{1,0:T(8,128)}, u32[]{:S(2)}) copy-start(f32[256,512]{1,0:T(8,128)} %subtract_convert_fusion.1) | copy-start | bytes 1572868
  96.6 36.9 %copy-start.13 = (pred[256,512]{1,0:T(8,128)(4,1)S(1)}, pred[256,512]{1,0:T(8,128)(4,1)}, u32[]{:S(2)}) copy-start(pred[256,512]{1,0:T(8,128)(4,1)} %get-tuple-element.53) | copy-start | bytes 393220
  96.6 37.0 %copy-start.31 = (f32[4]{0:T(128)S(1)}, f32[4]{0:T(128)}, u32[]{:S(2)}) copy-start(f32[4]{0:T(128)} %param.29) | copy-start | bytes 52
  135.5 3.0 copy-start.10
  140.5 2.3 copy-start.14
  140.5 3.1 copy-start.9
  146.4 26.1 %copy-start.7 = (bf16[2,4,2,1,8,2048]{5,4,3,2,1,0:T(8,128)(2,1)S(1)}, bf16[2,4,2,1,8,2048]{5,4,3,2,1,0:T(8,128)(2,1)}, u32[]{:S(2)}) copy-start(bf16[2,4,2,1,8,2048]{5,4,3,2,1,0:T(8,128)(2,1)} %get-tuple-element.43) | copy-start | bytes 1572868
  146.4 13.7 %collective-permute-start.4 = (bf16[2,4,2,8,2048]{4,3,1,0,2:T(8,128)(2,1)S(1)}, bf16[2,4,2,8,2048]{4,3,1,0,2:T(8,128)(2,1)}, u32[]{:S(2)}, u32[]{:S(2)}) collective-permute-start(bf16[2,4,2,8,2048]{4,3,1,0,2:T(8,128)(2,1)S(1)} %bitcast.187), channel_id=1, source_target_pairs={{0,1},{1,2},{2,3},{3,0},{4,5},{5,6},{6,7},{7,4},{8,9},{9,10},{10,1... | collective-permute-start | bytes 1572872 | tf_op jit(solution)/shard_map/ppermute | solution.py:58
  147.4 13.7 %collective-permute-start.5 = (bf16[2,4,2,8,2048]{4,3,1,0,2:T(8,128)(2,1)S(1)}, bf16[2,4,2,8,2048]{4,3,1,0,2:T(8,128)(2,1)S(1)}, u32[]{:S(2)}, u32[]{:S(2)}) collective-permute-start(bf16[2,4,2,8,2048]{4,3,1,0,2:T(8,128)(2,1)S(1)} %bitcast.188), channel_id=1, source_target_pairs={{0,2},{1,3},{2,0},{3,1},{4,6},{5,7},{6,4},{7,5},{8,10},{9,11},{10,... | collective-permute-start | bytes 1572872 | tf_op jit(solution)/shard_map/ppermute | solution.py:58
  147.5 26.5 %copy-start.25 = (bf16[2048]{0:T(1024)(128)(2,1)S(1)}, bf16[2048]{0:T(1024)(128)(2,1)}, u32[]{:S(2)}) copy-start(bf16[2048]{0:T(1024)(128)(2,1)} %param.31) | copy-start | bytes 12292
  147.5 26.5 %copy-start.30 = (s32[8]{0:T(128)S(1)}, s32[8]{0:T(128)}, u32[]{:S(2)}) copy-start(s32[8]{0:T(128)} %param.26) | copy-start | bytes 100
  147.5 24.9 %collective-permute-start.6 = (bf16[2,4,2,8,2048]{4,3,1,0,2:T(8,128)(2,1)S(1)}, bf16[2,4,2,8,2048]{4,3,1,0,2:T(8,128)(2,1)S(1)}, u32[]{:S(2)}, u32[]{:S(2)}) collective-permute-start(bf16[2,4,2,8,2048]{4,3,1,0,2:T(8,128)(2,1)S(1)} %bitcast.189), channel_id=1, source_target_pairs={{0,3},{1,0},{2,1},{3,2},{4,7},{5,4},{6,5},{7,6},{8,11},{9,8},{10,9... | collective-permute-start | bytes 1572872 | tf_op jit(solution)/shard_map/ppermute | solution.py:58
  173.9 14.3 %collective-permute-start.7 = (bf16[2,4,8,2048]{3,2,1,0:T(8,128)(2,1)S(1)}, bf16[2,4,8,2048]{3,2,1,0:T(8,128)(2,1)S(1)}, u32[]{:S(2)}, u32[]{:S(2)}) collective-permute-start(bf16[2,4,8,2048]{3,2,1,0:T(8,128)(2,1)S(1)} %fusion.64), channel_id=1, source_target_pairs={{0,4},{1,5},{2,6},{3,7},{4,0},{5,1},{6,2},{7,3},{8,12},{9,13},{10,... | collective-permute-start | bytes 786440 | tf_op jit(solution)/shard_map/ppermute | solution.py:64
  189.4 16.9 %copy-start.19 = (pred[2]{0:T(512)(128)(4,1)S(1)}, pred[2]{0:T(512)(128)(4,1)}, u32[]{:S(2)}) copy-start(pred[2]{0:T(512)(128)(4,1)} %copy-done.18) | copy-start | bytes 10
  189.7 19.1 %copy-start.16 = (pred[8,32]{1,0:T(8,128)(4,1)S(1)}, pred[8,32]{1,0:T(8,128)(4,1)}, u32[]{:S(2)}) copy-start(pred[8,32]{1,0:T(8,128)(4,1)} %copy-done.15) | copy-start | bytes 772
  189.7 19.1 %copy-start.21 = (pred[8]{0:T(512)(128)(4,1)S(1)}, pred[8]{0:T(512)(128)(4,1)}, u32[]{:S(2)}) copy-start(pred[8]{0:T(512)(128)(4,1)} %copy-done.20) | copy-start | bytes 28
  189.8 13.9 %collective-permute-start.8 = (bf16[2,4,8,2048]{3,2,1,0:T(8,128)(2,1)S(1)}, bf16[2,4,8,2048]{3,2,1,0:T(8,128)(2,1)S(1)}, u32[]{:S(2)}, u32[]{:S(2)}) collective-permute-start(bf16[2,4,8,2048]{3,2,1,0:T(8,128)(2,1)S(1)} %multiply_convert_fusion), channel_id=1, source_target_pairs={{0,4},{1,5},{2,6},{3,7},{4,0},{5,1},{6,2},{7,3},{8,12},{9,13},{10,... | collective-permute-start | bytes 786440 | tf_op jit(solution)/shard_map/ppermute | solution.py:76
  206.4 14.0 %collective-permute-start.9 = (bf16[2,2,4,8,2048]{4,3,2,1,0:T(8,128)(2,1)S(1)}, bf16[2,2,4,8,2048]{4,3,2,1,0:T(8,128)(2,1)S(1)}, u32[]{:S(2)}, u32[]{:S(2)}) collective-permute-start(bf16[2,2,4,8,2048]{4,3,2,1,0:T(8,128)(2,1)S(1)} %broadcast_select_fusion), channel_id=1, source_target_pairs={{0,1},{1,2},{2,3},{3,0},{4,5},{5,6},{6,7},{7,4},{8,9},{9,10},{10,1... | collective-permute-start | bytes 1572872 | tf_op jit(solution)/shard_map/ppermute | solution.py:81
  206.5 13.9 %collective-permute-start.10 = (bf16[2,2,4,8,2048]{4,3,2,1,0:T(8,128)(2,1)S(1)}, bf16[2,2,4,8,2048]{4,3,2,1,0:T(8,128)(2,1)S(1)}, u32[]{:S(2)}, u32[]{:S(2)}) collective-permute-start(bf16[2,2,4,8,2048]{4,3,2,1,0:T(8,128)(2,1)S(1)} %broadcast_select_fusion), channel_id=1, source_target_pairs={{0,2},{1,3},{2,0},{3,1},{4,6},{5,7},{6,4},{7,5},{8,10},{9,11},{10,... | collective-permute-start | bytes 1572872 | tf_op jit(solution)/shard_map/ppermute | solution.py:81
  206.5 25.9 %collective-permute-start.11 = (bf16[2,2,4,8,2048]{4,3,2,1,0:T(8,128)(2,1)S(1)}, bf16[2,2,4,8,2048]{4,3,2,1,0:T(8,128)(2,1)S(1)}, u32[]{:S(2)}, u32[]{:S(2)}) collective-permute-start(bf16[2,2,4,8,2048]{4,3,2,1,0:T(8,128)(2,1)S(1)} %broadcast_select_fusion), channel_id=1, source_target_pairs={{0,3},{1,0},{2,1},{3,2},{4,7},{5,4},{6,5},{7,6},{8,11},{9,8},{10,9... | collective-permute-start | bytes 1572872 | tf_op jit(solution)/shard_map/ppermute | solution.py:81
  232.7 2.1 copy-start.27
  238.3 74.7 %all-to-all-start.2 = ((bf16[32,2,32,4,128]{4,2,3,1,0:T(8,128)(2,1)}), bf16[32,2,32,4,128]{4,2,3,1,0:T(8,128)(2,1)S(1)}, u32[]{:S(2)}, u32[]{:S(2)}) async-start(bf16[32,2,32,4,128]{4,2,3,1,0:T(8,128)(2,1)} %bitcast.51), calls=%async_computation.2 | async-start | bytes 4194304 | tf_op jit(solution)/shard_map/all_to_all | solution.py:189
  257.9 31.5 %collective-permute-start.12 = (bf16[2,4,2,8,2048]{4,3,1,0,2:T(8,128)(2,1)S(1)}, bf16[2,4,2,8,2048]{4,3,1,0,2:T(8,128)(2,1)S(1)}, u32[]{:S(2)}, u32[]{:S(2)}) collective-permute-start(bf16[2,4,2,8,2048]{4,3,1,0,2:T(8,128)(2,1)S(1)} %bitcast.190), channel_id=1, source_target_pairs={{0,1},{1,2},{2,3},{3,0},{4,5},{5,6},{6,7},{7,4},{8,9},{9,10},{10,1... | collective-permute-start | bytes 1572872 | tf_op jit(solution)/shard_map/ppermute | solution.py:58
  259.4 30.0 %collective-permute-start.13 = (bf16[2,4,2,8,2048]{4,3,1,0,2:T(8,128)(2,1)S(1)}, bf16[2,4,2,8,2048]{4,3,1,0,2:T(8,128)(2,1)S(1)}, u32[]{:S(2)}, u32[]{:S(2)}) collective-permute-start(bf16[2,4,2,8,2048]{4,3,1,0,2:T(8,128)(2,1)S(1)} %bitcast.191), channel_id=1, source_target_pairs={{0,2},{1,3},{2,0},{3,1},{4,6},{5,7},{6,4},{7,5},{8,10},{9,11},{10,... | collective-permute-start | bytes 1572872 | tf_op jit(solution)/shard_map/ppermute | solution.py:58
  260.7 40.3 %copy-start.28 = (s32[2]{0:T(128)S(1)}, s32[2]{0:T(128)}, u32[]{:S(2)}) copy-start(s32[2]{0:T(128)} %get-tuple-element.55) | copy-start | bytes 28
  260.7 38.1 %collective-permute-start.14 = (bf16[2,4,2,8,2048]{4,3,1,0,2:T(8,128)(2,1)S(1)}, bf16[2,4,2,8,2048]{4,3,1,0,2:T(8,128)(2,1)S(1)}, u32[]{:S(2)}, u32[]{:S(2)}) collective-permute-start(bf16[2,4,2,8,2048]{4,3,1,0,2:T(8,128)(2,1)S(1)} %bitcast.192), channel_id=1, source_target_pairs={{0,3},{1,0},{2,1},{3,2},{4,7},{5,4},{6,5},{7,6},{8,11},{9,8},{10,9... | collective-permute-start | bytes 1572872 | tf_op jit(solution)/shard_map/ppermute | solution.py:58
  299.1 13.7 %collective-permute-start.15 = (bf16[2,4,8,2048]{3,2,1,0:T(8,128)(2,1)S(1)}, bf16[2,4,8,2048]{3,2,1,0:T(8,128)(2,1)S(1)}, u32[]{:S(2)}, u32[]{:S(2)}) collective-permute-start(bf16[2,4,8,2048]{3,2,1,0:T(8,128)(2,1)S(1)} %fusion.65), channel_id=1, source_target_pairs={{0,4},{1,5},{2,6},{3,7},{4,0},{5,1},{6,2},{7,3},{8,12},{9,13},{10,... | collective-permute-start | bytes 786440 | tf_op jit(solution)/shard_map/ppermute | solution.py:64
  318.0 12.9 %all-to-all-start.3 = ((bf16[2,4,8,2048]{3,2,0,1:T(8,128)(2,1)}), bf16[2,4,8,2048]{3,2,0,1:T(8,128)(2,1)S(1)}, u32[]{:S(2)}, u32[]{:S(2)}) async-start(bf16[2,4,8,2048]{3,2,0,1:T(8,128)(2,1)} %copy.130), calls=%async_computation.3 | async-start | bytes 524288 | tf_op jit(solution)/shard_map/all_to_all | solution.py:211
  322.9 10.9 %copy-start.1 = (bf16[2048,4,192]{0,2,1:T(8,128)(2,1)S(1)}, bf16[2048,4,192]{0,2,1:T(8,128)(2,1)}, u32[]{:S(2)}) copy-start(bf16[2048,4,192]{0,2,1:T(8,128)(2,1)} %param.28) | copy-start | bytes 9437188
  (4 other events, 4.3 us)

commit v14 on v13

--- a/solution.py
+++ b/solution.py
@@ -128,11 +128,6 @@
     slots = cache_prefill.shape[1]
     heads = cache_prefill.shape[3]
     devices = req_count * head_count
-    dealt_acts = jnp.take(stretch_acts, req_order, axis=0)
-    dealt_rows = lax.all_to_all(dealt_acts, "req", split_axis=0, concat_axis=1, tiled=True).reshape(
-        group_size, req_count, stretch_rows, features
-    )
-    gathered = head_gather(dealt_rows, head_count)
     chunks = []
     deferred = []
     later_layers = cache_prefill[1:]
@@ -149,13 +144,17 @@
             .reshape(devices, group_size, prefix_rows, heads // head_count, pair_width)
         )
         if layer == 0:
-            outgoing, gathered = lax.optimization_barrier((outgoing, gathered))
             incoming = lax.all_to_all(outgoing, ("req", "head"), 0, 0, tiled=True)
             incoming, later_layers = lax.optimization_barrier((incoming, later_layers))
             chunks.append(land(incoming, req_count, head_count))
         else:
             deferred.append(outgoing)
     current = chunks[0][0]
+    dealt_acts = jnp.take(stretch_acts, req_order, axis=0)
+    dealt_rows = lax.all_to_all(dealt_acts, "req", split_axis=0, concat_axis=1, tiled=True).reshape(
+        group_size, req_count, stretch_rows, features
+    )
+    gathered = lax.all_gather(dealt_rows, "head", axis=2, tiled=True)
     normed = (
         layer_norm(gathered.astype(jnp.float32), attn_gain)
         .astype(jnp.bfloat16)

time: 340 us -> 320 us (0.941); the launches traced: 334 us -> 319 us
  starting transfers between devices: 37.2 us -> 23.2 us
  between operations: 1.44 us -> 14.8 us
  other arithmetic: 34 us -> 23.1 us
  local copies, waits for them, and re-layouts: 60.7 us -> 50.1 us
  blocking collectives: 0 us -> 9.17 us
    all_gather x0 -> x1, waiting for transfers between devices: none -> 50.7 us  [local(): gathered = lax.all_gather(dealt_rows, 'head', axis=2, tiled=True)]
    all_to_all x1, waiting for transfers between devices: 35.6 us -> 1.45 us  [local(): incoming = lax.all_to_all(outgoing, ('req', 'head'), 0, 0, tiled=True)]
    ppermute x6 -> x3, waiting for transfers between devices: 36.1 us -> 20.2 us  [head_gather(): held.append(lax.ppermute(by_outer, 'head', pairs))]
    ppermute x2 -> x1, waiting for transfers between devices: 23.2 us -> 13.4 us  [head_gather(): held.append(lax.ppermute(rows, 'head', pairs))]
    all_to_all x0 -> x1, blocking collectives: none -> 9.17 us  [local(): lax.all_to_all(dealt_acts, 'req', split_axis=0, concat_axis=1, tiled=True)]
    ppermute x6, waiting for transfers between devices: 59.9 us -> 66.5 us  [head_sum(): lax.ppermute(sent, 'head', pairs).astype(jnp.float32)]
    another operation x7 -> x3, other arithmetic: 6.28 us -> 1.24 us  [head_gather(): jnp.stack(held)]
    all_to_all x1 -> x0, starting transfers between devices: 4.26 us -> none  [local(): lax.all_to_all(dealt_acts, 'req', split_axis=0, concat_axis=1, tiled=True)]
  transfers between devices with their start and end apart: 20 -> 16, of which waited for: 15 -> 12; matrix products, arithmetic and copies ran while one was open for 20% -> 19% of each run, Pallas kernels for 0% -> 0%
where the time goes in v14:
time: 320 us; the launch traced here: 319 us
  waiting for transfers between devices  173 us (54%)
  local copies, waits for them, and re-layouts  50.1 us (16%)
  matrix products  25.2 us (8%)
  starting transfers between devices  23.2 us (7%)
  other arithmetic  23.1 us (7%)
  between operations  14.8 us (5%)
  blocking collectives  9.17 us (3%)
    ppermute x6, waiting for transfers between devices, head_sum(): lax.ppermute(sent, 'head', pairs).astype(jnp.float32)  66.5 us
    all_gather x1, waiting for transfers between devices, local(): gathered = lax.all_gather(dealt_rows, 'head', axis=2, tiled=True)  50.7 us
    ppermute x2, waiting for transfers between devices, head_sum(): total = total + lax.ppermute(sent, 'head', pairs).astype(jnp.float32)  20.8 us
    ppermute x3, waiting for transfers between devices, head_gather(): held.append(lax.ppermute(by_outer, 'head', pairs))  20.2 us
    dot_general x1, matrix products, local(): jnp.dot(inner, down_weight, preferred_element_type=jnp.float32)  14.3 us
    ppermute x1, waiting for transfers between devices, head_gather(): held.append(lax.ppermute(rows, 'head', pairs))  13.4 us
    unnamed x41, local copies, waits for them, and re-layouts  10.7 us
    all_to_all x1, blocking collectives, local(): lax.all_to_all(dealt_acts, 'req', split_axis=0, concat_axis=1, tiled=True)  9.17 us
  transfers between devices with their start and end apart: 16, of which 12 were waited for; matrix products, arithmetic and copies ran while one was open for 19% of the time, Pallas kernels for 0%

profile of v14, /device:TPU:1, one launch (start us, length us, event | category | flops | bytes accessed | tf_op | source)
XLA Modules:
  0.0 318.7 jit_solution(14556338988563860502)
XLA Ops:
  8.0 1.4 gather_fusion
  10.1 1.5 gather_fusion.4
  11.7 9.2 %all_to_all.40 = bf16[8,8,2048]{2,1,0:T(8,128)(2,1)} all-to-all(bf16[8,8,2048]{2,1,0:T(8,128)(2,1)S(1)} %broadcast_select_fusion.2), channel_id=1, replica_groups=mesh['req'=4,'head'=8] {'req'}, dimensions={0} | all-to-all | bytes 524288 | tf_op jit(solution)/shard_map/all_to_all | solution.py:154
  20.9 5.2 %fusion.132 = (bf16[1,8,32,32,128]{4,3,2,1,0:T(8,128)(2,1)}, bf16[8,32,32,128]{3,2,1,0:T(8,128)(2,1)}) fusion(bf16[2,8,32,32,128]{4,3,2,1,0:T(8,128)(2,1)} %param.19), kind=kLoop, calls=%fused_computation.247 | loop fusion | bytes 8388608 | tf_op jit(solution)/shard_map/slice | solution.py:133
  26.1 3.7 %gather_fusion.5 = bf16[8,32,32,128]{3,2,1,0:T(8,128)(2,1)} fusion(bf16[8,32,32,128]{3,2,1,0:T(8,128)(2,1)} %get-tuple-element.28, s32[1024]{0:T(1024)S(1)} %pad_clamp_fusion.3), kind=kCustom, calls=%fused_computation.2.clone | custom fusion | bytes 4194336 | tf_op jit(solution)/shard_map/jit(_take)/gather | solution.py:138
  29.9 1.8 select_select_fusion.1
  32.6 1.8 copy.59
  34.4 6.1 %all-to-all-start.1 = ((bf16[32,2,32,4,128]{4,2,3,1,0:T(8,128)(2,1)}), bf16[32,2,32,4,128]{4,2,3,1,0:T(8,128)(2,1)}, u32[]{:S(2)}, u32[]{:S(2)}) async-start(bf16[32,2,32,4,128]{4,2,3,1,0:T(8,128)(2,1)} %bitcast.153), calls=%async_computation.1 | async-start | bytes 4194304 | tf_op jit(solution)/shard_map/all_to_all | solution.py:147
  43.3 1.2 iota_compare_fusion.1
  48.3 50.7 %all-gather.2.cloned.1.call-done = bf16[2,4,64,2048]{3,2,0,1:T(8,128)(2,1)} async-done(((bf16[2,4,8,2048]{3,2,0,1:T(8,128)(2,1)}), bf16[2,4,64,2048]{3,2,0,1:T(8,128)(2,1)}) %all-gather.2.cloned.1.call-update) | async-done | bytes 2097168 | tf_op jit(solution)/shard_map/all_gather | solution.py:157
  99.0 2.1 convert_reduce_fusion
  102.8 1.8 fusion.19
  105.6 1.5 all-to-all-done.1
  107.1 1.1 fusion.133
  108.3 2.0 fusion.136
  110.3 2.2 convolution_convert_fusion.3
  112.7 2.0 fusion.135
  114.7 2.2 convolution_convert_fusion.2
  117.8 1.0 constant_dynamic-slice_fusion.7
  118.9 1.2 collective-permute-start
  120.3 1.3 collective-permute-start.2
  121.6 11.0 %collective-permute-done = bf16[2,4,2,8,2048]{4,3,1,0,2:T(8,128)(2,1)} collective-permute-done((bf16[2,4,2,8,2048]{4,3,1,0,2:T(8,128)(2,1)S(1)}, bf16[2,4,2,8,2048]{4,3,1,0,2:T(8,128)(2,1)}, u32[]{:S(2)}, u32[]{:S(2)}) %collective-permute-start) | collective-permute-done | bytes 524320 | tf_op jit(solution)/shard_map/ppermute | solution.py:58
  133.6 11.3 %collective-permute-done.2 = bf16[2,4,2,8,2048]{4,3,1,0,2:T(8,128)(2,1)S(1)} collective-permute-done((bf16[2,4,2,8,2048]{4,3,1,0,2:T(8,128)(2,1)S(1)}, bf16[2,4,2,8,2048]{4,3,1,0,2:T(8,128)(2,1)S(1)}, u32[]{:S(2)}, u32[]{:S(2)}) %collective-permute-start.2) | collective-permute-done | bytes 524320 | tf_op jit(solution)/shard_map/ppermute | solution.py:58
  144.9 1.4 fusion.26
  147.6 2.6 gather_fusion.7
  150.2 10.8 %collective-permute-done.3 = bf16[2,4,8,2048]{3,2,0,1:T(8,128)(2,1)S(1)} collective-permute-done((bf16[2,4,8,2048]{3,2,0,1:T(8,128)(2,1)S(1)}, bf16[2,4,8,2048]{3,2,0,1:T(8,128)(2,1)S(1)}, u32[]{:S(2)}, u32[]{:S(2)}) %collective-permute-start.3) | collective-permute-done | bytes 262176 | tf_op jit(solution)/shard_map/ppermute | solution.py:64
  160.9 1.2 fusion.130
  162.7 13.4 %collective-permute-done.4 = bf16[2,4,8,2048]{3,2,0,1:T(8,128)(2,1)S(1)} collective-permute-done((bf16[2,4,8,2048]{3,2,0,1:T(8,128)(2,1)S(1)}, bf16[2,4,8,2048]{3,2,0,1:T(8,128)(2,1)S(1)}, u32[]{:S(2)}, u32[]{:S(2)}) %collective-permute-start.4) | collective-permute-done | bytes 262176 | tf_op jit(solution)/shard_map/ppermute | solution.py:76
  177.0 1.6 gather_fusion.1
  178.9 2.3 collective-permute-start.7
  182.5 2.0 copy.74
  184.6 8.2 %collective-permute-done.5 = bf16[2,2,4,8,2048]{4,3,1,2,0:T(8,128)(2,1)S(1)} collective-permute-done((bf16[2,2,4,8,2048]{4,3,1,2,0:T(8,128)(2,1)S(1)}, bf16[2,2,4,8,2048]{4,3,1,2,0:T(8,128)(2,1)S(1)}, u32[]{:S(2)}, u32[]{:S(2)}) %collective-permute-start.5) | collective-permute-done | bytes 524320 | tf_op jit(solution)/shard_map/ppermute | solution.py:81
  192.8 12.0 %collective-permute-done.7 = bf16[2,2,4,8,2048]{4,3,1,2,0:T(8,128)(2,1)S(1)} collective-permute-done((bf16[2,2,4,8,2048]{4,3,1,2,0:T(8,128)(2,1)S(1)}, bf16[2,2,4,8,2048]{4,3,1,2,0:T(8,128)(2,1)S(1)}, u32[]{:S(2)}, u32[]{:S(2)}) %collective-permute-start.7) | collective-permute-done | bytes 524320 | tf_op jit(solution)/shard_map/ppermute | solution.py:81
  205.1 2.0 gather_fusion.2
  207.1 1.9 select_bitcast_fusion
  208.9 1.6 copy.75
  210.5 3.7 %all-to-all-start.2 = ((bf16[32,2,32,4,128]{4,2,3,1,0:T(8,128)(2,1)}), bf16[32,2,32,4,128]{4,2,3,1,0:T(8,128)(2,1)S(1)}, u32[]{:S(2)}, u32[]{:S(2)}) async-start(bf16[32,2,32,4,128]{4,2,3,1,0:T(8,128)(2,1)} %bitcast.44), calls=%async_computation.2 | async-start | bytes 4194304 | tf_op jit(solution)/shard_map/all_to_all | solution.py:188
  214.2 14.3 %convolution_convert_fusion = bf16[512,2048]{1,0:T(8,128)(2,1)} fusion(bf16[1024,2048]{1,0:T(8,128)(2,1)} %param.29, bf16[512,2048]{1,0:T(8,128)(2,1)} %bitcast.163, bf16[2048,1024]{1,0:T(8,128)(2,1)} %param.28), kind=kOutput, calls=%fused_computation.22 | convolution fusion | flops 4330094592 | bytes 12582912 | tf_op jit(solution)/shard_map/dot_general | solution.py:198
  228.5 1.7 constant_dynamic-slice_fusion.3
  230.2 2.3 collective-permute-start.10
  233.6 31.9 %collective-permute-done.10 = bf16[2,4,2,8,2048]{4,3,1,0,2:T(8,128)(2,1)S(1)} collective-permute-done((bf16[2,4,2,8,2048]{4,3,1,0,2:T(8,128)(2,1)S(1)}, bf16[2,4,2,8,2048]{4,3,1,0,2:T(8,128)(2,1)S(1)}, u32[]{:S(2)}, u32[]{:S(2)}) %collective-permute-start.10) | collective-permute-done | bytes 524320 | tf_op jit(solution)/shard_map/ppermute | solution.py:58
  265.5 11.2 %collective-permute-done.9 = bf16[2,4,2,8,2048]{4,3,1,0,2:T(8,128)(2,1)S(1)} collective-permute-done((bf16[2,4,2,8,2048]{4,3,1,0,2:T(8,128)(2,1)S(1)}, bf16[2,4,2,8,2048]{4,3,1,0,2:T(8,128)(2,1)S(1)}, u32[]{:S(2)}, u32[]{:S(2)}) %collective-permute-start.9) | collective-permute-done | bytes 524320 | tf_op jit(solution)/shard_map/ppermute | solution.py:58
  277.3 3.5 %copy.72 = bf16[4,2,8,32,4,128]{5,3,2,4,1,0:T(8,128)(2,1)} copy(bf16[4,2,8,32,4,128]{5,3,4,1,2,0:T(8,128)(2,1)} %bitcast.7) | data formatting | bytes 4194304 | tf_op jit(solution)/shard_map/transpose | solution.py:89
  280.8 10.1 %collective-permute-done.11 = bf16[2,4,8,2048]{3,2,0,1:T(8,128)(2,1)S(1)} collective-permute-done((bf16[2,4,8,2048]{3,2,0,1:T(8,128)(2,1)S(1)}, bf16[2,4,8,2048]{3,2,0,1:T(8,128)(2,1)S(1)}, u32[]{:S(2)}, u32[]{:S(2)}) %collective-permute-start.11) | collective-permute-done | bytes 262176 | tf_op jit(solution)/shard_map/ppermute | solution.py:64
  292.9 2.2 copy.77
  295.9 5.0 %all-to-all-start.3 = ((bf16[2,4,8,2048]{3,2,0,1:T(8,128)(2,1)}), bf16[2,4,8,2048]{3,2,0,1:T(8,128)(2,1)S(1)}, u32[]{:S(2)}, u32[]{:S(2)}) async-start(bf16[2,4,8,2048]{3,2,0,1:T(8,128)(2,1)} %select_convert_fusion), calls=%async_computation.3 | async-start | bytes 524288 | tf_op jit(solution)/shard_map/all_to_all | solution.py:210
  300.9 7.9 %copy.84 = bf16[8,2,256,4,128]{4,3,2,1,0:T(4,128)(2,1)} copy(bf16[8,2,256,4,128]{4,2,3,1,0:T(8,128)(2,1)} %bitcast.152) | data formatting | bytes 8388608
  309.5 1.5 gather_fusion.8
  (133 shorter events, 24.5 us)
Async XLA Ops:
  7.2 95.7 %copy-start = (bf16[2048,4,192]{0,2,1:T(8,128)(2,1)S(1)}, bf16[2048,4,192]{0,2,1:T(8,128)(2,1)}, u32[]{:S(2)}) copy-start(bf16[2048,4,192]{0,2,1:T(8,128)(2,1)} %param.24) | copy-start | bytes 9437188
  7.2 91.9 %all-gather.2.cloned.1.call-start = ((), (), s32[]{:S(2)}) async-start(), calls=%async_computation.4 | async-start | bytes 2359296 | tf_op jit(solution)/shard_map/all_gather | solution.py:157
  34.4 6.2 %copy-start.16 = (s32[8]{0:T(128)S(1)}, s32[8]{0:T(128)}, u32[]{:S(2)}) copy-start(s32[8]{0:T(128)} %param.22) | copy-start | bytes 100
  34.4 6.3 %copy-start.2 = (s32[8]{0:T(128)S(1)}, s32[8]{0:T(128)}, u32[]{:S(2)}) copy-start(s32[8]{0:T(128)} %param.21) | copy-start | bytes 100
  34.4 7.0 %copy-start.3 = (s32[8]{0:T(128)S(1)}, s32[8]{0:T(128)}, u32[]{:S(2)}) copy-start(s32[8]{0:T(128)} %param.20) | copy-start | bytes 100
  34.4 7.6 %copy-start.14 = (bf16[2048]{0:T(1024)(128)(2,1)S(1)}, bf16[2048]{0:T(1024)(128)(2,1)}, u32[]{:S(2)}) copy-start(bf16[2048]{0:T(1024)(128)(2,1)} %param.23) | copy-start | bytes 12292
  34.4 72.7 %all-to-all-start.1 = ((bf16[32,2,32,4,128]{4,2,3,1,0:T(8,128)(2,1)}), bf16[32,2,32,4,128]{4,2,3,1,0:T(8,128)(2,1)}, u32[]{:S(2)}, u32[]{:S(2)}) async-start(bf16[32,2,32,4,128]{4,2,3,1,0:T(8,128)(2,1)} %bitcast.153), calls=%async_computation.1 | async-start | bytes 4194304 | tf_op jit(solution)/shard_map/all_to_all | solution.py:147
  99.0 2.2 copy-start.4
  104.7 0.9 copy-start.13
  105.6 2.8 copy-start.12
  105.6 2.8 copy-start.18
  110.3 2.4 copy-start.11
  112.7 2.0 copy-start.19
  114.7 2.4 copy-start.10
  118.9 26.1 %copy-start.8 = (bf16[2,4,2,1,8,2048]{5,4,3,2,1,0:T(8,128)(2,1)S(1)}, bf16[2,4,2,1,8,2048]{5,4,3,2,1,0:T(8,128)(2,1)}, u32[]{:S(2)}) copy-start(bf16[2,4,2,1,8,2048]{5,4,3,2,1,0:T(8,128)(2,1)} %get-tuple-element.33) | copy-start | bytes 1572868
  118.9 13.7 %collective-permute-start = (bf16[2,4,2,8,2048]{4,3,1,0,2:T(8,128)(2,1)S(1)}, bf16[2,4,2,8,2048]{4,3,1,0,2:T(8,128)(2,1)}, u32[]{:S(2)}, u32[]{:S(2)}) collective-permute-start(bf16[2,4,2,8,2048]{4,3,1,0,2:T(8,128)(2,1)S(1)} %bitcast.171), channel_id=1, source_target_pairs={{0,1},{1,2},{2,3},{3,0},{4,5},{5,6},{6,7},{7,4},{8,9},{9,10},{10,1... | collective-permute-start | bytes 1572872 | tf_op jit(solution)/shard_map/ppermute | solution.py:58
  120.1 13.5 %collective-permute-start.1 = (bf16[2,4,2,8,2048]{4,3,1,0,2:T(8,128)(2,1)S(1)}, bf16[2,4,2,8,2048]{4,3,1,0,2:T(8,128)(2,1)S(1)}, u32[]{:S(2)}, u32[]{:S(2)}) collective-permute-start(bf16[2,4,2,8,2048]{4,3,1,0,2:T(8,128)(2,1)S(1)} %bitcast.172), channel_id=1, source_target_pairs={{0,2},{1,3},{2,0},{3,1},{4,6},{5,7},{6,4},{7,5},{8,10},{9,11},{10,... | collective-permute-start | bytes 1572872 | tf_op jit(solution)/shard_map/ppermute | solution.py:58
  120.3 24.7 %collective-permute-start.2 = (bf16[2,4,2,8,2048]{4,3,1,0,2:T(8,128)(2,1)S(1)}, bf16[2,4,2,8,2048]{4,3,1,0,2:T(8,128)(2,1)S(1)}, u32[]{:S(2)}, u32[]{:S(2)}) collective-permute-start(bf16[2,4,2,8,2048]{4,3,1,0,2:T(8,128)(2,1)S(1)} %bitcast.173), channel_id=1, source_target_pairs={{0,3},{1,0},{2,1},{3,2},{4,7},{5,4},{6,5},{7,6},{8,11},{9,8},{10,9... | collective-permute-start | bytes 1572872 | tf_op jit(solution)/shard_map/ppermute | solution.py:58
  144.9 1.6 copy-start.15
  144.9 1.6 copy-start.17
  146.3 1.2 copy-start.6
  146.4 14.5 %collective-permute-start.3 = (bf16[2,4,8,2048]{3,2,0,1:T(8,128)(2,1)S(1)}, bf16[2,4,8,2048]{3,2,0,1:T(8,128)(2,1)S(1)}, u32[]{:S(2)}, u32[]{:S(2)}) collective-permute-start(bf16[2,4,8,2048]{3,2,0,1:T(8,128)(2,1)S(1)} %copy.70), channel_id=1, source_target_pairs={{0,4},{1,5},{2,6},{3,7},{4,0},{5,1},{6,2},{7,3},{8,12},{9,13},{10,... | collective-permute-start | bytes 786440 | tf_op jit(solution)/shard_map/ppermute | solution.py:64
  147.6 13.4 %copy-start.7 = (bf16[8,8,2048]{2,1,0:T(8,128)(2,1)S(1)}, bf16[8,8,2048]{2,1,0:T(8,128)(2,1)}, u32[]{:S(2)}) copy-start(bf16[8,8,2048]{2,1,0:T(8,128)(2,1)} %all_to_all.40) | copy-start | bytes 786436
  162.5 13.7 %collective-permute-start.4 = (bf16[2,4,8,2048]{3,2,0,1:T(8,128)(2,1)S(1)}, bf16[2,4,8,2048]{3,2,0,1:T(8,128)(2,1)S(1)}, u32[]{:S(2)}, u32[]{:S(2)}) collective-permute-start(bf16[2,4,8,2048]{3,2,0,1:T(8,128)(2,1)S(1)} %multiply_convert_fusion), channel_id=1, source_target_pairs={{0,4},{1,5},{2,6},{3,7},{4,0},{5,1},{6,2},{7,3},{8,12},{9,13},{10,... | collective-permute-start | bytes 786440 | tf_op jit(solution)/shard_map/ppermute | solution.py:76
  178.8 14.0 %collective-permute-start.5 = (bf16[2,2,4,8,2048]{4,3,1,2,0:T(8,128)(2,1)S(1)}, bf16[2,2,4,8,2048]{4,3,1,2,0:T(8,128)(2,1)S(1)}, u32[]{:S(2)}, u32[]{:S(2)}) collective-permute-start(bf16[2,2,4,8,2048]{4,3,1,2,0:T(8,128)(2,1)S(1)} %broadcast_select_fusion), channel_id=1, source_target_pairs={{0,1},{1,2},{2,3},{3,0},{4,5},{5,6},{6,7},{7,4},{8,9},{9,10},{10,1... | collective-permute-start | bytes 1572872 | tf_op jit(solution)/shard_map/ppermute | solution.py:81
  178.9 13.9 %collective-permute-start.6 = (bf16[2,2,4,8,2048]{4,3,1,2,0:T(8,128)(2,1)S(1)}, bf16[2,2,4,8,2048]{4,3,1,2,0:T(8,128)(2,1)S(1)}, u32[]{:S(2)}, u32[]{:S(2)}) collective-permute-start(bf16[2,2,4,8,2048]{4,3,1,2,0:T(8,128)(2,1)S(1)} %broadcast_select_fusion), channel_id=1, source_target_pairs={{0,2},{1,3},{2,0},{3,1},{4,6},{5,7},{6,4},{7,5},{8,10},{9,11},{10,... | collective-permute-start | bytes 1572872 | tf_op jit(solution)/shard_map/ppermute | solution.py:81
  178.9 25.9 %collective-permute-start.7 = (bf16[2,2,4,8,2048]{4,3,1,2,0:T(8,128)(2,1)S(1)}, bf16[2,2,4,8,2048]{4,3,1,2,0:T(8,128)(2,1)S(1)}, u32[]{:S(2)}, u32[]{:S(2)}) collective-permute-start(bf16[2,2,4,8,2048]{4,3,1,2,0:T(8,128)(2,1)S(1)} %broadcast_select_fusion), channel_id=1, source_target_pairs={{0,3},{1,0},{2,1},{3,2},{4,7},{5,4},{6,5},{7,6},{8,11},{9,8},{10,9... | collective-permute-start | bytes 1572872 | tf_op jit(solution)/shard_map/ppermute | solution.py:81
  210.5 80.4 %all-to-all-start.2 = ((bf16[32,2,32,4,128]{4,2,3,1,0:T(8,128)(2,1)}), bf16[32,2,32,4,128]{4,2,3,1,0:T(8,128)(2,1)S(1)}, u32[]{:S(2)}, u32[]{:S(2)}) async-start(bf16[32,2,32,4,128]{4,2,3,1,0:T(8,128)(2,1)} %bitcast.44), calls=%async_computation.2 | async-start | bytes 4194304 | tf_op jit(solution)/shard_map/all_to_all | solution.py:188
  230.2 35.3 %collective-permute-start.10 = (bf16[2,4,2,8,2048]{4,3,1,0,2:T(8,128)(2,1)S(1)}, bf16[2,4,2,8,2048]{4,3,1,0,2:T(8,128)(2,1)S(1)}, u32[]{:S(2)}, u32[]{:S(2)}) collective-permute-start(bf16[2,4,2,8,2048]{4,3,1,0,2:T(8,128)(2,1)S(1)} %bitcast.174), channel_id=1, source_target_pairs={{0,3},{1,0},{2,1},{3,2},{4,7},{5,4},{6,5},{7,6},{8,11},{9,8},{10,9... | collective-permute-start | bytes 1572872 | tf_op jit(solution)/shard_map/ppermute | solution.py:58
  232.6 33.0 %collective-permute-start.8 = (bf16[2,4,2,8,2048]{4,3,1,0,2:T(8,128)(2,1)S(1)}, bf16[2,4,2,8,2048]{4,3,1,0,2:T(8,128)(2,1)S(1)}, u32[]{:S(2)}, u32[]{:S(2)}) collective-permute-start(bf16[2,4,2,8,2048]{4,3,1,0,2:T(8,128)(2,1)S(1)} %bitcast.175), channel_id=1, source_target_pairs={{0,1},{1,2},{2,3},{3,0},{4,5},{5,6},{6,7},{7,4},{8,9},{9,10},{10,1... | collective-permute-start | bytes 1572872 | tf_op jit(solution)/shard_map/ppermute | solution.py:58
  232.9 43.8 %collective-permute-start.9 = (bf16[2,4,2,8,2048]{4,3,1,0,2:T(8,128)(2,1)S(1)}, bf16[2,4,2,8,2048]{4,3,1,0,2:T(8,128)(2,1)S(1)}, u32[]{:S(2)}, u32[]{:S(2)}) collective-permute-start(bf16[2,4,2,8,2048]{4,3,1,0,2:T(8,128)(2,1)S(1)} %bitcast.176), channel_id=1, source_target_pairs={{0,2},{1,3},{2,0},{3,1},{4,6},{5,7},{6,4},{7,5},{8,10},{9,11},{10,... | collective-permute-start | bytes 1572872 | tf_op jit(solution)/shard_map/ppermute | solution.py:58
  277.2 13.7 %collective-permute-start.11 = (bf16[2,4,8,2048]{3,2,0,1:T(8,128)(2,1)S(1)}, bf16[2,4,8,2048]{3,2,0,1:T(8,128)(2,1)S(1)}, u32[]{:S(2)}, u32[]{:S(2)}) collective-permute-start(bf16[2,4,8,2048]{3,2,0,1:T(8,128)(2,1)S(1)} %copy.82), channel_id=1, source_target_pairs={{0,4},{1,5},{2,6},{3,7},{4,0},{5,1},{6,2},{7,3},{8,12},{9,13},{10,... | collective-permute-start | bytes 786440 | tf_op jit(solution)/shard_map/ppermute | solution.py:64
  290.9 1.6 copy-start.5
  295.9 12.9 %all-to-all-start.3 = ((bf16[2,4,8,2048]{3,2,0,1:T(8,128)(2,1)}), bf16[2,4,8,2048]{3,2,0,1:T(8,128)(2,1)S(1)}, u32[]{:S(2)}, u32[]{:S(2)}) async-start(bf16[2,4,8,2048]{3,2,0,1:T(8,128)(2,1)} %select_convert_fusion), calls=%async_computation.3 | async-start | bytes 524288 | tf_op jit(solution)/shard_map/all_to_all | solution.py:210
  300.9 10.9 %copy-start.1 = (bf16[2048,4,192]{0,2,1:T(8,128)(2,1)S(1)}, bf16[2048,4,192]{0,2,1:T(8,128)(2,1)}, u32[]{:S(2)}) copy-start(bf16[2048,4,192]{0,2,1:T(8,128)(2,1)} %param.24) | copy-start | bytes 9437188
  308.8 0.7 copy-start.9
Sparse Core Ops, SparseCore 0:
  21.0 77.9 all-gather.1

commit v15 on v14

--- a/solution.py
+++ b/solution.py
@@ -82,6 +82,13 @@
     by_inner = jnp.take(jnp.stack(held), (inner_me - jnp.arange(inner_size)) % inner_size, axis=0)
     gathered = jnp.moveaxis(by_inner, (0, 1), (3, 2))
     return gathered.reshape(rows.shape[:2] + (head_count * rows.shape[2],) + rows.shape[3:])
+
+
+def assemble(chunks, req_count, head_count):
+    stacked = jnp.stack(chunks).reshape((len(chunks), req_count, head_count) + chunks[0].shape[1:])
+    ordered = stacked.transpose(1, 0, 3, 2, 4, 5, 6)
+    shape = ordered.shape
+    return ordered.reshape((shape[0] * shape[1], shape[2], shape[3] * shape[4]) + shape[5:])
 
 
 def land(incoming, req_count, head_count):
@@ -146,10 +153,10 @@
         if layer == 0:
             incoming = lax.all_to_all(outgoing, ("req", "head"), 0, 0, tiled=True)
             incoming, later_layers = lax.optimization_barrier((incoming, later_layers))
-            chunks.append(land(incoming, req_count, head_count))
+            chunks.append(incoming)
         else:
             deferred.append(outgoing)
-    current = chunks[0][0]
+    current = land(chunks[0][:head_count], 1, head_count)[0]
     dealt_acts = jnp.take(stretch_acts, req_order, axis=0)
     dealt_rows = lax.all_to_all(dealt_acts, "req", split_axis=0, concat_axis=1, tiled=True).reshape(
         group_size, req_count, stretch_rows, features
@@ -185,8 +192,8 @@
     normed_all = head_gather(normed_rows, head_count)
     deferred, normed_all = lax.optimization_barrier((deferred, normed_all))
     for outgoing in deferred:
-        chunks.append(land(lax.all_to_all(outgoing, ("req", "head"), 0, 0, tiled=True), req_count, head_count))
-    relaid = jnp.stack(chunks, axis=1).reshape((req_count * local_layers,) + chunks[0].shape[1:])
+        chunks.append(lax.all_to_all(outgoing, ("req", "head"), 0, 0, tiled=True))
+    relaid = assemble(chunks, req_count, head_count)
     inner = jax.nn.gelu(
         jnp.dot(
             normed_all.reshape(group_size * stretch_max, features),
@@ -199,7 +206,6 @@
         group_size, req_count, span_rows, features
     )
     mlp_rows = head_sum(partial_mlp, head_count, stretch_rows)
-    relaid, mlp_rows = lax.optimization_barrier((relaid, mlp_rows))
     row_number = (
         jnp.arange(req_count, dtype=jnp.int32)[:, None] * head_count + head_index
     ) * stretch_rows + jnp.arange(stretch_rows, dtype=jnp.int32)[None, :]

time: 320 us -> 342 us (1.069)
  waiting for transfers between devices: 173 us -> 204 us
  local copies, waits for them, and re-layouts: 50.1 us -> 38.9 us
  blocking collectives: 9.17 us -> 17.1 us
  starting transfers between devices: 23.2 us -> 17.7 us
    all_to_all x2 -> x1, waiting for transfers between devices: 0.01 us -> 47.1 us  [local(): chunks.append(lax.all_to_all(outgoing, ('req', 'head'), 0, 0, tiled=True))]
    ppermute x6, waiting for transfers between devices: 66.5 us -> 45.7 us  [head_sum(): lax.ppermute(sent, 'head', pairs).astype(jnp.float32)]
    all_to_all x0 -> x1, blocking collectives: none -> 7.93 us  [local(): lax.all_to_all(result, 'req', split_axis=1, concat_axis=0, tiled=True)]
    all_to_all x2 -> x1, starting transfers between devices: 8.62 us -> 4.41 us  [local(): chunks.append(lax.all_to_all(outgoing, ('req', 'head'), 0, 0, tiled=True))]
    ppermute x2, waiting for transfers between devices: 20.8 us -> 24.6 us  [head_sum(): total = total + lax.ppermute(sent, 'head', pairs).astype(jnp.float32)]
    unnamed x41 -> x37, local copies, waits for them, and re-layouts: 10.7 us -> 7.01 us
  transfers between devices with their start and end apart: 16 -> 15, of which waited for: 12 -> 13; matrix products, arithmetic and copies ran while one was open for 19% -> 10% of each run, Pallas kernels for 0% -> 0%
where the time goes in v15:
time: 342 us; the launch traced here: 340 us
  waiting for transfers between devices  204 us (60%)
  local copies, waits for them, and re-layouts  38.9 us (11%)
  other arithmetic  24.1 us (7%)
  matrix products  23.8 us (7%)
  starting transfers between devices  17.7 us (5%)
  blocking collectives  17.1 us (5%)
  between operations  14.8 us (4%)
    all_gather x1, waiting for transfers between devices, local(): gathered = lax.all_gather(dealt_rows, 'head', axis=2, tiled=True)  50.4 us
    all_to_all x1, waiting for transfers between devices, local(): chunks.append(lax.all_to_all(outgoing, ('req', 'head'), 0, 0, tiled=True))  47.1 us
    ppermute x6, waiting for transfers between devices, head_sum(): lax.ppermute(sent, 'head', pairs).astype(jnp.float32)  45.7 us
    ppermute x2, waiting for transfers between devices, head_sum(): total = total + lax.ppermute(sent, 'head', pairs).astype(jnp.float32)  24.6 us
    ppermute x3, waiting for transfers between devices, head_gather(): held.append(lax.ppermute(by_outer, 'head', pairs))  20.2 us
    ppermute x1, waiting for transfers between devices, head_gather(): held.append(lax.ppermute(rows, 'head', pairs))  14.3 us
    dot_general x1, matrix products, local(): jnp.dot(inner, down_weight, preferred_element_type=jnp.float32)  12.9 us
    all_to_all x1, blocking collectives, local(): lax.all_to_all(dealt_acts, 'req', split_axis=0, concat_axis=1, tiled=True)  9.17 us
  transfers between devices with their start and end apart: 15, of which 13 were waited for; matrix products, arithmetic and copies ran while one was open for 10% of the time, Pallas kernels for 0%

profile of v15, /device:TPU:1, one launch (start us, length us, event | category | flops | bytes accessed | tf_op | source)
XLA Modules:
  0.0 340.2 jit_solution(10780100981328044387)
XLA Ops:
  8.0 1.6 gather_fusion.4
  9.7 1.3 gather_fusion
  11.7 9.2 %all_to_all.40 = bf16[8,8,2048]{2,1,0:T(8,128)(2,1)} all-to-all(bf16[8,8,2048]{2,1,0:T(8,128)(2,1)S(1)} %broadcast_select_fusion.2), channel_id=1, replica_groups=mesh['req'=4,'head'=8] {'req'}, dimensions={0} | all-to-all | bytes 524288 | tf_op jit(solution)/shard_map/all_to_all | solution.py:161
  20.9 5.2 %fusion.135 = (bf16[1,8,32,32,128]{4,3,2,1,0:T(8,128)(2,1)}, bf16[8,32,32,128]{3,2,1,0:T(8,128)(2,1)}) fusion(bf16[2,8,32,32,128]{4,3,2,1,0:T(8,128)(2,1)} %param.19), kind=kLoop, calls=%fused_computation.250 | loop fusion | bytes 8388608 | tf_op jit(solution)/shard_map/slice | solution.py:140
  26.1 3.7 %gather_fusion.5 = bf16[8,32,32,128]{3,2,1,0:T(8,128)(2,1)} fusion(bf16[8,32,32,128]{3,2,1,0:T(8,128)(2,1)} %get-tuple-element.26, s32[1024]{0:T(1024)S(1)} %pad_clamp_fusion.3), kind=kCustom, calls=%fused_computation.2.clone | custom fusion | bytes 4194336 | tf_op jit(solution)/shard_map/jit(_take)/gather | solution.py:145
  29.9 1.8 select_select_fusion.1
  31.7 2.7 copy.77
  34.4 6.1 %all-to-all-start.1 = ((bf16[32,2,32,4,128]{4,2,3,1,0:T(8,128)(2,1)}), bf16[32,2,32,4,128]{4,2,3,1,0:T(8,128)(2,1)}, u32[]{:S(2)}, u32[]{:S(2)}) async-start(bf16[32,2,32,4,128]{4,2,3,1,0:T(8,128)(2,1)} %bitcast.154), calls=%async_computation.1 | async-start | bytes 4194304 | tf_op jit(solution)/shard_map/all_to_all | solution.py:154
  43.4 1.3 iota_compare_fusion.1
  48.6 50.4 %all-gather.2.cloned.1.call-done = bf16[2,4,64,2048]{3,2,0,1:T(8,128)(2,1)} async-done(((bf16[2,4,8,2048]{3,2,0,1:T(8,128)(2,1)}), bf16[2,4,64,2048]{3,2,0,1:T(8,128)(2,1)}) %all-gather.2.cloned.1.call-update) | async-done | bytes 2097168 | tf_op jit(solution)/shard_map/all_gather | solution.py:164
  99.0 2.1 convert_reduce_fusion
  102.8 1.8 fusion.19
  105.6 1.6 all-to-all-done.1
  107.1 1.1 slice_bitcast_fusion.1
  108.4 2.0 fusion.138
  110.4 2.2 convolution_convert_fusion.2
  112.8 2.0 fusion.139
  114.8 2.2 convolution_convert_fusion.3
  117.9 1.0 constant_dynamic-slice_fusion.7
  119.1 2.4 collective-permute-start.1
  121.7 10.1 %collective-permute-done.2 = bf16[2,4,2,8,2048]{4,3,1,0,2:T(8,128)(2,1)} collective-permute-done((bf16[2,4,2,8,2048]{4,3,1,0,2:T(8,128)(2,1)S(1)}, bf16[2,4,2,8,2048]{4,3,1,0,2:T(8,128)(2,1)}, u32[]{:S(2)}, u32[]{:S(2)}) %collective-permute-start.2) | collective-permute-done | bytes 524320 | tf_op jit(solution)/shard_map/ppermute | solution.py:58
  131.7 13.1 %collective-permute-done.1 = bf16[2,4,2,8,2048]{4,3,1,0,2:T(8,128)(2,1)S(1)} collective-permute-done((bf16[2,4,2,8,2048]{4,3,1,0,2:T(8,128)(2,1)S(1)}, bf16[2,4,2,8,2048]{4,3,1,0,2:T(8,128)(2,1)S(1)}, u32[]{:S(2)}, u32[]{:S(2)}) %collective-permute-start.1) | collective-permute-done | bytes 524320 | tf_op jit(solution)/shard_map/ppermute | solution.py:58
  144.8 1.4 fusion.26
  147.2 2.6 gather_fusion.7
  149.8 10.4 %collective-permute-done.3 = bf16[2,4,8,2048]{3,2,0,1:T(8,128)(2,1)S(1)} collective-permute-done((bf16[2,4,8,2048]{3,2,0,1:T(8,128)(2,1)S(1)}, bf16[2,4,8,2048]{3,2,0,1:T(8,128)(2,1)S(1)}, u32[]{:S(2)}, u32[]{:S(2)}) %collective-permute-start.3) | collective-permute-done | bytes 262176 | tf_op jit(solution)/shard_map/ppermute | solution.py:64
  160.1 1.2 fusion.133
  162.0 14.3 %collective-permute-done.4 = bf16[2,4,8,2048]{3,2,0,1:T(8,128)(2,1)S(1)} collective-permute-done((bf16[2,4,8,2048]{3,2,0,1:T(8,128)(2,1)S(1)}, bf16[2,4,8,2048]{3,2,0,1:T(8,128)(2,1)S(1)}, u32[]{:S(2)}, u32[]{:S(2)}) %collective-permute-start.4) | collective-permute-done | bytes 262176 | tf_op jit(solution)/shard_map/ppermute | solution.py:76
  177.1 1.6 gather_fusion.1
  178.9 1.1 collective-permute-start.6
  181.6 2.0 copy.90
  183.7 8.1 %collective-permute-done.7 = bf16[2,2,4,8,2048]{4,3,1,2,0:T(8,128)(2,1)S(1)} collective-permute-done((bf16[2,2,4,8,2048]{4,3,1,2,0:T(8,128)(2,1)S(1)}, bf16[2,2,4,8,2048]{4,3,1,2,0:T(8,128)(2,1)S(1)}, u32[]{:S(2)}, u32[]{:S(2)}) %collective-permute-start.7) | collective-permute-done | bytes 524320 | tf_op jit(solution)/shard_map/ppermute | solution.py:81
  191.9 11.0 %collective-permute-done.6 = bf16[2,2,4,8,2048]{4,3,1,2,0:T(8,128)(2,1)S(1)} collective-permute-done((bf16[2,2,4,8,2048]{4,3,1,2,0:T(8,128)(2,1)S(1)}, bf16[2,2,4,8,2048]{4,3,1,2,0:T(8,128)(2,1)S(1)}, u32[]{:S(2)}, u32[]{:S(2)}) %collective-permute-start.6) | collective-permute-done | bytes 524320 | tf_op jit(solution)/shard_map/ppermute | solution.py:81
  202.8 1.1 collective-permute-done.5
  204.2 2.0 gather_fusion.2
  206.2 1.9 select_bitcast_fusion
  208.1 1.6 copy.91
  209.7 12.9 %convolution_convert_fusion = bf16[512,2048]{1,0:T(8,128)(2,1)S(1)} fusion(bf16[1024,2048]{1,0:T(8,128)(2,1)} %param.29, bf16[512,2048]{1,0:T(8,128)(2,1)} %bitcast.162, bf16[2048,1024]{1,0:T(8,128)(2,1)} %param.28), kind=kOutput, calls=%fused_computation.22 | convolution fusion | flops 4330094592 | bytes 12582912 | tf_op jit(solution)/shard_map/dot_general | solution.py:205
  223.8 1.2 collective-permute-start.9
  225.2 9.5 %collective-permute-done.10 = bf16[2,4,2,8,2048]{4,3,1,0,2:T(8,128)(2,1)S(1)} collective-permute-done((bf16[2,4,2,8,2048]{4,3,1,0,2:T(8,128)(2,1)S(1)}, bf16[2,4,2,8,2048]{4,3,1,0,2:T(8,128)(2,1)S(1)}, u32[]{:S(2)}, u32[]{:S(2)}) %collective-permute-start.10) | collective-permute-done | bytes 524320 | tf_op jit(solution)/shard_map/ppermute | solution.py:58
  234.7 13.1 %collective-permute-done.9 = bf16[2,4,2,8,2048]{4,3,1,0,2:T(8,128)(2,1)S(1)} collective-permute-done((bf16[2,4,2,8,2048]{4,3,1,0,2:T(8,128)(2,1)S(1)}, bf16[2,4,2,8,2048]{4,3,1,0,2:T(8,128)(2,1)S(1)}, u32[]{:S(2)}, u32[]{:S(2)}) %collective-permute-start.9) | collective-permute-done | bytes 524320 | tf_op jit(solution)/shard_map/ppermute | solution.py:58
  248.7 14.2 %collective-permute-done.11 = bf16[2,4,8,2048]{3,2,0,1:T(8,128)(2,1)S(1)} collective-permute-done((bf16[2,4,8,2048]{3,2,0,1:T(8,128)(2,1)S(1)}, bf16[2,4,8,2048]{3,2,0,1:T(8,128)(2,1)S(1)}, u32[]{:S(2)}, u32[]{:S(2)}) %collective-permute-start.11) | collective-permute-done | bytes 262176 | tf_op jit(solution)/shard_map/ppermute | solution.py:64
  263.0 7.9 %all_to_all.41 = bf16[2,4,8,2048]{3,2,0,1:T(8,128)(2,1)S(1)} all-to-all(bf16[2,4,8,2048]{3,2,0,1:T(8,128)(2,1)S(1)} %fusion.59), channel_id=1, replica_groups=mesh['req'=4,'head'=8] {'req'}, dimensions={1} | all-to-all | bytes 524288 | tf_op jit(solution)/shard_map/all_to_all | solution.py:216
  270.9 4.4 %all-to-all-start.3 = ((bf16[32,2,32,4,128]{4,2,3,1,0:T(8,128)(2,1)}), bf16[32,2,32,4,128]{4,2,3,1,0:T(8,128)(2,1)S(1)}, u32[]{:S(2)}, u32[]{:S(2)}) async-start(bf16[32,2,32,4,128]{4,2,3,1,0:T(8,128)(2,1)} %bitcast.43), calls=%async_computation.3 | async-start | bytes 4194304 | tf_op jit(solution)/shard_map/all_to_all | solution.py:195
  275.4 1.0 sort.17
  277.7 47.1 %all-to-all-done.3 = bf16[32,2,32,4,128]{4,2,3,1,0:T(8,128)(2,1)S(1)} async-done(((bf16[32,2,32,4,128]{4,2,3,1,0:T(8,128)(2,1)}), bf16[32,2,32,4,128]{4,2,3,1,0:T(8,128)(2,1)S(1)}, u32[]{:S(2)}, u32[]{:S(2)}) %all-to-all-start.3) | async-done | bytes 2097184 | tf_op jit(solution)/shard_map/all_to_all | solution.py:195
  324.8 2.0 maximum_bitcast_fusion
  326.8 1.1 copy.98
  327.9 5.5 %copy.99 = bf16[8,2,256,4,128]{4,3,2,1,0:T(4,128)(2,1)} copy(bf16[8,2,256,4,128]{4,2,3,1,0:T(8,128)(2,1)S(1)} %bitcast.152) | data formatting | bytes 8388608
  (123 shorter events, 20.7 us)
Async XLA Ops:
  7.2 95.6 %copy-start = (bf16[2048,4,192]{0,2,1:T(8,128)(2,1)S(1)}, bf16[2048,4,192]{0,2,1:T(8,128)(2,1)}, u32[]{:S(2)}) copy-start(bf16[2048,4,192]{0,2,1:T(8,128)(2,1)} %param.24) | copy-start | bytes 9437188
  7.2 91.8 %all-gather.2.cloned.1.call-start = ((), (), s32[]{:S(2)}) async-start(), calls=%async_computation.4 | async-start | bytes 2359296 | tf_op jit(solution)/shard_map/all_gather | solution.py:164
  34.4 6.2 %copy-start.14 = (s32[8]{0:T(128)S(1)}, s32[8]{0:T(128)}, u32[]{:S(2)}) copy-start(s32[8]{0:T(128)} %param.22) | copy-start | bytes 100
  34.4 6.3 %copy-start.2 = (s32[8]{0:T(128)S(1)}, s32[8]{0:T(128)}, u32[]{:S(2)}) copy-start(s32[8]{0:T(128)} %param.21) | copy-start | bytes 100
  34.4 6.9 %copy-start.3 = (s32[8]{0:T(128)S(1)}, s32[8]{0:T(128)}, u32[]{:S(2)}) copy-start(s32[8]{0:T(128)} %param.20) | copy-start | bytes 100
  34.4 7.6 %copy-start.12 = (bf16[2048]{0:T(1024)(128)(2,1)S(1)}, bf16[2048]{0:T(1024)(128)(2,1)}, u32[]{:S(2)}) copy-start(bf16[2048]{0:T(1024)(128)(2,1)} %param.23) | copy-start | bytes 12292
  34.4 72.7 %all-to-all-start.1 = ((bf16[32,2,32,4,128]{4,2,3,1,0:T(8,128)(2,1)}), bf16[32,2,32,4,128]{4,2,3,1,0:T(8,128)(2,1)}, u32[]{:S(2)}, u32[]{:S(2)}) async-start(bf16[32,2,32,4,128]{4,2,3,1,0:T(8,128)(2,1)} %bitcast.154), calls=%async_computation.1 | async-start | bytes 4194304 | tf_op jit(solution)/shard_map/all_to_all | solution.py:154
  99.0 2.2 copy-start.4
  104.6 0.9 copy-start.11
  105.5 2.9 copy-start.10
  105.5 2.9 copy-start.16
  110.4 2.4 copy-start.9
  112.8 2.0 copy-start.17
  114.8 2.4 copy-start.8
  118.9 25.8 %copy-start.7 = (bf16[2,4,2,1,8,2048]{5,4,3,2,1,0:T(8,128)(2,1)S(1)}, bf16[2,4,2,1,8,2048]{5,4,3,2,1,0:T(8,128)(2,1)}, u32[]{:S(2)}) copy-start(bf16[2,4,2,1,8,2048]{5,4,3,2,1,0:T(8,128)(2,1)} %get-tuple-element.31) | copy-start | bytes 1572868
  119.0 12.7 %collective-permute-start.2 = (bf16[2,4,2,8,2048]{4,3,1,0,2:T(8,128)(2,1)S(1)}, bf16[2,4,2,8,2048]{4,3,1,0,2:T(8,128)(2,1)}, u32[]{:S(2)}, u32[]{:S(2)}) collective-permute-start(bf16[2,4,2,8,2048]{4,3,1,0,2:T(8,128)(2,1)S(1)} %bitcast.169), channel_id=1, source_target_pairs={{0,3},{1,0},{2,1},{3,2},{4,7},{5,4},{6,5},{7,6},{8,11},{9,8},{10,9... | collective-permute-start | bytes 1572872 | tf_op jit(solution)/shard_map/ppermute | solution.py:58
  119.1 25.7 %collective-permute-start.1 = (bf16[2,4,2,8,2048]{4,3,1,0,2:T(8,128)(2,1)S(1)}, bf16[2,4,2,8,2048]{4,3,1,0,2:T(8,128)(2,1)S(1)}, u32[]{:S(2)}, u32[]{:S(2)}) collective-permute-start(bf16[2,4,2,8,2048]{4,3,1,0,2:T(8,128)(2,1)S(1)} %bitcast.170), channel_id=1, source_target_pairs={{0,2},{1,3},{2,0},{3,1},{4,6},{5,7},{6,4},{7,5},{8,10},{9,11},{10,... | collective-permute-start | bytes 1572872 | tf_op jit(solution)/shard_map/ppermute | solution.py:58
  121.5 23.3 %collective-permute-start = (bf16[2,4,2,8,2048]{4,3,1,0,2:T(8,128)(2,1)S(1)}, bf16[2,4,2,8,2048]{4,3,1,0,2:T(8,128)(2,1)S(1)}, u32[]{:S(2)}, u32[]{:S(2)}) collective-permute-start(bf16[2,4,2,8,2048]{4,3,1,0,2:T(8,128)(2,1)S(1)} %bitcast.171), channel_id=1, source_target_pairs={{0,1},{1,2},{2,3},{3,0},{4,5},{5,6},{6,7},{7,4},{8,9},{9,10},{10,1... | collective-permute-start | bytes 1572872 | tf_op jit(solution)/shard_map/ppermute | solution.py:58
  144.8 1.9 copy-start.13
  146.2 1.0 copy-start.5
  146.2 13.9 %collective-permute-start.3 = (bf16[2,4,8,2048]{3,2,0,1:T(8,128)(2,1)S(1)}, bf16[2,4,8,2048]{3,2,0,1:T(8,128)(2,1)S(1)}, u32[]{:S(2)}, u32[]{:S(2)}) collective-permute-start(bf16[2,4,8,2048]{3,2,0,1:T(8,128)(2,1)S(1)} %copy.87), channel_id=1, source_target_pairs={{0,4},{1,5},{2,6},{3,7},{4,0},{5,1},{6,2},{7,3},{8,12},{9,13},{10,... | collective-permute-start | bytes 786440 | tf_op jit(solution)/shard_map/ppermute | solution.py:64
  147.2 13.0 %copy-start.6 = (bf16[8,8,2048]{2,1,0:T(8,128)(2,1)S(1)}, bf16[8,8,2048]{2,1,0:T(8,128)(2,1)}, u32[]{:S(2)}) copy-start(bf16[8,8,2048]{2,1,0:T(8,128)(2,1)} %all_to_all.40) | copy-start | bytes 786436
  161.7 14.5 %collective-permute-start.4 = (bf16[2,4,8,2048]{3,2,0,1:T(8,128)(2,1)S(1)}, bf16[2,4,8,2048]{3,2,0,1:T(8,128)(2,1)S(1)}, u32[]{:S(2)}, u32[]{:S(2)}) collective-permute-start(bf16[2,4,8,2048]{3,2,0,1:T(8,128)(2,1)S(1)} %multiply_convert_fusion), channel_id=1, source_target_pairs={{0,4},{1,5},{2,6},{3,7},{4,0},{5,1},{6,2},{7,3},{8,12},{9,13},{10,... | collective-permute-start | bytes 786440 | tf_op jit(solution)/shard_map/ppermute | solution.py:76
  178.8 13.1 %collective-permute-start.7 = (bf16[2,2,4,8,2048]{4,3,1,2,0:T(8,128)(2,1)S(1)}, bf16[2,2,4,8,2048]{4,3,1,2,0:T(8,128)(2,1)S(1)}, u32[]{:S(2)}, u32[]{:S(2)}) collective-permute-start(bf16[2,2,4,8,2048]{4,3,1,2,0:T(8,128)(2,1)S(1)} %broadcast_select_fusion), channel_id=1, source_target_pairs={{0,3},{1,0},{2,1},{3,2},{4,7},{5,4},{6,5},{7,6},{8,11},{9,8},{10,9... | collective-permute-start | bytes 1572872 | tf_op jit(solution)/shard_map/ppermute | solution.py:81
  178.9 23.9 %collective-permute-start.6 = (bf16[2,2,4,8,2048]{4,3,1,2,0:T(8,128)(2,1)S(1)}, bf16[2,2,4,8,2048]{4,3,1,2,0:T(8,128)(2,1)S(1)}, u32[]{:S(2)}, u32[]{:S(2)}) collective-permute-start(bf16[2,2,4,8,2048]{4,3,1,2,0:T(8,128)(2,1)S(1)} %broadcast_select_fusion), channel_id=1, source_target_pairs={{0,2},{1,3},{2,0},{3,1},{4,6},{5,7},{6,4},{7,5},{8,10},{9,11},{10,... | collective-permute-start | bytes 1572872 | tf_op jit(solution)/shard_map/ppermute | solution.py:81
  180.0 24.0 %collective-permute-start.5 = (bf16[2,2,4,8,2048]{4,3,1,2,0:T(8,128)(2,1)S(1)}, bf16[2,2,4,8,2048]{4,3,1,2,0:T(8,128)(2,1)S(1)}, u32[]{:S(2)}, u32[]{:S(2)}) collective-permute-start(bf16[2,2,4,8,2048]{4,3,1,2,0:T(8,128)(2,1)S(1)} %broadcast_select_fusion), channel_id=1, source_target_pairs={{0,1},{1,2},{2,3},{3,0},{4,5},{5,6},{6,7},{7,4},{8,9},{9,10},{10,1... | collective-permute-start | bytes 1572872 | tf_op jit(solution)/shard_map/ppermute | solution.py:81
  222.8 11.8 %collective-permute-start.10 = (bf16[2,4,2,8,2048]{4,3,1,0,2:T(8,128)(2,1)S(1)}, bf16[2,4,2,8,2048]{4,3,1,0,2:T(8,128)(2,1)S(1)}, u32[]{:S(2)}, u32[]{:S(2)}) collective-permute-start(bf16[2,4,2,8,2048]{4,3,1,0,2:T(8,128)(2,1)S(1)} %bitcast.172), channel_id=1, source_target_pairs={{0,3},{1,0},{2,1},{3,2},{4,7},{5,4},{6,5},{7,6},{8,11},{9,8},{10,9... | collective-permute-start | bytes 1572872 | tf_op jit(solution)/shard_map/ppermute | solution.py:58
  223.8 23.9 %collective-permute-start.9 = (bf16[2,4,2,8,2048]{4,3,1,0,2:T(8,128)(2,1)S(1)}, bf16[2,4,2,8,2048]{4,3,1,0,2:T(8,128)(2,1)S(1)}, u32[]{:S(2)}, u32[]{:S(2)}) collective-permute-start(bf16[2,4,2,8,2048]{4,3,1,0,2:T(8,128)(2,1)S(1)} %bitcast.173), channel_id=1, source_target_pairs={{0,2},{1,3},{2,0},{3,1},{4,6},{5,7},{6,4},{7,5},{8,10},{9,11},{10,... | collective-permute-start | bytes 1572872 | tf_op jit(solution)/shard_map/ppermute | solution.py:58
  225.1 22.6 %collective-permute-start.8 = (bf16[2,4,2,8,2048]{4,3,1,0,2:T(8,128)(2,1)S(1)}, bf16[2,4,2,8,2048]{4,3,1,0,2:T(8,128)(2,1)S(1)}, u32[]{:S(2)}, u32[]{:S(2)}) collective-permute-start(bf16[2,4,2,8,2048]{4,3,1,0,2:T(8,128)(2,1)S(1)} %bitcast.174), channel_id=1, source_target_pairs={{0,1},{1,2},{2,3},{3,0},{4,5},{5,6},{6,7},{7,4},{8,9},{9,10},{10,1... | collective-permute-start | bytes 1572872 | tf_op jit(solution)/shard_map/ppermute | solution.py:58
  248.1 14.8 %collective-permute-start.11 = (bf16[2,4,8,2048]{3,2,0,1:T(8,128)(2,1)S(1)}, bf16[2,4,8,2048]{3,2,0,1:T(8,128)(2,1)S(1)}, u32[]{:S(2)}, u32[]{:S(2)}) collective-permute-start(bf16[2,4,8,2048]{3,2,0,1:T(8,128)(2,1)S(1)} %copy.96), channel_id=1, source_target_pairs={{0,4},{1,5},{2,6},{3,7},{4,0},{5,1},{6,2},{7,3},{8,12},{9,13},{10,... | collective-permute-start | bytes 786440 | tf_op jit(solution)/shard_map/ppermute | solution.py:64
  270.9 4.4 %copy-start.15 = (s32[8]{0:T(128)S(1)}, s32[8]{0:T(128)}, u32[]{:S(2)}) copy-start(s32[8]{0:T(128)} %param.22) | copy-start | bytes 100
  270.9 53.9 %all-to-all-start.3 = ((bf16[32,2,32,4,128]{4,2,3,1,0:T(8,128)(2,1)}), bf16[32,2,32,4,128]{4,2,3,1,0:T(8,128)(2,1)S(1)}, u32[]{:S(2)}, u32[]{:S(2)}) async-start(bf16[32,2,32,4,128]{4,2,3,1,0:T(8,128)(2,1)} %bitcast.43), calls=%async_computation.3 | async-start | bytes 4194304 | tf_op jit(solution)/shard_map/all_to_all | solution.py:195
  327.9 5.5 %copy-start.1 = (bf16[2048,4,192]{0,2,1:T(8,128)(2,1)S(1)}, bf16[2048,4,192]{0,2,1:T(8,128)(2,1)}, u32[]{:S(2)}) copy-start(bf16[2048,4,192]{0,2,1:T(8,128)(2,1)} %param.24) | copy-start | bytes 9437188
Sparse Core Ops, SparseCore 0:
  21.0 77.9 all-gather.1

commit v16 on v15

--- a/solution.py
+++ b/solution.py
@@ -206,6 +206,7 @@
         group_size, req_count, span_rows, features
     )
     mlp_rows = head_sum(partial_mlp, head_count, stretch_rows)
+    relaid, mlp_rows = lax.optimization_barrier((relaid, mlp_rows))
     row_number = (
         jnp.arange(req_count, dtype=jnp.int32)[:, None] * head_count + head_index
     ) * stretch_rows + jnp.arange(stretch_rows, dtype=jnp.int32)[None, :]

time: 342 us -> 321 us (0.939)
  waiting for transfers between devices: 204 us -> 176 us
  blocking collectives: 17.1 us -> 9.17 us
  local copies, waits for them, and re-layouts: 38.9 us -> 46.1 us
  starting transfers between devices: 17.7 us -> 23.2 us
    all_to_all x1, waiting for transfers between devices: 47.1 us -> 0.01 us  [local(): chunks.append(lax.all_to_all(outgoing, ('req', 'head'), 0, 0, tiled=True))]
    ppermute x6, waiting for transfers between devices: 45.7 us -> 66.5 us  [head_sum(): lax.ppermute(sent, 'head', pairs).astype(jnp.float32)]
    all_to_all x1 -> x0, blocking collectives: 7.93 us -> none  [local(): lax.all_to_all(result, 'req', split_axis=1, concat_axis=0, tiled=True)]
    all_to_all x0 -> x1, starting transfers between devices: none -> 4.96 us  [local(): lax.all_to_all(result, 'req', split_axis=1, concat_axis=0, tiled=True)]
    unnamed x37 -> x39, local copies, waits for them, and re-layouts: 7.01 us -> 9.67 us
  transfers between devices with their start and end apart: 15 -> 16, of which waited for: 13 -> 12; matrix products, arithmetic and copies ran while one was open for 10% -> 18% of each run, Pallas kernels for 0% -> 0%
where the time goes in v16:
time: 321 us; the launch traced here: 320 us
  waiting for transfers between devices  176 us (55%)
  local copies, waits for them, and re-layouts  46.1 us (14%)
  matrix products  25.2 us (8%)
  other arithmetic  25 us (8%)
  starting transfers between devices  23.2 us (7%)
  between operations  14.8 us (5%)
  blocking collectives  9.17 us (3%)
    ppermute x6, waiting for transfers between devices, head_sum(): lax.ppermute(sent, 'head', pairs).astype(jnp.float32)  66.5 us
    all_gather x1, waiting for transfers between devices, local(): gathered = lax.all_gather(dealt_rows, 'head', axis=2, tiled=True)  50.2 us
    ppermute x2, waiting for transfers between devices, head_sum(): total = total + lax.ppermute(sent, 'head', pairs).astype(jnp.float32)  24.3 us
    ppermute x3, waiting for transfers between devices, head_gather(): held.append(lax.ppermute(by_outer, 'head', pairs))  20.2 us
    dot_general x1, matrix products, local(): jnp.dot(inner, down_weight, preferred_element_type=jnp.float32)  14.3 us
    ppermute x1, waiting for transfers between devices, head_gather(): held.append(lax.ppermute(rows, 'head', pairs))  13.5 us
    unnamed x39, local copies, waits for them, and re-layouts  9.67 us
    all_to_all x1, blocking collectives, local(): lax.all_to_all(dealt_acts, 'req', split_axis=0, concat_axis=1, tiled=True)  9.17 us
  transfers between devices with their start and end apart: 16, of which 12 were waited for; matrix products, arithmetic and copies ran while one was open for 18% of the time, Pallas kernels for 0%

profile of v16, /device:TPU:1, one launch (start us, length us, event | category | flops | bytes accessed | tf_op | source)
XLA Modules:
  0.0 319.7 jit_solution(8028452332238456965)
XLA Ops:
  8.0 1.4 gather_fusion
  10.1 1.5 gather_fusion.4
  11.7 9.2 %all_to_all.40 = bf16[8,8,2048]{2,1,0:T(8,128)(2,1)} all-to-all(bf16[8,8,2048]{2,1,0:T(8,128)(2,1)S(1)} %broadcast_select_fusion.2), channel_id=1, replica_groups=mesh['req'=4,'head'=8] {'req'}, dimensions={0} | all-to-all | bytes 524288 | tf_op jit(solution)/shard_map/all_to_all | solution.py:161
  20.9 5.2 %fusion.132 = (bf16[1,8,32,32,128]{4,3,2,1,0:T(8,128)(2,1)}, bf16[8,32,32,128]{3,2,1,0:T(8,128)(2,1)}) fusion(bf16[2,8,32,32,128]{4,3,2,1,0:T(8,128)(2,1)} %param.19), kind=kLoop, calls=%fused_computation.248 | loop fusion | bytes 8388608 | tf_op jit(solution)/shard_map/slice | solution.py:140
  26.1 3.7 %gather_fusion.5 = bf16[8,32,32,128]{3,2,1,0:T(8,128)(2,1)} fusion(bf16[8,32,32,128]{3,2,1,0:T(8,128)(2,1)} %get-tuple-element.30, s32[1024]{0:T(1024)S(1)} %pad_clamp_fusion.3), kind=kCustom, calls=%fused_computation.2.clone | custom fusion | bytes 4194336 | tf_op jit(solution)/shard_map/jit(_take)/gather | solution.py:145
  29.9 1.8 select_select_fusion.1
  31.7 2.7 copy.77
  34.4 6.1 %all-to-all-start.1 = ((bf16[32,2,32,4,128]{4,2,3,1,0:T(8,128)(2,1)}), bf16[32,2,32,4,128]{4,2,3,1,0:T(8,128)(2,1)}, u32[]{:S(2)}, u32[]{:S(2)}) async-start(bf16[32,2,32,4,128]{4,2,3,1,0:T(8,128)(2,1)} %bitcast.154), calls=%async_computation.1 | async-start | bytes 4194304 | tf_op jit(solution)/shard_map/all_to_all | solution.py:154
  43.4 1.3 iota_compare_fusion.1
  48.8 50.2 %all-gather.2.cloned.1.call-done = bf16[2,4,64,2048]{3,2,0,1:T(8,128)(2,1)} async-done(((bf16[2,4,8,2048]{3,2,0,1:T(8,128)(2,1)}), bf16[2,4,64,2048]{3,2,0,1:T(8,128)(2,1)}) %all-gather.2.cloned.1.call-update) | async-done | bytes 2097168 | tf_op jit(solution)/shard_map/all_gather | solution.py:164
  99.0 2.1 convert_reduce_fusion
  102.8 1.8 fusion.19
  105.6 1.6 all-to-all-done.1
  107.1 1.1 slice_bitcast_fusion.1
  108.4 2.0 fusion.136
  110.4 2.2 convolution_convert_fusion.3
  112.8 2.0 fusion.135
  114.8 2.2 convolution_convert_fusion.2
  117.9 1.0 constant_dynamic-slice_fusion.7
  119.0 1.2 collective-permute-start
  120.3 1.3 collective-permute-start.2
  121.7 11.0 %collective-permute-done = bf16[2,4,2,8,2048]{4,3,1,0,2:T(8,128)(2,1)} collective-permute-done((bf16[2,4,2,8,2048]{4,3,1,0,2:T(8,128)(2,1)S(1)}, bf16[2,4,2,8,2048]{4,3,1,0,2:T(8,128)(2,1)}, u32[]{:S(2)}, u32[]{:S(2)}) %collective-permute-start) | collective-permute-done | bytes 524320 | tf_op jit(solution)/shard_map/ppermute | solution.py:58
  133.7 11.3 %collective-permute-done.2 = bf16[2,4,2,8,2048]{4,3,1,0,2:T(8,128)(2,1)S(1)} collective-permute-done((bf16[2,4,2,8,2048]{4,3,1,0,2:T(8,128)(2,1)S(1)}, bf16[2,4,2,8,2048]{4,3,1,0,2:T(8,128)(2,1)S(1)}, u32[]{:S(2)}, u32[]{:S(2)}) %collective-permute-start.2) | collective-permute-done | bytes 524320 | tf_op jit(solution)/shard_map/ppermute | solution.py:58
  145.0 1.4 fusion.26
  147.6 2.6 gather_fusion.7
  150.2 10.8 %collective-permute-done.3 = bf16[2,4,8,2048]{3,2,0,1:T(8,128)(2,1)S(1)} collective-permute-done((bf16[2,4,8,2048]{3,2,0,1:T(8,128)(2,1)S(1)}, bf16[2,4,8,2048]{3,2,0,1:T(8,128)(2,1)S(1)}, u32[]{:S(2)}, u32[]{:S(2)}) %collective-permute-start.3) | collective-permute-done | bytes 262176 | tf_op jit(solution)/shard_map/ppermute | solution.py:64
  161.0 1.2 fusion.130
  162.8 13.5 %collective-permute-done.4 = bf16[2,4,8,2048]{3,2,0,1:T(8,128)(2,1)S(1)} collective-permute-done((bf16[2,4,8,2048]{3,2,0,1:T(8,128)(2,1)S(1)}, bf16[2,4,8,2048]{3,2,0,1:T(8,128)(2,1)S(1)}, u32[]{:S(2)}, u32[]{:S(2)}) %collective-permute-start.4) | collective-permute-done | bytes 262176 | tf_op jit(solution)/shard_map/ppermute | solution.py:76
  177.1 1.6 gather_fusion.1
  179.0 2.3 collective-permute-start.7
  182.5 2.0 copy.90
  184.6 8.2 %collective-permute-done.5 = bf16[2,2,4,8,2048]{4,3,1,2,0:T(8,128)(2,1)S(1)} collective-permute-done((bf16[2,2,4,8,2048]{4,3,1,2,0:T(8,128)(2,1)S(1)}, bf16[2,2,4,8,2048]{4,3,1,2,0:T(8,128)(2,1)S(1)}, u32[]{:S(2)}, u32[]{:S(2)}) %collective-permute-start.5) | collective-permute-done | bytes 524320 | tf_op jit(solution)/shard_map/ppermute | solution.py:81
  192.8 12.0 %collective-permute-done.7 = bf16[2,2,4,8,2048]{4,3,1,2,0:T(8,128)(2,1)S(1)} collective-permute-done((bf16[2,2,4,8,2048]{4,3,1,2,0:T(8,128)(2,1)S(1)}, bf16[2,2,4,8,2048]{4,3,1,2,0:T(8,128)(2,1)S(1)}, u32[]{:S(2)}, u32[]{:S(2)}) %collective-permute-start.7) | collective-permute-done | bytes 524320 | tf_op jit(solution)/shard_map/ppermute | solution.py:81
  205.1 2.0 gather_fusion.2
  207.1 1.9 select_bitcast_fusion
  209.0 1.6 copy.91
  210.6 3.7 %all-to-all-start.2 = ((bf16[32,2,32,4,128]{4,2,3,1,0:T(8,128)(2,1)}), bf16[32,2,32,4,128]{4,2,3,1,0:T(8,128)(2,1)S(1)}, u32[]{:S(2)}, u32[]{:S(2)}) async-start(bf16[32,2,32,4,128]{4,2,3,1,0:T(8,128)(2,1)} %bitcast.44), calls=%async_computation.2 | async-start | bytes 4194304 | tf_op jit(solution)/shard_map/all_to_all | solution.py:195
  214.2 14.3 %convolution_convert_fusion = bf16[512,2048]{1,0:T(8,128)(2,1)} fusion(bf16[1024,2048]{1,0:T(8,128)(2,1)} %param.29, bf16[512,2048]{1,0:T(8,128)(2,1)} %bitcast.161, bf16[2048,1024]{1,0:T(8,128)(2,1)} %param.28), kind=kOutput, calls=%fused_computation.22 | convolution fusion | flops 4330094592 | bytes 12582912 | tf_op jit(solution)/shard_map/dot_general | solution.py:205
  228.5 1.7 constant_dynamic-slice_fusion.3
  230.2 2.3 collective-permute-start.10
  233.7 31.9 %collective-permute-done.10 = bf16[2,4,2,8,2048]{4,3,1,0,2:T(8,128)(2,1)S(1)} collective-permute-done((bf16[2,4,2,8,2048]{4,3,1,0,2:T(8,128)(2,1)S(1)}, bf16[2,4,2,8,2048]{4,3,1,0,2:T(8,128)(2,1)S(1)}, u32[]{:S(2)}, u32[]{:S(2)}) %collective-permute-start.10) | collective-permute-done | bytes 524320 | tf_op jit(solution)/shard_map/ppermute | solution.py:58
  265.6 11.2 %collective-permute-done.9 = bf16[2,4,2,8,2048]{4,3,1,0,2:T(8,128)(2,1)S(1)} collective-permute-done((bf16[2,4,2,8,2048]{4,3,1,0,2:T(8,128)(2,1)S(1)}, bf16[2,4,2,8,2048]{4,3,1,0,2:T(8,128)(2,1)S(1)}, u32[]{:S(2)}, u32[]{:S(2)}) %collective-permute-start.9) | collective-permute-done | bytes 524320 | tf_op jit(solution)/shard_map/ppermute | solution.py:58
  277.4 13.6 %collective-permute-done.11 = bf16[2,4,8,2048]{3,2,0,1:T(8,128)(2,1)S(1)} collective-permute-done((bf16[2,4,8,2048]{3,2,0,1:T(8,128)(2,1)S(1)}, bf16[2,4,8,2048]{3,2,0,1:T(8,128)(2,1)S(1)}, u32[]{:S(2)}, u32[]{:S(2)}) %collective-permute-start.11) | collective-permute-done | bytes 262176 | tf_op jit(solution)/shard_map/ppermute | solution.py:64
  291.0 2.0 maximum_bitcast_fusion
  293.0 3.2 copy.92
  296.9 5.0 %all-to-all-start.3 = ((bf16[2,4,8,2048]{3,2,0,1:T(8,128)(2,1)}), bf16[2,4,8,2048]{3,2,0,1:T(8,128)(2,1)S(1)}, u32[]{:S(2)}, u32[]{:S(2)}) async-start(bf16[2,4,8,2048]{3,2,0,1:T(8,128)(2,1)} %select_convert_fusion), calls=%async_computation.3 | async-start | bytes 524288 | tf_op jit(solution)/shard_map/all_to_all | solution.py:217
  301.9 7.9 %copy.99 = bf16[8,2,256,4,128]{4,3,2,1,0:T(4,128)(2,1)} copy(bf16[8,2,256,4,128]{4,2,3,1,0:T(8,128)(2,1)} %bitcast.152) | data formatting | bytes 8388608
  310.5 1.5 gather_fusion.8
  (127 shorter events, 22.0 us)
Async XLA Ops:
  7.2 95.6 %copy-start = (bf16[2048,4,192]{0,2,1:T(8,128)(2,1)S(1)}, bf16[2048,4,192]{0,2,1:T(8,128)(2,1)}, u32[]{:S(2)}) copy-start(bf16[2048,4,192]{0,2,1:T(8,128)(2,1)} %param.24) | copy-start | bytes 9437188
  7.2 91.8 %all-gather.2.cloned.1.call-start = ((), (), s32[]{:S(2)}) async-start(), calls=%async_computation.4 | async-start | bytes 2359296 | tf_op jit(solution)/shard_map/all_gather | solution.py:164
  34.4 6.2 %copy-start.15 = (s32[8]{0:T(128)S(1)}, s32[8]{0:T(128)}, u32[]{:S(2)}) copy-start(s32[8]{0:T(128)} %param.22) | copy-start | bytes 100
  34.4 6.3 %copy-start.2 = (s32[8]{0:T(128)S(1)}, s32[8]{0:T(128)}, u32[]{:S(2)}) copy-start(s32[8]{0:T(128)} %param.21) | copy-start | bytes 100
  34.4 6.9 %copy-start.3 = (s32[8]{0:T(128)S(1)}, s32[8]{0:T(128)}, u32[]{:S(2)}) copy-start(s32[8]{0:T(128)} %param.20) | copy-start | bytes 100
  34.4 7.6 %copy-start.13 = (bf16[2048]{0:T(1024)(128)(2,1)S(1)}, bf16[2048]{0:T(1024)(128)(2,1)}, u32[]{:S(2)}) copy-start(bf16[2048]{0:T(1024)(128)(2,1)} %param.23) | copy-start | bytes 12292
  34.4 72.7 %all-to-all-start.1 = ((bf16[32,2,32,4,128]{4,2,3,1,0:T(8,128)(2,1)}), bf16[32,2,32,4,128]{4,2,3,1,0:T(8,128)(2,1)}, u32[]{:S(2)}, u32[]{:S(2)}) async-start(bf16[32,2,32,4,128]{4,2,3,1,0:T(8,128)(2,1)} %bitcast.154), calls=%async_computation.1 | async-start | bytes 4194304 | tf_op jit(solution)/shard_map/all_to_all | solution.py:154
  99.0 2.2 copy-start.4
  104.6 0.9 copy-start.12
  105.5 2.9 copy-start.11
  105.5 2.9 copy-start.17
  110.4 2.4 copy-start.10
  112.8 2.0 copy-start.18
  114.7 2.4 copy-start.9
  118.9 26.1 %copy-start.7 = (bf16[2,4,2,1,8,2048]{5,4,3,2,1,0:T(8,128)(2,1)S(1)}, bf16[2,4,2,1,8,2048]{5,4,3,2,1,0:T(8,128)(2,1)}, u32[]{:S(2)}) copy-start(bf16[2,4,2,1,8,2048]{5,4,3,2,1,0:T(8,128)(2,1)} %get-tuple-element.35) | copy-start | bytes 1572868
  119.0 13.7 %collective-permute-start = (bf16[2,4,2,8,2048]{4,3,1,0,2:T(8,128)(2,1)S(1)}, bf16[2,4,2,8,2048]{4,3,1,0,2:T(8,128)(2,1)}, u32[]{:S(2)}, u32[]{:S(2)}) collective-permute-start(bf16[2,4,2,8,2048]{4,3,1,0,2:T(8,128)(2,1)S(1)} %bitcast.169), channel_id=1, source_target_pairs={{0,1},{1,2},{2,3},{3,0},{4,5},{5,6},{6,7},{7,4},{8,9},{9,10},{10,1... | collective-permute-start | bytes 1572872 | tf_op jit(solution)/shard_map/ppermute | solution.py:58
  120.2 13.5 %collective-permute-start.1 = (bf16[2,4,2,8,2048]{4,3,1,0,2:T(8,128)(2,1)S(1)}, bf16[2,4,2,8,2048]{4,3,1,0,2:T(8,128)(2,1)S(1)}, u32[]{:S(2)}, u32[]{:S(2)}) collective-permute-start(bf16[2,4,2,8,2048]{4,3,1,0,2:T(8,128)(2,1)S(1)} %bitcast.170), channel_id=1, source_target_pairs={{0,2},{1,3},{2,0},{3,1},{4,6},{5,7},{6,4},{7,5},{8,10},{9,11},{10,... | collective-permute-start | bytes 1572872 | tf_op jit(solution)/shard_map/ppermute | solution.py:58
  120.3 24.7 %collective-permute-start.2 = (bf16[2,4,2,8,2048]{4,3,1,0,2:T(8,128)(2,1)S(1)}, bf16[2,4,2,8,2048]{4,3,1,0,2:T(8,128)(2,1)S(1)}, u32[]{:S(2)}, u32[]{:S(2)}) collective-permute-start(bf16[2,4,2,8,2048]{4,3,1,0,2:T(8,128)(2,1)S(1)} %bitcast.171), channel_id=1, source_target_pairs={{0,3},{1,0},{2,1},{3,2},{4,7},{5,4},{6,5},{7,6},{8,11},{9,8},{10,9... | collective-permute-start | bytes 1572872 | tf_op jit(solution)/shard_map/ppermute | solution.py:58
  145.0 1.6 copy-start.14
  145.0 1.6 copy-start.16
  146.4 1.2 copy-start.5
  146.5 14.5 %collective-permute-start.3 = (bf16[2,4,8,2048]{3,2,0,1:T(8,128)(2,1)S(1)}, bf16[2,4,8,2048]{3,2,0,1:T(8,128)(2,1)S(1)}, u32[]{:S(2)}, u32[]{:S(2)}) collective-permute-start(bf16[2,4,8,2048]{3,2,0,1:T(8,128)(2,1)S(1)} %copy.87), channel_id=1, source_target_pairs={{0,4},{1,5},{2,6},{3,7},{4,0},{5,1},{6,2},{7,3},{8,12},{9,13},{10,... | collective-permute-start | bytes 786440 | tf_op jit(solution)/shard_map/ppermute | solution.py:64
  147.6 13.4 %copy-start.6 = (bf16[8,8,2048]{2,1,0:T(8,128)(2,1)S(1)}, bf16[8,8,2048]{2,1,0:T(8,128)(2,1)}, u32[]{:S(2)}) copy-start(bf16[8,8,2048]{2,1,0:T(8,128)(2,1)} %all_to_all.40) | copy-start | bytes 786436
  162.6 13.7 %collective-permute-start.4 = (bf16[2,4,8,2048]{3,2,0,1:T(8,128)(2,1)S(1)}, bf16[2,4,8,2048]{3,2,0,1:T(8,128)(2,1)S(1)}, u32[]{:S(2)}, u32[]{:S(2)}) collective-permute-start(bf16[2,4,8,2048]{3,2,0,1:T(8,128)(2,1)S(1)} %multiply_convert_fusion), channel_id=1, source_target_pairs={{0,4},{1,5},{2,6},{3,7},{4,0},{5,1},{6,2},{7,3},{8,12},{9,13},{10,... | collective-permute-start | bytes 786440 | tf_op jit(solution)/shard_map/ppermute | solution.py:76
  178.8 14.0 %collective-permute-start.5 = (bf16[2,2,4,8,2048]{4,3,1,2,0:T(8,128)(2,1)S(1)}, bf16[2,2,4,8,2048]{4,3,1,2,0:T(8,128)(2,1)S(1)}, u32[]{:S(2)}, u32[]{:S(2)}) collective-permute-start(bf16[2,2,4,8,2048]{4,3,1,2,0:T(8,128)(2,1)S(1)} %broadcast_select_fusion), channel_id=1, source_target_pairs={{0,1},{1,2},{2,3},{3,0},{4,5},{5,6},{6,7},{7,4},{8,9},{9,10},{10,1... | collective-permute-start | bytes 1572872 | tf_op jit(solution)/shard_map/ppermute | solution.py:81
  178.9 13.9 %collective-permute-start.6 = (bf16[2,2,4,8,2048]{4,3,1,2,0:T(8,128)(2,1)S(1)}, bf16[2,2,4,8,2048]{4,3,1,2,0:T(8,128)(2,1)S(1)}, u32[]{:S(2)}, u32[]{:S(2)}) collective-permute-start(bf16[2,2,4,8,2048]{4,3,1,2,0:T(8,128)(2,1)S(1)} %broadcast_select_fusion), channel_id=1, source_target_pairs={{0,2},{1,3},{2,0},{3,1},{4,6},{5,7},{6,4},{7,5},{8,10},{9,11},{10,... | collective-permute-start | bytes 1572872 | tf_op jit(solution)/shard_map/ppermute | solution.py:81
  179.0 25.9 %collective-permute-start.7 = (bf16[2,2,4,8,2048]{4,3,1,2,0:T(8,128)(2,1)S(1)}, bf16[2,2,4,8,2048]{4,3,1,2,0:T(8,128)(2,1)S(1)}, u32[]{:S(2)}, u32[]{:S(2)}) collective-permute-start(bf16[2,2,4,8,2048]{4,3,1,2,0:T(8,128)(2,1)S(1)} %broadcast_select_fusion), channel_id=1, source_target_pairs={{0,3},{1,0},{2,1},{3,2},{4,7},{5,4},{6,5},{7,6},{8,11},{9,8},{10,9... | collective-permute-start | bytes 1572872 | tf_op jit(solution)/shard_map/ppermute | solution.py:81
  210.6 80.4 %all-to-all-start.2 = ((bf16[32,2,32,4,128]{4,2,3,1,0:T(8,128)(2,1)}), bf16[32,2,32,4,128]{4,2,3,1,0:T(8,128)(2,1)S(1)}, u32[]{:S(2)}, u32[]{:S(2)}) async-start(bf16[32,2,32,4,128]{4,2,3,1,0:T(8,128)(2,1)} %bitcast.44), calls=%async_computation.2 | async-start | bytes 4194304 | tf_op jit(solution)/shard_map/all_to_all | solution.py:195
  230.2 35.3 %collective-permute-start.10 = (bf16[2,4,2,8,2048]{4,3,1,0,2:T(8,128)(2,1)S(1)}, bf16[2,4,2,8,2048]{4,3,1,0,2:T(8,128)(2,1)S(1)}, u32[]{:S(2)}, u32[]{:S(2)}) collective-permute-start(bf16[2,4,2,8,2048]{4,3,1,0,2:T(8,128)(2,1)S(1)} %bitcast.172), channel_id=1, source_target_pairs={{0,3},{1,0},{2,1},{3,2},{4,7},{5,4},{6,5},{7,6},{8,11},{9,8},{10,9... | collective-permute-start | bytes 1572872 | tf_op jit(solution)/shard_map/ppermute | solution.py:58
  232.6 33.0 %collective-permute-start.8 = (bf16[2,4,2,8,2048]{4,3,1,0,2:T(8,128)(2,1)S(1)}, bf16[2,4,2,8,2048]{4,3,1,0,2:T(8,128)(2,1)S(1)}, u32[]{:S(2)}, u32[]{:S(2)}) collective-permute-start(bf16[2,4,2,8,2048]{4,3,1,0,2:T(8,128)(2,1)S(1)} %bitcast.173), channel_id=1, source_target_pairs={{0,1},{1,2},{2,3},{3,0},{4,5},{5,6},{6,7},{7,4},{8,9},{9,10},{10,1... | collective-permute-start | bytes 1572872 | tf_op jit(solution)/shard_map/ppermute | solution.py:58
  233.0 43.8 %collective-permute-start.9 = (bf16[2,4,2,8,2048]{4,3,1,0,2:T(8,128)(2,1)S(1)}, bf16[2,4,2,8,2048]{4,3,1,0,2:T(8,128)(2,1)S(1)}, u32[]{:S(2)}, u32[]{:S(2)}) collective-permute-start(bf16[2,4,2,8,2048]{4,3,1,0,2:T(8,128)(2,1)S(1)} %bitcast.174), channel_id=1, source_target_pairs={{0,2},{1,3},{2,0},{3,1},{4,6},{5,7},{6,4},{7,5},{8,10},{9,11},{10,... | collective-permute-start | bytes 1572872 | tf_op jit(solution)/shard_map/ppermute | solution.py:58
  277.2 13.7 %collective-permute-start.11 = (bf16[2,4,8,2048]{3,2,0,1:T(8,128)(2,1)S(1)}, bf16[2,4,8,2048]{3,2,0,1:T(8,128)(2,1)S(1)}, u32[]{:S(2)}, u32[]{:S(2)}) collective-permute-start(bf16[2,4,8,2048]{3,2,0,1:T(8,128)(2,1)S(1)} %copy.97), channel_id=1, source_target_pairs={{0,4},{1,5},{2,6},{3,7},{4,0},{5,1},{6,2},{7,3},{8,12},{9,13},{10,... | collective-permute-start | bytes 786440 | tf_op jit(solution)/shard_map/ppermute | solution.py:64
  296.9 12.9 %all-to-all-start.3 = ((bf16[2,4,8,2048]{3,2,0,1:T(8,128)(2,1)}), bf16[2,4,8,2048]{3,2,0,1:T(8,128)(2,1)S(1)}, u32[]{:S(2)}, u32[]{:S(2)}) async-start(bf16[2,4,8,2048]{3,2,0,1:T(8,128)(2,1)} %select_convert_fusion), calls=%async_computation.3 | async-start | bytes 524288 | tf_op jit(solution)/shard_map/all_to_all | solution.py:217
  301.9 10.9 %copy-start.1 = (bf16[2048,4,192]{0,2,1:T(8,128)(2,1)S(1)}, bf16[2048,4,192]{0,2,1:T(8,128)(2,1)}, u32[]{:S(2)}) copy-start(bf16[2048,4,192]{0,2,1:T(8,128)(2,1)} %param.24) | copy-start | bytes 9437188
  309.8 0.7 copy-start.8
Sparse Core Ops, SparseCore 0:
  21.0 77.9 all-gather.1

commit v17 on v14

--- a/solution.py
+++ b/solution.py
@@ -88,6 +88,17 @@
     shape = (req_count, head_count) + incoming.shape[1:]
     landed = incoming.reshape(shape).transpose(0, 2, 1, 3, 4, 5)
     return landed.reshape(landed.shape[:2] + (-1,) + landed.shape[4:])
+
+
+def req_exchange(dealt_acts, req_count):
+    me = lax.axis_index("req")
+    blocks = dealt_acts.reshape((req_count, -1) + dealt_acts.shape[1:])
+    held = [lax.dynamic_index_in_dim(blocks, me, 0, False)]
+    for shift in range(1, req_count):
+        pairs = [(a, (a + shift) % req_count) for a in range(req_count)]
+        held.append(lax.ppermute(lax.dynamic_index_in_dim(blocks, (me + shift) % req_count, 0, False), "req", pairs))
+    ordered = jnp.take(jnp.stack(held), (me - jnp.arange(req_count)) % req_count, axis=0)
+    return ordered.transpose(1, 0, 2, 3)
 
 
 def local(
@@ -151,9 +162,7 @@
             deferred.append(outgoing)
     current = chunks[0][0]
     dealt_acts = jnp.take(stretch_acts, req_order, axis=0)
-    dealt_rows = lax.all_to_all(dealt_acts, "req", split_axis=0, concat_axis=1, tiled=True).reshape(
-        group_size, req_count, stretch_rows, features
-    )
+    dealt_rows = req_exchange(dealt_acts, req_count)
     gathered = lax.all_gather(dealt_rows, "head", axis=2, tiled=True)
     normed = (
         layer_norm(gathered.astype(jnp.float32), attn_gain)

time: 320 us -> 323 us (level); the launches traced: 319 us -> 318 us
  blocking collectives: 9.17 us -> 0 us
  waiting for transfers between devices: 173 us -> 167 us
  starting transfers between devices: 23.2 us -> 28.4 us
  other arithmetic: 23.1 us -> 27.9 us
    all_to_all x1 -> x0, blocking collectives: 9.17 us -> none  [local(): lax.all_to_all(dealt_acts, 'req', split_axis=0, concat_axis=1, tiled=True)]
    ppermute x6, waiting for transfers between devices: 66.5 us -> 59.9 us  [head_sum(): lax.ppermute(sent, 'head', pairs).astype(jnp.float32)]
    all_gather x1, waiting for transfers between devices: 50.7 us -> 46.7 us  [local(): gathered = lax.all_gather(dealt_rows, 'head', axis=2, tiled=True)]
    unnamed x41 -> x61, local copies, waits for them, and re-layouts: 10.7 us -> 11.3 us
  transfers between devices with their start and end apart: 16 -> 19, of which waited for: 12 -> 15; matrix products, arithmetic and copies ran while one was open for 19% -> 20% of each run, Pallas kernels for 0% -> 0%
where the time goes in v17:
time: 323 us; the launch traced here: 318 us
  waiting for transfers between devices  167 us (52%)
  local copies, waits for them, and re-layouts  53 us (16%)
  starting transfers between devices  28.4 us (9%)
  other arithmetic  27.9 us (9%)
  matrix products  26.8 us (8%)
  between operations  14.9 us (5%)
    ppermute x6, waiting for transfers between devices, head_sum(): lax.ppermute(sent, 'head', pairs).astype(jnp.float32)  59.9 us
    all_gather x1, waiting for transfers between devices, local(): gathered = lax.all_gather(dealt_rows, 'head', axis=2, tiled=True)  46.7 us
    ppermute x3, waiting for transfers between devices, head_gather(): held.append(lax.ppermute(by_outer, 'head', pairs))  20.2 us
    ppermute x2, waiting for transfers between devices, head_sum(): total = total + lax.ppermute(sent, 'head', pairs).astype(jnp.float32)  18.8 us
    dot_general x1, matrix products, local(): jnp.dot(inner, down_weight, preferred_element_type=jnp.float32)  14.3 us
    ppermute x1, waiting for transfers between devices, head_gather(): held.append(lax.ppermute(rows, 'head', pairs))  13.7 us
    unnamed x61, local copies, waits for them, and re-layouts  11.3 us
    ppermute x6, starting transfers between devices, head_sum(): lax.ppermute(sent, 'head', pairs).astype(jnp.float32)  6.73 us
  transfers between devices with their start and end apart: 19, of which 15 were waited for; matrix products, arithmetic and copies ran while one was open for 20% of the time, Pallas kernels for 0%

profile of v17, /device:TPU:1, one launch (start us, length us, event | category | flops | bytes accessed | tf_op | source)
XLA Modules:
  0.0 317.6 jit_solution(765861211936342946)
XLA Ops:
  10.7 1.5 gather_fusion.5
  12.3 2.7 collective-permute-start
  16.3 1.9 collective-permute-done.1
  18.9 1.6 pad_maximum_fusion.7
  20.5 1.5 gather_fusion
  22.8 5.2 %fusion.135 = (bf16[1,8,32,32,128]{4,3,2,1,0:T(8,128)(2,1)}, bf16[8,32,32,128]{3,2,1,0:T(8,128)(2,1)}) fusion(bf16[2,8,32,32,128]{4,3,2,1,0:T(8,128)(2,1)} %param.19), kind=kLoop, calls=%fused_computation.267 | loop fusion | bytes 8388608 | tf_op jit(solution)/shard_map/slice | solution.py:144
  28.1 3.7 %gather_fusion.6 = bf16[8,32,32,128]{3,2,1,0:T(8,128)(2,1)} fusion(bf16[8,32,32,128]{3,2,1,0:T(8,128)(2,1)} %get-tuple-element.28, s32[1024]{0:T(1024)S(1)} %pad_clamp_fusion.4), kind=kCustom, calls=%fused_computation.2.clone | custom fusion | bytes 4194336 | tf_op jit(solution)/shard_map/jit(_take)/gather | solution.py:149
  32.5 1.8 select_select_fusion.1
  35.2 1.8 copy.59
  37.0 5.9 %all-to-all-start = ((bf16[32,2,32,4,128]{4,2,3,1,0:T(8,128)(2,1)}), bf16[32,2,32,4,128]{4,2,3,1,0:T(8,128)(2,1)}, u32[]{:S(2)}, u32[]{:S(2)}) async-start(bf16[32,2,32,4,128]{4,2,3,1,0:T(8,128)(2,1)} %bitcast.166), calls=%async_computation | async-start | bytes 4194304 | tf_op jit(solution)/shard_map/all_to_all | solution.py:158
  52.0 46.7 %all-gather.2.cloned.1.call-done = bf16[2,4,64,2048]{3,2,0,1:T(8,128)(2,1)} async-done(((bf16[2,4,8,2048]{3,2,0,1:T(8,128)(2,1)}), bf16[2,4,64,2048]{3,2,0,1:T(8,128)(2,1)}) %all-gather.2.cloned.1.call-update) | async-done | bytes 2097168 | tf_op jit(solution)/shard_map/all_gather | solution.py:166
  98.7 2.1 convert_reduce_fusion
  102.5 1.8 fusion.19
  105.2 4.3 %all-to-all-done = bf16[32,2,32,4,128]{4,2,3,1,0:T(8,128)(2,1)} async-done(((bf16[32,2,32,4,128]{4,2,3,1,0:T(8,128)(2,1)}), bf16[32,2,32,4,128]{4,2,3,1,0:T(8,128)(2,1)}, u32[]{:S(2)}, u32[]{:S(2)}) %all-to-all-start) | async-done | bytes 2097184 | tf_op jit(solution)/shard_map/all_to_all | solution.py:158
  110.9 2.0 fusion.139
  112.8 2.9 convolution_convert_fusion.3
  115.9 2.0 fusion.138
  117.9 2.2 convolution_convert_fusion.2
  121.0 1.7 convolution_convert_fusion.1
  124.7 1.7 collective-permute-start.5
  126.4 11.1 %collective-permute-done.3 = bf16[2,4,2,8,2048]{4,3,1,0,2:T(8,128)(2,1)} collective-permute-done((bf16[2,4,2,8,2048]{4,3,1,0,2:T(8,128)(2,1)S(1)}, bf16[2,4,2,8,2048]{4,3,1,0,2:T(8,128)(2,1)}, u32[]{:S(2)}, u32[]{:S(2)}) %collective-permute-start.3) | collective-permute-done | bytes 524320 | tf_op jit(solution)/shard_map/ppermute | solution.py:58
  138.1 11.7 %collective-permute-done.5 = bf16[2,4,2,8,2048]{4,3,1,0,2:T(8,128)(2,1)S(1)} collective-permute-done((bf16[2,4,2,8,2048]{4,3,1,0,2:T(8,128)(2,1)S(1)}, bf16[2,4,2,8,2048]{4,3,1,0,2:T(8,128)(2,1)S(1)}, u32[]{:S(2)}, u32[]{:S(2)}) %collective-permute-start.5) | collective-permute-done | bytes 524320 | tf_op jit(solution)/shard_map/ppermute | solution.py:58
  149.8 1.4 fusion.26
  152.4 2.7 gather_fusion.8
  155.1 10.4 %collective-permute-done.6 = bf16[2,4,8,2048]{3,2,0,1:T(8,128)(2,1)S(1)} collective-permute-done((bf16[2,4,8,2048]{3,2,0,1:T(8,128)(2,1)S(1)}, bf16[2,4,8,2048]{3,2,0,1:T(8,128)(2,1)S(1)}, u32[]{:S(2)}, u32[]{:S(2)}) %collective-permute-start.6) | collective-permute-done | bytes 262176 | tf_op jit(solution)/shard_map/ppermute | solution.py:64
  167.4 13.7 %collective-permute-done.7 = bf16[2,4,8,2048]{3,2,0,1:T(8,128)(2,1)S(1)} collective-permute-done((bf16[2,4,8,2048]{3,2,0,1:T(8,128)(2,1)S(1)}, bf16[2,4,8,2048]{3,2,0,1:T(8,128)(2,1)S(1)}, u32[]{:S(2)}, u32[]{:S(2)}) %collective-permute-start.7) | collective-permute-done | bytes 262176 | tf_op jit(solution)/shard_map/ppermute | solution.py:76
  182.0 1.6 gather_fusion.2
  183.9 2.3 collective-permute-start.10
  187.4 2.0 copy.74
  189.5 8.2 %collective-permute-done.8 = bf16[2,2,4,8,2048]{4,3,1,2,0:T(8,128)(2,1)S(1)} collective-permute-done((bf16[2,2,4,8,2048]{4,3,1,2,0:T(8,128)(2,1)S(1)}, bf16[2,2,4,8,2048]{4,3,1,2,0:T(8,128)(2,1)S(1)}, u32[]{:S(2)}, u32[]{:S(2)}) %collective-permute-start.8) | collective-permute-done | bytes 524320 | tf_op jit(solution)/shard_map/ppermute | solution.py:81
  197.7 12.0 %collective-permute-done.10 = bf16[2,2,4,8,2048]{4,3,1,2,0:T(8,128)(2,1)S(1)} collective-permute-done((bf16[2,2,4,8,2048]{4,3,1,2,0:T(8,128)(2,1)S(1)}, bf16[2,2,4,8,2048]{4,3,1,2,0:T(8,128)(2,1)S(1)}, u32[]{:S(2)}, u32[]{:S(2)}) %collective-permute-start.10) | collective-permute-done | bytes 524320 | tf_op jit(solution)/shard_map/ppermute | solution.py:81
  210.0 2.0 gather_fusion.3
  212.0 1.9 select_bitcast_fusion
  213.9 1.6 copy.75
  215.4 3.3 %all-to-all-start.1 = ((bf16[32,2,32,4,128]{4,2,3,1,0:T(8,128)(2,1)}), bf16[32,2,32,4,128]{4,2,3,1,0:T(8,128)(2,1)S(1)}, u32[]{:S(2)}, u32[]{:S(2)}) async-start(bf16[32,2,32,4,128]{4,2,3,1,0:T(8,128)(2,1)} %bitcast.50), calls=%async_computation.1 | async-start | bytes 4194304 | tf_op jit(solution)/shard_map/all_to_all | solution.py:197
  218.7 14.3 %convolution_convert_fusion = bf16[512,2048]{1,0:T(8,128)(2,1)} fusion(bf16[1024,2048]{1,0:T(8,128)(2,1)} %param.29, bf16[512,2048]{1,0:T(8,128)(2,1)} %bitcast.174, bf16[2048,1024]{1,0:T(8,128)(2,1)} %param.28), kind=kOutput, calls=%fused_computation.23 | convolution fusion | flops 4330094592 | bytes 12582912 | tf_op jit(solution)/shard_map/dot_general | solution.py:207
  233.1 1.7 constant_dynamic-slice_fusion.3
  234.8 1.4 collective-permute-start.11
  237.6 1.5 collective-permute-start.13
  239.1 27.1 %collective-permute-done.11 = bf16[2,4,2,8,2048]{4,3,1,0,2:T(8,128)(2,1)S(1)} collective-permute-done((bf16[2,4,2,8,2048]{4,3,1,0,2:T(8,128)(2,1)S(1)}, bf16[2,4,2,8,2048]{4,3,1,0,2:T(8,128)(2,1)S(1)}, u32[]{:S(2)}, u32[]{:S(2)}) %collective-permute-start.11) | collective-permute-done | bytes 524320 | tf_op jit(solution)/shard_map/ppermute | solution.py:58
  266.3 9.4 %collective-permute-done.13 = bf16[2,4,2,8,2048]{4,3,1,0,2:T(8,128)(2,1)S(1)} collective-permute-done((bf16[2,4,2,8,2048]{4,3,1,0,2:T(8,128)(2,1)S(1)}, bf16[2,4,2,8,2048]{4,3,1,0,2:T(8,128)(2,1)S(1)}, u32[]{:S(2)}, u32[]{:S(2)}) %collective-permute-start.13) | collective-permute-done | bytes 524320 | tf_op jit(solution)/shard_map/ppermute | solution.py:58
  276.1 1.8 collective-permute-start.14
  277.9 3.5 %copy.72 = bf16[4,2,8,32,4,128]{5,3,2,4,1,0:T(8,128)(2,1)} copy(bf16[4,2,8,32,4,128]{5,3,4,1,2,0:T(8,128)(2,1)} %bitcast.14) | data formatting | bytes 4194304 | tf_op jit(solution)/shard_map/transpose | solution.py:89
  281.4 8.4 %collective-permute-done.14 = bf16[2,4,8,2048]{3,2,0,1:T(8,128)(2,1)S(1)} collective-permute-done((bf16[2,4,8,2048]{3,2,0,1:T(8,128)(2,1)S(1)}, bf16[2,4,8,2048]{3,2,0,1:T(8,128)(2,1)S(1)}, u32[]{:S(2)}, u32[]{:S(2)}) %collective-permute-start.14) | collective-permute-done | bytes 262176 | tf_op jit(solution)/shard_map/ppermute | solution.py:64
  291.8 2.2 copy.77
  294.9 4.9 %all-to-all-start.2 = ((bf16[2,4,8,2048]{3,2,0,1:T(8,128)(2,1)}), bf16[2,4,8,2048]{3,2,0,1:T(8,128)(2,1)S(1)}, u32[]{:S(2)}, u32[]{:S(2)}) async-start(bf16[2,4,8,2048]{3,2,0,1:T(8,128)(2,1)} %select_convert_fusion), calls=%async_computation.2 | async-start | bytes 524288 | tf_op jit(solution)/shard_map/all_to_all | solution.py:219
  299.8 7.9 %copy.84 = bf16[8,2,256,4,128]{4,3,2,1,0:T(4,128)(2,1)} copy(bf16[8,2,256,4,128]{4,2,3,1,0:T(8,128)(2,1)} %bitcast.165) | data formatting | bytes 8388608
  308.4 1.5 gather_fusion.9
  (164 shorter events, 36.3 us)
Async XLA Ops:
  7.2 95.3 %copy-start = (bf16[2048,4,192]{0,2,1:T(8,128)(2,1)S(1)}, bf16[2048,4,192]{0,2,1:T(8,128)(2,1)}, u32[]{:S(2)}) copy-start(bf16[2048,4,192]{0,2,1:T(8,128)(2,1)} %param.24) | copy-start | bytes 9437188
  7.2 91.5 %all-gather.2.cloned.1.call-start = ((), (), s32[]{:S(2)}) async-start(), calls=%async_computation.3 | async-start | bytes 2359296 | tf_op jit(solution)/shard_map/all_gather | solution.py:166
  8.1 20.0 %copy-start.17 = (s32[1024]{0:T(1024)}, s32[1024]{0:T(1024)S(1)}, u32[]{:S(2)}) copy-start(s32[1024]{0:T(1024)S(1)} %pad_clamp_fusion.4) | copy-start | bytes 12292
  10.7 21.2 %copy-start.18 = (pred[8]{0:T(512)(128)(4,1)}, pred[8]{0:T(512)(128)(4,1)S(1)}, u32[]{:S(2)}) copy-start(pred[8]{0:T(512)(128)(4,1)S(1)} %get-tuple-element.26) | copy-start | bytes 28
  12.3 4.0 %collective-permute-start = (bf16[2,8,2048]{2,1,0:T(8,128)(2,1)S(1)}, bf16[2,8,2048]{2,1,0:T(8,128)(2,1)S(1)}, u32[]{:S(2)}, u32[]{:S(2)}) collective-permute-start(bf16[2,8,2048]{2,1,0:T(8,128)(2,1)S(1)} %get-tuple-element.44), channel_id=1, source_target_pairs={{0,8},{8,16},{16,24},{24,0},{1,9},{9,17},{17,25},{25,1},{2,10},{10... | collective-permute-start | bytes 196616 | tf_op jit(solution)/shard_map/ppermute | solution.py:99
  15.0 3.3 %collective-permute-start.1 = (bf16[2,8,2048]{2,1,0:T(8,128)(2,1)S(1)}, bf16[2,8,2048]{2,1,0:T(8,128)(2,1)S(1)}, u32[]{:S(2)}, u32[]{:S(2)}) collective-permute-start(bf16[2,8,2048]{2,1,0:T(8,128)(2,1)S(1)} %get-tuple-element.43), channel_id=1, source_target_pairs={{0,16},{8,24},{16,0},{24,8},{1,17},{9,25},{17,1},{25,9},{2,18},{10... | collective-permute-start | bytes 196616 | tf_op jit(solution)/shard_map/ppermute | solution.py:99
  15.0 3.9 %collective-permute-start.2 = (bf16[2,8,2048]{2,1,0:T(8,128)(2,1)S(1)}, bf16[2,8,2048]{2,1,0:T(8,128)(2,1)}, u32[]{:S(2)}, u32[]{:S(2)}) collective-permute-start(bf16[2,8,2048]{2,1,0:T(8,128)(2,1)S(1)} %get-tuple-element.42), channel_id=1, source_target_pairs={{0,24},{8,0},{16,8},{24,16},{1,25},{9,1},{17,9},{25,17},{2,26},{10... | collective-permute-start | bytes 196616 | tf_op jit(solution)/shard_map/ppermute | solution.py:99
  16.0 12.0 %copy-start.20 = (pred[4]{0:T(512)(128)(4,1)}, pred[4]{0:T(512)(128)(4,1)S(1)}, u32[]{:S(2)}) copy-start(pred[4]{0:T(512)(128)(4,1)S(1)} %get-tuple-element.52) | copy-start | bytes 16
  28.0 3.8 %copy-start.28 = (s32[8]{0:T(128)S(1)}, s32[8]{0:T(128)}, u32[]{:S(2)}) copy-start(s32[8]{0:T(128)} %get-tuple-element.25) | copy-start | bytes 100
  37.0 6.0 %copy-start.22 = (bf16[2048]{0:T(1024)(128)(2,1)S(1)}, bf16[2048]{0:T(1024)(128)(2,1)}, u32[]{:S(2)}) copy-start(bf16[2048]{0:T(1024)(128)(2,1)} %param.23) | copy-start | bytes 12292
  37.0 6.0 %copy-start.26 = (s32[8]{0:T(128)S(1)}, s32[8]{0:T(128)}, u32[]{:S(2)}) copy-start(s32[8]{0:T(128)} %param.22) | copy-start | bytes 100
  37.0 6.1 %copy-start.2 = (s32[8]{0:T(128)S(1)}, s32[8]{0:T(128)}, u32[]{:S(2)}) copy-start(s32[8]{0:T(128)} %param.21) | copy-start | bytes 100
  37.0 6.7 %copy-start.3 = (s32[8]{0:T(128)S(1)}, s32[8]{0:T(128)}, u32[]{:S(2)}) copy-start(s32[8]{0:T(128)} %param.20) | copy-start | bytes 100
  37.0 72.6 %all-to-all-start = ((bf16[32,2,32,4,128]{4,2,3,1,0:T(8,128)(2,1)}), bf16[32,2,32,4,128]{4,2,3,1,0:T(8,128)(2,1)}, u32[]{:S(2)}, u32[]{:S(2)}) async-start(bf16[32,2,32,4,128]{4,2,3,1,0:T(8,128)(2,1)} %bitcast.166), calls=%async_computation | async-start | bytes 4194304 | tf_op jit(solution)/shard_map/all_to_all | solution.py:158
  98.7 2.2 copy-start.4
  104.3 0.9 copy-start.12
  105.2 5.7 %copy-start.11 = (f32[256,512]{1,0:T(8,128)S(1)}, f32[256,512]{1,0:T(8,128)}, u32[]{:S(2)}) copy-start(f32[256,512]{1,0:T(8,128)} %subtract_convert_fusion.1) | copy-start | bytes 1572868
  105.2 5.7 %copy-start.13 = (pred[256,512]{1,0:T(8,128)(4,1)S(1)}, pred[256,512]{1,0:T(8,128)(4,1)}, u32[]{:S(2)}) copy-start(pred[256,512]{1,0:T(8,128)(4,1)} %get-tuple-element.45) | copy-start | bytes 393220
  105.2 5.7 %copy-start.29 = (f32[4]{0:T(128)S(1)}, f32[4]{0:T(128)}, u32[]{:S(2)}) copy-start(f32[4]{0:T(128)} %param.25) | copy-start | bytes 52
  112.8 3.0 copy-start.10
  117.9 2.3 copy-start.14
  117.9 3.1 copy-start.9
  123.7 26.1 %copy-start.7 = (bf16[2,4,2,1,8,2048]{5,4,3,2,1,0:T(8,128)(2,1)S(1)}, bf16[2,4,2,1,8,2048]{5,4,3,2,1,0:T(8,128)(2,1)}, u32[]{:S(2)}) copy-start(bf16[2,4,2,1,8,2048]{5,4,3,2,1,0:T(8,128)(2,1)} %get-tuple-element.33) | copy-start | bytes 1572868
  123.8 13.8 %collective-permute-start.3 = (bf16[2,4,2,8,2048]{4,3,1,0,2:T(8,128)(2,1)S(1)}, bf16[2,4,2,8,2048]{4,3,1,0,2:T(8,128)(2,1)}, u32[]{:S(2)}, u32[]{:S(2)}) collective-permute-start(bf16[2,4,2,8,2048]{4,3,1,0,2:T(8,128)(2,1)S(1)} %bitcast.183), channel_id=1, source_target_pairs={{0,1},{1,2},{2,3},{3,0},{4,5},{5,6},{6,7},{7,4},{8,9},{9,10},{10,1... | collective-permute-start | bytes 1572872 | tf_op jit(solution)/shard_map/ppermute | solution.py:58
  124.6 13.5 %collective-permute-start.4 = (bf16[2,4,2,8,2048]{4,3,1,0,2:T(8,128)(2,1)S(1)}, bf16[2,4,2,8,2048]{4,3,1,0,2:T(8,128)(2,1)S(1)}, u32[]{:S(2)}, u32[]{:S(2)}) collective-permute-start(bf16[2,4,2,8,2048]{4,3,1,0,2:T(8,128)(2,1)S(1)} %bitcast.184), channel_id=1, source_target_pairs={{0,2},{1,3},{2,0},{3,1},{4,6},{5,7},{6,4},{7,5},{8,10},{9,11},{10,... | collective-permute-start | bytes 1572872 | tf_op jit(solution)/shard_map/ppermute | solution.py:58
  124.7 25.1 %collective-permute-start.5 = (bf16[2,4,2,8,2048]{4,3,1,0,2:T(8,128)(2,1)S(1)}, bf16[2,4,2,8,2048]{4,3,1,0,2:T(8,128)(2,1)S(1)}, u32[]{:S(2)}, u32[]{:S(2)}) collective-permute-start(bf16[2,4,2,8,2048]{4,3,1,0,2:T(8,128)(2,1)S(1)} %bitcast.185), channel_id=1, source_target_pairs={{0,3},{1,0},{2,1},{3,2},{4,7},{5,4},{6,5},{7,6},{8,11},{9,8},{10,9... | collective-permute-start | bytes 1572872 | tf_op jit(solution)/shard_map/ppermute | solution.py:58
  149.8 1.6 copy-start.23
  149.8 1.6 copy-start.27
  151.2 1.2 copy-start.6
  151.3 14.2 %collective-permute-start.6 = (bf16[2,4,8,2048]{3,2,0,1:T(8,128)(2,1)S(1)}, bf16[2,4,8,2048]{3,2,0,1:T(8,128)(2,1)S(1)}, u32[]{:S(2)}, u32[]{:S(2)}) collective-permute-start(bf16[2,4,8,2048]{3,2,0,1:T(8,128)(2,1)S(1)} %copy.70), channel_id=1, source_target_pairs={{0,4},{1,5},{2,6},{3,7},{4,0},{5,1},{6,2},{7,3},{8,12},{9,13},{10,... | collective-permute-start | bytes 786440 | tf_op jit(solution)/shard_map/ppermute | solution.py:64
  152.4 13.1 %copy-start.21 = (pred[4]{0:T(512)(128)(4,1)S(1)}, pred[4]{0:T(512)(128)(4,1)}, u32[]{:S(2)}) copy-start(pred[4]{0:T(512)(128)(4,1)} %copy-done.20) | copy-start | bytes 16
  167.1 19.0 %copy-start.16 = (pred[8,32]{1,0:T(8,128)(4,1)S(1)}, pred[8,32]{1,0:T(8,128)(4,1)}, u32[]{:S(2)}) copy-start(pred[8,32]{1,0:T(8,128)(4,1)} %copy-done.15) | copy-start | bytes 772
  167.1 19.0 %copy-start.19 = (pred[8]{0:T(512)(128)(4,1)S(1)}, pred[8]{0:T(512)(128)(4,1)}, u32[]{:S(2)}) copy-start(pred[8]{0:T(512)(128)(4,1)} %copy-done.18) | copy-start | bytes 28
  167.2 14.0 %collective-permute-start.7 = (bf16[2,4,8,2048]{3,2,0,1:T(8,128)(2,1)S(1)}, bf16[2,4,8,2048]{3,2,0,1:T(8,128)(2,1)S(1)}, u32[]{:S(2)}, u32[]{:S(2)}) collective-permute-start(bf16[2,4,8,2048]{3,2,0,1:T(8,128)(2,1)S(1)} %multiply_convert_fusion), channel_id=1, source_target_pairs={{0,4},{1,5},{2,6},{3,7},{4,0},{5,1},{6,2},{7,3},{8,12},{9,13},{10,... | collective-permute-start | bytes 786440 | tf_op jit(solution)/shard_map/ppermute | solution.py:76
  183.7 14.0 %collective-permute-start.8 = (bf16[2,2,4,8,2048]{4,3,1,2,0:T(8,128)(2,1)S(1)}, bf16[2,2,4,8,2048]{4,3,1,2,0:T(8,128)(2,1)S(1)}, u32[]{:S(2)}, u32[]{:S(2)}) collective-permute-start(bf16[2,2,4,8,2048]{4,3,1,2,0:T(8,128)(2,1)S(1)} %broadcast_select_fusion), channel_id=1, source_target_pairs={{0,1},{1,2},{2,3},{3,0},{4,5},{5,6},{6,7},{7,4},{8,9},{9,10},{10,1... | collective-permute-start | bytes 1572872 | tf_op jit(solution)/shard_map/ppermute | solution.py:81
  183.8 13.9 %collective-permute-start.9 = (bf16[2,2,4,8,2048]{4,3,1,2,0:T(8,128)(2,1)S(1)}, bf16[2,2,4,8,2048]{4,3,1,2,0:T(8,128)(2,1)S(1)}, u32[]{:S(2)}, u32[]{:S(2)}) collective-permute-start(bf16[2,2,4,8,2048]{4,3,1,2,0:T(8,128)(2,1)S(1)} %broadcast_select_fusion), channel_id=1, source_target_pairs={{0,2},{1,3},{2,0},{3,1},{4,6},{5,7},{6,4},{7,5},{8,10},{9,11},{10,... | collective-permute-start | bytes 1572872 | tf_op jit(solution)/shard_map/ppermute | solution.py:81
  183.9 25.9 %collective-permute-start.10 = (bf16[2,2,4,8,2048]{4,3,1,2,0:T(8,128)(2,1)S(1)}, bf16[2,2,4,8,2048]{4,3,1,2,0:T(8,128)(2,1)S(1)}, u32[]{:S(2)}, u32[]{:S(2)}) collective-permute-start(bf16[2,2,4,8,2048]{4,3,1,2,0:T(8,128)(2,1)S(1)} %broadcast_select_fusion), channel_id=1, source_target_pairs={{0,3},{1,0},{2,1},{3,2},{4,7},{5,4},{6,5},{7,6},{8,11},{9,8},{10,9... | collective-permute-start | bytes 1572872 | tf_op jit(solution)/shard_map/ppermute | solution.py:81
  210.0 2.0 copy-start.24
  215.4 74.4 %all-to-all-start.1 = ((bf16[32,2,32,4,128]{4,2,3,1,0:T(8,128)(2,1)}), bf16[32,2,32,4,128]{4,2,3,1,0:T(8,128)(2,1)S(1)}, u32[]{:S(2)}, u32[]{:S(2)}) async-start(bf16[32,2,32,4,128]{4,2,3,1,0:T(8,128)(2,1)} %bitcast.50), calls=%async_computation.1 | async-start | bytes 4194304 | tf_op jit(solution)/shard_map/all_to_all | solution.py:197
  234.8 31.5 %collective-permute-start.11 = (bf16[2,4,2,8,2048]{4,3,1,0,2:T(8,128)(2,1)S(1)}, bf16[2,4,2,8,2048]{4,3,1,0,2:T(8,128)(2,1)S(1)}, u32[]{:S(2)}, u32[]{:S(2)}) collective-permute-start(bf16[2,4,2,8,2048]{4,3,1,0,2:T(8,128)(2,1)S(1)} %bitcast.186), channel_id=1, source_target_pairs={{0,1},{1,2},{2,3},{3,0},{4,5},{5,6},{6,7},{7,4},{8,9},{9,10},{10,1... | collective-permute-start | bytes 1572872 | tf_op jit(solution)/shard_map/ppermute | solution.py:58
  236.3 30.0 %collective-permute-start.12 = (bf16[2,4,2,8,2048]{4,3,1,0,2:T(8,128)(2,1)S(1)}, bf16[2,4,2,8,2048]{4,3,1,0,2:T(8,128)(2,1)S(1)}, u32[]{:S(2)}, u32[]{:S(2)}) collective-permute-start(bf16[2,4,2,8,2048]{4,3,1,0,2:T(8,128)(2,1)S(1)} %bitcast.187), channel_id=1, source_target_pairs={{0,2},{1,3},{2,0},{3,1},{4,6},{5,7},{6,4},{7,5},{8,10},{9,11},{10,... | collective-permute-start | bytes 1572872 | tf_op jit(solution)/shard_map/ppermute | solution.py:58
  237.6 38.1 %collective-permute-start.13 = (bf16[2,4,2,8,2048]{4,3,1,0,2:T(8,128)(2,1)S(1)}, bf16[2,4,2,8,2048]{4,3,1,0,2:T(8,128)(2,1)S(1)}, u32[]{:S(2)}, u32[]{:S(2)}) collective-permute-start(bf16[2,4,2,8,2048]{4,3,1,0,2:T(8,128)(2,1)S(1)} %bitcast.188), channel_id=1, source_target_pairs={{0,3},{1,0},{2,1},{3,2},{4,7},{5,4},{6,5},{7,6},{8,11},{9,8},{10,9... | collective-permute-start | bytes 1572872 | tf_op jit(solution)/shard_map/ppermute | solution.py:58
  275.7 2.2 copy-start.25
  276.1 13.7 %collective-permute-start.14 = (bf16[2,4,8,2048]{3,2,0,1:T(8,128)(2,1)S(1)}, bf16[2,4,8,2048]{3,2,0,1:T(8,128)(2,1)S(1)}, u32[]{:S(2)}, u32[]{:S(2)}) collective-permute-start(bf16[2,4,8,2048]{3,2,0,1:T(8,128)(2,1)S(1)} %copy.82), channel_id=1, source_target_pairs={{0,4},{1,5},{2,6},{3,7},{4,0},{5,1},{6,2},{7,3},{8,12},{9,13},{10,... | collective-permute-start | bytes 786440 | tf_op jit(solution)/shard_map/ppermute | solution.py:64
  289.9 1.6 copy-start.5
  294.9 12.9 %all-to-all-start.2 = ((bf16[2,4,8,2048]{3,2,0,1:T(8,128)(2,1)}), bf16[2,4,8,2048]{3,2,0,1:T(8,128)(2,1)S(1)}, u32[]{:S(2)}, u32[]{:S(2)}) async-start(bf16[2,4,8,2048]{3,2,0,1:T(8,128)(2,1)} %select_convert_fusion), calls=%async_computation.2 | async-start | bytes 524288 | tf_op jit(solution)/shard_map/all_to_all | solution.py:219
  299.8 10.9 %copy-start.1 = (bf16[2048,4,192]{0,2,1:T(8,128)(2,1)S(1)}, bf16[2048,4,192]{0,2,1:T(8,128)(2,1)}, u32[]{:S(2)}) copy-start(bf16[2048,4,192]{0,2,1:T(8,128)(2,1)} %param.24) | copy-start | bytes 9437188
  307.7 0.7 copy-start.8
  (1 other events, 0.6 us)
Sparse Core Ops, SparseCore 0:
  23.0 75.6 all-gather.1

commit v18 on v14

--- a/solution.py
+++ b/solution.py
@@ -187,18 +187,21 @@
     for outgoing in deferred:
         chunks.append(land(lax.all_to_all(outgoing, ("req", "head"), 0, 0, tiled=True), req_count, head_count))
     relaid = jnp.stack(chunks, axis=1).reshape((req_count * local_layers,) + chunks[0].shape[1:])
-    inner = jax.nn.gelu(
-        jnp.dot(
-            normed_all.reshape(group_size * stretch_max, features),
-            up_weight,
-            preferred_element_type=jnp.float32,
-        ),
-        approximate=False,
-    ).astype(jnp.bfloat16)
-    partial_mlp = jnp.dot(inner, down_weight, preferred_element_type=jnp.float32).reshape(
-        group_size, req_count, span_rows, features
-    )
-    mlp_rows = head_sum(partial_mlp, head_count, stretch_rows)
+    member_sums = []
+    for member in range(group_size):
+        inner = jax.nn.gelu(
+            jnp.dot(
+                normed_all[member].reshape(stretch_max, features),
+                up_weight,
+                preferred_element_type=jnp.float32,
+            ),
+            approximate=False,
+        ).astype(jnp.bfloat16)
+        partial_mlp = jnp.dot(inner, down_weight, preferred_element_type=jnp.float32).reshape(
+            1, req_count, span_rows, features
+        )
+        member_sums.append(head_sum(partial_mlp, head_count, stretch_rows))
+    mlp_rows = jnp.concatenate(member_sums, axis=0)
     relaid, mlp_rows = lax.optimization_barrier((relaid, mlp_rows))
     row_number = (
         jnp.arange(req_count, dtype=jnp.int32)[:, None] * head_count + head_index

time: 320 us -> 317 us (level)
  waiting for transfers between devices: 173 us -> 157 us
  starting transfers between devices: 23.2 us -> 36.3 us
  blocking collectives: 9.17 us -> 0 us
  other arithmetic: 23.1 us -> 27.3 us
  matrix products: 25.2 us -> 28.5 us
    ppermute x6 -> x9, waiting for transfers between devices: 66.5 us -> 54 us  [head_sum(): lax.ppermute(sent, 'head', pairs).astype(jnp.float32)]
    all_to_all x1 -> x0, blocking collectives: 9.17 us -> none  [local(): lax.all_to_all(dealt_acts, 'req', split_axis=0, concat_axis=1, tiled=True)]
    ppermute x2 -> x3, starting transfers between devices: 0.14 us -> 5.84 us  [head_sum(): total = total + lax.ppermute(sent, 'head', pairs).astype(jnp.float32)]
    all_to_all x0 -> x1, waiting for transfers between devices: none -> 5.06 us  [local(): lax.all_to_all(dealt_acts, 'req', split_axis=0, concat_axis=1, tiled=True)]
    all_to_all x0 -> x1, starting transfers between devices: none -> 4.26 us  [local(): lax.all_to_all(dealt_acts, 'req', split_axis=0, concat_axis=1, tiled=True)]
    all_gather x1, waiting for transfers between devices: 50.7 us -> 47.2 us  [local(): gathered = lax.all_gather(dealt_rows, 'head', axis=2, tiled=True)]
    ppermute x3, waiting for transfers between devices: 20.2 us -> 16.7 us  [head_gather(): held.append(lax.ppermute(by_outer, 'head', pairs))]
    dot_general x1 -> x2, matrix products: 14.3 us -> 17.6 us  [local(): jnp.dot(inner, down_weight, preferred_element_type=jnp.float32)]
  transfers between devices with their start and end apart: 16 -> 21, of which waited for: 12 -> 13; matrix products, arithmetic and copies ran while one was open for 19% -> 19% of each run, Pallas kernels for 0% -> 0%
where the time goes in v18:
time: 317 us; the launch traced here: 315 us
  waiting for transfers between devices  157 us (50%)
  local copies, waits for them, and re-layouts  50.5 us (16%)
  starting transfers between devices  36.3 us (11%)
  matrix products  28.5 us (9%)
  other arithmetic  27.3 us (9%)
  between operations  14.8 us (5%)
    ppermute x9, waiting for transfers between devices, head_sum(): lax.ppermute(sent, 'head', pairs).astype(jnp.float32)  54 us
    all_gather x1, waiting for transfers between devices, local(): gathered = lax.all_gather(dealt_rows, 'head', axis=2, tiled=True)  47.2 us
    ppermute x3, waiting for transfers between devices, head_sum(): total = total + lax.ppermute(sent, 'head', pairs).astype(jnp.float32)  19.3 us
    dot_general x2, matrix products, local(): jnp.dot(inner, down_weight, preferred_element_type=jnp.float32)  17.6 us
    ppermute x3, waiting for transfers between devices, head_gather(): held.append(lax.ppermute(by_outer, 'head', pairs))  16.7 us
    ppermute x1, waiting for transfers between devices, head_gather(): held.append(lax.ppermute(rows, 'head', pairs))  13.5 us
    unnamed x49, local copies, waits for them, and re-layouts  12.1 us
    ppermute x9, starting transfers between devices, head_sum(): lax.ppermute(sent, 'head', pairs).astype(jnp.float32)  7.86 us
  transfers between devices with their start and end apart: 21, of which 13 were waited for; matrix products, arithmetic and copies ran while one was open for 19% of the time, Pallas kernels for 0%

profile of v18, /device:TPU:1, one launch (start us, length us, event | category | flops | bytes accessed | tf_op | source)
XLA Modules:
  0.0 314.5 jit_solution(13197907204091428827)
XLA Ops:
  8.0 1.4 gather_fusion
  10.1 1.5 gather_fusion.4
  12.4 4.3 %all-to-all-start = ((bf16[8,8,2048]{2,1,0:T(8,128)(2,1)}), bf16[8,8,2048]{2,1,0:T(8,128)(2,1)S(1)}, u32[]{:S(2)}, u32[]{:S(2)}) async-start(bf16[8,8,2048]{2,1,0:T(8,128)(2,1)} %broadcast_select_fusion.2), calls=%async_computation | async-start | bytes 524288 | tf_op jit(solution)/shard_map/all_to_all | solution.py:154
  16.7 5.1 %all-to-all-done = bf16[8,8,2048]{2,1,0:T(8,128)(2,1)S(1)} async-done(((bf16[8,8,2048]{2,1,0:T(8,128)(2,1)}), bf16[8,8,2048]{2,1,0:T(8,128)(2,1)S(1)}, u32[]{:S(2)}, u32[]{:S(2)}) %all-to-all-start) | async-done | bytes 262176 | tf_op jit(solution)/shard_map/all_to_all | solution.py:154
  22.5 5.2 %fusion.206 = (bf16[1,8,32,32,128]{4,3,2,1,0:T(8,128)(2,1)}, bf16[8,32,32,128]{3,2,1,0:T(8,128)(2,1)}) fusion(bf16[2,8,32,32,128]{4,3,2,1,0:T(8,128)(2,1)} %param.19), kind=kLoop, calls=%fused_computation.331 | loop fusion | bytes 8388608 | tf_op jit(solution)/shard_map/slice | solution.py:133
  27.6 3.8 %gather_fusion.5 = bf16[8,32,32,128]{3,2,1,0:T(8,128)(2,1)} fusion(bf16[8,32,32,128]{3,2,1,0:T(8,128)(2,1)} %get-tuple-element.28, s32[1024]{0:T(1024)S(1)} %pad_clamp_fusion.3), kind=kCustom, calls=%fused_computation.2.clone | custom fusion | bytes 4194336 | tf_op jit(solution)/shard_map/jit(_take)/gather | solution.py:138
  31.5 1.8 select_select_fusion.1
  34.1 1.8 copy.49
  36.0 6.3 %all-to-all-start.1 = ((bf16[32,2,32,4,128]{4,2,3,1,0:T(8,128)(2,1)}), bf16[32,2,32,4,128]{4,2,3,1,0:T(8,128)(2,1)}, u32[]{:S(2)}, u32[]{:S(2)}) async-start(bf16[32,2,32,4,128]{4,2,3,1,0:T(8,128)(2,1)} %bitcast.165), calls=%async_computation.1 | async-start | bytes 4194304 | tf_op jit(solution)/shard_map/all_to_all | solution.py:147
  47.8 1.3 iota_compare_fusion.1
  53.6 47.2 %all-gather.2.cloned.1.call-done = bf16[2,4,64,2048]{3,2,0,1:T(8,128)(2,1)} async-done(((bf16[2,4,8,2048]{3,2,0,1:T(8,128)(2,1)}), bf16[2,4,64,2048]{3,2,0,1:T(8,128)(2,1)}) %all-gather.2.cloned.1.call-update) | async-done | bytes 2097168 | tf_op jit(solution)/shard_map/all_gather | solution.py:157
  100.8 2.1 convert_reduce_fusion
  104.6 1.8 fusion.9
  107.3 1.4 all-to-all-done.1
  110.1 2.0 fusion.211
  112.0 2.2 convolution_convert_fusion.4
  114.5 2.0 fusion.210
  116.4 2.2 convolution_convert_fusion.3
  121.2 1.3 collective-permute-start.2
  122.6 10.8 %collective-permute-done = bf16[2,4,2,8,2048]{4,3,1,0,2:T(8,128)(2,1)S(1)} collective-permute-done((bf16[2,4,2,8,2048]{4,3,1,0,2:T(8,128)(2,1)S(1)}, bf16[2,4,2,8,2048]{4,3,1,0,2:T(8,128)(2,1)S(1)}, u32[]{:S(2)}, u32[]{:S(2)}) %collective-permute-start) | collective-permute-done | bytes 524320 | tf_op jit(solution)/shard_map/ppermute | solution.py:58
  134.5 11.4 %collective-permute-done.2 = bf16[2,4,2,8,2048]{4,3,1,0,2:T(8,128)(2,1)S(1)} collective-permute-done((bf16[2,4,2,8,2048]{4,3,1,0,2:T(8,128)(2,1)S(1)}, bf16[2,4,2,8,2048]{4,3,1,0,2:T(8,128)(2,1)S(1)}, u32[]{:S(2)}, u32[]{:S(2)}) %collective-permute-start.2) | collective-permute-done | bytes 524320 | tf_op jit(solution)/shard_map/ppermute | solution.py:58
  147.2 2.6 gather_fusion.7
  149.8 11.0 %collective-permute-done.3 = bf16[2,4,8,2048]{3,2,0,1:T(8,128)(2,1)S(1)} collective-permute-done((bf16[2,4,8,2048]{3,2,0,1:T(8,128)(2,1)S(1)}, bf16[2,4,8,2048]{3,2,0,1:T(8,128)(2,1)S(1)}, u32[]{:S(2)}, u32[]{:S(2)}) %collective-permute-start.3) | collective-permute-done | bytes 262176 | tf_op jit(solution)/shard_map/ppermute | solution.py:64
  162.6 13.5 %collective-permute-done.4 = bf16[2,4,8,2048]{3,2,0,1:T(8,128)(2,1)S(1)} collective-permute-done((bf16[2,4,8,2048]{3,2,0,1:T(8,128)(2,1)S(1)}, bf16[2,4,8,2048]{3,2,0,1:T(8,128)(2,1)S(1)}, u32[]{:S(2)}, u32[]{:S(2)}) %collective-permute-start.4) | collective-permute-done | bytes 262176 | tf_op jit(solution)/shard_map/ppermute | solution.py:76
  176.9 1.7 gather_fusion.1
  178.9 2.3 collective-permute-start.7
  181.7 3.5 %copy.62 = bf16[4,2,8,32,4,128]{5,3,2,4,1,0:T(8,128)(2,1)} copy(bf16[4,2,8,32,4,128]{5,3,4,1,2,0:T(8,128)(2,1)} %bitcast.7) | data formatting | bytes 4194304 | tf_op jit(solution)/shard_map/transpose | solution.py:89
  185.9 2.0 copy.64
  188.1 4.7 %collective-permute-done.5 = bf16[2,2,4,8,2048]{4,3,1,2,0:T(8,128)(2,1)S(1)} collective-permute-done((bf16[2,2,4,8,2048]{4,3,1,2,0:T(8,128)(2,1)S(1)}, bf16[2,2,4,8,2048]{4,3,1,2,0:T(8,128)(2,1)S(1)}, u32[]{:S(2)}, u32[]{:S(2)}) %collective-permute-start.5) | collective-permute-done | bytes 524320 | tf_op jit(solution)/shard_map/ppermute | solution.py:81
  192.8 12.0 %collective-permute-done.7 = bf16[2,2,4,8,2048]{4,3,1,2,0:T(8,128)(2,1)S(1)} collective-permute-done((bf16[2,2,4,8,2048]{4,3,1,2,0:T(8,128)(2,1)S(1)}, bf16[2,2,4,8,2048]{4,3,1,2,0:T(8,128)(2,1)S(1)}, u32[]{:S(2)}, u32[]{:S(2)}) %collective-permute-start.7) | collective-permute-done | bytes 524320 | tf_op jit(solution)/shard_map/ppermute | solution.py:81
  205.1 2.0 gather_fusion.2
  207.1 1.9 select_bitcast_fusion
  209.1 1.6 fusion.207
  210.7 8.3 %convolution_convert_fusion.2 = bf16[256,2048]{1,0:T(8,128)(2,1)S(1)} fusion(bf16[1024,2048]{1,0:T(8,128)(2,1)} %param.29, bf16[256,2048]{1,0:T(8,128)(2,1)} %bitcast.186, bf16[2048,1024]{1,0:T(8,128)(2,1)} %param.28), kind=kOutput, calls=%fused_computation.23 | convolution fusion | flops 2165047296 | bytes 10485760 | tf_op jit(solution)/shard_map/dot_general | solution.py:200
  219.1 1.5 collective-permute-start.8
  220.6 5.7 %all-to-all-start.2 = ((bf16[32,2,32,4,128]{4,2,3,1,0:T(8,128)(2,1)}), bf16[32,2,32,4,128]{4,2,3,1,0:T(8,128)(2,1)S(1)}, u32[]{:S(2)}, u32[]{:S(2)}) async-start(bf16[32,2,32,4,128]{4,2,3,1,0:T(8,128)(2,1)} %bitcast.44), calls=%async_computation.2 | async-start | bytes 4194304 | tf_op jit(solution)/shard_map/all_to_all | solution.py:188
  226.3 9.3 %convolution_convert_fusion.1 = bf16[256,2048]{1,0:T(8,128)(2,1)} fusion(bf16[1024,2048]{1,0:T(8,128)(2,1)} %param.29, bf16[256,2048]{1,0:T(8,128)(2,1)} %bitcast.185, bf16[2048,1024]{1,0:T(8,128)(2,1)} %param.28), kind=kOutput, calls=%fused_computation.22 | convolution fusion | flops 2165047296 | bytes 10485760 | tf_op jit(solution)/shard_map/dot_general | solution.py:200
  236.8 1.4 collective-permute-start.12
  240.6 1.3 fusion.39
  241.9 2.2 collective-permute-start.11
  244.1 26.6 %collective-permute-done.12 = bf16[1,4,2,8,2048]{4,3,2,1,0:T(8,128)(2,1)S(1)} collective-permute-done((bf16[1,4,2,8,2048]{4,3,2,1,0:T(8,128)(2,1)S(1)}, bf16[1,4,2,8,2048]{4,3,2,1,0:T(8,128)(2,1)S(1)}, u32[]{:S(2)}, u32[]{:S(2)}) %collective-permute-start.12) | collective-permute-done | bytes 262176 | tf_op jit(solution)/shard_map/ppermute | solution.py:58
  270.8 4.1 %collective-permute-done.14 = bf16[1,4,2,8,2048]{4,3,2,1,0:T(8,128)(2,1)S(1)} collective-permute-done((bf16[1,4,2,8,2048]{4,3,2,1,0:T(8,128)(2,1)S(1)}, bf16[1,4,2,8,2048]{4,3,2,1,0:T(8,128)(2,1)S(1)}, u32[]{:S(2)}, u32[]{:S(2)}) %collective-permute-start.14) | collective-permute-done | bytes 262176 | tf_op jit(solution)/shard_map/ppermute | solution.py:58
  276.0 3.6 %collective-permute-start.15 = (bf16[1,4,8,2048]{3,2,0,1:T(8,128)(2,1)S(1)}, bf16[1,4,8,2048]{3,2,0,1:T(8,128)(2,1)S(1)}, u32[]{:S(2)}, u32[]{:S(2)}) collective-permute-start(bf16[1,4,8,2048]{3,2,0,1:T(8,128)(2,1)S(1)} %fusion.111), channel_id=1, source_target_pairs={{0,4},{1,5},{2,6},{3,7},{4,0},{5,1},{6,2},{7,3},{8,12},{9,13},{10,... | collective-permute-start | bytes 393224 | tf_op jit(solution)/shard_map/ppermute | solution.py:64
  279.6 8.2 %collective-permute-done.15 = bf16[1,4,8,2048]{3,2,0,1:T(8,128)(2,1)S(1)} collective-permute-done((bf16[1,4,8,2048]{3,2,0,1:T(8,128)(2,1)S(1)}, bf16[1,4,8,2048]{3,2,0,1:T(8,128)(2,1)S(1)}, u32[]{:S(2)}, u32[]{:S(2)}) %collective-permute-start.15) | collective-permute-done | bytes 131104 | tf_op jit(solution)/shard_map/ppermute | solution.py:64
  289.9 2.2 copy.67
  292.9 3.9 %all-to-all-start.3 = ((bf16[2,4,8,2048]{3,2,0,1:T(8,128)(2,1)}), bf16[2,4,8,2048]{3,2,0,1:T(8,128)(2,1)S(1)}, u32[]{:S(2)}, u32[]{:S(2)}) async-start(bf16[2,4,8,2048]{3,2,0,1:T(8,128)(2,1)} %select_convert_fusion), calls=%async_computation.3 | async-start | bytes 524288 | tf_op jit(solution)/shard_map/all_to_all | solution.py:213
  296.8 7.9 %copy.68 = bf16[8,2,256,4,128]{4,3,2,1,0:T(4,128)(2,1)} copy(bf16[8,2,256,4,128]{4,2,3,1,0:T(8,128)(2,1)} %bitcast.164) | data formatting | bytes 8388608
  305.4 1.5 gather_fusion.8
  (153 shorter events, 36.5 us)
Async XLA Ops:
  7.2 97.4 %copy-start = (bf16[2048,4,192]{0,2,1:T(8,128)(2,1)S(1)}, bf16[2048,4,192]{0,2,1:T(8,128)(2,1)}, u32[]{:S(2)}) copy-start(bf16[2048,4,192]{0,2,1:T(8,128)(2,1)} %param.24) | copy-start | bytes 9437188
  12.4 9.3 %all-to-all-start = ((bf16[8,8,2048]{2,1,0:T(8,128)(2,1)}), bf16[8,8,2048]{2,1,0:T(8,128)(2,1)S(1)}, u32[]{:S(2)}, u32[]{:S(2)}) async-start(bf16[8,8,2048]{2,1,0:T(8,128)(2,1)} %broadcast_select_fusion.2), calls=%async_computation | async-start | bytes 524288 | tf_op jit(solution)/shard_map/all_to_all | solution.py:154
  16.7 84.1 %all-gather.2.cloned.1.call-start = ((), (), s32[]{:S(2)}) async-start(), calls=%async_computation.4 | async-start | bytes 2359296 | tf_op jit(solution)/shard_map/all_gather | solution.py:157
  21.7 0.7 copy-start.7
  36.0 6.4 %copy-start.19 = (s32[8]{0:T(128)S(1)}, s32[8]{0:T(128)}, u32[]{:S(2)}) copy-start(s32[8]{0:T(128)} %param.22) | copy-start | bytes 100
  36.0 6.5 %copy-start.2 = (s32[8]{0:T(128)S(1)}, s32[8]{0:T(128)}, u32[]{:S(2)}) copy-start(s32[8]{0:T(128)} %param.21) | copy-start | bytes 100
  36.0 7.1 %copy-start.3 = (s32[8]{0:T(128)S(1)}, s32[8]{0:T(128)}, u32[]{:S(2)}) copy-start(s32[8]{0:T(128)} %param.20) | copy-start | bytes 100
  36.0 7.8 %copy-start.15 = (bf16[2048]{0:T(1024)(128)(2,1)S(1)}, bf16[2048]{0:T(1024)(128)(2,1)}, u32[]{:S(2)}) copy-start(bf16[2048]{0:T(1024)(128)(2,1)} %param.23) | copy-start | bytes 12292
  36.0 72.8 %all-to-all-start.1 = ((bf16[32,2,32,4,128]{4,2,3,1,0:T(8,128)(2,1)}), bf16[32,2,32,4,128]{4,2,3,1,0:T(8,128)(2,1)}, u32[]{:S(2)}, u32[]{:S(2)}) async-start(bf16[32,2,32,4,128]{4,2,3,1,0:T(8,128)(2,1)} %bitcast.165), calls=%async_computation.1 | async-start | bytes 4194304 | tf_op jit(solution)/shard_map/all_to_all | solution.py:147
  100.8 2.2 copy-start.4
  106.4 0.9 copy-start.14
  107.3 2.8 copy-start.13
  107.3 2.8 copy-start.21
  112.0 2.4 copy-start.12
  114.4 2.0 copy-start.22
  116.4 2.4 copy-start.10
  119.8 2.7 copy-start.23
  119.8 2.7 copy-start.20
  119.9 13.6 %collective-permute-start = (bf16[2,4,2,8,2048]{4,3,1,0,2:T(8,128)(2,1)S(1)}, bf16[2,4,2,8,2048]{4,3,1,0,2:T(8,128)(2,1)S(1)}, u32[]{:S(2)}, u32[]{:S(2)}) collective-permute-start(bf16[2,4,2,8,2048]{4,3,1,0,2:T(8,128)(2,1)S(1)} %bitcast.188), channel_id=1, source_target_pairs={{0,1},{1,2},{2,3},{3,0},{4,5},{5,6},{6,7},{7,4},{8,9},{9,10},{10,1... | collective-permute-start | bytes 1572872 | tf_op jit(solution)/shard_map/ppermute | solution.py:58
  121.1 13.4 %collective-permute-start.1 = (bf16[2,4,2,8,2048]{4,3,1,0,2:T(8,128)(2,1)S(1)}, bf16[2,4,2,8,2048]{4,3,1,0,2:T(8,128)(2,1)S(1)}, u32[]{:S(2)}, u32[]{:S(2)}) collective-permute-start(bf16[2,4,2,8,2048]{4,3,1,0,2:T(8,128)(2,1)S(1)} %bitcast.189), channel_id=1, source_target_pairs={{0,2},{1,3},{2,0},{3,1},{4,6},{5,7},{6,4},{7,5},{8,10},{9,11},{10,... | collective-permute-start | bytes 1572872 | tf_op jit(solution)/shard_map/ppermute | solution.py:58
  121.2 24.7 %collective-permute-start.2 = (bf16[2,4,2,8,2048]{4,3,1,0,2:T(8,128)(2,1)S(1)}, bf16[2,4,2,8,2048]{4,3,1,0,2:T(8,128)(2,1)S(1)}, u32[]{:S(2)}, u32[]{:S(2)}) collective-permute-start(bf16[2,4,2,8,2048]{4,3,1,0,2:T(8,128)(2,1)S(1)} %bitcast.190), channel_id=1, source_target_pairs={{0,3},{1,0},{2,1},{3,2},{4,7},{5,4},{6,5},{7,6},{8,11},{9,8},{10,9... | collective-permute-start | bytes 1572872 | tf_op jit(solution)/shard_map/ppermute | solution.py:58
  145.9 0.7 copy-start.16
  145.9 0.7 copy-start.18
  146.2 1.0 copy-start.6
  146.3 14.5 %collective-permute-start.3 = (bf16[2,4,8,2048]{3,2,0,1:T(8,128)(2,1)S(1)}, bf16[2,4,8,2048]{3,2,0,1:T(8,128)(2,1)S(1)}, u32[]{:S(2)}, u32[]{:S(2)}) collective-permute-start(bf16[2,4,8,2048]{3,2,0,1:T(8,128)(2,1)S(1)} %copy.60), channel_id=1, source_target_pairs={{0,4},{1,5},{2,6},{3,7},{4,0},{5,1},{6,2},{7,3},{8,12},{9,13},{10,... | collective-permute-start | bytes 786440 | tf_op jit(solution)/shard_map/ppermute | solution.py:64
  147.2 13.6 %copy-start.8 = (bf16[8,8,2048]{2,1,0:T(8,128)(2,1)S(1)}, bf16[8,8,2048]{2,1,0:T(8,128)(2,1)}, u32[]{:S(2)}) copy-start(bf16[8,8,2048]{2,1,0:T(8,128)(2,1)} %copy-done.7) | copy-start | bytes 786436
  162.0 16.6 %copy-start.17 = (pred[2]{0:T(512)(128)(4,1)S(1)}, pred[2]{0:T(512)(128)(4,1)}, u32[]{:S(2)}) copy-start(pred[2]{0:T(512)(128)(4,1)} %compare_and_fusion.3) | copy-start | bytes 10
  162.4 13.7 %collective-permute-start.4 = (bf16[2,4,8,2048]{3,2,0,1:T(8,128)(2,1)S(1)}, bf16[2,4,8,2048]{3,2,0,1:T(8,128)(2,1)S(1)}, u32[]{:S(2)}, u32[]{:S(2)}) collective-permute-start(bf16[2,4,8,2048]{3,2,0,1:T(8,128)(2,1)S(1)} %multiply_convert_fusion), channel_id=1, source_target_pairs={{0,4},{1,5},{2,6},{3,7},{4,0},{5,1},{6,2},{7,3},{8,12},{9,13},{10,... | collective-permute-start | bytes 786440 | tf_op jit(solution)/shard_map/ppermute | solution.py:76
  178.8 14.0 %collective-permute-start.5 = (bf16[2,2,4,8,2048]{4,3,1,2,0:T(8,128)(2,1)S(1)}, bf16[2,2,4,8,2048]{4,3,1,2,0:T(8,128)(2,1)S(1)}, u32[]{:S(2)}, u32[]{:S(2)}) collective-permute-start(bf16[2,2,4,8,2048]{4,3,1,2,0:T(8,128)(2,1)S(1)} %broadcast_select_fusion), channel_id=1, source_target_pairs={{0,1},{1,2},{2,3},{3,0},{4,5},{5,6},{6,7},{7,4},{8,9},{9,10},{10,1... | collective-permute-start | bytes 1572872 | tf_op jit(solution)/shard_map/ppermute | solution.py:81
  178.8 13.9 %collective-permute-start.6 = (bf16[2,2,4,8,2048]{4,3,1,2,0:T(8,128)(2,1)S(1)}, bf16[2,2,4,8,2048]{4,3,1,2,0:T(8,128)(2,1)S(1)}, u32[]{:S(2)}, u32[]{:S(2)}) collective-permute-start(bf16[2,2,4,8,2048]{4,3,1,2,0:T(8,128)(2,1)S(1)} %broadcast_select_fusion), channel_id=1, source_target_pairs={{0,2},{1,3},{2,0},{3,1},{4,6},{5,7},{6,4},{7,5},{8,10},{9,11},{10,... | collective-permute-start | bytes 1572872 | tf_op jit(solution)/shard_map/ppermute | solution.py:81
  178.9 25.9 %collective-permute-start.7 = (bf16[2,2,4,8,2048]{4,3,1,2,0:T(8,128)(2,1)S(1)}, bf16[2,2,4,8,2048]{4,3,1,2,0:T(8,128)(2,1)S(1)}, u32[]{:S(2)}, u32[]{:S(2)}) collective-permute-start(bf16[2,2,4,8,2048]{4,3,1,2,0:T(8,128)(2,1)S(1)} %broadcast_select_fusion), channel_id=1, source_target_pairs={{0,3},{1,0},{2,1},{3,2},{4,7},{5,4},{6,5},{7,6},{8,11},{9,8},{10,9... | collective-permute-start | bytes 1572872 | tf_op jit(solution)/shard_map/ppermute | solution.py:81
  219.0 1.6 copy-start.11
  219.1 20.3 %collective-permute-start.10 = (bf16[1,4,2,8,2048]{4,3,2,1,0:T(8,128)(2,1)S(1)}, bf16[1,4,2,8,2048]{4,3,2,1,0:T(8,128)(2,1)}, u32[]{:S(2)}, u32[]{:S(2)}) collective-permute-start(bf16[1,4,2,8,2048]{4,3,2,1,0:T(8,128)(2,1)S(1)} %get-tuple-element.38), channel_id=1, source_target_pairs={{0,3},{1,0},{2,1},{3,2},{4,7},{5,4},{6,5},{7,6},{8,11},{9,8},{10,9... | collective-permute-start | bytes 786440 | tf_op jit(solution)/shard_map/ppermute | solution.py:58
  219.1 21.4 %collective-permute-start.8 = (bf16[1,4,2,8,2048]{4,3,2,1,0:T(8,128)(2,1)S(1)}, bf16[1,4,2,8,2048]{4,3,2,1,0:T(8,128)(2,1)}, u32[]{:S(2)}, u32[]{:S(2)}) collective-permute-start(bf16[1,4,2,8,2048]{4,3,2,1,0:T(8,128)(2,1)S(1)} %get-tuple-element.37), channel_id=1, source_target_pairs={{0,1},{1,2},{2,3},{3,0},{4,5},{5,6},{6,7},{7,4},{8,9},{9,10},{10,1... | collective-permute-start | bytes 786440 | tf_op jit(solution)/shard_map/ppermute | solution.py:58
  220.6 20.0 %collective-permute-start.9 = (bf16[1,4,2,8,2048]{4,3,2,1,0:T(8,128)(2,1)S(1)}, bf16[1,4,2,8,2048]{4,3,2,1,0:T(8,128)(2,1)}, u32[]{:S(2)}, u32[]{:S(2)}) collective-permute-start(bf16[1,4,2,8,2048]{4,3,2,1,0:T(8,128)(2,1)S(1)} %get-tuple-element.39), channel_id=1, source_target_pairs={{0,2},{1,3},{2,0},{3,1},{4,6},{5,7},{6,4},{7,5},{8,10},{9,11},{10,... | collective-permute-start | bytes 786440 | tf_op jit(solution)/shard_map/ppermute | solution.py:58
  220.6 67.3 %all-to-all-start.2 = ((bf16[32,2,32,4,128]{4,2,3,1,0:T(8,128)(2,1)}), bf16[32,2,32,4,128]{4,2,3,1,0:T(8,128)(2,1)S(1)}, u32[]{:S(2)}, u32[]{:S(2)}) async-start(bf16[32,2,32,4,128]{4,2,3,1,0:T(8,128)(2,1)} %bitcast.44), calls=%async_computation.2 | async-start | bytes 4194304 | tf_op jit(solution)/shard_map/all_to_all | solution.py:188
  236.8 34.0 %collective-permute-start.12 = (bf16[1,4,2,8,2048]{4,3,2,1,0:T(8,128)(2,1)S(1)}, bf16[1,4,2,8,2048]{4,3,2,1,0:T(8,128)(2,1)S(1)}, u32[]{:S(2)}, u32[]{:S(2)}) collective-permute-start(bf16[1,4,2,8,2048]{4,3,2,1,0:T(8,128)(2,1)S(1)} %get-tuple-element.40), channel_id=1, source_target_pairs={{0,1},{1,2},{2,3},{3,0},{4,5},{5,6},{6,7},{7,4},{8,9},{9,10},{10,1... | collective-permute-start | bytes 786440 | tf_op jit(solution)/shard_map/ppermute | solution.py:58
  238.2 32.6 %collective-permute-start.13 = (bf16[1,4,2,8,2048]{4,3,2,1,0:T(8,128)(2,1)S(1)}, bf16[1,4,2,8,2048]{4,3,2,1,0:T(8,128)(2,1)S(1)}, u32[]{:S(2)}, u32[]{:S(2)}) collective-permute-start(bf16[1,4,2,8,2048]{4,3,2,1,0:T(8,128)(2,1)S(1)} %get-tuple-element.42), channel_id=1, source_target_pairs={{0,2},{1,3},{2,0},{3,1},{4,6},{5,7},{6,4},{7,5},{8,10},{9,11},{10,... | collective-permute-start | bytes 786440 | tf_op jit(solution)/shard_map/ppermute | solution.py:58
  239.4 35.5 %collective-permute-start.14 = (bf16[1,4,2,8,2048]{4,3,2,1,0:T(8,128)(2,1)S(1)}, bf16[1,4,2,8,2048]{4,3,2,1,0:T(8,128)(2,1)S(1)}, u32[]{:S(2)}, u32[]{:S(2)}) collective-permute-start(bf16[1,4,2,8,2048]{4,3,2,1,0:T(8,128)(2,1)S(1)} %get-tuple-element.41), channel_id=1, source_target_pairs={{0,3},{1,0},{2,1},{3,2},{4,7},{5,4},{6,5},{7,6},{8,11},{9,8},{10,9... | collective-permute-start | bytes 786440 | tf_op jit(solution)/shard_map/ppermute | solution.py:58
  241.9 37.6 %collective-permute-start.11 = (bf16[1,4,8,2048]{3,2,0,1:T(8,128)(2,1)S(1)}, bf16[1,4,8,2048]{3,2,0,1:T(8,128)(2,1)S(1)}, u32[]{:S(2)}, u32[]{:S(2)}) collective-permute-start(bf16[1,4,8,2048]{3,2,0,1:T(8,128)(2,1)S(1)} %fusion.110), channel_id=1, source_target_pairs={{0,4},{1,5},{2,6},{3,7},{4,0},{5,1},{6,2},{7,3},{8,12},{9,13},{10,... | collective-permute-start | bytes 393224 | tf_op jit(solution)/shard_map/ppermute | solution.py:64
  276.0 11.8 %collective-permute-start.15 = (bf16[1,4,8,2048]{3,2,0,1:T(8,128)(2,1)S(1)}, bf16[1,4,8,2048]{3,2,0,1:T(8,128)(2,1)S(1)}, u32[]{:S(2)}, u32[]{:S(2)}) collective-permute-start(bf16[1,4,8,2048]{3,2,0,1:T(8,128)(2,1)S(1)} %fusion.111), channel_id=1, source_target_pairs={{0,4},{1,5},{2,6},{3,7},{4,0},{5,1},{6,2},{7,3},{8,12},{9,13},{10,... | collective-permute-start | bytes 393224 | tf_op jit(solution)/shard_map/ppermute | solution.py:64
  287.9 1.6 copy-start.5
  292.9 11.8 %all-to-all-start.3 = ((bf16[2,4,8,2048]{3,2,0,1:T(8,128)(2,1)}), bf16[2,4,8,2048]{3,2,0,1:T(8,128)(2,1)S(1)}, u32[]{:S(2)}, u32[]{:S(2)}) async-start(bf16[2,4,8,2048]{3,2,0,1:T(8,128)(2,1)} %select_convert_fusion), calls=%async_computation.3 | async-start | bytes 524288 | tf_op jit(solution)/shard_map/all_to_all | solution.py:213
  296.8 10.9 %copy-start.1 = (bf16[2048,4,192]{0,2,1:T(8,128)(2,1)S(1)}, bf16[2048,4,192]{0,2,1:T(8,128)(2,1)}, u32[]{:S(2)}) copy-start(bf16[2048,4,192]{0,2,1:T(8,128)(2,1)} %param.24) | copy-start | bytes 9437188
  304.7 0.7 copy-start.9
Sparse Core Ops, SparseCore 0:
  22.6 78.1 all-gather.1

commit v19 on v18

--- a/solution.py
+++ b/solution.py
@@ -166,20 +166,18 @@
         preferred_element_type=jnp.float32,
     )
     mixed = mixed.reshape(group_size, stretch_max, heads_here, 3 * head_dim).astype(jnp.bfloat16)
-    contexts = []
+    attn_sums = []
     for member in range(group_size):
         pairs = jnp.concatenate([current[member], mixed[member, :, :, head_dim:]], axis=0)
-        contexts.append(
-            attend(mixed[member, :, :, :head_dim], pairs, member_prefix[member], slopes, head_dim)
-        )
-    context = jnp.concatenate(contexts, axis=0)
-    partial_attn = jnp.dot(
-        context,
-        out_weight.reshape(heads_here * head_dim, features),
-        preferred_element_type=jnp.float32,
-    )
-    partial_attn = partial_attn.reshape(group_size, req_count, span_rows, features)
-    attn_rows = head_sum(partial_attn, head_count, stretch_rows)
+        context = attend(mixed[member, :, :, :head_dim], pairs, member_prefix[member], slopes, head_dim)
+        partial_attn = jnp.dot(
+            context,
+            out_weight.reshape(heads_here * head_dim, features),
+            preferred_element_type=jnp.float32,
+        )
+        partial_attn = partial_attn.reshape(1, req_count, span_rows, features)
+        attn_sums.append(head_sum(partial_attn, head_count, stretch_rows))
+    attn_rows = jnp.concatenate(attn_sums, axis=0)
     residual_rows = dealt_rows.astype(jnp.float32) + attn_rows
     normed_rows = layer_norm(residual_rows, mlp_gain).astype(jnp.bfloat16)
     normed_all = head_gather(normed_rows, head_count)

time: 317 us -> 316 us (level)
  waiting for transfers between devices: 157 us -> 140 us
  starting transfers between devices: 36.3 us -> 44.3 us
  local copies, waits for them, and re-layouts: 50.5 us -> 54.2 us
    ppermute x9 -> x12, waiting for transfers between devices: 54 us -> 39.5 us  [head_sum(): lax.ppermute(sent, 'head', pairs).astype(jnp.float32)]
    all_gather x1, waiting for transfers between devices: 47.2 us -> 58 us  [local(): gathered = lax.all_gather(dealt_rows, 'head', axis=2, tiled=True)]
    ppermute x9 -> x12, starting transfers between devices: 7.86 us -> 13.4 us  [head_sum(): lax.ppermute(sent, 'head', pairs).astype(jnp.float32)]
    all_to_all x1, waiting for transfers between devices: 5.06 us -> 0.01 us  [local(): lax.all_to_all(dealt_acts, 'req', split_axis=0, concat_axis=1, tiled=True)]
    ppermute x3 -> x4, waiting for transfers between devices: 19.3 us -> 15 us  [head_sum(): total = total + lax.ppermute(sent, 'head', pairs).astype(jnp.float32)]
    all_to_all x1, starting transfers between devices: 3.87 us -> 7.65 us  [local(): lax.all_to_all(result, 'req', split_axis=1, concat_axis=0, tiled=True)]
    unnamed x49 -> x63, local copies, waits for them, and re-layouts: 12.1 us -> 10.7 us
  transfers between devices with their start and end apart: 21 -> 25, of which waited for: 13 -> 14; matrix products, arithmetic and copies ran while one was open for 19% -> 23% of each run, Pallas kernels for 0% -> 0%
where the time goes in v19:
time: 316 us; the launch traced here: 312 us
  waiting for transfers between devices  140 us (44%)
  local copies, waits for them, and re-layouts  54.2 us (17%)
  starting transfers between devices  44.3 us (14%)
  other arithmetic  29.5 us (9%)
  matrix products  28.8 us (9%)
  between operations  14.8 us (5%)
    all_gather x1, waiting for transfers between devices, local(): gathered = lax.all_gather(dealt_rows, 'head', axis=2, tiled=True)  58 us
    ppermute x12, waiting for transfers between devices, head_sum(): lax.ppermute(sent, 'head', pairs).astype(jnp.float32)  39.5 us
    dot_general x2, matrix products, local(): jnp.dot(inner, down_weight, preferred_element_type=jnp.float32)  17.6 us
    ppermute x3, waiting for transfers between devices, head_gather(): held.append(lax.ppermute(by_outer, 'head', pairs))  15.6 us
    ppermute x4, waiting for transfers between devices, head_sum(): total = total + lax.ppermute(sent, 'head', pairs).astype(jnp.float32)  15 us
    ppermute x12, starting transfers between devices, head_sum(): lax.ppermute(sent, 'head', pairs).astype(jnp.float32)  13.4 us
    ppermute x1, waiting for transfers between devices, head_gather(): held.append(lax.ppermute(rows, 'head', pairs))  12 us
    unnamed x63, local copies, waits for them, and re-layouts  10.7 us
  transfers between devices with their start and end apart: 25, of which 14 were waited for; matrix products, arithmetic and copies ran while one was open for 23% of the time, Pallas kernels for 0%

profile of v19, /device:TPU:1, one launch (start us, length us, event | category | flops | bytes accessed | tf_op | source)
XLA Modules:
  0.0 311.8 jit_solution(17273246853366420590)
XLA Ops:
  8.0 1.4 gather_fusion
  10.1 1.5 gather_fusion.4
  12.4 4.3 %all-to-all-start = ((bf16[8,8,2048]{2,1,0:T(8,128)(2,1)}), bf16[8,8,2048]{2,1,0:T(8,128)(2,1)S(1)}, u32[]{:S(2)}, u32[]{:S(2)}) async-start(bf16[8,8,2048]{2,1,0:T(8,128)(2,1)} %broadcast_select_fusion.2), calls=%async_computation | async-start | bytes 524288 | tf_op jit(solution)/shard_map/all_to_all | solution.py:154
  16.7 5.2 %fusion.211 = (bf16[1,8,32,32,128]{4,3,2,1,0:T(8,128)(2,1)}, bf16[8,32,32,128]{3,2,1,0:T(8,128)(2,1)}) fusion(bf16[2,8,32,32,128]{4,3,2,1,0:T(8,128)(2,1)} %param.19), kind=kLoop, calls=%fused_computation.339 | loop fusion | bytes 8388608 | tf_op jit(solution)/shard_map/slice | solution.py:133
  21.9 3.8 %gather_fusion.5 = bf16[8,32,32,128]{3,2,1,0:T(8,128)(2,1)} fusion(bf16[8,32,32,128]{3,2,1,0:T(8,128)(2,1)} %get-tuple-element.30, s32[1024]{0:T(1024)S(1)} %pad_clamp_fusion.3), kind=kCustom, calls=%fused_computation.2.clone | custom fusion | bytes 4194336 | tf_op jit(solution)/shard_map/jit(_take)/gather | solution.py:138
  26.5 1.8 select_select_fusion.1
  29.1 1.8 copy.75
  30.9 6.8 %all-to-all-start.1 = ((bf16[32,2,32,4,128]{4,2,3,1,0:T(8,128)(2,1)}), bf16[32,2,32,4,128]{4,2,3,1,0:T(8,128)(2,1)}, u32[]{:S(2)}, u32[]{:S(2)}) async-start(bf16[32,2,32,4,128]{4,2,3,1,0:T(8,128)(2,1)} %bitcast.194), calls=%async_computation.1 | async-start | bytes 4194304 | tf_op jit(solution)/shard_map/all_to_all | solution.py:147
  51.1 58.0 %all-gather.2.cloned.1.call-done = bf16[2,4,64,2048]{3,2,1,0:T(8,128)(2,1)} async-done(((bf16[2,4,8,2048]{3,2,1,0:T(8,128)(2,1)}), bf16[2,4,64,2048]{3,2,1,0:T(8,128)(2,1)}) %all-gather.2.cloned.1.call-update) | async-done | bytes 2097168 | tf_op jit(solution)/shard_map/all_gather | solution.py:157
  109.1 2.1 convert_reduce_fusion
  112.7 1.8 fusion.9
  117.5 2.0 fusion.216
  119.4 2.2 fusion.12
  123.3 2.4 collective-permute-start.2
  125.9 2.1 fusion.215
  128.0 2.2 fusion.13
  133.2 2.7 gather_fusion.7
  135.9 2.4 collective-permute-start.6
  139.2 1.3 fusion.43
  140.6 4.1 %collective-permute-done.4 = bf16[1,4,2,8,2048]{4,3,2,1,0:T(8,128)(2,1)} collective-permute-done((bf16[1,4,2,8,2048]{4,3,2,1,0:T(8,128)(2,1)}, bf16[1,4,2,8,2048]{4,3,2,1,0:T(8,128)(2,1)}, u32[]{:S(2)}, u32[]{:S(2)}) %collective-permute-start.4) | collective-permute-done | bytes 262176 | tf_op jit(solution)/shard_map/ppermute | solution.py:58
  144.7 4.7 %collective-permute-done.6 = bf16[1,4,2,8,2048]{4,3,2,1,0:T(8,128)(2,1)S(1)} collective-permute-done((bf16[1,4,2,8,2048]{4,3,2,1,0:T(8,128)(2,1)S(1)}, bf16[1,4,2,8,2048]{4,3,2,1,0:T(8,128)(2,1)S(1)}, u32[]{:S(2)}, u32[]{:S(2)}) %collective-permute-start.6) | collective-permute-done | bytes 262176 | tf_op jit(solution)/shard_map/ppermute | solution.py:58
  150.8 8.8 %collective-permute-done.7 = bf16[1,4,8,2048]{3,2,1,0:T(8,128)(2,1)S(1)} collective-permute-done((bf16[1,4,8,2048]{3,2,1,0:T(8,128)(2,1)S(1)}, bf16[1,4,8,2048]{3,2,1,0:T(8,128)(2,1)S(1)}, u32[]{:S(2)}, u32[]{:S(2)}) %collective-permute-start.7) | collective-permute-done | bytes 131104 | tf_op jit(solution)/shard_map/ppermute | solution.py:64
  160.4 12.0 %collective-permute-done.8 = bf16[2,4,8,2048]{3,2,1,0:T(8,128)(2,1)S(1)} collective-permute-done((bf16[2,4,8,2048]{3,2,1,0:T(8,128)(2,1)S(1)}, bf16[2,4,8,2048]{3,2,1,0:T(8,128)(2,1)S(1)}, u32[]{:S(2)}, u32[]{:S(2)}) %collective-permute-start.8) | collective-permute-done | bytes 262176 | tf_op jit(solution)/shard_map/ppermute | solution.py:76
  173.3 1.7 gather_fusion.1
  175.2 2.2 collective-permute-start.9
  179.1 3.5 %copy.82 = bf16[4,2,8,32,4,128]{5,3,2,4,1,0:T(8,128)(2,1)} copy(bf16[4,2,8,32,4,128]{5,3,4,1,2,0:T(8,128)(2,1)} %bitcast.7) | data formatting | bytes 4194304 | tf_op jit(solution)/shard_map/transpose | solution.py:89
  183.5 2.0 copy.84
  185.6 3.6 %collective-permute-done.9 = bf16[2,2,4,8,2048]{4,3,2,1,0:T(8,128)(2,1)S(1)} collective-permute-done((bf16[2,2,4,8,2048]{4,3,2,1,0:T(8,128)(2,1)S(1)}, bf16[2,2,4,8,2048]{4,3,2,1,0:T(8,128)(2,1)S(1)}, u32[]{:S(2)}, u32[]{:S(2)}) %collective-permute-start.9) | collective-permute-done | bytes 524320 | tf_op jit(solution)/shard_map/ppermute | solution.py:81
  190.1 11.1 %collective-permute-done.11 = bf16[2,2,4,8,2048]{4,3,2,1,0:T(8,128)(2,1)S(1)} collective-permute-done((bf16[2,2,4,8,2048]{4,3,2,1,0:T(8,128)(2,1)S(1)}, bf16[2,2,4,8,2048]{4,3,2,1,0:T(8,128)(2,1)S(1)}, u32[]{:S(2)}, u32[]{:S(2)}) %collective-permute-start.11) | collective-permute-done | bytes 524320 | tf_op jit(solution)/shard_map/ppermute | solution.py:81
  201.5 2.1 gather_fusion.2
  203.6 1.9 select_bitcast_fusion
  205.6 1.6 fusion.212
  207.2 8.3 %convolution_convert_fusion.1 = bf16[256,2048]{1,0:T(8,128)(2,1)S(1)} fusion(bf16[1024,2048]{1,0:T(8,128)(2,1)} %param.29, bf16[256,2048]{1,0:T(8,128)(2,1)} %bitcast.217, bf16[2048,1024]{1,0:T(8,128)(2,1)} %param.28), kind=kOutput, calls=%fused_computation.22 | convolution fusion | flops 2165047296 | bytes 10485760 | tf_op jit(solution)/shard_map/dot_general | solution.py:198
  216.4 1.3 collective-permute-start.12
  218.1 1.7 collective-permute-start.14
  219.8 5.0 %all-to-all-start.2 = ((bf16[32,2,32,4,128]{4,2,3,1,0:T(8,128)(2,1)}), bf16[32,2,32,4,128]{4,2,3,1,0:T(8,128)(2,1)S(1)}, u32[]{:S(2)}, u32[]{:S(2)}) async-start(bf16[32,2,32,4,128]{4,2,3,1,0:T(8,128)(2,1)} %bitcast.47), calls=%async_computation.2 | async-start | bytes 4194304 | tf_op jit(solution)/shard_map/all_to_all | solution.py:186
  224.8 9.3 %convolution_convert_fusion = bf16[256,2048]{1,0:T(8,128)(2,1)} fusion(bf16[1024,2048]{1,0:T(8,128)(2,1)} %param.29, bf16[256,2048]{1,0:T(8,128)(2,1)} %bitcast.216, bf16[2048,1024]{1,0:T(8,128)(2,1)} %param.28), kind=kOutput, calls=%fused_computation.21 | convolution fusion | flops 2165047296 | bytes 10485760 | tf_op jit(solution)/shard_map/dot_general | solution.py:198
  235.3 1.4 collective-permute-start.16
  239.1 1.3 fusion.39
  240.5 3.3 %collective-permute-start.15 = (bf16[1,4,8,2048]{3,2,1,0:T(8,128)(2,1)S(1)}, bf16[1,4,8,2048]{3,2,1,0:T(8,128)(2,1)S(1)}, u32[]{:S(2)}, u32[]{:S(2)}) collective-permute-start(bf16[1,4,8,2048]{3,2,1,0:T(8,128)(2,1)S(1)} %fusion.116), channel_id=1, source_target_pairs={{0,4},{1,5},{2,6},{3,7},{4,0},{5,1},{6,2},{7,3},{8,12},{9,13},{10,... | collective-permute-start | bytes 393224 | tf_op jit(solution)/shard_map/ppermute | solution.py:64
  243.8 23.5 %collective-permute-done.16 = bf16[1,4,2,8,2048]{4,3,2,1,0:T(8,128)(2,1)S(1)} collective-permute-done((bf16[1,4,2,8,2048]{4,3,2,1,0:T(8,128)(2,1)S(1)}, bf16[1,4,2,8,2048]{4,3,2,1,0:T(8,128)(2,1)S(1)}, u32[]{:S(2)}, u32[]{:S(2)}) %collective-permute-start.16) | collective-permute-done | bytes 262176 | tf_op jit(solution)/shard_map/ppermute | solution.py:58
  268.0 5.6 %collective-permute-done.18 = bf16[1,4,2,8,2048]{4,3,2,1,0:T(8,128)(2,1)S(1)} collective-permute-done((bf16[1,4,2,8,2048]{4,3,2,1,0:T(8,128)(2,1)S(1)}, bf16[1,4,2,8,2048]{4,3,2,1,0:T(8,128)(2,1)S(1)}, u32[]{:S(2)}, u32[]{:S(2)}) %collective-permute-start.18) | collective-permute-done | bytes 262176 | tf_op jit(solution)/shard_map/ppermute | solution.py:58
  274.8 1.6 collective-permute-done.15
  276.4 4.6 %collective-permute-done.19 = bf16[1,4,8,2048]{3,2,1,0:T(8,128)(2,1)S(1)} collective-permute-done((bf16[1,4,8,2048]{3,2,1,0:T(8,128)(2,1)S(1)}, bf16[1,4,8,2048]{3,2,1,0:T(8,128)(2,1)S(1)}, u32[]{:S(2)}, u32[]{:S(2)}) %collective-permute-start.19) | collective-permute-done | bytes 131104 | tf_op jit(solution)/shard_map/ppermute | solution.py:64
  283.1 2.2 copy.87
  286.2 7.6 %all-to-all-start.3 = ((bf16[2,4,8,2048]{3,2,0,1:T(8,128)(2,1)}), bf16[2,4,8,2048]{3,2,0,1:T(8,128)(2,1)S(1)}, u32[]{:S(2)}, u32[]{:S(2)}) async-start(bf16[2,4,8,2048]{3,2,0,1:T(8,128)(2,1)} %copy.88), calls=%async_computation.3 | async-start | bytes 524288 | tf_op jit(solution)/shard_map/all_to_all | solution.py:211
  293.9 7.9 %copy.89 = bf16[8,2,256,4,128]{4,3,2,1,0:T(4,128)(2,1)} copy(bf16[8,2,256,4,128]{4,2,3,1,0:T(8,128)(2,1)} %bitcast.191) | data formatting | bytes 8388608
  302.5 1.6 gather_fusion.8
  (178 shorter events, 45.4 us)
Async XLA Ops:
  7.2 105.6 %copy-start = (bf16[2048,4,192]{0,2,1:T(8,128)(2,1)S(1)}, bf16[2048,4,192]{0,2,1:T(8,128)(2,1)}, u32[]{:S(2)}) copy-start(bf16[2048,4,192]{0,2,1:T(8,128)(2,1)} %param.24) | copy-start | bytes 9437188
  8.0 13.9 %copy-start.19 = (s32[1024]{0:T(1024)}, s32[1024]{0:T(1024)S(1)}, u32[]{:S(2)}) copy-start(s32[1024]{0:T(1024)S(1)} %pad_clamp_fusion.3) | copy-start | bytes 12292
  10.1 16.3 %copy-start.20 = (pred[8]{0:T(512)(128)(4,1)}, pred[8]{0:T(512)(128)(4,1)S(1)}, u32[]{:S(2)}) copy-start(pred[8]{0:T(512)(128)(4,1)S(1)} %get-tuple-element.28) | copy-start | bytes 28
  12.4 13.3 %all-to-all-start = ((bf16[8,8,2048]{2,1,0:T(8,128)(2,1)}), bf16[8,8,2048]{2,1,0:T(8,128)(2,1)S(1)}, u32[]{:S(2)}, u32[]{:S(2)}) async-start(bf16[8,8,2048]{2,1,0:T(8,128)(2,1)} %broadcast_select_fusion.2), calls=%async_computation | async-start | bytes 524288 | tf_op jit(solution)/shard_map/all_to_all | solution.py:154
  16.7 92.4 %all-gather.2.cloned.1.call-start = ((), (), s32[]{:S(2)}) async-start(), calls=%async_computation.4 | async-start | bytes 2359296 | tf_op jit(solution)/shard_map/all_gather | solution.py:157
  25.7 2.6 copy-start.17
  30.9 6.9 %copy-start.26 = (s32[8]{0:T(128)S(1)}, s32[8]{0:T(128)}, u32[]{:S(2)}) copy-start(s32[8]{0:T(128)} %param.22) | copy-start | bytes 100
  30.9 7.0 %copy-start.2 = (s32[8]{0:T(128)S(1)}, s32[8]{0:T(128)}, u32[]{:S(2)}) copy-start(s32[8]{0:T(128)} %param.21) | copy-start | bytes 100
  30.9 7.7 %copy-start.3 = (s32[8]{0:T(128)S(1)}, s32[8]{0:T(128)}, u32[]{:S(2)}) copy-start(s32[8]{0:T(128)} %param.20) | copy-start | bytes 100
  30.9 8.3 %copy-start.22 = (bf16[2048]{0:T(1024)(128)(2,1)S(1)}, bf16[2048]{0:T(1024)(128)(2,1)}, u32[]{:S(2)}) copy-start(bf16[2048]{0:T(1024)(128)(2,1)} %param.23) | copy-start | bytes 12292
  30.9 8.3 %copy-start.23 = (bf16[2048]{0:T(1024)(128)(2,1)S(1)}, bf16[2048]{0:T(1024)(128)(2,1)}, u32[]{:S(2)}) copy-start(bf16[2048]{0:T(1024)(128)(2,1)} %param.27) | copy-start | bytes 12292
  30.9 85.2 %all-to-all-start.1 = ((bf16[32,2,32,4,128]{4,2,3,1,0:T(8,128)(2,1)}), bf16[32,2,32,4,128]{4,2,3,1,0:T(8,128)(2,1)}, u32[]{:S(2)}, u32[]{:S(2)}) async-start(bf16[32,2,32,4,128]{4,2,3,1,0:T(8,128)(2,1)} %bitcast.194), calls=%async_computation.1 | async-start | bytes 4194304 | tf_op jit(solution)/shard_map/all_to_all | solution.py:147
  40.2 8.3 %copy-start.29 = (s32[8]{0:T(128)}, s32[8]{0:T(128)S(1)}, u32[]{:S(2)}) copy-start(s32[8]{0:T(128)S(1)} %get-tuple-element.17) | copy-start | bytes 100
  49.3 76.6 %copy-start.15 = (pred[256,512]{1,0:T(8,128)(4,1)}, pred[256,512]{1,0:T(8,128)(4,1)S(1)}, u32[]{:S(2)}) copy-start(pred[256,512]{1,0:T(8,128)(4,1)S(1)} %get-tuple-element.50) | copy-start | bytes 393220
  109.1 2.2 copy-start.4
  119.4 2.4 copy-start.6
  121.9 4.0 %copy-start.11 = (f32[256,512]{1,0:T(8,128)S(1)}, f32[256,512]{1,0:T(8,128)}, u32[]{:S(2)}) copy-start(f32[256,512]{1,0:T(8,128)} %subtract_convert_fusion) | copy-start | bytes 1572868
  122.3 5.7 %copy-start.7 = (bf16[4,64,2048]{2,1,0:T(8,128)(2,1)}, bf16[4,64,2048]{2,1,0:T(8,128)(2,1)S(1)}, u32[]{:S(2)}) copy-start(bf16[4,64,2048]{2,1,0:T(8,128)(2,1)S(1)} %convolution_convert_fusion.3) | copy-start | bytes 3145732
  123.3 12.6 %collective-permute-start = (bf16[1,4,2,8,2048]{4,3,2,1,0:T(8,128)(2,1)}, bf16[1,4,2,8,2048]{4,3,2,1,0:T(8,128)(2,1)}, u32[]{:S(2)}, u32[]{:S(2)}) collective-permute-start(bf16[1,4,2,8,2048]{4,3,2,1,0:T(8,128)(2,1)} %get-tuple-element.41), channel_id=1, source_target_pairs={{0,1},{1,2},{2,3},{3,0},{4,5},{5,6},{6,7},{7,4},{8,9},{9,10},{10,1... | collective-permute-start | bytes 786440 | tf_op jit(solution)/shard_map/ppermute | solution.py:58
  123.3 15.0 %collective-permute-start.1 = (bf16[1,4,2,8,2048]{4,3,2,1,0:T(8,128)(2,1)}, bf16[1,4,2,8,2048]{4,3,2,1,0:T(8,128)(2,1)}, u32[]{:S(2)}, u32[]{:S(2)}) collective-permute-start(bf16[1,4,2,8,2048]{4,3,2,1,0:T(8,128)(2,1)} %get-tuple-element.43), channel_id=1, source_target_pairs={{0,2},{1,3},{2,0},{3,1},{4,6},{5,7},{6,4},{7,5},{8,10},{9,11},{10,... | collective-permute-start | bytes 786440 | tf_op jit(solution)/shard_map/ppermute | solution.py:58
  123.3 15.8 %collective-permute-start.2 = (bf16[1,4,2,8,2048]{4,3,2,1,0:T(8,128)(2,1)}, bf16[1,4,2,8,2048]{4,3,2,1,0:T(8,128)(2,1)}, u32[]{:S(2)}, u32[]{:S(2)}) collective-permute-start(bf16[1,4,2,8,2048]{4,3,2,1,0:T(8,128)(2,1)} %get-tuple-element.42), channel_id=1, source_target_pairs={{0,3},{1,0},{2,1},{3,2},{4,7},{5,4},{6,5},{7,6},{8,11},{9,8},{10,9... | collective-permute-start | bytes 786440 | tf_op jit(solution)/shard_map/ppermute | solution.py:58
  130.9 2.4 copy-start.8
  131.8 12.9 %collective-permute-start.4 = (bf16[1,4,2,8,2048]{4,3,2,1,0:T(8,128)(2,1)}, bf16[1,4,2,8,2048]{4,3,2,1,0:T(8,128)(2,1)}, u32[]{:S(2)}, u32[]{:S(2)}) collective-permute-start(bf16[1,4,2,8,2048]{4,3,2,1,0:T(8,128)(2,1)} %get-tuple-element.44), channel_id=1, source_target_pairs={{0,1},{1,2},{2,3},{3,0},{4,5},{5,6},{6,7},{7,4},{8,9},{9,10},{10,1... | collective-permute-start | bytes 786440 | tf_op jit(solution)/shard_map/ppermute | solution.py:58
  132.0 12.7 %collective-permute-start.5 = (bf16[1,4,2,8,2048]{4,3,2,1,0:T(8,128)(2,1)S(1)}, bf16[1,4,2,8,2048]{4,3,2,1,0:T(8,128)(2,1)}, u32[]{:S(2)}, u32[]{:S(2)}) collective-permute-start(bf16[1,4,2,8,2048]{4,3,2,1,0:T(8,128)(2,1)S(1)} %get-tuple-element.46), channel_id=1, source_target_pairs={{0,2},{1,3},{2,0},{3,1},{4,6},{5,7},{6,4},{7,5},{8,10},{9,11},{10,... | collective-permute-start | bytes 786440 | tf_op jit(solution)/shard_map/ppermute | solution.py:58
  135.9 13.5 %collective-permute-start.6 = (bf16[1,4,2,8,2048]{4,3,2,1,0:T(8,128)(2,1)S(1)}, bf16[1,4,2,8,2048]{4,3,2,1,0:T(8,128)(2,1)S(1)}, u32[]{:S(2)}, u32[]{:S(2)}) collective-permute-start(bf16[1,4,2,8,2048]{4,3,2,1,0:T(8,128)(2,1)S(1)} %get-tuple-element.45), channel_id=1, source_target_pairs={{0,3},{1,0},{2,1},{3,2},{4,7},{5,4},{6,5},{7,6},{8,11},{9,8},{10,9... | collective-permute-start | bytes 786440 | tf_op jit(solution)/shard_map/ppermute | solution.py:58
  140.5 10.3 %collective-permute-start.3 = (bf16[1,4,8,2048]{3,2,1,0:T(8,128)(2,1)S(1)}, bf16[1,4,8,2048]{3,2,1,0:T(8,128)(2,1)S(1)}, u32[]{:S(2)}, u32[]{:S(2)}) collective-permute-start(bf16[1,4,8,2048]{3,2,1,0:T(8,128)(2,1)S(1)} %fusion.114), channel_id=1, source_target_pairs={{0,4},{1,5},{2,6},{3,7},{4,0},{5,1},{6,2},{7,3},{8,12},{9,13},{10,... | collective-permute-start | bytes 393224 | tf_op jit(solution)/shard_map/ppermute | solution.py:64
  150.7 8.9 %collective-permute-start.7 = (bf16[1,4,8,2048]{3,2,1,0:T(8,128)(2,1)S(1)}, bf16[1,4,8,2048]{3,2,1,0:T(8,128)(2,1)S(1)}, u32[]{:S(2)}, u32[]{:S(2)}) collective-permute-start(bf16[1,4,8,2048]{3,2,1,0:T(8,128)(2,1)S(1)} %fusion.115), channel_id=1, source_target_pairs={{0,4},{1,5},{2,6},{3,7},{4,0},{5,1},{6,2},{7,3},{8,12},{9,13},{10,... | collective-permute-start | bytes 393224 | tf_op jit(solution)/shard_map/ppermute | solution.py:64
  160.0 15.0 %copy-start.25 = (pred[2]{0:T(512)(128)(4,1)S(1)}, pred[2]{0:T(512)(128)(4,1)}, u32[]{:S(2)}) copy-start(pred[2]{0:T(512)(128)(4,1)} %compare_and_fusion.3) | copy-start | bytes 10
  160.2 18.5 %copy-start.18 = (pred[8,32]{1,0:T(8,128)(4,1)S(1)}, pred[8,32]{1,0:T(8,128)(4,1)}, u32[]{:S(2)}) copy-start(pred[8,32]{1,0:T(8,128)(4,1)} %copy-done.17) | copy-start | bytes 772
  160.2 18.5 %copy-start.21 = (pred[8]{0:T(512)(128)(4,1)S(1)}, pred[8]{0:T(512)(128)(4,1)}, u32[]{:S(2)}) copy-start(pred[8]{0:T(512)(128)(4,1)} %copy-done.20) | copy-start | bytes 28
  160.2 12.2 %collective-permute-start.8 = (bf16[2,4,8,2048]{3,2,1,0:T(8,128)(2,1)S(1)}, bf16[2,4,8,2048]{3,2,1,0:T(8,128)(2,1)S(1)}, u32[]{:S(2)}, u32[]{:S(2)}) collective-permute-start(bf16[2,4,8,2048]{3,2,1,0:T(8,128)(2,1)S(1)} %multiply_convert_fusion), channel_id=1, source_target_pairs={{0,4},{1,5},{2,6},{3,7},{4,0},{5,1},{6,2},{7,3},{8,12},{9,13},{10,... | collective-permute-start | bytes 786440 | tf_op jit(solution)/shard_map/ppermute | solution.py:76
  175.2 14.0 %collective-permute-start.9 = (bf16[2,2,4,8,2048]{4,3,2,1,0:T(8,128)(2,1)S(1)}, bf16[2,2,4,8,2048]{4,3,2,1,0:T(8,128)(2,1)S(1)}, u32[]{:S(2)}, u32[]{:S(2)}) collective-permute-start(bf16[2,2,4,8,2048]{4,3,2,1,0:T(8,128)(2,1)S(1)} %broadcast_select_fusion), channel_id=1, source_target_pairs={{0,1},{1,2},{2,3},{3,0},{4,5},{5,6},{6,7},{7,4},{8,9},{9,10},{10,1... | collective-permute-start | bytes 1572872 | tf_op jit(solution)/shard_map/ppermute | solution.py:81
  177.4 12.7 %collective-permute-start.10 = (bf16[2,2,4,8,2048]{4,3,2,1,0:T(8,128)(2,1)S(1)}, bf16[2,2,4,8,2048]{4,3,2,1,0:T(8,128)(2,1)S(1)}, u32[]{:S(2)}, u32[]{:S(2)}) collective-permute-start(bf16[2,2,4,8,2048]{4,3,2,1,0:T(8,128)(2,1)S(1)} %broadcast_select_fusion), channel_id=1, source_target_pairs={{0,2},{1,3},{2,0},{3,1},{4,6},{5,7},{6,4},{7,5},{8,10},{9,11},{10,... | collective-permute-start | bytes 1572872 | tf_op jit(solution)/shard_map/ppermute | solution.py:81
  177.4 23.8 %collective-permute-start.11 = (bf16[2,2,4,8,2048]{4,3,2,1,0:T(8,128)(2,1)S(1)}, bf16[2,2,4,8,2048]{4,3,2,1,0:T(8,128)(2,1)S(1)}, u32[]{:S(2)}, u32[]{:S(2)}) collective-permute-start(bf16[2,2,4,8,2048]{4,3,2,1,0:T(8,128)(2,1)S(1)} %broadcast_select_fusion), channel_id=1, source_target_pairs={{0,3},{1,0},{2,1},{3,2},{4,7},{5,4},{6,5},{7,6},{8,11},{9,8},{10,9... | collective-permute-start | bytes 1572872 | tf_op jit(solution)/shard_map/ppermute | solution.py:81
  215.5 4.3 %copy-start.10 = (bf16[256,2048]{1,0:T(8,128)(2,1)}, bf16[256,2048]{1,0:T(8,128)(2,1)S(1)}, u32[]{:S(2)}) copy-start(bf16[256,2048]{1,0:T(8,128)(2,1)S(1)} %convolution_convert_fusion.1) | copy-start | bytes 3145732
  216.4 21.5 %collective-permute-start.12 = (bf16[1,4,2,8,2048]{4,3,2,1,0:T(8,128)(2,1)}, bf16[1,4,2,8,2048]{4,3,2,1,0:T(8,128)(2,1)}, u32[]{:S(2)}, u32[]{:S(2)}) collective-permute-start(bf16[1,4,2,8,2048]{4,3,2,1,0:T(8,128)(2,1)} %get-tuple-element.35), channel_id=1, source_target_pairs={{0,1},{1,2},{2,3},{3,0},{4,5},{5,6},{6,7},{7,4},{8,9},{9,10},{10,1... | collective-permute-start | bytes 786440 | tf_op jit(solution)/shard_map/ppermute | solution.py:58
  217.7 21.4 %collective-permute-start.13 = (bf16[1,4,2,8,2048]{4,3,2,1,0:T(8,128)(2,1)S(1)}, bf16[1,4,2,8,2048]{4,3,2,1,0:T(8,128)(2,1)}, u32[]{:S(2)}, u32[]{:S(2)}) collective-permute-start(bf16[1,4,2,8,2048]{4,3,2,1,0:T(8,128)(2,1)S(1)} %get-tuple-element.37), channel_id=1, source_target_pairs={{0,2},{1,3},{2,0},{3,1},{4,6},{5,7},{6,4},{7,5},{8,10},{9,11},{10,... | collective-permute-start | bytes 786440 | tf_op jit(solution)/shard_map/ppermute | solution.py:58
  218.1 21.0 %collective-permute-start.14 = (bf16[1,4,2,8,2048]{4,3,2,1,0:T(8,128)(2,1)S(1)}, bf16[1,4,2,8,2048]{4,3,2,1,0:T(8,128)(2,1)}, u32[]{:S(2)}, u32[]{:S(2)}) collective-permute-start(bf16[1,4,2,8,2048]{4,3,2,1,0:T(8,128)(2,1)S(1)} %get-tuple-element.36), channel_id=1, source_target_pairs={{0,3},{1,0},{2,1},{3,2},{4,7},{5,4},{6,5},{7,6},{8,11},{9,8},{10,9... | collective-permute-start | bytes 786440 | tf_op jit(solution)/shard_map/ppermute | solution.py:58
  219.8 61.3 %all-to-all-start.2 = ((bf16[32,2,32,4,128]{4,2,3,1,0:T(8,128)(2,1)}), bf16[32,2,32,4,128]{4,2,3,1,0:T(8,128)(2,1)S(1)}, u32[]{:S(2)}, u32[]{:S(2)}) async-start(bf16[32,2,32,4,128]{4,2,3,1,0:T(8,128)(2,1)} %bitcast.47), calls=%async_computation.2 | async-start | bytes 4194304 | tf_op jit(solution)/shard_map/all_to_all | solution.py:186
  235.3 31.9 %collective-permute-start.16 = (bf16[1,4,2,8,2048]{4,3,2,1,0:T(8,128)(2,1)S(1)}, bf16[1,4,2,8,2048]{4,3,2,1,0:T(8,128)(2,1)S(1)}, u32[]{:S(2)}, u32[]{:S(2)}) collective-permute-start(bf16[1,4,2,8,2048]{4,3,2,1,0:T(8,128)(2,1)S(1)} %get-tuple-element.38), channel_id=1, source_target_pairs={{0,1},{1,2},{2,3},{3,0},{4,5},{5,6},{6,7},{7,4},{8,9},{9,10},{10,1... | collective-permute-start | bytes 786440 | tf_op jit(solution)/shard_map/ppermute | solution.py:58
  236.7 31.2 %collective-permute-start.17 = (bf16[1,4,2,8,2048]{4,3,2,1,0:T(8,128)(2,1)S(1)}, bf16[1,4,2,8,2048]{4,3,2,1,0:T(8,128)(2,1)S(1)}, u32[]{:S(2)}, u32[]{:S(2)}) collective-permute-start(bf16[1,4,2,8,2048]{4,3,2,1,0:T(8,128)(2,1)S(1)} %get-tuple-element.40), channel_id=1, source_target_pairs={{0,2},{1,3},{2,0},{3,1},{4,6},{5,7},{6,4},{7,5},{8,10},{9,11},{10,... | collective-permute-start | bytes 786440 | tf_op jit(solution)/shard_map/ppermute | solution.py:58
  237.9 35.7 %collective-permute-start.18 = (bf16[1,4,2,8,2048]{4,3,2,1,0:T(8,128)(2,1)S(1)}, bf16[1,4,2,8,2048]{4,3,2,1,0:T(8,128)(2,1)S(1)}, u32[]{:S(2)}, u32[]{:S(2)}) collective-permute-start(bf16[1,4,2,8,2048]{4,3,2,1,0:T(8,128)(2,1)S(1)} %get-tuple-element.39), channel_id=1, source_target_pairs={{0,3},{1,0},{2,1},{3,2},{4,7},{5,4},{6,5},{7,6},{8,11},{9,8},{10,9... | collective-permute-start | bytes 786440 | tf_op jit(solution)/shard_map/ppermute | solution.py:58
  240.5 35.9 %collective-permute-start.15 = (bf16[1,4,8,2048]{3,2,1,0:T(8,128)(2,1)S(1)}, bf16[1,4,8,2048]{3,2,1,0:T(8,128)(2,1)S(1)}, u32[]{:S(2)}, u32[]{:S(2)}) collective-permute-start(bf16[1,4,8,2048]{3,2,1,0:T(8,128)(2,1)S(1)} %fusion.116), channel_id=1, source_target_pairs={{0,4},{1,5},{2,6},{3,7},{4,0},{5,1},{6,2},{7,3},{8,12},{9,13},{10,... | collective-permute-start | bytes 393224 | tf_op jit(solution)/shard_map/ppermute | solution.py:64
  274.7 6.3 %collective-permute-start.19 = (bf16[1,4,8,2048]{3,2,1,0:T(8,128)(2,1)S(1)}, bf16[1,4,8,2048]{3,2,1,0:T(8,128)(2,1)S(1)}, u32[]{:S(2)}, u32[]{:S(2)}) collective-permute-start(bf16[1,4,8,2048]{3,2,1,0:T(8,128)(2,1)S(1)} %fusion.117), channel_id=1, source_target_pairs={{0,4},{1,5},{2,6},{3,7},{4,0},{5,1},{6,2},{7,3},{8,12},{9,13},{10,... | collective-permute-start | bytes 393224 | tf_op jit(solution)/shard_map/ppermute | solution.py:64
  283.1 2.3 copy-start.24
  285.3 8.5 %copy-start.30 = (s32[8]{0:T(128)S(1)}, s32[8]{0:T(128)}, u32[]{:S(2)}) copy-start(s32[8]{0:T(128)} %copy-done.29) | copy-start | bytes 100
  286.2 15.6 %all-to-all-start.3 = ((bf16[2,4,8,2048]{3,2,0,1:T(8,128)(2,1)}), bf16[2,4,8,2048]{3,2,0,1:T(8,128)(2,1)S(1)}, u32[]{:S(2)}, u32[]{:S(2)}) async-start(bf16[2,4,8,2048]{3,2,0,1:T(8,128)(2,1)} %copy.88), calls=%async_computation.3 | async-start | bytes 524288 | tf_op jit(solution)/shard_map/all_to_all | solution.py:211
  293.9 11.0 %copy-start.1 = (bf16[2048,4,192]{0,2,1:T(8,128)(2,1)S(1)}, bf16[2048,4,192]{0,2,1:T(8,128)(2,1)}, u32[]{:S(2)}) copy-start(bf16[2048,4,192]{0,2,1:T(8,128)(2,1)} %param.24) | copy-start | bytes 9437188
  (8 other events, 13.5 us)
Sparse Core Ops, SparseCore 0:
  26.6 82.4 all-gather.1
